TPU v7x, 256 devices: a whole 4x4x8 slice. The times are simulated.
256 devices in a mesh: req: 32 (over x_hi, z, core), mlp: 8 (over x_lo, y).
Axes of the slice: x: 4 (x_hi: 2, x_lo: 2; x = x_hi * 2 + x_lo), y: 4, z: 8, core: 2. Of those that a mesh axis runs over, the one named last changes fastest.
Arguments:
- tokens: bfloat16 [768, 1536], P('req')
- lengths: int32 [768], replicated, may hold values from 1 to 16384, as said below
- leaving: int32 [32, 13], replicated, may hold values from 0 to 23, as said below
- owner: int32 [32, 13], replicated, may hold values from 0 to 31, as said below
- cache: bfloat16 [768, 1024, 256], P('req', 'mlp'), as said below
- conv_state: bfloat16 [768, 3, 2048], P('req', None, 'mlp'), may hold values from -6 to 6
- lru_state: bfloat16 [768, 2048], P('req', 'mlp'), may hold values from -6 to 6
- gain_rec: float32 [1536], replicated, may hold values from 0.25 to 1.75
- w_input: bfloat16 [1536, 2048], P(None, 'mlp'), may hold values from -0.15625 to 0.15625
- w_branch: bfloat16 [1536, 2048], P(None, 'mlp'), may hold values from -0.15625 to 0.15625
- conv_weight: float32 [4, 2048], P(None, 'mlp'), may hold values from -3 to 3
- conv_bias: float32 [2048], P('mlp'), may hold values from -3 to 3
- gate_weight: bfloat16 [2, 16, 128, 128], P(None, 'mlp'), may hold values from -0.5 to 0.5
- gate_bias: float32 [2, 2048], P(None, 'mlp'), may hold values from -4 to 4
- decay_param: float32 [2048], P('mlp'), may hold values from 1 to 6
- w_rec_out: bfloat16 [2048, 1536], P('mlp'), may hold values from -0.125 to 0.125
- gain_att: float32 [1536], replicated, may hold values from 0.25 to 1.75
- w_query: bfloat16 [1536, 1536], P('mlp'), may hold values from -0.15625 to 0.15625
- w_keyval: bfloat16 [1536, 256], replicated, may hold values from -0.15625 to 0.15625
- w_attn_out: bfloat16 [1536, 1536], P('mlp'), may hold values from -0.25 to 0.25
- gain_mlp: float32 [1536], replicated, may hold values from 0.25 to 1.75
- w_gate: bfloat16 [1536, 4608], P(None, 'mlp'), may hold values from -0.15625 to 0.15625
- w_up: bfloat16 [1536, 4608], P(None, 'mlp'), may hold values from -0.15625 to 0.15625
- w_down: bfloat16 [4608, 1536], P('mlp'), may hold values from -0.09375 to 0.09375
Outputs:
- hidden_out: bfloat16 [768, 1536], P('req', 'mlp')
- cache_out: bfloat16 [768, 1024, 256], P('req', 'mlp')
- conv_out: bfloat16 [768, 3, 2048], P('req', None, 'mlp')
- lru_out: bfloat16 [768, 2048], P('req', 'mlp')
Inputs may be any that keep to these rules, and one draw needn't show every extreme that they name: lengths[0] is 16384 and lengths[1] is 1. `leaving`: row d holds 13 different slot numbers within req index d. `owner`: each row holds 13 different req indices, none equal to the row's own index, and each column holds every req index once. `cache`: keys are stored already rotated for the positions they hold.
All inputs are finite; a program needn't handle non-finite values.
Results may differ from a plain program's by a relative error of at most 0.03.
Values may be sent and summed in bfloat16 or wider, within the bound.
No kernel may reach another device: no remote copies, remote signals or barrier semaphores. Data moves between devices by JAX's collectives and lax.ppermute only.
A program may use at most 128 MiB of HBM per device.

v0:
```python
import math

import jax
import jax.numpy as jnp
from jax import lax
from jax.sharding import PartitionSpec as P

epsilon = 1e-06


def joined(value, axis, join):
    pieces = jax.tree.map(lambda part: lax.all_gather(part, axis), value)
    head = jax.tree.map(lambda part: part[0], pieces)
    tail = jax.tree.map(lambda part: part[1:], pieces)
    so_far, _ = lax.scan(lambda so_far, piece: (join(so_far, piece), None), head, tail)
    return so_far


def rms_norm(values, gain_vec):
    mean_square = jnp.mean(values * values, axis=-1, keepdims=True)
    return (values * lax.rsqrt(mean_square + epsilon) * gain_vec).astype(jnp.bfloat16)


def rotate(vectors, positions):
    half_size = vectors.shape[-1] // 2
    frequency = 10000.0 ** (-2.0 * jnp.arange(half_size, dtype=jnp.float32) / vectors.shape[-1])
    angles = positions[:, None] * frequency[None, :]
    cos_part = jnp.cos(angles)[:, None, :]
    sin_part = jnp.sin(angles)[:, None, :]
    first_half = vectors[..., :half_size]
    second = vectors[..., half_size:]
    return jnp.concatenate(
        [first_half * cos_part - second * sin_part, second * cos_part + first_half * sin_part],
        axis=-1,
    )


def combine_parts(first_part, second_part):
    first_top, first_sum, first_acc = first_part
    second_top, second_sum, second_acc = second_part
    larger = jnp.maximum(first_top, second_top)
    first_factor = jnp.exp(first_top - larger)
    second_factor = jnp.exp(second_top - larger)
    return (
        larger,
        first_sum * first_factor + second_sum * second_factor,
        first_acc * first_factor[..., None] + second_acc * second_factor[..., None],
    )


def across_mlp(partial_value):
    return lax.psum(partial_value, "mlp")


def per_device(
    tokens,
    lengths,
    leaving,
    owner,
    cache,
    conv_state,
    lru_state,
    gain_rec,
    w_input,
    w_branch,
    conv_weight,
    conv_bias,
    gate_weight,
    gate_bias,
    decay_param,
    w_rec_out,
    gain_att,
    w_query,
    w_keyval,
    w_attn_out,
    gain_mlp,
    w_gate,
    w_up,
    w_down,
):
    req_rows = tokens.shape[0]
    width = tokens.shape[1]
    leavers = leaving.shape[1]
    groups = lax.axis_size("req")
    own_group = lax.axis_index("req")
    mlp_id = lax.axis_index("mlp")
    rank_ids = jnp.arange(leavers, dtype=jnp.int32)
    group_ids = jnp.arange(groups, dtype=jnp.int32)
    my_leave = leaving[own_group]
    anchor = jnp.sum(jnp.where(owner == own_group, group_ids[:, None], 0), axis=0)
    leave_cache = jnp.take(cache, my_leave, axis=0)
    leave_conv = jnp.take(conv_state, my_leave, axis=0)
    leave_lru = jnp.take(lru_state, my_leave, axis=0)
    got_cache, got_conv, got_lru = (
        lax.all_gather(leave_cache, "req", axis=0, tiled=True),
        lax.all_gather(leave_conv, "req", axis=0, tiled=True),
        lax.all_gather(leave_lru, "req", axis=0, tiled=True),
    )
    pick_rows = anchor * leavers + rank_ids
    arrive_cache = jnp.take(got_cache, pick_rows, axis=0)
    arrive_conv = jnp.take(got_conv, pick_rows, axis=0)
    arrive_lru = jnp.take(got_lru, pick_rows, axis=0)
    local_ids = jnp.arange(req_rows, dtype=jnp.int32)
    match_slot = my_leave[None, :] == local_ids[:, None]
    arrive_rank = jnp.sum(jnp.where(match_slot, rank_ids[None, :], 0), axis=1)
    arriving = jnp.any(match_slot, axis=1)
    pick_local = jnp.where(arriving, req_rows + arrive_rank, local_ids)
    moved_cache = jnp.take(jnp.concatenate([cache, arrive_cache], axis=0), pick_local, axis=0)
    moved_conv = jnp.take(jnp.concatenate([conv_state, arrive_conv], axis=0), pick_local, axis=0)
    moved_lru = jnp.take(jnp.concatenate([lru_state, arrive_lru], axis=0), pick_local, axis=0)
    arrive_anchor = anchor[arrive_rank]
    anchor_slot = arrive_anchor * req_rows + leaving[arrive_anchor, arrive_rank]
    source_slot = jnp.where(arriving, anchor_slot, own_group * req_rows + local_ids)
    position = lengths[source_slot]
    inputs = tokens.astype(jnp.float32)
    normed = rms_norm(inputs, gain_rec)
    branch_in = jnp.dot(normed, w_input, preferred_element_type=jnp.float32).astype(jnp.bfloat16)
    branch = jax.nn.gelu(
        jnp.dot(normed, w_branch, preferred_element_type=jnp.float32), approximate=True
    )
    history = moved_conv.astype(jnp.float32)
    conv_in = (
        jnp.sum(conv_weight[:-1][None] * history, axis=1)
        + conv_weight[-1] * branch_in.astype(jnp.float32)
        + conv_bias
    )
    channels = conv_in.shape[1]
    block_size = gate_weight.shape[2]
    blocks = channels // block_size
    gate_pre = (
        jnp.einsum(
            "snb,gnbc->gsnc",
            conv_in.reshape(req_rows, blocks, block_size),
            gate_weight.astype(jnp.float32),
        ).reshape(2, req_rows, channels)
        + gate_bias[:, None, :]
    )
    rate_gate = jax.nn.sigmoid(gate_pre[0])
    admit_gate = jax.nn.sigmoid(gate_pre[1])
    log_decay = -8.0 * rate_gate * jax.nn.softplus(-decay_param)
    new_state = (
        jnp.exp(log_decay) * moved_lru.astype(jnp.float32)
        + jnp.sqrt(-jnp.expm1(2.0 * log_decay)) * admit_gate * conv_in
    )
    lru_out = new_state.astype(jnp.bfloat16)
    conv_out = jnp.concatenate([moved_conv[:, 1:], branch_in[:, None, :]], axis=1)
    gated_rec = (new_state * branch).astype(jnp.bfloat16)
    resid_one = inputs + across_mlp(
        jnp.dot(gated_rec, w_rec_out, preferred_element_type=jnp.float32)
    )
    head_size = w_keyval.shape[1] // 2
    heads = width // head_size
    slice_rows = w_query.shape[0]
    normed_att = rms_norm(resid_one, gain_att)
    query_part = jnp.dot(
        lax.dynamic_slice_in_dim(normed_att, mlp_id * slice_rows, slice_rows, 1),
        w_query,
        preferred_element_type=jnp.float32,
    )
    query_full = across_mlp(query_part)
    where_pos = position.astype(jnp.float32)
    queries = rotate(query_full.reshape(req_rows, heads, head_size), where_pos).astype(jnp.bfloat16)
    key_value = jnp.dot(normed_att, w_keyval, preferred_element_type=jnp.float32)
    key_new = rotate(key_value[:, None, :head_size], where_pos)[:, 0].astype(jnp.bfloat16)
    value_new = key_value[:, head_size:].astype(jnp.bfloat16)
    page_rows = moved_cache.shape[1]
    window = page_rows * lax.axis_size("mlp")
    score_scale = 1.0 / math.sqrt(head_size)
    scores = (
        jnp.einsum(
            "shd,swd->shw",
            queries,
            moved_cache[..., :head_size],
            preferred_element_type=jnp.float32,
        )
        * score_scale
    )
    slot_ids = mlp_id * page_rows + jnp.arange(page_rows, dtype=jnp.int32)[None, :]
    current = position[:, None]
    held_pos = current - 1 - jnp.mod(current - 1 - slot_ids, window)
    usable = ((held_pos >= 0) & (held_pos != current - window))[:, None, :]
    local_top = jnp.max(jnp.where(usable, scores, -1e30), axis=-1)
    weights = jnp.where(usable, jnp.exp(scores - local_top[..., None]), 0.0)
    local_sum = jnp.sum(weights, axis=-1)
    local_acc = jnp.einsum(
        "shw,swd->shd",
        weights.astype(jnp.bfloat16),
        moved_cache[..., head_size:],
        preferred_element_type=jnp.float32,
    )
    merged_top, merged_sum, merged_acc = joined(
        (local_top, local_sum, local_acc), "mlp", combine_parts
    )
    own_score = (
        jnp.sum(queries.astype(jnp.float32) * key_new.astype(jnp.float32)[:, None, :], axis=-1)
        * score_scale
    )
    top_score = jnp.maximum(merged_top, own_score)
    rescale = jnp.exp(merged_top - top_score)
    own_weight = jnp.exp(own_score - top_score)
    own_rounded = lax.optimization_barrier(own_weight.astype(jnp.bfloat16)).astype(jnp.float32)
    denominator = merged_sum * rescale + own_weight
    numerator = (
        merged_acc * rescale[..., None]
        + own_rounded[..., None] * value_new.astype(jnp.float32)[:, None, :]
    )
    attended = (numerator / denominator[..., None]).reshape(req_rows, width).astype(jnp.bfloat16)
    attn_part = jnp.dot(
        lax.dynamic_slice_in_dim(attended, mlp_id * slice_rows, slice_rows, 1),
        w_attn_out,
        preferred_element_type=jnp.float32,
    )
    resid_two = resid_one + across_mlp(attn_part)
    normed_mlp = rms_norm(resid_two, gain_mlp)
    gate_act = jax.nn.gelu(
        jnp.dot(normed_mlp, w_gate, preferred_element_type=jnp.float32), approximate=True
    )
    hidden = (gate_act * jnp.dot(normed_mlp, w_up, preferred_element_type=jnp.float32)).astype(
        jnp.bfloat16
    )
    down_part = jnp.dot(hidden, w_down, preferred_element_type=jnp.float32)
    share = lax.psum_scatter(down_part, "mlp", scatter_dimension=1, tiled=True)
    share_cols = share.shape[1]
    hidden_out = (
        lax.dynamic_slice_in_dim(resid_two, mlp_id * share_cols, share_cols, 1) + share
    ).astype(jnp.bfloat16)
    write_row = jnp.concatenate([key_new, value_new], axis=-1)
    row_hit = slot_ids == jnp.mod(current, window)
    cache_out = jnp.where(row_hit[:, :, None], write_row[:, None, :], moved_cache)
    return (hidden_out, cache_out, conv_out, lru_out)


def solution(mesh):
    placed = (
        P("req", None),
        P(),
        P(),
        P(),
        P("req", "mlp", None),
        P("req", None, "mlp"),
        P("req", "mlp"),
        P(),
        P(None, "mlp"),
        P(None, "mlp"),
        P(None, "mlp"),
        P("mlp"),
        P(None, "mlp", None, None),
        P(None, "mlp"),
        P("mlp"),
        P("mlp", None),
        P(),
        P("mlp", None),
        P(),
        P("mlp", None),
        P(),
        P(None, "mlp"),
        P(None, "mlp"),
        P("mlp", None),
    )
    return jax.shard_map(
        per_device,
        mesh=mesh,
        in_specs=placed,
        out_specs=(P("req", "mlp"), P("req", "mlp", None), P("req", None, "mlp"), P("req", "mlp")),
        check_vma=False,
    )
```

profile of v0, /device:TPU:32, one launch (start us, length us, event | category | flops | bytes accessed | tf_op | source)
XLA Modules:
  0.0 605.6 jit_solution(1500225180897330372)
XLA Ops:
  14.7 42.5 %all_gather.27 = bf16[416,3,256]{2,1,0:T(4,128)(2,1)S(1)} all-gather(bf16[13,3,256]{2,1,0:T(4,128)(2,1)S(1)} %copy.92), channel_id=1, replica_groups=mesh['req'=32,'mlp'=8] {'req'}, dimensions={0}, use_global_device_ids=true | all-gather | bytes 658944 | tf_op jit(solution)/shard_map/all_gather | solution.py:96
  61.7 44.3 %all-gather.3 = bf16[32,13,256]{2,1,0:T(8,128)(2,1)} all-gather(bf16[1,13,256]{2,1,0:T(8,128)(2,1)S(1)} %select_bitcast_fusion), channel_id=1, replica_groups=mesh['req'=32,'mlp'=8] {'req'}, dimensions={0}, use_global_device_ids=true | all-gather | bytes 219648 | tf_op jit(solution)/shard_map/all_gather | solution.py:97
  106.0 1.7 reshape.577
  107.8 1.5 gather_fusion.4
  113.1 2.7 fusion.59
  117.4 70.8 %all-reduce.4.cloned.1.call-done = f32[24,1536]{1,0:T(8,128)} async-done(((f32[24,1536]{1,0:T(8,128)}), f32[24,1536]{1,0:T(8,128)}) %all-reduce.4.cloned.1.call-update) | async-done | bytes 147472 | tf_op jit(solution)/shard_map/psum | solution.py:52
  190.3 2.0 fusion.73
  192.3 1.6 reshape.469
  194.0 2.2 broadcast_select_fusion.2
  200.6 149.9 %all-reduce.6.cloned.1.call-done = f32[24,12,128]{2,1,0:T(8,128)} async-done(((f32[24,12,128]{2,1,0:T(8,128)}), f32[24,12,128]{2,1,0:T(8,128)}) %all-reduce.6.cloned.1.call-update) | async-done | bytes 147472 | tf_op jit(solution)/shard_map/psum | solution.py:52
  350.5 1.8 subtract_convert_fusion
  352.3 36.1 %all-gather.9.cloned.1.call-done = bf16[416,128,256]{2,1,0:T(8,128)(2,1)} async-done(((bf16[13,128,256]{2,1,0:T(8,128)(2,1)}), bf16[416,128,256]{2,1,0:T(8,128)(2,1)}) %all-gather.9.cloned.1.call-update) | async-done | bytes 27262992 | tf_op jit(solution)/shard_map/all_gather | solution.py:95
  388.4 10.3 %gather_fusion.10 = bf16[13,128,256]{2,1,0:T(8,128)(2,1)} fusion(bf16[416,128,256]{2,1,0:T(8,128)(2,1)} %all-gather.9.cloned.1.call-done, s32[1024]{0:T(1024)S(1)} %pad_clamp_fusion.3), kind=kCustom, calls=%fused_computation.10 | custom fusion | bytes 1703988 | tf_op jit(solution)/shard_map/jit(_take)/gather | solution.py:100
  400.0 1.7 pad_maximum_fusion
  401.7 2.5 gather_fusion.11
  404.1 2.2 broadcast_select_fusion.1
  408.9 28.2 %all-gather.5 = f32[8,24,12]{1,2,0:T(8,128)S(1)} all-gather(f32[1,24,12]{1,2,0:T(8,128)S(1)} %copy.100), channel_id=3, replica_groups=mesh['req'=32,'mlp'=8] {'mlp'}, dimensions={0}, use_global_device_ids=true | all-gather | bytes 10368 | tf_op jit(solution)/shard_map/all_gather | solution.py:12
  437.2 28.1 %all-gather.4 = f32[8,24,12]{1,2,0:T(8,128)S(1)} all-gather(f32[1,24,12]{1,2,0:T(8,128)S(1)} %copy.99), channel_id=2, replica_groups=mesh['req'=32,'mlp'=8] {'mlp'}, dimensions={0}, use_global_device_ids=true | all-gather | bytes 10368 | tf_op jit(solution)/shard_map/all_gather | solution.py:12
  466.6 3.1 while.14
  470.3 2.0 fusion.71
  472.3 75.0 %all-reduce.8.cloned.1.call-done = f32[24,1536]{1,0:T(8,128)} async-done(((f32[24,1536]{1,0:T(8,128)}), f32[24,1536]{1,0:T(8,128)}) %all-reduce.8.cloned.1.call-update) | async-done | bytes 147472 | tf_op jit(solution)/shard_map/psum | solution.py:52
  549.1 2.7 fusion.106
  551.8 3.0 convolution_bitcast_fusion
  556.4 39.6 %reduce-scatter.4.cloned.1.call-done = f32[192,24]{1,0:T(8,128)} async-done(((f32[1536,24]{1,0:T(8,128)}), f32[192,24]{1,0:T(8,128)}) %reduce-scatter.4.cloned.1.call-update) | async-done | bytes 18448
  (178 shorter events, 37.1 us)
Async XLA Ops:
  8.0 543.8 %copy-start = (bf16[576,1536]{1,0:T(8,128)(2,1)S(1)}, bf16[576,1536]{1,0:T(8,128)(2,1)}, u32[]{:S(2)}) copy-start(bf16[576,1536]{1,0:T(8,128)(2,1)} %param.49) | copy-start | bytes 5308420
  8.0 49.9 %copy-start.3 = (bf16[24,1536]{1,0:T(8,128)(2,1)S(1)}, bf16[24,1536]{1,0:T(8,128)(2,1)}, u32[]{:S(2)}) copy-start(bf16[24,1536]{1,0:T(8,128)(2,1)} %param.26) | copy-start | bytes 221188
  8.0 50.0 %copy-start.14 = (f32[4,256]{1,0:T(4,128)S(1)}, f32[4,256]{1,0:T(4,128)}, u32[]{:S(2)}) copy-start(f32[4,256]{1,0:T(4,128)} %param.36) | copy-start | bytes 12292
  8.0 51.5 %copy-start.11 = (f32[1536]{0:T(1024)S(1)}, f32[1536]{0:T(1024)}, u32[]{:S(2)}) copy-start(f32[1536]{0:T(1024)} %param.33) | copy-start | bytes 18436
  8.0 51.5 %copy-start.19 = (f32[256]{0:T(256)S(1)}, f32[256]{0:T(256)}, u32[]{:S(2)}) copy-start(f32[256]{0:T(256)} %param.37) | copy-start | bytes 3076
  8.1 180.2 %all-reduce.4.cloned.1.call-start = ((), (), s32[]{:S(2)}) async-start(), calls=%async_computation.1 | async-start | bytes 294912 | tf_op jit(solution)/shard_map/psum | solution.py:52
  10.1 99.1 %copy-start.15 = (pred[13]{0:T(512)(128)(4,1)}, pred[13]{0:T(512)(128)(4,1)S(1)}, u32[]{:S(2)}) copy-start(pred[13]{0:T(512)(128)(4,1)S(1)} %compare_and_fusion.2) | copy-start | bytes 43
  10.9 50.2 %copy-start.9 = (bf16[24,256]{1,0:T(8,128)(2,1)S(1)}, bf16[24,256]{1,0:T(8,128)(2,1)}, u32[]{:S(2)}) copy-start(bf16[24,256]{1,0:T(8,128)(2,1)} %param.32) | copy-start | bytes 36868
  57.9 57.9 %copy-start.16 = (pred[24]{0:T(512)(128)(4,1)}, pred[24]{0:T(512)(128)(4,1)S(1)}, u32[]{:S(2)}) copy-start(pred[24]{0:T(512)(128)(4,1)S(1)} %compare_and_fusion.3) | copy-start | bytes 76
  58.1 2.9 copy-start.18
  58.1 57.7 %copy-start.13 = (s32[1024]{0:T(1024)}, s32[1024]{0:T(1024)S(1)}, u32[]{:S(2)}) copy-start(s32[1024]{0:T(1024)S(1)} %get-tuple-element.133) | copy-start | bytes 12292
  61.0 54.9 %copy-start.2 = (bf16[24,128,256]{2,1,0:T(8,128)(2,1)S(1)}, bf16[24,128,256]{2,1,0:T(8,128)(2,1)}, u32[]{:S(2)}) copy-start(bf16[24,128,256]{2,1,0:T(8,128)(2,1)} %param.30) | copy-start | bytes 4718596
  113.1 76.2 %copy-start.12 = (f32[1536]{0:T(1024)S(1)}, f32[1536]{0:T(1024)}, u32[]{:S(2)}) copy-start(f32[1536]{0:T(1024)} %param.42) | copy-start | bytes 18436
  115.9 234.7 %all-reduce.6.cloned.1.call-start = ((), (), s32[]{:S(2)}) async-start(), calls=%async_computation.2 | async-start | bytes 393216 | tf_op jit(solution)/shard_map/psum | solution.py:52
  190.3 6.0 copy-start.1
  193.9 194.5 %all-gather.9.cloned.1.call-start = ((), (), s32[]{:S(2)}) async-start(), calls=%async_computation.3 | async-start | bytes 28114944 | tf_op jit(solution)/shard_map/all_gather | solution.py:95
  196.2 269.1 %all-gather.11.cloned.1.call-start = ((), (), s32[]{:S(2)}) async-start(), calls=%async_computation.5 | async-start | bytes 1327104 | tf_op jit(solution)/shard_map/all_gather | solution.py:12
  401.7 2.5 copy-start.17
  404.1 2.3 copy-start.7
  408.2 139.2 %all-reduce.8.cloned.1.call-start = ((), (), s32[]{:S(2)}) async-start(), calls=%async_computation.4 | async-start | bytes 294912 | tf_op jit(solution)/shard_map/psum | solution.py:52
  466.6 3.4 copy-start.10
  466.6 80.7 %copy-start.6 = (f32[24,1536]{1,0:T(8,128)S(1)}, f32[24,1536]{1,0:T(8,128)}, u32[]{:S(2)}) copy-start(f32[24,1536]{1,0:T(8,128)} %all-reduce.4.cloned.1.call-done) | copy-start | bytes 442372
  472.3 123.8 %reduce-scatter.4.cloned.1.call-start = ((), (), s32[]{:S(2)}) async-start(), calls=%async_computation.6 | async-start | bytes 884736
  548.4 3.4 copy-start.4
  (3 other events, 3.9 us)
Sparse Core Ops, SparseCore 0:
  116.0 72.2 all-reduce.3
  194.1 156.4 all-reduce.5
  408.3 40.2 all-gather.10
  472.4 74.9 all-reduce.7
  555.0 41.0 reduce-scatter.3
Sparse Core Ops, SparseCore 1:
  197.8 190.6 all-gather.8
where the time goes:
time: 607 us; the launch traced here: 606 us
  waiting for transfers between devices  372 us (61%)
  blocking collectives  143 us (24%)
  local copies, waits for them, and re-layouts  34.5 us (6%)
  other arithmetic  22.9 us (4%)
  matrix products  17.3 us (3%)
  between operations  15.7 us (3%)
    psum x3, waiting for transfers between devices, across_mlp(): return lax.psum(partial_value, 'mlp')  296 us
    all_gather x2, blocking collectives, joined(): pieces = jax.tree.map(lambda part: lax.all_gather(part, axis), value)  56.3 us
    all_gather x1, blocking collectives, per_device(): lax.all_gather(leave_lru, 'req', axis=0, tiled=True)  44.3 us
    all_gather x1, blocking collectives, per_device(): lax.all_gather(leave_conv, 'req', axis=0, tiled=True)  42.5 us
    unnamed x7, waiting for transfers between devices  39.7 us
    all_gather x1, waiting for transfers between devices, per_device(): lax.all_gather(leave_cache, 'req', axis=0, tiled=True)  36.1 us
  transfers between devices with their start and end apart: 6, of which 5 were waited for; matrix products, arithmetic and copies ran while one was open for 2% of the time, Pallas kernels for 0%

commit v1 on v0

--- a/solution.py
+++ b/solution.py
@@ -8,12 +8,42 @@
 epsilon = 1e-06
 
 
+def partner_swap(value, axis, bit):
+    size = lax.axis_size(axis)
+    pairs = [(j, j ^ bit) for j in range(size)]
+    return jax.tree.map(lambda part: lax.ppermute(part, axis, pairs), value)
+
+
+def axis_bits(axis):
+    size = lax.axis_size(axis)
+    assert size & (size - 1) == 0
+    bits = []
+    bit = 1
+    while bit < size:
+        bits.append(bit)
+        bit *= 2
+    return bits
+
+
 def joined(value, axis, join):
-    pieces = jax.tree.map(lambda part: lax.all_gather(part, axis), value)
-    head = jax.tree.map(lambda part: part[0], pieces)
-    tail = jax.tree.map(lambda part: part[1:], pieces)
-    so_far, _ = lax.scan(lambda so_far, piece: (join(so_far, piece), None), head, tail)
-    return so_far
+    for bit in axis_bits(axis):
+        value = join(value, partner_swap(value, axis, bit))
+    return value
+
+
+def scatter_sum(value, axis):
+    size = lax.axis_size(axis)
+    rows, cols = value.shape
+    me = lax.axis_index(axis)
+    held = value.reshape(rows, size, cols // size)
+    for bit in reversed(axis_bits(axis)):
+        half = held.shape[1] // 2
+        lower, upper = held[:, :half], held[:, half:]
+        mine_upper = (me & bit) != 0
+        keep = jnp.where(mine_upper, upper, lower)
+        send = jnp.where(mine_upper, lower, upper)
+        held = keep + partner_swap(send, axis, bit)
+    return held.reshape(rows, cols // size)
 
 
 def rms_norm(values, gain_vec):
@@ -49,7 +79,7 @@
 
 
 def across_mlp(partial_value):
-    return lax.psum(partial_value, "mlp")
+    return joined(partial_value, "mlp", lambda first, second: first + second)
 
 
 def per_device(
@@ -88,26 +118,22 @@
     group_ids = jnp.arange(groups, dtype=jnp.int32)
     my_leave = leaving[own_group]
     anchor = jnp.sum(jnp.where(owner == own_group, group_ids[:, None], 0), axis=0)
-    leave_cache = jnp.take(cache, my_leave, axis=0)
-    leave_conv = jnp.take(conv_state, my_leave, axis=0)
-    leave_lru = jnp.take(lru_state, my_leave, axis=0)
-    got_cache, got_conv, got_lru = (
-        lax.all_gather(leave_cache, "req", axis=0, tiled=True),
-        lax.all_gather(leave_conv, "req", axis=0, tiled=True),
-        lax.all_gather(leave_lru, "req", axis=0, tiled=True),
-    )
-    pick_rows = anchor * leavers + rank_ids
-    arrive_cache = jnp.take(got_cache, pick_rows, axis=0)
-    arrive_conv = jnp.take(got_conv, pick_rows, axis=0)
-    arrive_lru = jnp.take(got_lru, pick_rows, axis=0)
+    page_rows = cache.shape[1]
+    conv_rows = conv_state.shape[1]
+    combined = jnp.concatenate([cache, conv_state, lru_state[:, None, :]], axis=1)
+    to_group = owner[own_group][None, :] == group_ids[:, None]
+    send_slot = jnp.sum(jnp.where(to_group, my_leave[None, :], 0), axis=1)
+    send = jnp.take(combined, send_slot, axis=0)
+    got = lax.all_to_all(send, "req", 0, 0, tiled=True)
     local_ids = jnp.arange(req_rows, dtype=jnp.int32)
     match_slot = my_leave[None, :] == local_ids[:, None]
     arrive_rank = jnp.sum(jnp.where(match_slot, rank_ids[None, :], 0), axis=1)
     arriving = jnp.any(match_slot, axis=1)
-    pick_local = jnp.where(arriving, req_rows + arrive_rank, local_ids)
-    moved_cache = jnp.take(jnp.concatenate([cache, arrive_cache], axis=0), pick_local, axis=0)
-    moved_conv = jnp.take(jnp.concatenate([conv_state, arrive_conv], axis=0), pick_local, axis=0)
-    moved_lru = jnp.take(jnp.concatenate([lru_state, arrive_lru], axis=0), pick_local, axis=0)
+    arrived = jnp.take(got, anchor[arrive_rank], axis=0)
+    moved = jnp.where(arriving[:, None, None], arrived, combined)
+    moved_cache = moved[:, :page_rows]
+    moved_conv = moved[:, page_rows : page_rows + conv_rows]
+    moved_lru = moved[:, page_rows + conv_rows]
     arrive_anchor = anchor[arrive_rank]
     anchor_slot = arrive_anchor * req_rows + leaving[arrive_anchor, arrive_rank]
     source_slot = jnp.where(arriving, anchor_slot, own_group * req_rows + local_ids)
@@ -163,7 +189,6 @@
     key_value = jnp.dot(normed_att, w_keyval, preferred_element_type=jnp.float32)
     key_new = rotate(key_value[:, None, :head_size], where_pos)[:, 0].astype(jnp.bfloat16)
     value_new = key_value[:, head_size:].astype(jnp.bfloat16)
-    page_rows = moved_cache.shape[1]
     window = page_rows * lax.axis_size("mlp")
     score_scale = 1.0 / math.sqrt(head_size)
     scores = (
@@ -219,7 +244,7 @@
         jnp.bfloat16
     )
     down_part = jnp.dot(hidden, w_down, preferred_element_type=jnp.float32)
-    share = lax.psum_scatter(down_part, "mlp", scatter_dimension=1, tiled=True)
+    share = scatter_sum(down_part, "mlp")
     share_cols = share.shape[1]
     hidden_out = (
         lax.dynamic_slice_in_dim(resid_two, mlp_id * share_cols, share_cols, 1) + share

time: 607 us -> 206 us (0.34)
  waiting for transfers between devices: 372 us -> 96.6 us
  blocking collectives: 143 us -> 0 us
  starting transfers between devices: 0.25 us -> 50.9 us
  between operations: 15.7 us -> 1.13 us
  local copies, waits for them, and re-layouts: 34.5 us -> 22.4 us
    psum x3 -> x0, waiting for transfers between devices: 296 us -> none  [across_mlp(): return lax.psum(partial_value, 'mlp')]
    all_gather x4 -> x0, blocking collectives: 143 us -> none  [the longest x2 56.3 us: joined(): pieces = jax.tree.map(lambda part: lax.all_gather(part, axis), value)]
    all_to_all x0 -> x1, waiting for transfers between devices: none -> 52 us  [per_device(): got = lax.all_to_all(send, 'req', 0, 0, tiled=True)]
    ppermute x0 -> x21, waiting for transfers between devices: none -> 44.6 us  [partner_swap(): return jax.tree.map(lambda part: lax.ppermute(part, axis, pairs), value)]
    unnamed x7 -> x0, waiting for transfers between devices: 39.7 us -> none
    ppermute x0 -> x21, starting transfers between devices: none -> 39.5 us  [partner_swap(): return jax.tree.map(lambda part: lax.ppermute(part, axis, pairs), value)]
    all_gather x2 -> x0, waiting for transfers between devices: 36.1 us -> none  [the longest x1 36.1 us: per_device(): lax.all_gather(leave_cache, 'req', axis=0, tiled=True)]
    gather x10 -> x3, local copies, waits for them, and re-layouts: 20.3 us -> 7.73 us  [the longest x2 4.23 us: per_device(): arrived = jnp.take(got, anchor[arrive_rank], axis=0)]
  transfers between devices with their start and end apart: 6 -> 22, of which waited for: 5 -> 17; matrix products, arithmetic and copies ran while one was open for 2% -> 7% of each run, Pallas kernels for 0% -> 0%
where the time goes in v1:
time: 206 us; the launch traced here: 205 us
  waiting for transfers between devices  96.6 us (47%)
  starting transfers between devices  50.9 us (25%)
  local copies, waits for them, and re-layouts  22.4 us (11%)
  other arithmetic  20.4 us (10%)
  matrix products  13.3 us (6%)
    all_to_all x1, waiting for transfers between devices, per_device(): got = lax.all_to_all(send, 'req', 0, 0, tiled=True)  52 us
    ppermute x21, waiting for transfers between devices, partner_swap(): return jax.tree.map(lambda part: lax.ppermute(part, axis, pairs), value)  44.6 us
    ppermute x21, starting transfers between devices, partner_swap(): return jax.tree.map(lambda part: lax.ppermute(part, axis, pairs), value)  39.5 us
    all_to_all x1, starting transfers between devices, per_device(): got = lax.all_to_all(send, 'req', 0, 0, tiled=True)  11.4 us
    unnamed x57, local copies, waits for them, and re-layouts  5.07 us
    gather x2, local copies, waits for them, and re-layouts, per_device(): arrived = jnp.take(got, anchor[arrive_rank], axis=0)  4.23 us
  transfers between devices with their start and end apart: 22, of which 17 were waited for; matrix products, arithmetic and copies ran while one was open for 7% of the time, Pallas kernels for 0%

profile of v1, /device:TPU:32, one launch (start us, length us, event | category | flops | bytes accessed | tf_op | source)
XLA Modules:
  0.0 204.7 jit_solution(17902380396634566742)
XLA Ops:
  5.9 3.5 %gather_fusion.1 = bf16[32,132,256]{2,1,0:T(8,128)(2,1)} fusion(bf16[24,132,256]{2,1,0:T(8,128)(2,1)} %copy.49, s32[1024]{0:T(1024)S(1)} %pad_clamp_fusion.2), kind=kCustom, calls=%fused_computation.1 | custom fusion | bytes 4325504 | tf_op jit(solution)/shard_map/jit(_take)/gather | solution.py:126
  9.4 3.3 %broadcast_select_fusion = bf16[32,132,256]{2,1,0:T(8,128)(2,1)} fusion(bf16[32,132,256]{2,1,0:T(8,128)(2,1)} %gather_fusion.1, pred[32]{0:T(512)(128)(4,1)S(1)} %compare_and_fusion.1), kind=kLoop, calls=%fused_computation.5 | loop fusion | flops 1081344 | bytes 4325408 | tf_op jit(solution)/shard_map/jit(_take)/select_n | solution.py:126
  12.7 11.4 %all-to-all-start = ((bf16[32,132,256]{2,1,0:T(8,128)(2,1)}), bf16[32,132,256]{2,1,0:T(8,128)(2,1)}, u32[]{:S(2)}, u32[]{:S(2)}) async-start(bf16[32,132,256]{2,1,0:T(8,128)(2,1)} %broadcast_select_fusion), calls=%async_computation | async-start | bytes 4456448 | tf_op jit(solution)/shard_map/all_to_all | solution.py:127
  27.9 52.0 %all-to-all-done = bf16[32,132,256]{2,1,0:T(8,128)(2,1)} async-done(((bf16[32,132,256]{2,1,0:T(8,128)(2,1)}), bf16[32,132,256]{2,1,0:T(8,128)(2,1)}, u32[]{:S(2)}, u32[]{:S(2)}) %all-to-all-start) | async-done | bytes 2162720 | tf_op jit(solution)/shard_map/all_to_all | solution.py:127
  79.9 3.5 %gather_fusion.2 = bf16[24,132,256]{2,1,0:T(8,128)(2,1)} fusion(bf16[32,132,256]{2,1,0:T(8,128)(2,1)} %all-to-all-done, s32[1024]{0:T(1024)S(1)} %pad_clamp_fusion.1), kind=kCustom, calls=%fused_computation.2 | custom fusion | bytes 3244128 | tf_op jit(solution)/shard_map/jit(_take)/gather | solution.py:132
  98.0 3.3 %collective-permute-start.1 = (f32[24,1536]{1,0:T(8,128)S(1)}, f32[24,1536]{1,0:T(8,128)S(1)}, u32[]{:S(2)}, u32[]{:S(2)}) collective-permute-start(f32[24,1536]{1,0:T(8,128)S(1)} %add.303), channel_id=1, source_target_pairs={{0,2},{1,3},{2,0},{3,1},{4,6},{5,7},{6,4},{7,5},{8,10},{9,11},{10,... | collective-permute-start | bytes 442376 | tf_op jit(solution)/shard_map/ppermute | solution.py:14
  102.0 2.7 %collective-permute-done.1 = f32[24,1536]{1,0:T(8,128)S(1)} collective-permute-done((f32[24,1536]{1,0:T(8,128)S(1)}, f32[24,1536]{1,0:T(8,128)S(1)}, u32[]{:S(2)}, u32[]{:S(2)}) %collective-permute-start.1) | collective-permute-done | bytes 147488 | tf_op jit(solution)/shard_map/ppermute | solution.py:14
  106.9 3.1 %collective-permute-done.2 = f32[24,1536]{1,0:T(8,128)S(1)} collective-permute-done((f32[24,1536]{1,0:T(8,128)S(1)}, f32[24,1536]{1,0:T(8,128)S(1)}, u32[]{:S(2)}, u32[]{:S(2)}) %collective-permute-start.2) | collective-permute-done | bytes 147488 | tf_op jit(solution)/shard_map/ppermute | solution.py:14
  113.7 2.8 %collective-permute-done.3 = f32[24,1536]{1,0:T(8,128)S(1)} collective-permute-done((f32[24,1536]{1,0:T(8,128)S(1)}, f32[24,1536]{1,0:T(8,128)S(1)}, u32[]{:S(2)}, u32[]{:S(2)}) %collective-permute-start.3) | collective-permute-done | bytes 147488 | tf_op jit(solution)/shard_map/ppermute | solution.py:14
  116.5 4.7 %collective-permute-start.4 = (f32[24,1536]{1,0:T(8,128)S(1)}, f32[24,1536]{1,0:T(8,128)S(1)}, u32[]{:S(2)}, u32[]{:S(2)}) collective-permute-start(f32[24,1536]{1,0:T(8,128)S(1)} %add.316), channel_id=1, source_target_pairs={{0,2},{1,3},{2,0},{3,1},{4,6},{5,7},{6,4},{7,5},{8,10},{9,11},{10,... | collective-permute-start | bytes 442376 | tf_op jit(solution)/shard_map/ppermute | solution.py:14
  121.2 3.1 %collective-permute-done.4 = f32[24,1536]{1,0:T(8,128)S(1)} collective-permute-done((f32[24,1536]{1,0:T(8,128)S(1)}, f32[24,1536]{1,0:T(8,128)S(1)}, u32[]{:S(2)}, u32[]{:S(2)}) %collective-permute-start.4) | collective-permute-done | bytes 147488 | tf_op jit(solution)/shard_map/ppermute | solution.py:14
  125.9 3.7 %collective-permute-done.5 = f32[24,1536]{1,0:T(8,128)S(1)} collective-permute-done((f32[24,1536]{1,0:T(8,128)S(1)}, f32[24,1536]{1,0:T(8,128)S(1)}, u32[]{:S(2)}, u32[]{:S(2)}) %collective-permute-start.5) | collective-permute-done | bytes 147488 | tf_op jit(solution)/shard_map/ppermute | solution.py:14
  137.1 4.9 %collective-permute-done.12 = f32[24,12]{1,0:T(8,128)S(1)} collective-permute-done((f32[24,12]{1,0:T(8,128)S(1)}, f32[24,12]{1,0:T(8,128)S(1)}, u32[]{:S(2)}, u32[]{:S(2)}) %collective-permute-start.12) | collective-permute-done | bytes 1184 | tf_op jit(solution)/shard_map/ppermute | solution.py:14
  142.0 3.4 %collective-permute-start.13 = (f32[24,12]{1,0:T(8,128)S(1)}, f32[24,12]{1,0:T(8,128)S(1)}, u32[]{:S(2)}, u32[]{:S(2)}) collective-permute-start(f32[24,12]{1,0:T(8,128)S(1)} %get-tuple-element.30), channel_id=1, source_target_pairs={{0,2},{1,3},{2,0},{3,1},{4,6},{5,7},{6,4},{7,5},{8,10},{9,11},{10,... | collective-permute-start | bytes 3464 | tf_op jit(solution)/shard_map/ppermute | solution.py:14
  145.9 3.2 %collective-permute-start.9 = (f32[24,12,128]{2,1,0:T(8,128)S(1)}, f32[24,12,128]{2,1,0:T(8,128)S(1)}, u32[]{:S(2)}, u32[]{:S(2)}) collective-permute-start(f32[24,12,128]{2,1,0:T(8,128)S(1)} %multiply_add_fusion.1), channel_id=1, source_target_pairs={{0,2},{1,3},{2,0},{3,1},{4,6},{5,7},{6,4},{7,5},{8,10},{9,11},{10,... | collective-permute-start | bytes 442376 | tf_op jit(solution)/shard_map/ppermute | solution.py:14
  155.0 4.5 %collective-permute-done.11 = f32[24,12,128]{2,1,0:T(8,128)S(1)} collective-permute-done((f32[24,12,128]{2,1,0:T(8,128)S(1)}, f32[24,12,128]{2,1,0:T(8,128)S(1)}, u32[]{:S(2)}, u32[]{:S(2)}) %collective-permute-start.11) | collective-permute-done | bytes 147488 | tf_op jit(solution)/shard_map/ppermute | solution.py:14
  160.1 2.8 %collective-permute-start.15 = (f32[24,1536]{1,0:T(8,128)S(1)}, f32[24,1536]{1,0:T(8,128)S(1)}, u32[]{:S(2)}, u32[]{:S(2)}) collective-permute-start(f32[24,1536]{1,0:T(8,128)S(1)} %fusion.71), channel_id=1, source_target_pairs={{0,1},{1,0},{2,3},{3,2},{4,5},{5,4},{6,7},{7,6},{8,9},{9,8},{10,11... | collective-permute-start | bytes 442376 | tf_op jit(solution)/shard_map/ppermute | solution.py:14
  163.0 3.1 %collective-permute-done.15 = f32[24,1536]{1,0:T(8,128)S(1)} collective-permute-done((f32[24,1536]{1,0:T(8,128)S(1)}, f32[24,1536]{1,0:T(8,128)S(1)}, u32[]{:S(2)}, u32[]{:S(2)}) %collective-permute-start.15) | collective-permute-done | bytes 147488 | tf_op jit(solution)/shard_map/ppermute | solution.py:14
  166.1 3.6 %collective-permute-start.16 = (f32[24,1536]{1,0:T(8,128)S(1)}, f32[24,1536]{1,0:T(8,128)S(1)}, u32[]{:S(2)}, u32[]{:S(2)}) collective-permute-start(f32[24,1536]{1,0:T(8,128)S(1)} %add.329), channel_id=1, source_target_pairs={{0,2},{1,3},{2,0},{3,1},{4,6},{5,7},{6,4},{7,5},{8,10},{9,11},{10,... | collective-permute-start | bytes 442376 | tf_op jit(solution)/shard_map/ppermute | solution.py:14
  169.7 3.2 %collective-permute-done.16 = f32[24,1536]{1,0:T(8,128)S(1)} collective-permute-done((f32[24,1536]{1,0:T(8,128)S(1)}, f32[24,1536]{1,0:T(8,128)S(1)}, u32[]{:S(2)}, u32[]{:S(2)}) %collective-permute-start.16) | collective-permute-done | bytes 147488 | tf_op jit(solution)/shard_map/ppermute | solution.py:14
  174.9 3.3 %collective-permute-done.17 = f32[24,1536]{1,0:T(8,128)} collective-permute-done((f32[24,1536]{1,0:T(8,128)S(1)}, f32[24,1536]{1,0:T(8,128)}, u32[]{:S(2)}, u32[]{:S(2)}) %collective-permute-start.17) | collective-permute-done | bytes 147488 | tf_op jit(solution)/shard_map/ppermute | solution.py:14
  182.6 3.2 %fusion.2 = f32[24,1536]{1,0:T(8,128)} fusion(bf16[576,1536]{1,0:T(8,128)(2,1)S(1)} %copy-done, bf16[1536,576]{0,1:T(8,128)(2,1)} %param.46, f32[24,576]{1,0:T(8,128)} %fusion.99, f32[24,1536]{1,0:T(8,128)S(1)} %get-tuple-element.19, f32[1536]{0:T(1024)} %param.44, f32[24]{0:T(128)} %copy-done.23), kind=kOutput, calls=%fused_computation.14 | convolution fusion | flops 85183488 | bytes 3895392 | tf_op jit(solution)/shard_map/dot_general | solution.py:246
  190.1 3.2 %collective-permute-done.18 = f32[24,4,192]{2,0,1:T(8,128)S(1)} collective-permute-done((f32[24,4,192]{2,0,1:T(8,128)S(1)}, f32[24,4,192]{2,0,1:T(8,128)S(1)}, u32[]{:S(2)}, u32[]{:S(2)}) %collective-permute-start.18) | collective-permute-done | bytes 73760 | tf_op jit(solution)/shard_map/ppermute | solution.py:14
  193.4 4.6 %collective-permute-start.19 = (f32[24,2,192]{2,0,1:T(8,128)S(1)}, f32[24,2,192]{2,0,1:T(8,128)S(1)}, u32[]{:S(2)}, u32[]{:S(2)}) collective-permute-start(f32[24,2,192]{2,0,1:T(8,128)S(1)} %slice_select_fusion.1), channel_id=1, source_target_pairs={{0,2},{1,3},{2,0},{3,1},{4,6},{5,7},{6,4},{7,5},{8,10},{9,11},{10,... | collective-permute-start | bytes 110600 | tf_op jit(solution)/shard_map/ppermute | solution.py:14
  (166 shorter events, 63.5 us)
Async XLA Ops:
  0.6 182.0 %copy-start = (bf16[576,1536]{1,0:T(8,128)(2,1)S(1)}, bf16[576,1536]{1,0:T(8,128)(2,1)}, u32[]{:S(2)}) copy-start(bf16[576,1536]{1,0:T(8,128)(2,1)} %param.47) | copy-start | bytes 5308420
  12.7 67.2 %all-to-all-start = ((bf16[32,132,256]{2,1,0:T(8,128)(2,1)}), bf16[32,132,256]{2,1,0:T(8,128)(2,1)}, u32[]{:S(2)}, u32[]{:S(2)}) async-start(bf16[32,132,256]{2,1,0:T(8,128)(2,1)} %broadcast_select_fusion), calls=%async_computation | async-start | bytes 4456448 | tf_op jit(solution)/shard_map/all_to_all | solution.py:127
  91.3 5.7 %collective-permute-start = (f32[24,1536]{1,0:T(8,128)}, f32[24,1536]{1,0:T(8,128)}, u32[]{:S(2)}, u32[]{:S(2)}) collective-permute-start(f32[24,1536]{1,0:T(8,128)} %fusion.59), channel_id=1, source_target_pairs={{0,1},{1,0},{2,3},{3,2},{4,5},{5,4},{6,7},{7,6},{8,9},{9,8},{10,11... | collective-permute-start | bytes 442376 | tf_op jit(solution)/shard_map/ppermute | solution.py:14
  98.0 6.7 %collective-permute-start.1 = (f32[24,1536]{1,0:T(8,128)S(1)}, f32[24,1536]{1,0:T(8,128)S(1)}, u32[]{:S(2)}, u32[]{:S(2)}) collective-permute-start(f32[24,1536]{1,0:T(8,128)S(1)} %add.303), channel_id=1, source_target_pairs={{0,2},{1,3},{2,0},{3,1},{4,6},{5,7},{6,4},{7,5},{8,10},{9,11},{10,... | collective-permute-start | bytes 442376 | tf_op jit(solution)/shard_map/ppermute | solution.py:14
  104.8 5.2 %collective-permute-start.2 = (f32[24,1536]{1,0:T(8,128)S(1)}, f32[24,1536]{1,0:T(8,128)S(1)}, u32[]{:S(2)}, u32[]{:S(2)}) collective-permute-start(f32[24,1536]{1,0:T(8,128)S(1)} %add.304), channel_id=1, source_target_pairs={{0,4},{1,5},{2,6},{3,7},{4,0},{5,1},{6,2},{7,3},{8,12},{9,13},{10,... | collective-permute-start | bytes 442376 | tf_op jit(solution)/shard_map/ppermute | solution.py:14
  111.2 5.3 %collective-permute-start.3 = (f32[24,1536]{1,0:T(8,128)S(1)}, f32[24,1536]{1,0:T(8,128)S(1)}, u32[]{:S(2)}, u32[]{:S(2)}) collective-permute-start(f32[24,1536]{1,0:T(8,128)S(1)} %fusion.73), channel_id=1, source_target_pairs={{0,1},{1,0},{2,3},{3,2},{4,5},{5,4},{6,7},{7,6},{8,9},{9,8},{10,11... | collective-permute-start | bytes 442376 | tf_op jit(solution)/shard_map/ppermute | solution.py:14
  116.5 7.8 %collective-permute-start.4 = (f32[24,1536]{1,0:T(8,128)S(1)}, f32[24,1536]{1,0:T(8,128)S(1)}, u32[]{:S(2)}, u32[]{:S(2)}) collective-permute-start(f32[24,1536]{1,0:T(8,128)S(1)} %add.316), channel_id=1, source_target_pairs={{0,2},{1,3},{2,0},{3,1},{4,6},{5,7},{6,4},{7,5},{8,10},{9,11},{10,... | collective-permute-start | bytes 442376 | tf_op jit(solution)/shard_map/ppermute | solution.py:14
  124.4 5.2 %collective-permute-start.5 = (f32[24,1536]{1,0:T(8,128)S(1)}, f32[24,1536]{1,0:T(8,128)S(1)}, u32[]{:S(2)}, u32[]{:S(2)}) collective-permute-start(f32[24,1536]{1,0:T(8,128)S(1)} %add.317), channel_id=1, source_target_pairs={{0,4},{1,5},{2,6},{3,7},{4,0},{5,1},{6,2},{7,3},{8,12},{9,13},{10,... | collective-permute-start | bytes 442376 | tf_op jit(solution)/shard_map/ppermute | solution.py:14
  133.3 26.2 %copy-start.16 = (f32[24,128]{1,0:T(8,128)S(1)}, f32[24,128]{1,0:T(8,128)}, u32[]{:S(2)}) copy-start(f32[24,128]{1,0:T(8,128)} %get-tuple-element.20) | copy-start | bytes 36868
  133.3 8.6 %collective-permute-start.6 = (f32[24,12]{1,0:T(8,128)S(1)}, f32[24,12]{1,0:T(8,128)S(1)}, u32[]{:S(2)}, u32[]{:S(2)}) collective-permute-start(f32[24,12]{1,0:T(8,128)S(1)} %get-tuple-element.57), channel_id=1, source_target_pairs={{0,1},{1,0},{2,3},{3,2},{4,5},{5,4},{6,7},{7,6},{8,9},{9,8},{10,11... | collective-permute-start | bytes 3464 | tf_op jit(solution)/shard_map/ppermute | solution.py:14
  134.8 11.0 %collective-permute-start.7 = (f32[24,12,128]{2,1,0:T(8,128)S(1)}, f32[24,12,128]{2,1,0:T(8,128)S(1)}, u32[]{:S(2)}, u32[]{:S(2)}) collective-permute-start(f32[24,12,128]{2,1,0:T(8,128)S(1)} %fusion.3), channel_id=1, source_target_pairs={{0,1},{1,0},{2,3},{3,2},{4,5},{5,4},{6,7},{7,6},{8,9},{9,8},{10,11... | collective-permute-start | bytes 442376 | tf_op jit(solution)/shard_map/ppermute | solution.py:14
  136.1 5.8 %collective-permute-start.12 = (f32[24,12]{1,0:T(8,128)S(1)}, f32[24,12]{1,0:T(8,128)S(1)}, u32[]{:S(2)}, u32[]{:S(2)}) collective-permute-start(f32[24,12]{1,0:T(8,128)S(1)} %fusion.6), channel_id=1, source_target_pairs={{0,1},{1,0},{2,3},{3,2},{4,5},{5,4},{6,7},{7,6},{8,9},{9,8},{10,11... | collective-permute-start | bytes 3464 | tf_op jit(solution)/shard_map/ppermute | solution.py:14
  142.0 7.2 %collective-permute-start.13 = (f32[24,12]{1,0:T(8,128)S(1)}, f32[24,12]{1,0:T(8,128)S(1)}, u32[]{:S(2)}, u32[]{:S(2)}) collective-permute-start(f32[24,12]{1,0:T(8,128)S(1)} %get-tuple-element.30), channel_id=1, source_target_pairs={{0,2},{1,3},{2,0},{3,1},{4,6},{5,7},{6,4},{7,5},{8,10},{9,11},{10,... | collective-permute-start | bytes 3464 | tf_op jit(solution)/shard_map/ppermute | solution.py:14
  145.4 5.2 %collective-permute-start.8 = (f32[24,12]{1,0:T(8,128)S(1)}, f32[24,12]{1,0:T(8,128)S(1)}, u32[]{:S(2)}, u32[]{:S(2)}) collective-permute-start(f32[24,12]{1,0:T(8,128)S(1)} %get-tuple-element.33), channel_id=1, source_target_pairs={{0,2},{1,3},{2,0},{3,1},{4,6},{5,7},{6,4},{7,5},{8,10},{9,11},{10,... | collective-permute-start | bytes 3464 | tf_op jit(solution)/shard_map/ppermute | solution.py:14
  145.9 7.7 %collective-permute-start.9 = (f32[24,12,128]{2,1,0:T(8,128)S(1)}, f32[24,12,128]{2,1,0:T(8,128)S(1)}, u32[]{:S(2)}, u32[]{:S(2)}) collective-permute-start(f32[24,12,128]{2,1,0:T(8,128)S(1)} %multiply_add_fusion.1), channel_id=1, source_target_pairs={{0,2},{1,3},{2,0},{3,1},{4,6},{5,7},{6,4},{7,5},{8,10},{9,11},{10,... | collective-permute-start | bytes 442376 | tf_op jit(solution)/shard_map/ppermute | solution.py:14
  150.6 3.9 %collective-permute-start.14 = (f32[24,12]{1,0:T(8,128)S(1)}, f32[24,12]{1,0:T(8,128)S(1)}, u32[]{:S(2)}, u32[]{:S(2)}) collective-permute-start(f32[24,12]{1,0:T(8,128)S(1)} %get-tuple-element.26), channel_id=1, source_target_pairs={{0,4},{1,5},{2,6},{3,7},{4,0},{5,1},{6,2},{7,3},{8,12},{9,13},{10,... | collective-permute-start | bytes 3464 | tf_op jit(solution)/shard_map/ppermute | solution.py:14
  151.3 3.7 %collective-permute-start.10 = (f32[24,12]{1,0:T(8,128)S(1)}, f32[24,12]{1,0:T(8,128)S(1)}, u32[]{:S(2)}, u32[]{:S(2)}) collective-permute-start(f32[24,12]{1,0:T(8,128)S(1)} %get-tuple-element.29), channel_id=1, source_target_pairs={{0,4},{1,5},{2,6},{3,7},{4,0},{5,1},{6,2},{7,3},{8,12},{9,13},{10,... | collective-permute-start | bytes 3464 | tf_op jit(solution)/shard_map/ppermute | solution.py:14
  153.8 5.8 %collective-permute-start.11 = (f32[24,12,128]{2,1,0:T(8,128)S(1)}, f32[24,12,128]{2,1,0:T(8,128)S(1)}, u32[]{:S(2)}, u32[]{:S(2)}) collective-permute-start(f32[24,12,128]{2,1,0:T(8,128)S(1)} %multiply_add_fusion), channel_id=1, source_target_pairs={{0,4},{1,5},{2,6},{3,7},{4,0},{5,1},{6,2},{7,3},{8,12},{9,13},{10,... | collective-permute-start | bytes 442376 | tf_op jit(solution)/shard_map/ppermute | solution.py:14
  160.1 5.9 %collective-permute-start.15 = (f32[24,1536]{1,0:T(8,128)S(1)}, f32[24,1536]{1,0:T(8,128)S(1)}, u32[]{:S(2)}, u32[]{:S(2)}) collective-permute-start(f32[24,1536]{1,0:T(8,128)S(1)} %fusion.71), channel_id=1, source_target_pairs={{0,1},{1,0},{2,3},{3,2},{4,5},{5,4},{6,7},{7,6},{8,9},{9,8},{10,11... | collective-permute-start | bytes 442376 | tf_op jit(solution)/shard_map/ppermute | solution.py:14
  166.1 6.7 %collective-permute-start.16 = (f32[24,1536]{1,0:T(8,128)S(1)}, f32[24,1536]{1,0:T(8,128)S(1)}, u32[]{:S(2)}, u32[]{:S(2)}) collective-permute-start(f32[24,1536]{1,0:T(8,128)S(1)} %add.329), channel_id=1, source_target_pairs={{0,2},{1,3},{2,0},{3,1},{4,6},{5,7},{6,4},{7,5},{8,10},{9,11},{10,... | collective-permute-start | bytes 442376 | tf_op jit(solution)/shard_map/ppermute | solution.py:14
  172.9 5.3 %collective-permute-start.17 = (f32[24,1536]{1,0:T(8,128)S(1)}, f32[24,1536]{1,0:T(8,128)}, u32[]{:S(2)}, u32[]{:S(2)}) collective-permute-start(f32[24,1536]{1,0:T(8,128)S(1)} %add.330), channel_id=1, source_target_pairs={{0,4},{1,5},{2,6},{3,7},{4,0},{5,1},{6,2},{7,3},{8,12},{9,13},{10,... | collective-permute-start | bytes 442376 | tf_op jit(solution)/shard_map/ppermute | solution.py:14
  188.6 4.7 %collective-permute-start.18 = (f32[24,4,192]{2,0,1:T(8,128)S(1)}, f32[24,4,192]{2,0,1:T(8,128)S(1)}, u32[]{:S(2)}, u32[]{:S(2)}) collective-permute-start(f32[24,4,192]{2,0,1:T(8,128)S(1)} %copy_select_fusion.1), channel_id=1, source_target_pairs={{0,4},{1,5},{2,6},{3,7},{4,0},{5,1},{6,2},{7,3},{8,12},{9,13},{10,... | collective-permute-start | bytes 221192 | tf_op jit(solution)/shard_map/ppermute | solution.py:14
  193.4 6.6 %collective-permute-start.19 = (f32[24,2,192]{2,0,1:T(8,128)S(1)}, f32[24,2,192]{2,0,1:T(8,128)S(1)}, u32[]{:S(2)}, u32[]{:S(2)}) collective-permute-start(f32[24,2,192]{2,0,1:T(8,128)S(1)} %slice_select_fusion.1), channel_id=1, source_target_pairs={{0,2},{1,3},{2,0},{3,1},{4,6},{5,7},{6,4},{7,5},{8,10},{9,11},{10,... | collective-permute-start | bytes 110600 | tf_op jit(solution)/shard_map/ppermute | solution.py:14
  200.0 4.0 %collective-permute-start.20 = (f32[24,1,192]{2,0,1:T(8,128)S(1)}, f32[24,1,192]{2,0,1:T(8,128)S(1)}, u32[]{:S(2)}, u32[]{:S(2)}) collective-permute-start(f32[24,1,192]{2,0,1:T(8,128)S(1)} %slice_select_fusion.2), channel_id=1, source_target_pairs={{0,1},{1,0},{2,3},{3,2},{4,5},{5,4},{6,7},{7,6},{8,9},{9,8},{10,11... | collective-permute-start | bytes 55304 | tf_op jit(solution)/shard_map/ppermute | solution.py:14
  (25 other events, 149.9 us)

commit v2 on v1

--- a/solution.py
+++ b/solution.py
@@ -120,20 +120,24 @@
     anchor = jnp.sum(jnp.where(owner == own_group, group_ids[:, None], 0), axis=0)
     page_rows = cache.shape[1]
     conv_rows = conv_state.shape[1]
-    combined = jnp.concatenate([cache, conv_state, lru_state[:, None, :]], axis=1)
+    states = jnp.concatenate([conv_state, lru_state[:, None, :]], axis=1)
     to_group = owner[own_group][None, :] == group_ids[:, None]
     send_slot = jnp.sum(jnp.where(to_group, my_leave[None, :], 0), axis=1)
-    send = jnp.take(combined, send_slot, axis=0)
-    got = lax.all_to_all(send, "req", 0, 0, tiled=True)
+    got_states = lax.all_to_all(jnp.take(states, send_slot, axis=0), "req", 0, 0, tiled=True)
+    got_cache = lax.all_to_all(jnp.take(cache, send_slot, axis=0), "req", 0, 0, tiled=True)
     local_ids = jnp.arange(req_rows, dtype=jnp.int32)
     match_slot = my_leave[None, :] == local_ids[:, None]
     arrive_rank = jnp.sum(jnp.where(match_slot, rank_ids[None, :], 0), axis=1)
     arriving = jnp.any(match_slot, axis=1)
-    arrived = jnp.take(got, anchor[arrive_rank], axis=0)
-    moved = jnp.where(arriving[:, None, None], arrived, combined)
-    moved_cache = moved[:, :page_rows]
-    moved_conv = moved[:, page_rows : page_rows + conv_rows]
-    moved_lru = moved[:, page_rows + conv_rows]
+    arrive_from = anchor[arrive_rank]
+    moved_states = jnp.where(
+        arriving[:, None, None], jnp.take(got_states, arrive_from, axis=0), states
+    )
+    moved_cache = jnp.where(
+        arriving[:, None, None], jnp.take(got_cache, arrive_from, axis=0), cache
+    )
+    moved_conv = moved_states[:, :conv_rows]
+    moved_lru = moved_states[:, conv_rows]
     arrive_anchor = anchor[arrive_rank]
     anchor_slot = arrive_anchor * req_rows + leaving[arrive_anchor, arrive_rank]
     source_slot = jnp.where(arriving, anchor_slot, own_group * req_rows + local_ids)

time: 206 us -> 163 us (0.79)
  waiting for transfers between devices: 96.6 us -> 50.3 us
  local copies, waits for them, and re-layouts: 22.4 us -> 13.7 us
  starting transfers between devices: 50.9 us -> 58.8 us
  other arithmetic: 20.4 us -> 25.4 us
    all_to_all x1 -> x2, waiting for transfers between devices: 52 us -> 0.01 us  [the longest x1 0.01 us: per_device(): lax.all_to_all(jnp.take(states, send_slot, axis=0), 'req', 0, 0, tiled=True)]
    all_to_all x1 -> x2, starting transfers between devices: 11.4 us -> 21.1 us  [the longest x1 11.2 us: per_device(): lax.all_to_all(jnp.take(states, send_slot, axis=0), 'req', 0, 0, tiled=True)]
    ppermute x21, waiting for transfers between devices: 44.6 us -> 50.3 us  [partner_swap(): return jax.tree.map(lambda part: lax.ppermute(part, axis, pairs), value)]
    unnamed x57 -> x51, local copies, waits for them, and re-layouts: 5.07 us -> 0.77 us
    add x7, other arithmetic: 1.1 us -> 3.34 us  [across_mlp(): return joined(partial_value, 'mlp', lambda first, second: first + second)]
    select_n x1, other arithmetic: 0.56 us -> 2.71 us  [per_device(): jnp.where(row_hit[:, :, None], write_row[:, None, :], moved_cache)]
    gather x3 -> x5, local copies, waits for them, and re-layouts: 7.73 us -> 7.47 us  [the longest x1 3.55 us: per_device(): jnp.take(got_cache, arrive_from, axis=0)]
  transfers between devices with their start and end apart: 22 -> 23, of which waited for: 17 -> 19; matrix products, arithmetic and copies ran while one was open for 7% -> 21% of each run, Pallas kernels for 0% -> 0%
where the time goes in v2:
time: 163 us; the launch traced here: 162 us
  starting transfers between devices  58.8 us (36%)
  waiting for transfers between devices  50.3 us (31%)
  other arithmetic  25.4 us (16%)
  local copies, waits for them, and re-layouts  13.7 us (8%)
  matrix products  12.5 us (8%)
    ppermute x21, waiting for transfers between devices, partner_swap(): return jax.tree.map(lambda part: lax.ppermute(part, axis, pairs), value)  50.3 us
    ppermute x21, starting transfers between devices, partner_swap(): return jax.tree.map(lambda part: lax.ppermute(part, axis, pairs), value)  37.7 us
    all_to_all x1, starting transfers between devices, per_device(): lax.all_to_all(jnp.take(states, send_slot, axis=0), 'req', 0, 0, tiled=True)  11.2 us
    all_to_all x1, starting transfers between devices, per_device(): lax.all_to_all(jnp.take(cache, send_slot, axis=0), 'req', 0, 0, tiled=True)  9.88 us
    gather x1, local copies, waits for them, and re-layouts, per_device(): jnp.take(got_cache, arrive_from, axis=0)  3.55 us
    add x7, other arithmetic, across_mlp(): return joined(partial_value, 'mlp', lambda first, second: first + second)  3.34 us
  transfers between devices with their start and end apart: 23, of which 19 were waited for; matrix products, arithmetic and copies ran while one was open for 21% of the time, Pallas kernels for 0%

profile of v2, /device:TPU:32, one launch (start us, length us, event | category | flops | bytes accessed | tf_op | source)
XLA Modules:
  0.0 161.8 jit_solution(968529819773307994)
XLA Ops:
  4.0 11.2 %all-to-all-start = ((bf16[32,4,256]{2,1,0:T(4,128)(2,1)}), bf16[32,4,256]{2,1,0:T(4,128)(2,1)S(1)}, u32[]{:S(2)}, u32[]{:S(2)}) async-start(bf16[32,4,256]{2,1,0:T(4,128)(2,1)} %broadcast_select_fusion.2), calls=%async_computation | async-start | bytes 131072 | tf_op jit(solution)/shard_map/all_to_all | solution.py:126
  22.3 3.2 %broadcast_select_fusion = bf16[32,128,256]{2,1,0:T(8,128)(2,1)} fusion(bf16[32,128,256]{2,1,0:T(8,128)(2,1)} %gather_fusion.5, pred[32]{0:T(512)(128)(4,1)S(1)} %compare_and_fusion.1), kind=kLoop, calls=%fused_computation.7 | loop fusion | flops 1048576 | bytes 4194336 | tf_op jit(solution)/shard_map/jit(_take)/select_n | solution.py:127
  27.4 9.9 %all-to-all-start.1 = ((bf16[32,128,256]{2,1,0:T(8,128)(2,1)}), bf16[32,128,256]{2,1,0:T(8,128)(2,1)}, u32[]{:S(2)}, u32[]{:S(2)}) async-start(bf16[32,128,256]{2,1,0:T(8,128)(2,1)} %broadcast_select_fusion), calls=%async_computation.1 | async-start | bytes 4194304 | tf_op jit(solution)/shard_map/all_to_all | solution.py:127
  43.3 2.7 %fusion.57 = f32[24,1536]{1,0:T(8,128)} fusion(bf16[256,1536]{1,0:T(8,128)(2,1)} %param.39, f32[24,256]{1,0:T(8,128)S(1)} %get-tuple-element.5, bf16[1536,256]{1,0:T(8,128)(2,1)} %param.33, bf16[24,1536]{1,0:T(8,128)(2,1)S(1)} %copy-done.5, f32[1536]{0:T(1024)} %param.31, f32[24]{0:T(128)} %add_rsqrt_fusion.2), kind=kOutput, calls=%fused_computation.111 | convolution fusion | flops 37957632 | bytes 1824864 | tf_op jit(solution)/shard_map/dot_general | solution.py:179
  48.4 3.8 %collective-permute-done = f32[24,1536]{1,0:T(8,128)S(1)} collective-permute-done((f32[24,1536]{1,0:T(8,128)}, f32[24,1536]{1,0:T(8,128)S(1)}, u32[]{:S(2)}, u32[]{:S(2)}) %collective-permute-start) | collective-permute-done | bytes 147488 | tf_op jit(solution)/shard_map/ppermute | solution.py:14
  53.7 3.2 %collective-permute-start.1 = (f32[24,1536]{1,0:T(8,128)}, f32[24,1536]{1,0:T(8,128)}, u32[]{:S(2)}, u32[]{:S(2)}) collective-permute-start(f32[24,1536]{1,0:T(8,128)} %add.309), channel_id=1, source_target_pairs={{0,2},{1,3},{2,0},{3,1},{4,6},{5,7},{6,4},{7,5},{8,10},{9,11},{10,... | collective-permute-start | bytes 442376 | tf_op jit(solution)/shard_map/ppermute | solution.py:14
  57.7 3.1 %collective-permute-done.1 = f32[24,1536]{1,0:T(8,128)} collective-permute-done((f32[24,1536]{1,0:T(8,128)}, f32[24,1536]{1,0:T(8,128)}, u32[]{:S(2)}, u32[]{:S(2)}) %collective-permute-start.1) | collective-permute-done | bytes 147488 | tf_op jit(solution)/shard_map/ppermute | solution.py:14
  63.1 4.8 %collective-permute-done.2 = f32[24,1536]{1,0:T(8,128)S(1)} collective-permute-done((f32[24,1536]{1,0:T(8,128)S(1)}, f32[24,1536]{1,0:T(8,128)S(1)}, u32[]{:S(2)}, u32[]{:S(2)}) %collective-permute-start.2) | collective-permute-done | bytes 147488 | tf_op jit(solution)/shard_map/ppermute | solution.py:14
  71.9 2.7 %collective-permute-done.3 = f32[24,1536]{1,0:T(8,128)S(1)} collective-permute-done((f32[24,1536]{1,0:T(8,128)S(1)}, f32[24,1536]{1,0:T(8,128)S(1)}, u32[]{:S(2)}, u32[]{:S(2)}) %collective-permute-start.3) | collective-permute-done | bytes 147488 | tf_op jit(solution)/shard_map/ppermute | solution.py:14
  74.6 3.5 %collective-permute-start.4 = (f32[24,1536]{1,0:T(8,128)S(1)}, f32[24,1536]{1,0:T(8,128)S(1)}, u32[]{:S(2)}, u32[]{:S(2)}) collective-permute-start(f32[24,1536]{1,0:T(8,128)S(1)} %add.322), channel_id=1, source_target_pairs={{0,2},{1,3},{2,0},{3,1},{4,6},{5,7},{6,4},{7,5},{8,10},{9,11},{10,... | collective-permute-start | bytes 442376 | tf_op jit(solution)/shard_map/ppermute | solution.py:14
  78.4 3.0 %collective-permute-done.4 = f32[24,1536]{1,0:T(8,128)S(1)} collective-permute-done((f32[24,1536]{1,0:T(8,128)S(1)}, f32[24,1536]{1,0:T(8,128)S(1)}, u32[]{:S(2)}, u32[]{:S(2)}) %collective-permute-start.4) | collective-permute-done | bytes 147488 | tf_op jit(solution)/shard_map/ppermute | solution.py:14
  83.3 3.4 %collective-permute-done.5 = f32[24,1536]{1,0:T(8,128)S(1)} collective-permute-done((f32[24,1536]{1,0:T(8,128)S(1)}, f32[24,1536]{1,0:T(8,128)S(1)}, u32[]{:S(2)}, u32[]{:S(2)}) %collective-permute-start.5) | collective-permute-done | bytes 147488 | tf_op jit(solution)/shard_map/ppermute | solution.py:14
  90.9 3.6 %gather_fusion.6 = bf16[24,128,256]{2,1,0:T(8,128)(2,1)} fusion(bf16[32,128,256]{2,1,0:T(8,128)(2,1)} %all-to-all-done.1, s32[1024]{0:T(1024)} %copy-done.20), kind=kCustom, calls=%fused_computation.6 | custom fusion | bytes 3145824 | tf_op jit(solution)/shard_map/jit(_take)/gather | solution.py:137
  94.5 2.7 %broadcast_select_fusion.1 = (bf16[24,128,256]{2,1,0:T(8,128)(2,1)}, bf16[24,128,256]{2,1,0:T(8,128)(2,1)S(1)}) fusion(pred[24,128]{1,0:T(8,128)(4,1)S(1)} %copy-done.17, bf16[24,256]{1,0:T(8,128)(2,1)S(1)} %copy-done.13, bf16[24,128,256]{2,1,0:T(8,128)(2,1)S(1)} %copy-done.2, bf16[24,128,256]{2,1,0:T(8,128)(2,1)} %gather_fusion.6, ...), kind=kLoop, calls=%fused_computation.9 | loop fusion | flops 2359296 | bytes 6306864 | tf_op jit(solution)/shard_map/jit(_where)/select_n | solution.py:258
  97.8 2.8 %collective-permute-start.6 = (f32[24,12]{1,0:T(8,128)S(1)}, f32[24,12]{1,0:T(8,128)S(1)}, u32[]{:S(2)}, u32[]{:S(2)}) collective-permute-start(f32[24,12]{1,0:T(8,128)S(1)} %get-tuple-element.45), channel_id=1, source_target_pairs={{0,1},{1,0},{2,3},{3,2},{4,5},{5,4},{6,7},{7,6},{8,9},{9,8},{10,11... | collective-permute-start | bytes 3464 | tf_op jit(solution)/shard_map/ppermute | solution.py:14
  104.7 4.3 %collective-permute-start.13 = (f32[24,12]{1,0:T(8,128)S(1)}, f32[24,12]{1,0:T(8,128)S(1)}, u32[]{:S(2)}, u32[]{:S(2)}) collective-permute-start(f32[24,12]{1,0:T(8,128)S(1)} %get-tuple-element.20), channel_id=1, source_target_pairs={{0,2},{1,3},{2,0},{3,1},{4,6},{5,7},{6,4},{7,5},{8,10},{9,11},{10,... | collective-permute-start | bytes 3464 | tf_op jit(solution)/shard_map/ppermute | solution.py:14
  109.3 3.7 %collective-permute-start.9 = (f32[24,12,128]{2,1,0:T(8,128)S(1)}, f32[24,12,128]{2,1,0:T(8,128)S(1)}, u32[]{:S(2)}, u32[]{:S(2)}) collective-permute-start(f32[24,12,128]{2,1,0:T(8,128)S(1)} %multiply_add_fusion.1), channel_id=1, source_target_pairs={{0,2},{1,3},{2,0},{3,1},{4,6},{5,7},{6,4},{7,5},{8,10},{9,11},{10,... | collective-permute-start | bytes 442376 | tf_op jit(solution)/shard_map/ppermute | solution.py:14
  118.6 4.0 %collective-permute-done.11 = f32[24,12,128]{2,1,0:T(8,128)S(1)} collective-permute-done((f32[24,12,128]{2,1,0:T(8,128)S(1)}, f32[24,12,128]{2,1,0:T(8,128)S(1)}, u32[]{:S(2)}, u32[]{:S(2)}) %collective-permute-start.11) | collective-permute-done | bytes 147488 | tf_op jit(solution)/shard_map/ppermute | solution.py:14
  125.1 3.4 %collective-permute-done.15 = f32[24,1536]{1,0:T(8,128)S(1)} collective-permute-done((f32[24,1536]{1,0:T(8,128)S(1)}, f32[24,1536]{1,0:T(8,128)S(1)}, u32[]{:S(2)}, u32[]{:S(2)}) %collective-permute-start.15) | collective-permute-done | bytes 147488 | tf_op jit(solution)/shard_map/ppermute | solution.py:14
  128.5 3.9 %collective-permute-start.16 = (f32[24,1536]{1,0:T(8,128)S(1)}, f32[24,1536]{1,0:T(8,128)S(1)}, u32[]{:S(2)}, u32[]{:S(2)}) collective-permute-start(f32[24,1536]{1,0:T(8,128)S(1)} %add.335), channel_id=1, source_target_pairs={{0,2},{1,3},{2,0},{3,1},{4,6},{5,7},{6,4},{7,5},{8,10},{9,11},{10,... | collective-permute-start | bytes 442376 | tf_op jit(solution)/shard_map/ppermute | solution.py:14
  132.4 3.1 %collective-permute-done.16 = f32[24,1536]{1,0:T(8,128)S(1)} collective-permute-done((f32[24,1536]{1,0:T(8,128)S(1)}, f32[24,1536]{1,0:T(8,128)S(1)}, u32[]{:S(2)}, u32[]{:S(2)}) %collective-permute-start.16) | collective-permute-done | bytes 147488 | tf_op jit(solution)/shard_map/ppermute | solution.py:14
  136.2 5.6 %collective-permute-done.17 = f32[24,1536]{1,0:T(8,128)S(1)} collective-permute-done((f32[24,1536]{1,0:T(8,128)S(1)}, f32[24,1536]{1,0:T(8,128)S(1)}, u32[]{:S(2)}, u32[]{:S(2)}) %collective-permute-start.17) | collective-permute-done | bytes 147488 | tf_op jit(solution)/shard_map/ppermute | solution.py:14
  147.4 4.0 %collective-permute-done.18 = f32[24,4,192]{2,0,1:T(8,128)S(1)} collective-permute-done((f32[24,4,192]{2,0,1:T(8,128)S(1)}, f32[24,4,192]{2,0,1:T(8,128)S(1)}, u32[]{:S(2)}, u32[]{:S(2)}) %collective-permute-start.18) | collective-permute-done | bytes 73760 | tf_op jit(solution)/shard_map/ppermute | solution.py:14
  154.1 3.1 %collective-permute-done.19 = f32[24,2,192]{2,0,1:T(8,128)S(1)} collective-permute-done((f32[24,2,192]{2,0,1:T(8,128)S(1)}, f32[24,2,192]{2,0,1:T(8,128)S(1)}, u32[]{:S(2)}, u32[]{:S(2)}) %collective-permute-start.19) | collective-permute-done | bytes 36896 | tf_op jit(solution)/shard_map/ppermute | solution.py:14
  (164 shorter events, 62.0 us)
Async XLA Ops:
  0.6 143.4 %copy-start = (bf16[576,1536]{1,0:T(8,128)(2,1)S(1)}, bf16[576,1536]{1,0:T(8,128)(2,1)}, u32[]{:S(2)}) copy-start(bf16[576,1536]{1,0:T(8,128)(2,1)} %param.47) | copy-start | bytes 5308420
  4.0 23.3 %all-to-all-start = ((bf16[32,4,256]{2,1,0:T(4,128)(2,1)}), bf16[32,4,256]{2,1,0:T(4,128)(2,1)S(1)}, u32[]{:S(2)}, u32[]{:S(2)}) async-start(bf16[32,4,256]{2,1,0:T(4,128)(2,1)} %broadcast_select_fusion.2), calls=%async_computation | async-start | bytes 131072 | tf_op jit(solution)/shard_map/all_to_all | solution.py:126
  27.4 63.5 %all-to-all-start.1 = ((bf16[32,128,256]{2,1,0:T(8,128)(2,1)}), bf16[32,128,256]{2,1,0:T(8,128)(2,1)}, u32[]{:S(2)}, u32[]{:S(2)}) async-start(bf16[32,128,256]{2,1,0:T(8,128)(2,1)} %broadcast_select_fusion), calls=%async_computation.1 | async-start | bytes 4194304 | tf_op jit(solution)/shard_map/all_to_all | solution.py:127
  46.0 6.1 %collective-permute-start = (f32[24,1536]{1,0:T(8,128)}, f32[24,1536]{1,0:T(8,128)S(1)}, u32[]{:S(2)}, u32[]{:S(2)}) collective-permute-start(f32[24,1536]{1,0:T(8,128)} %fusion.57), channel_id=1, source_target_pairs={{0,1},{1,0},{2,3},{3,2},{4,5},{5,4},{6,7},{7,6},{8,9},{9,8},{10,11... | collective-permute-start | bytes 442376 | tf_op jit(solution)/shard_map/ppermute | solution.py:14
  53.7 7.0 %collective-permute-start.1 = (f32[24,1536]{1,0:T(8,128)}, f32[24,1536]{1,0:T(8,128)}, u32[]{:S(2)}, u32[]{:S(2)}) collective-permute-start(f32[24,1536]{1,0:T(8,128)} %add.309), channel_id=1, source_target_pairs={{0,2},{1,3},{2,0},{3,1},{4,6},{5,7},{6,4},{7,5},{8,10},{9,11},{10,... | collective-permute-start | bytes 442376 | tf_op jit(solution)/shard_map/ppermute | solution.py:14
  61.7 6.1 %collective-permute-start.2 = (f32[24,1536]{1,0:T(8,128)S(1)}, f32[24,1536]{1,0:T(8,128)S(1)}, u32[]{:S(2)}, u32[]{:S(2)}) collective-permute-start(f32[24,1536]{1,0:T(8,128)S(1)} %add.310), channel_id=1, source_target_pairs={{0,4},{1,5},{2,6},{3,7},{4,0},{5,1},{6,2},{7,3},{8,12},{9,13},{10,... | collective-permute-start | bytes 442376 | tf_op jit(solution)/shard_map/ppermute | solution.py:14
  69.4 5.2 %collective-permute-start.3 = (f32[24,1536]{1,0:T(8,128)S(1)}, f32[24,1536]{1,0:T(8,128)S(1)}, u32[]{:S(2)}, u32[]{:S(2)}) collective-permute-start(f32[24,1536]{1,0:T(8,128)S(1)} %fusion.73), channel_id=1, source_target_pairs={{0,1},{1,0},{2,3},{3,2},{4,5},{5,4},{6,7},{7,6},{8,9},{9,8},{10,11... | collective-permute-start | bytes 442376 | tf_op jit(solution)/shard_map/ppermute | solution.py:14
  74.6 6.7 %collective-permute-start.4 = (f32[24,1536]{1,0:T(8,128)S(1)}, f32[24,1536]{1,0:T(8,128)S(1)}, u32[]{:S(2)}, u32[]{:S(2)}) collective-permute-start(f32[24,1536]{1,0:T(8,128)S(1)} %add.322), channel_id=1, source_target_pairs={{0,2},{1,3},{2,0},{3,1},{4,6},{5,7},{6,4},{7,5},{8,10},{9,11},{10,... | collective-permute-start | bytes 442376 | tf_op jit(solution)/shard_map/ppermute | solution.py:14
  81.4 5.4 %collective-permute-start.5 = (f32[24,1536]{1,0:T(8,128)S(1)}, f32[24,1536]{1,0:T(8,128)S(1)}, u32[]{:S(2)}, u32[]{:S(2)}) collective-permute-start(f32[24,1536]{1,0:T(8,128)S(1)} %add.323), channel_id=1, source_target_pairs={{0,4},{1,5},{2,6},{3,7},{4,0},{5,1},{6,2},{7,3},{8,12},{9,13},{10,... | collective-permute-start | bytes 442376 | tf_op jit(solution)/shard_map/ppermute | solution.py:14
  97.8 6.9 %collective-permute-start.6 = (f32[24,12]{1,0:T(8,128)S(1)}, f32[24,12]{1,0:T(8,128)S(1)}, u32[]{:S(2)}, u32[]{:S(2)}) collective-permute-start(f32[24,12]{1,0:T(8,128)S(1)} %get-tuple-element.45), channel_id=1, source_target_pairs={{0,1},{1,0},{2,3},{3,2},{4,5},{5,4},{6,7},{7,6},{8,9},{9,8},{10,11... | collective-permute-start | bytes 3464 | tf_op jit(solution)/shard_map/ppermute | solution.py:14
  100.9 3.8 %collective-permute-start.12 = (f32[24,12]{1,0:T(8,128)S(1)}, f32[24,12]{1,0:T(8,128)S(1)}, u32[]{:S(2)}, u32[]{:S(2)}) collective-permute-start(f32[24,12]{1,0:T(8,128)S(1)} %fusion.5), channel_id=1, source_target_pairs={{0,1},{1,0},{2,3},{3,2},{4,5},{5,4},{6,7},{7,6},{8,9},{9,8},{10,11... | collective-permute-start | bytes 3464 | tf_op jit(solution)/shard_map/ppermute | solution.py:14
  101.4 7.7 %collective-permute-start.7 = (f32[24,12,128]{2,1,0:T(8,128)S(1)}, f32[24,12,128]{2,1,0:T(8,128)S(1)}, u32[]{:S(2)}, u32[]{:S(2)}) collective-permute-start(f32[24,12,128]{2,1,0:T(8,128)S(1)} %fusion.2), channel_id=1, source_target_pairs={{0,1},{1,0},{2,3},{3,2},{4,5},{5,4},{6,7},{7,6},{8,9},{9,8},{10,11... | collective-permute-start | bytes 442376 | tf_op jit(solution)/shard_map/ppermute | solution.py:14
  104.7 8.4 %collective-permute-start.13 = (f32[24,12]{1,0:T(8,128)S(1)}, f32[24,12]{1,0:T(8,128)S(1)}, u32[]{:S(2)}, u32[]{:S(2)}) collective-permute-start(f32[24,12]{1,0:T(8,128)S(1)} %get-tuple-element.20), channel_id=1, source_target_pairs={{0,2},{1,3},{2,0},{3,1},{4,6},{5,7},{6,4},{7,5},{8,10},{9,11},{10,... | collective-permute-start | bytes 3464 | tf_op jit(solution)/shard_map/ppermute | solution.py:14
  109.0 5.2 %collective-permute-start.8 = (f32[24,12]{1,0:T(8,128)S(1)}, f32[24,12]{1,0:T(8,128)S(1)}, u32[]{:S(2)}, u32[]{:S(2)}) collective-permute-start(f32[24,12]{1,0:T(8,128)S(1)} %get-tuple-element.23), channel_id=1, source_target_pairs={{0,2},{1,3},{2,0},{3,1},{4,6},{5,7},{6,4},{7,5},{8,10},{9,11},{10,... | collective-permute-start | bytes 3464 | tf_op jit(solution)/shard_map/ppermute | solution.py:14
  109.3 7.4 %collective-permute-start.9 = (f32[24,12,128]{2,1,0:T(8,128)S(1)}, f32[24,12,128]{2,1,0:T(8,128)S(1)}, u32[]{:S(2)}, u32[]{:S(2)}) collective-permute-start(f32[24,12,128]{2,1,0:T(8,128)S(1)} %multiply_add_fusion.1), channel_id=1, source_target_pairs={{0,2},{1,3},{2,0},{3,1},{4,6},{5,7},{6,4},{7,5},{8,10},{9,11},{10,... | collective-permute-start | bytes 442376 | tf_op jit(solution)/shard_map/ppermute | solution.py:14
  114.2 3.8 %collective-permute-start.14 = (f32[24,12]{1,0:T(8,128)S(1)}, f32[24,12]{1,0:T(8,128)S(1)}, u32[]{:S(2)}, u32[]{:S(2)}) collective-permute-start(f32[24,12]{1,0:T(8,128)S(1)} %get-tuple-element.16), channel_id=1, source_target_pairs={{0,4},{1,5},{2,6},{3,7},{4,0},{5,1},{6,2},{7,3},{8,12},{9,13},{10,... | collective-permute-start | bytes 3464 | tf_op jit(solution)/shard_map/ppermute | solution.py:14
  114.9 3.7 %collective-permute-start.10 = (f32[24,12]{1,0:T(8,128)S(1)}, f32[24,12]{1,0:T(8,128)S(1)}, u32[]{:S(2)}, u32[]{:S(2)}) collective-permute-start(f32[24,12]{1,0:T(8,128)S(1)} %get-tuple-element.19), channel_id=1, source_target_pairs={{0,4},{1,5},{2,6},{3,7},{4,0},{5,1},{6,2},{7,3},{8,12},{9,13},{10,... | collective-permute-start | bytes 3464 | tf_op jit(solution)/shard_map/ppermute | solution.py:14
  116.9 5.8 %collective-permute-start.11 = (f32[24,12,128]{2,1,0:T(8,128)S(1)}, f32[24,12,128]{2,1,0:T(8,128)S(1)}, u32[]{:S(2)}, u32[]{:S(2)}) collective-permute-start(f32[24,12,128]{2,1,0:T(8,128)S(1)} %multiply_add_fusion), channel_id=1, source_target_pairs={{0,4},{1,5},{2,6},{3,7},{4,0},{5,1},{6,2},{7,3},{8,12},{9,13},{10,... | collective-permute-start | bytes 442376 | tf_op jit(solution)/shard_map/ppermute | solution.py:14
  123.3 5.2 %collective-permute-start.15 = (f32[24,1536]{1,0:T(8,128)S(1)}, f32[24,1536]{1,0:T(8,128)S(1)}, u32[]{:S(2)}, u32[]{:S(2)}) collective-permute-start(f32[24,1536]{1,0:T(8,128)S(1)} %fusion.71), channel_id=1, source_target_pairs={{0,1},{1,0},{2,3},{3,2},{4,5},{5,4},{6,7},{7,6},{8,9},{9,8},{10,11... | collective-permute-start | bytes 442376 | tf_op jit(solution)/shard_map/ppermute | solution.py:14
  128.5 7.1 %collective-permute-start.16 = (f32[24,1536]{1,0:T(8,128)S(1)}, f32[24,1536]{1,0:T(8,128)S(1)}, u32[]{:S(2)}, u32[]{:S(2)}) collective-permute-start(f32[24,1536]{1,0:T(8,128)S(1)} %add.335), channel_id=1, source_target_pairs={{0,2},{1,3},{2,0},{3,1},{4,6},{5,7},{6,4},{7,5},{8,10},{9,11},{10,... | collective-permute-start | bytes 442376 | tf_op jit(solution)/shard_map/ppermute | solution.py:14
  135.6 6.3 %collective-permute-start.17 = (f32[24,1536]{1,0:T(8,128)S(1)}, f32[24,1536]{1,0:T(8,128)S(1)}, u32[]{:S(2)}, u32[]{:S(2)}) collective-permute-start(f32[24,1536]{1,0:T(8,128)S(1)} %add.336), channel_id=1, source_target_pairs={{0,4},{1,5},{2,6},{3,7},{4,0},{5,1},{6,2},{7,3},{8,12},{9,13},{10,... | collective-permute-start | bytes 442376 | tf_op jit(solution)/shard_map/ppermute | solution.py:14
  146.8 4.7 %collective-permute-start.18 = (f32[24,4,192]{2,0,1:T(8,128)S(1)}, f32[24,4,192]{2,0,1:T(8,128)S(1)}, u32[]{:S(2)}, u32[]{:S(2)}) collective-permute-start(f32[24,4,192]{2,0,1:T(8,128)S(1)} %copy_select_fusion), channel_id=1, source_target_pairs={{0,4},{1,5},{2,6},{3,7},{4,0},{5,1},{6,2},{7,3},{8,12},{9,13},{10,... | collective-permute-start | bytes 221192 | tf_op jit(solution)/shard_map/ppermute | solution.py:14
  151.5 5.7 %collective-permute-start.19 = (f32[24,2,192]{2,0,1:T(8,128)S(1)}, f32[24,2,192]{2,0,1:T(8,128)S(1)}, u32[]{:S(2)}, u32[]{:S(2)}) collective-permute-start(f32[24,2,192]{2,0,1:T(8,128)S(1)} %slice_select_fusion), channel_id=1, source_target_pairs={{0,2},{1,3},{2,0},{3,1},{4,6},{5,7},{6,4},{7,5},{8,10},{9,11},{10,... | collective-permute-start | bytes 110600 | tf_op jit(solution)/shard_map/ppermute | solution.py:14
  157.2 3.9 %collective-permute-start.20 = (f32[24,1,192]{2,0,1:T(8,128)S(1)}, f32[24,1,192]{2,0,1:T(8,128)S(1)}, u32[]{:S(2)}, u32[]{:S(2)}) collective-permute-start(f32[24,1,192]{2,0,1:T(8,128)S(1)} %slice_select_fusion.1), channel_id=1, source_target_pairs={{0,1},{1,0},{2,3},{3,2},{4,5},{5,4},{6,7},{7,6},{8,9},{9,8},{10,11... | collective-permute-start | bytes 55304 | tf_op jit(solution)/shard_map/ppermute | solution.py:14
  (25 other events, 323.9 us)

commit v3 on v2

--- a/solution.py
+++ b/solution.py
@@ -25,9 +25,17 @@
     return bits
 
 
+def axis_stages(axis):
+    stages = []
+    for bit in axis_bits(axis):
+        mask = bit | (bit // 2) if bit == 2 else bit
+        stages.append((mask, bit))
+    return stages
+
+
 def joined(value, axis, join):
-    for bit in axis_bits(axis):
-        value = join(value, partner_swap(value, axis, bit))
+    for mask, _ in axis_stages(axis):
+        value = join(value, partner_swap(value, axis, mask))
     return value
 
 
@@ -36,13 +44,13 @@
     rows, cols = value.shape
     me = lax.axis_index(axis)
     held = value.reshape(rows, size, cols // size)
-    for bit in reversed(axis_bits(axis)):
+    for mask, bit in reversed(axis_stages(axis)):
         half = held.shape[1] // 2
         lower, upper = held[:, :half], held[:, half:]
         mine_upper = (me & bit) != 0
         keep = jnp.where(mine_upper, upper, lower)
         send = jnp.where(mine_upper, lower, upper)
-        held = keep + partner_swap(send, axis, bit)
+        held = keep + partner_swap(send, axis, mask)
     return held.reshape(rows, cols // size)
 
 
@@ -66,15 +74,20 @@
 
 
 def combine_parts(first_part, second_part):
-    first_top, first_sum, first_acc = first_part
-    second_top, second_sum, second_acc = second_part
+    head_size = first_part.shape[-1] - 2
+    first_top, first_sum = first_part[..., head_size], first_part[..., head_size + 1]
+    second_top, second_sum = second_part[..., head_size], second_part[..., head_size + 1]
     larger = jnp.maximum(first_top, second_top)
     first_factor = jnp.exp(first_top - larger)
     second_factor = jnp.exp(second_top - larger)
-    return (
-        larger,
-        first_sum * first_factor + second_sum * second_factor,
-        first_acc * first_factor[..., None] + second_acc * second_factor[..., None],
+    return jnp.concatenate(
+        [
+            first_part[..., :head_size] * first_factor[..., None]
+            + second_part[..., :head_size] * second_factor[..., None],
+            larger[..., None],
+            (first_sum * first_factor + second_sum * second_factor)[..., None],
+        ],
+        axis=-1,
     )
 
 
@@ -217,9 +230,14 @@
         moved_cache[..., head_size:],
         preferred_element_type=jnp.float32,
     )
-    merged_top, merged_sum, merged_acc = joined(
-        (local_top, local_sum, local_acc), "mlp", combine_parts
-    )
+    merged = joined(
+        jnp.concatenate([local_acc, local_top[..., None], local_sum[..., None]], axis=-1),
+        "mlp",
+        combine_parts,
+    )
+    merged_acc = merged[..., :head_size]
+    merged_top = merged[..., head_size]
+    merged_sum = merged[..., head_size + 1]
     own_score = (
         jnp.sum(queries.astype(jnp.float32) * key_new.astype(jnp.float32)[:, None, :], axis=-1)
         * score_scale

time: 163 us -> 172 us (1.055)
  starting transfers between devices: 58.8 us -> 44.1 us
  waiting for transfers between devices: 50.3 us -> 64.3 us
  local copies, waits for them, and re-layouts: 13.7 us -> 20 us
    ppermute x21 -> x15, starting transfers between devices: 37.7 us -> 22.9 us  [partner_swap(): return jax.tree.map(lambda part: lax.ppermute(part, axis, pairs), value)]
    ppermute x21 -> x15, waiting for transfers between devices: 50.3 us -> 63.8 us  [partner_swap(): return jax.tree.map(lambda part: lax.ppermute(part, axis, pairs), value)]
    concatenate x0 -> x3, other arithmetic: none -> 2.07 us  [the longest x2 1.96 us: combine_parts(): jnp.concatenate([first_part[..., :head_size] * first_factor[..., None] +...]
    unnamed x51 -> x62, local copies, waits for them, and re-layouts: 0.77 us -> 2.6 us
  transfers between devices with their start and end apart: 23 -> 17, of which waited for: 19 -> 16; matrix products, arithmetic and copies ran while one was open for 21% -> 20% of each run, Pallas kernels for 0% -> 0%
where the time goes in v3:
time: 172 us; the launch traced here: 171 us
  waiting for transfers between devices  64.3 us (37%)
  starting transfers between devices  44.1 us (26%)
  other arithmetic  27 us (16%)
  local copies, waits for them, and re-layouts  20 us (12%)
  matrix products  14.2 us (8%)
    ppermute x15, waiting for transfers between devices, partner_swap(): return jax.tree.map(lambda part: lax.ppermute(part, axis, pairs), value)  63.8 us
    ppermute x15, starting transfers between devices, partner_swap(): return jax.tree.map(lambda part: lax.ppermute(part, axis, pairs), value)  22.9 us
    all_to_all x1, starting transfers between devices, per_device(): lax.all_to_all(jnp.take(states, send_slot, axis=0), 'req', 0, 0, tiled=True)  11.2 us
    all_to_all x1, starting transfers between devices, per_device(): lax.all_to_all(jnp.take(cache, send_slot, axis=0), 'req', 0, 0, tiled=True)  10 us
    gather x1, local copies, waits for them, and re-layouts, per_device(): jnp.take(got_cache, arrive_from, axis=0)  3.55 us
  transfers between devices with their start and end apart: 17, of which 16 were waited for; matrix products, arithmetic and copies ran while one was open for 20% of the time, Pallas kernels for 0%

profile of v3, /device:TPU:32, one launch (start us, length us, event | category | flops | bytes accessed | tf_op | source)
XLA Modules:
  0.0 170.7 jit_solution(2614065160251861100)
XLA Ops:
  4.0 11.2 %all-to-all-start = ((bf16[32,4,256]{2,1,0:T(4,128)(2,1)}), bf16[32,4,256]{2,1,0:T(4,128)(2,1)S(1)}, u32[]{:S(2)}, u32[]{:S(2)}) async-start(bf16[32,4,256]{2,1,0:T(4,128)(2,1)} %broadcast_select_fusion.2), calls=%async_computation | async-start | bytes 131072 | tf_op jit(solution)/shard_map/all_to_all | solution.py:139
  22.3 3.2 %broadcast_select_fusion = bf16[32,128,256]{2,1,0:T(8,128)(2,1)} fusion(bf16[32,128,256]{2,1,0:T(8,128)(2,1)} %gather_fusion.5, pred[32]{0:T(512)(128)(4,1)S(1)} %compare_and_fusion.1), kind=kLoop, calls=%fused_computation.7 | loop fusion | flops 1048576 | bytes 4194336 | tf_op jit(solution)/shard_map/jit(_take)/select_n | solution.py:140
  28.6 10.0 %all-to-all-start.1 = ((bf16[32,128,256]{2,1,0:T(8,128)(2,1)}), bf16[32,128,256]{2,1,0:T(8,128)(2,1)}, u32[]{:S(2)}, u32[]{:S(2)}) async-start(bf16[32,128,256]{2,1,0:T(8,128)(2,1)} %broadcast_select_fusion), calls=%async_computation.1 | async-start | bytes 4194304 | tf_op jit(solution)/shard_map/all_to_all | solution.py:140
  49.7 4.5 %collective-permute-done = f32[24,1536]{1,0:T(8,128)S(1)} collective-permute-done((f32[24,1536]{1,0:T(8,128)}, f32[24,1536]{1,0:T(8,128)S(1)}, u32[]{:S(2)}, u32[]{:S(2)}) %collective-permute-start) | collective-permute-done | bytes 147488 | tf_op jit(solution)/shard_map/ppermute | solution.py:14
  55.8 3.0 %collective-permute-start.1 = (f32[24,1536]{1,0:T(8,128)}, f32[24,1536]{1,0:T(8,128)}, u32[]{:S(2)}, u32[]{:S(2)}) collective-permute-start(f32[24,1536]{1,0:T(8,128)} %add.316), channel_id=1, source_target_pairs={{0,3},{1,2},{2,1},{3,0},{4,7},{5,6},{6,5},{7,4},{8,11},{9,10},{10,... | collective-permute-start | bytes 442376 | tf_op jit(solution)/shard_map/ppermute | solution.py:14
  59.5 2.9 %collective-permute-done.1 = f32[24,1536]{1,0:T(8,128)} collective-permute-done((f32[24,1536]{1,0:T(8,128)}, f32[24,1536]{1,0:T(8,128)}, u32[]{:S(2)}, u32[]{:S(2)}) %collective-permute-start.1) | collective-permute-done | bytes 147488 | tf_op jit(solution)/shard_map/ppermute | solution.py:14
  64.8 4.6 %collective-permute-done.2 = f32[24,1536]{1,0:T(8,128)S(1)} collective-permute-done((f32[24,1536]{1,0:T(8,128)S(1)}, f32[24,1536]{1,0:T(8,128)S(1)}, u32[]{:S(2)}, u32[]{:S(2)}) %collective-permute-start.2) | collective-permute-done | bytes 147488 | tf_op jit(solution)/shard_map/ppermute | solution.py:14
  72.3 3.8 %collective-permute-done.3 = f32[24,1536]{1,0:T(8,128)S(1)} collective-permute-done((f32[24,1536]{1,0:T(8,128)S(1)}, f32[24,1536]{1,0:T(8,128)S(1)}, u32[]{:S(2)}, u32[]{:S(2)}) %collective-permute-start.3) | collective-permute-done | bytes 147488 | tf_op jit(solution)/shard_map/ppermute | solution.py:14
  76.2 3.1 %collective-permute-start.4 = (f32[24,1536]{1,0:T(8,128)S(1)}, f32[24,1536]{1,0:T(8,128)S(1)}, u32[]{:S(2)}, u32[]{:S(2)}) collective-permute-start(f32[24,1536]{1,0:T(8,128)S(1)} %add.329), channel_id=1, source_target_pairs={{0,3},{1,2},{2,1},{3,0},{4,7},{5,6},{6,5},{7,4},{8,11},{9,10},{10,... | collective-permute-start | bytes 442376 | tf_op jit(solution)/shard_map/ppermute | solution.py:14
  79.4 3.2 %collective-permute-done.4 = f32[24,1536]{1,0:T(8,128)S(1)} collective-permute-done((f32[24,1536]{1,0:T(8,128)S(1)}, f32[24,1536]{1,0:T(8,128)S(1)}, u32[]{:S(2)}, u32[]{:S(2)}) %collective-permute-start.4) | collective-permute-done | bytes 147488 | tf_op jit(solution)/shard_map/ppermute | solution.py:14
  83.6 4.3 %collective-permute-done.5 = f32[24,1536]{1,0:T(8,128)S(1)} collective-permute-done((f32[24,1536]{1,0:T(8,128)S(1)}, f32[24,1536]{1,0:T(8,128)S(1)}, u32[]{:S(2)}, u32[]{:S(2)}) %collective-permute-start.5) | collective-permute-done | bytes 147488 | tf_op jit(solution)/shard_map/ppermute | solution.py:14
  91.6 3.6 %gather_fusion.6 = bf16[24,128,256]{2,1,0:T(8,128)(2,1)} fusion(bf16[32,128,256]{2,1,0:T(8,128)(2,1)} %all-to-all-done.1, s32[1024]{0:T(1024)} %pad_clamp_fusion.1), kind=kCustom, calls=%fused_computation.6 | custom fusion | bytes 3145824 | tf_op jit(solution)/shard_map/jit(_take)/gather | solution.py:150
  95.2 2.8 %broadcast_select_fusion.1 = (bf16[24,128,256]{2,1,0:T(8,128)(2,1)}, bf16[24,128,256]{2,1,0:T(8,128)(2,1)S(1)}) fusion(pred[24,128]{1,0:T(8,128)(4,1)} %get-tuple-element.45, bf16[24,256]{1,0:T(8,128)(2,1)S(1)} %pad_maximum_fusion.7, bf16[24,128,256]{2,1,0:T(8,128)(2,1)S(1)} %copy-done.2, bf16[24,128,256]{2,1,0:T(8,128)(2,1)} %gather_fusion.6, ...), kind=kLoop, calls=%fused_computation.9 | loop fusion | flops 2359296 | bytes 6306864 | tf_op jit(solution)/shard_map/jit(_where)/select_n | solution.py:276
  103.8 7.0 %collective-permute-done.6 = f32[24,12,130]{2,0,1:T(8,128)S(1)} collective-permute-done((f32[24,12,130]{2,0,1:T(8,128)S(1)}, f32[24,12,130]{2,0,1:T(8,128)S(1)}, u32[]{:S(2)}, u32[]{:S(2)}) %collective-permute-start.6) | collective-permute-done | bytes 149792 | tf_op jit(solution)/shard_map/ppermute | solution.py:14
  112.1 3.1 %collective-permute-start.7 = (f32[24,12,130]{2,0,1:T(8,128)S(1)}, f32[24,12,130]{2,0,1:T(8,128)S(1)}, u32[]{:S(2)}, u32[]{:S(2)}) collective-permute-start(f32[24,12,130]{2,0,1:T(8,128)S(1)} %pad_maximum_fusion.1), channel_id=1, source_target_pairs={{0,3},{1,2},{2,1},{3,0},{4,7},{5,6},{6,5},{7,4},{8,11},{9,10},{10,... | collective-permute-start | bytes 449288 | tf_op jit(solution)/shard_map/ppermute | solution.py:14
  115.2 5.9 %collective-permute-done.7 = f32[24,12,130]{2,0,1:T(8,128)S(1)} collective-permute-done((f32[24,12,130]{2,0,1:T(8,128)S(1)}, f32[24,12,130]{2,0,1:T(8,128)S(1)}, u32[]{:S(2)}, u32[]{:S(2)}) %collective-permute-start.7) | collective-permute-done | bytes 149792 | tf_op jit(solution)/shard_map/ppermute | solution.py:14
  127.4 5.0 %collective-permute-done.8 = f32[24,12,130]{2,0,1:T(8,128)S(1)} collective-permute-done((f32[24,12,130]{2,0,1:T(8,128)}, f32[24,12,130]{2,0,1:T(8,128)S(1)}, u32[]{:S(2)}, u32[]{:S(2)}) %collective-permute-start.8) | collective-permute-done | bytes 149792 | tf_op jit(solution)/shard_map/ppermute | solution.py:14
  134.5 4.9 %collective-permute-done.9 = f32[24,1536]{1,0:T(8,128)S(1)} collective-permute-done((f32[24,1536]{1,0:T(8,128)S(1)}, f32[24,1536]{1,0:T(8,128)S(1)}, u32[]{:S(2)}, u32[]{:S(2)}) %collective-permute-start.9) | collective-permute-done | bytes 147488 | tf_op jit(solution)/shard_map/ppermute | solution.py:14
  139.4 3.0 %collective-permute-start.10 = (f32[24,1536]{1,0:T(8,128)S(1)}, f32[24,1536]{1,0:T(8,128)S(1)}, u32[]{:S(2)}, u32[]{:S(2)}) collective-permute-start(f32[24,1536]{1,0:T(8,128)S(1)} %add.342), channel_id=1, source_target_pairs={{0,3},{1,2},{2,1},{3,0},{4,7},{5,6},{6,5},{7,4},{8,11},{9,10},{10,... | collective-permute-start | bytes 442376 | tf_op jit(solution)/shard_map/ppermute | solution.py:14
  142.4 3.5 %collective-permute-done.10 = f32[24,1536]{1,0:T(8,128)S(1)} collective-permute-done((f32[24,1536]{1,0:T(8,128)S(1)}, f32[24,1536]{1,0:T(8,128)S(1)}, u32[]{:S(2)}, u32[]{:S(2)}) %collective-permute-start.10) | collective-permute-done | bytes 147488 | tf_op jit(solution)/shard_map/ppermute | solution.py:14
  146.5 4.5 %collective-permute-done.11 = f32[24,1536]{1,0:T(8,128)S(1)} collective-permute-done((f32[24,1536]{1,0:T(8,128)S(1)}, f32[24,1536]{1,0:T(8,128)S(1)}, u32[]{:S(2)}, u32[]{:S(2)}) %collective-permute-start.11) | collective-permute-done | bytes 147488 | tf_op jit(solution)/shard_map/ppermute | solution.py:14
  156.7 4.0 %collective-permute-done.12 = f32[24,4,192]{2,0,1:T(8,128)S(1)} collective-permute-done((f32[24,4,192]{2,0,1:T(8,128)S(1)}, f32[24,4,192]{2,0,1:T(8,128)S(1)}, u32[]{:S(2)}, u32[]{:S(2)}) %collective-permute-start.12) | collective-permute-done | bytes 73760 | tf_op jit(solution)/shard_map/ppermute | solution.py:14
  160.7 3.0 %collective-permute-start.13 = (f32[24,2,192]{2,0,1:T(8,128)S(1)}, f32[24,2,192]{2,0,1:T(8,128)S(1)}, u32[]{:S(2)}, u32[]{:S(2)}) collective-permute-start(f32[24,2,192]{2,0,1:T(8,128)S(1)} %slice_select_fusion), channel_id=1, source_target_pairs={{0,3},{1,2},{2,1},{3,0},{4,7},{5,6},{6,5},{7,4},{8,11},{9,10},{10,... | collective-permute-start | bytes 110600 | tf_op jit(solution)/shard_map/ppermute | solution.py:14
  166.9 3.2 %collective-permute-done.14 = f32[24,1,192]{2,0,1:T(8,128)S(1)} collective-permute-done((f32[24,1,192]{2,0,1:T(8,128)S(1)}, f32[24,1,192]{2,0,1:T(8,128)S(1)}, u32[]{:S(2)}, u32[]{:S(2)}) %collective-permute-start.14) | collective-permute-done | bytes 18464 | tf_op jit(solution)/shard_map/ppermute | solution.py:14
  (193 shorter events, 62.3 us)
Async XLA Ops:
  0.6 152.7 %copy-start = (bf16[576,1536]{1,0:T(8,128)(2,1)S(1)}, bf16[576,1536]{1,0:T(8,128)(2,1)}, u32[]{:S(2)}) copy-start(bf16[576,1536]{1,0:T(8,128)(2,1)} %param.47) | copy-start | bytes 5308420
  0.6 18.4 %copy-start.6 = (bf16[24,1536]{1,0:T(8,128)(2,1)S(1)}, bf16[24,1536]{1,0:T(8,128)(2,1)}, u32[]{:S(2)}) copy-start(bf16[24,1536]{1,0:T(8,128)(2,1)} %param.24) | copy-start | bytes 221188
  0.7 19.1 %copy-start.25 = (f32[256]{0:T(256)S(1)}, f32[256]{0:T(256)}, u32[]{:S(2)}) copy-start(f32[256]{0:T(256)} %param.38) | copy-start | bytes 3076
  0.7 19.7 %copy-start.2 = (bf16[24,128,256]{2,1,0:T(8,128)(2,1)S(1)}, bf16[24,128,256]{2,1,0:T(8,128)(2,1)}, u32[]{:S(2)}) copy-start(bf16[24,128,256]{2,1,0:T(8,128)(2,1)} %param.28) | copy-start | bytes 4718596
  4.0 24.5 %all-to-all-start = ((bf16[32,4,256]{2,1,0:T(4,128)(2,1)}), bf16[32,4,256]{2,1,0:T(4,128)(2,1)S(1)}, u32[]{:S(2)}, u32[]{:S(2)}) async-start(bf16[32,4,256]{2,1,0:T(4,128)(2,1)} %broadcast_select_fusion.2), calls=%async_computation | async-start | bytes 131072 | tf_op jit(solution)/shard_map/all_to_all | solution.py:139
  28.6 63.0 %all-to-all-start.1 = ((bf16[32,128,256]{2,1,0:T(8,128)(2,1)}), bf16[32,128,256]{2,1,0:T(8,128)(2,1)}, u32[]{:S(2)}, u32[]{:S(2)}) async-start(bf16[32,128,256]{2,1,0:T(8,128)(2,1)} %broadcast_select_fusion), calls=%async_computation.1 | async-start | bytes 4194304 | tf_op jit(solution)/shard_map/all_to_all | solution.py:140
  43.3 26.2 %copy-start.21 = (f32[1536]{0:T(1024)S(1)}, f32[1536]{0:T(1024)}, u32[]{:S(2)}) copy-start(f32[1536]{0:T(1024)} %param.40) | copy-start | bytes 18436
  48.1 6.1 %collective-permute-start = (f32[24,1536]{1,0:T(8,128)}, f32[24,1536]{1,0:T(8,128)S(1)}, u32[]{:S(2)}, u32[]{:S(2)}) collective-permute-start(f32[24,1536]{1,0:T(8,128)} %fusion.64), channel_id=1, source_target_pairs={{0,1},{1,0},{2,3},{3,2},{4,5},{5,4},{6,7},{7,6},{8,9},{9,8},{10,11... | collective-permute-start | bytes 442376 | tf_op jit(solution)/shard_map/ppermute | solution.py:14
  55.8 6.7 %collective-permute-start.1 = (f32[24,1536]{1,0:T(8,128)}, f32[24,1536]{1,0:T(8,128)}, u32[]{:S(2)}, u32[]{:S(2)}) collective-permute-start(f32[24,1536]{1,0:T(8,128)} %add.316), channel_id=1, source_target_pairs={{0,3},{1,2},{2,1},{3,0},{4,7},{5,6},{6,5},{7,4},{8,11},{9,10},{10,... | collective-permute-start | bytes 442376 | tf_op jit(solution)/shard_map/ppermute | solution.py:14
  63.4 5.9 %collective-permute-start.2 = (f32[24,1536]{1,0:T(8,128)S(1)}, f32[24,1536]{1,0:T(8,128)S(1)}, u32[]{:S(2)}, u32[]{:S(2)}) collective-permute-start(f32[24,1536]{1,0:T(8,128)S(1)} %add.317), channel_id=1, source_target_pairs={{0,4},{1,5},{2,6},{3,7},{4,0},{5,1},{6,2},{7,3},{8,12},{9,13},{10,... | collective-permute-start | bytes 442376 | tf_op jit(solution)/shard_map/ppermute | solution.py:14
  69.5 18.4 %copy-start.4 = (f32[24,1536]{1,0:T(8,128)}, f32[24,1536]{1,0:T(8,128)S(1)}, u32[]{:S(2)}) copy-start(f32[24,1536]{1,0:T(8,128)S(1)} %get-tuple-element.21) | copy-start | bytes 442372
  70.9 5.2 %collective-permute-start.3 = (f32[24,1536]{1,0:T(8,128)S(1)}, f32[24,1536]{1,0:T(8,128)S(1)}, u32[]{:S(2)}, u32[]{:S(2)}) collective-permute-start(f32[24,1536]{1,0:T(8,128)S(1)} %fusion.78), channel_id=1, source_target_pairs={{0,1},{1,0},{2,3},{3,2},{4,5},{5,4},{6,7},{7,6},{8,9},{9,8},{10,11... | collective-permute-start | bytes 442376 | tf_op jit(solution)/shard_map/ppermute | solution.py:14
  76.2 6.4 %collective-permute-start.4 = (f32[24,1536]{1,0:T(8,128)S(1)}, f32[24,1536]{1,0:T(8,128)S(1)}, u32[]{:S(2)}, u32[]{:S(2)}) collective-permute-start(f32[24,1536]{1,0:T(8,128)S(1)} %add.329), channel_id=1, source_target_pairs={{0,3},{1,2},{2,1},{3,0},{4,7},{5,6},{6,5},{7,4},{8,11},{9,10},{10,... | collective-permute-start | bytes 442376 | tf_op jit(solution)/shard_map/ppermute | solution.py:14
  82.6 5.3 %collective-permute-start.5 = (f32[24,1536]{1,0:T(8,128)S(1)}, f32[24,1536]{1,0:T(8,128)S(1)}, u32[]{:S(2)}, u32[]{:S(2)}) collective-permute-start(f32[24,1536]{1,0:T(8,128)S(1)} %add.330), channel_id=1, source_target_pairs={{0,4},{1,5},{2,6},{3,7},{4,0},{5,1},{6,2},{7,3},{8,12},{9,13},{10,... | collective-permute-start | bytes 442376 | tf_op jit(solution)/shard_map/ppermute | solution.py:14
  102.2 8.6 %collective-permute-start.6 = (f32[24,12,130]{2,0,1:T(8,128)S(1)}, f32[24,12,130]{2,0,1:T(8,128)S(1)}, u32[]{:S(2)}, u32[]{:S(2)}) collective-permute-start(f32[24,12,130]{2,0,1:T(8,128)S(1)} %pad_maximum_fusion), channel_id=1, source_target_pairs={{0,1},{1,0},{2,3},{3,2},{4,5},{5,4},{6,7},{7,6},{8,9},{9,8},{10,11... | collective-permute-start | bytes 449288 | tf_op jit(solution)/shard_map/ppermute | solution.py:14
  112.1 9.0 %collective-permute-start.7 = (f32[24,12,130]{2,0,1:T(8,128)S(1)}, f32[24,12,130]{2,0,1:T(8,128)S(1)}, u32[]{:S(2)}, u32[]{:S(2)}) collective-permute-start(f32[24,12,130]{2,0,1:T(8,128)S(1)} %pad_maximum_fusion.1), channel_id=1, source_target_pairs={{0,3},{1,2},{2,1},{3,0},{4,7},{5,6},{6,5},{7,4},{8,11},{9,10},{10,... | collective-permute-start | bytes 449288 | tf_op jit(solution)/shard_map/ppermute | solution.py:14
  125.4 7.0 %collective-permute-start.8 = (f32[24,12,130]{2,0,1:T(8,128)}, f32[24,12,130]{2,0,1:T(8,128)S(1)}, u32[]{:S(2)}, u32[]{:S(2)}) collective-permute-start(f32[24,12,130]{2,0,1:T(8,128)} %pad_maximum_fusion.2), channel_id=1, source_target_pairs={{0,4},{1,5},{2,6},{3,7},{4,0},{5,1},{6,2},{7,3},{8,12},{9,13},{10,... | collective-permute-start | bytes 449288 | tf_op jit(solution)/shard_map/ppermute | solution.py:14
  132.5 18.5 %copy-start.5 = (f32[24,1536]{1,0:T(8,128)S(1)}, f32[24,1536]{1,0:T(8,128)}, u32[]{:S(2)}) copy-start(f32[24,1536]{1,0:T(8,128)} %copy-done.4) | copy-start | bytes 442372
  134.1 5.2 %collective-permute-start.9 = (f32[24,1536]{1,0:T(8,128)S(1)}, f32[24,1536]{1,0:T(8,128)S(1)}, u32[]{:S(2)}, u32[]{:S(2)}) collective-permute-start(f32[24,1536]{1,0:T(8,128)S(1)} %fusion.76), channel_id=1, source_target_pairs={{0,1},{1,0},{2,3},{3,2},{4,5},{5,4},{6,7},{7,6},{8,9},{9,8},{10,11... | collective-permute-start | bytes 442376 | tf_op jit(solution)/shard_map/ppermute | solution.py:14
  139.4 6.4 %collective-permute-start.10 = (f32[24,1536]{1,0:T(8,128)S(1)}, f32[24,1536]{1,0:T(8,128)S(1)}, u32[]{:S(2)}, u32[]{:S(2)}) collective-permute-start(f32[24,1536]{1,0:T(8,128)S(1)} %add.342), channel_id=1, source_target_pairs={{0,3},{1,2},{2,1},{3,0},{4,7},{5,6},{6,5},{7,4},{8,11},{9,10},{10,... | collective-permute-start | bytes 442376 | tf_op jit(solution)/shard_map/ppermute | solution.py:14
  145.8 5.2 %collective-permute-start.11 = (f32[24,1536]{1,0:T(8,128)S(1)}, f32[24,1536]{1,0:T(8,128)S(1)}, u32[]{:S(2)}, u32[]{:S(2)}) collective-permute-start(f32[24,1536]{1,0:T(8,128)S(1)} %add.343), channel_id=1, source_target_pairs={{0,4},{1,5},{2,6},{3,7},{4,0},{5,1},{6,2},{7,3},{8,12},{9,13},{10,... | collective-permute-start | bytes 442376 | tf_op jit(solution)/shard_map/ppermute | solution.py:14
  156.0 4.7 %collective-permute-start.12 = (f32[24,4,192]{2,0,1:T(8,128)S(1)}, f32[24,4,192]{2,0,1:T(8,128)S(1)}, u32[]{:S(2)}, u32[]{:S(2)}) collective-permute-start(f32[24,4,192]{2,0,1:T(8,128)S(1)} %copy_select_fusion), channel_id=1, source_target_pairs={{0,4},{1,5},{2,6},{3,7},{4,0},{5,1},{6,2},{7,3},{8,12},{9,13},{10,... | collective-permute-start | bytes 221192 | tf_op jit(solution)/shard_map/ppermute | solution.py:14
  160.7 5.4 %collective-permute-start.13 = (f32[24,2,192]{2,0,1:T(8,128)S(1)}, f32[24,2,192]{2,0,1:T(8,128)S(1)}, u32[]{:S(2)}, u32[]{:S(2)}) collective-permute-start(f32[24,2,192]{2,0,1:T(8,128)S(1)} %slice_select_fusion), channel_id=1, source_target_pairs={{0,3},{1,2},{2,1},{3,0},{4,7},{5,6},{6,5},{7,4},{8,11},{9,10},{10,... | collective-permute-start | bytes 110600 | tf_op jit(solution)/shard_map/ppermute | solution.py:14
  166.2 3.9 %collective-permute-start.14 = (f32[24,1,192]{2,0,1:T(8,128)S(1)}, f32[24,1,192]{2,0,1:T(8,128)S(1)}, u32[]{:S(2)}, u32[]{:S(2)}) collective-permute-start(f32[24,1,192]{2,0,1:T(8,128)S(1)} %slice_select_fusion.1), channel_id=1, source_target_pairs={{0,1},{1,0},{2,3},{3,2},{4,5},{5,4},{6,7},{7,6},{8,9},{9,8},{10,11... | collective-permute-start | bytes 55304 | tf_op jit(solution)/shard_map/ppermute | solution.py:14
  (20 other events, 182.0 us)

commit v4 on v3

--- a/solution.py
+++ b/solution.py
@@ -50,7 +50,7 @@
         mine_upper = (me & bit) != 0
         keep = jnp.where(mine_upper, upper, lower)
         send = jnp.where(mine_upper, lower, upper)
-        held = keep + partner_swap(send, axis, mask)
+        held = keep + partner_swap(send.astype(jnp.bfloat16), axis, mask).astype(jnp.float32)
     return held.reshape(rows, cols // size)
 
 
@@ -74,25 +74,36 @@
 
 
 def combine_parts(first_part, second_part):
-    head_size = first_part.shape[-1] - 2
-    first_top, first_sum = first_part[..., head_size], first_part[..., head_size + 1]
-    second_top, second_sum = second_part[..., head_size], second_part[..., head_size + 1]
+    width = first_part.shape[-1] - 128
+    heads = width // 128
+    first_top, first_sum = first_part[:, width : width + heads], first_part[:, width + heads : width + 2 * heads]
+    second_top = second_part[:, width : width + heads]
+    second_sum = second_part[:, width + heads : width + 2 * heads]
     larger = jnp.maximum(first_top, second_top)
     first_factor = jnp.exp(first_top - larger)
     second_factor = jnp.exp(second_top - larger)
-    return jnp.concatenate(
-        [
-            first_part[..., :head_size] * first_factor[..., None]
-            + second_part[..., :head_size] * second_factor[..., None],
-            larger[..., None],
-            (first_sum * first_factor + second_sum * second_factor)[..., None],
-        ],
+    rows = first_part.shape[0]
+    head_size = width // heads
+    acc = (
+        first_part[:, :width].reshape(rows, heads, head_size) * first_factor[..., None]
+        + second_part[:, :width].reshape(rows, heads, head_size) * second_factor[..., None]
+    )
+    stats = jnp.concatenate(
+        [larger, first_sum * first_factor + second_sum * second_factor, first_part[:, width + 2 * heads :]],
         axis=-1,
     )
+    return jnp.concatenate([acc.reshape(rows, width), stats], axis=-1)
 
 
 def across_mlp(partial_value):
     return joined(partial_value, "mlp", lambda first, second: first + second)
+
+
+def across_mlp_narrow(partial_value):
+    for mask, _ in axis_stages("mlp"):
+        sent = partner_swap(partial_value.astype(jnp.bfloat16), "mlp", mask)
+        partial_value = partial_value + sent.astype(jnp.float32)
+    return partial_value
 
 
 def per_device(
@@ -230,14 +241,17 @@
         moved_cache[..., head_size:],
         preferred_element_type=jnp.float32,
     )
+    stat_pad = jnp.zeros((req_rows, 128 - 2 * heads), jnp.float32)
     merged = joined(
-        jnp.concatenate([local_acc, local_top[..., None], local_sum[..., None]], axis=-1),
+        jnp.concatenate(
+            [local_acc.reshape(req_rows, width), local_top, local_sum, stat_pad], axis=-1
+        ),
         "mlp",
         combine_parts,
     )
-    merged_acc = merged[..., :head_size]
-    merged_top = merged[..., head_size]
-    merged_sum = merged[..., head_size + 1]
+    merged_acc = merged[:, :width].reshape(req_rows, heads, head_size)
+    merged_top = merged[:, width : width + heads]
+    merged_sum = merged[:, width + heads : width + 2 * heads]
     own_score = (
         jnp.sum(queries.astype(jnp.float32) * key_new.astype(jnp.float32)[:, None, :], axis=-1)
         * score_scale
@@ -257,7 +271,7 @@
         w_attn_out,
         preferred_element_type=jnp.float32,
     )
-    resid_two = resid_one + across_mlp(attn_part)
+    resid_two = resid_one + across_mlp_narrow(attn_part)
     normed_mlp = rms_norm(resid_two, gain_mlp)
     gate_act = jax.nn.gelu(
         jnp.dot(normed_mlp, w_gate, preferred_element_type=jnp.float32), approximate=True

time: 172 us -> 156 us (0.907)
  waiting for transfers between devices: 64.3 us -> 54.9 us
  local copies, waits for them, and re-layouts: 20 us -> 15 us
  other arithmetic: 27 us -> 25 us
    ppermute x15, waiting for transfers between devices: 63.8 us -> 54.3 us  [partner_swap(): return jax.tree.map(lambda part: lax.ppermute(part, axis, pairs), value)]
    unnamed x62 -> x52, local copies, waits for them, and re-layouts: 2.6 us -> 0.28 us
    concatenate x3 -> x0, other arithmetic: 2.07 us -> none  [the longest x2 1.96 us: combine_parts(): jnp.concatenate([first_part[..., :head_size] * first_factor[..., None] +...]
  transfers between devices with their start and end apart: 17 -> 17, of which waited for: 16 -> 16; matrix products, arithmetic and copies ran while one was open for 20% -> 22% of each run, Pallas kernels for 0% -> 0%
where the time goes in v4:
time: 156 us; the launch traced here: 154 us
  waiting for transfers between devices  54.9 us (35%)
  starting transfers between devices  44.5 us (29%)
  other arithmetic  25 us (16%)
  local copies, waits for them, and re-layouts  15 us (10%)
  matrix products  13.1 us (8%)
    ppermute x15, waiting for transfers between devices, partner_swap(): return jax.tree.map(lambda part: lax.ppermute(part, axis, pairs), value)  54.3 us
    ppermute x15, starting transfers between devices, partner_swap(): return jax.tree.map(lambda part: lax.ppermute(part, axis, pairs), value)  23.3 us
    all_to_all x1, starting transfers between devices, per_device(): lax.all_to_all(jnp.take(states, send_slot, axis=0), 'req', 0, 0, tiled=True)  11.2 us
    all_to_all x1, starting transfers between devices, per_device(): lax.all_to_all(jnp.take(cache, send_slot, axis=0), 'req', 0, 0, tiled=True)  10 us
    gather x1, local copies, waits for them, and re-layouts, per_device(): jnp.take(got_cache, arrive_from, axis=0)  3.55 us
    add x5, other arithmetic, across_mlp(): return joined(partial_value, 'mlp', lambda first, second: first + second)  3.31 us
    select_n x1, other arithmetic, per_device(): jnp.take(cache, send_slot, axis=0)  3.16 us
  transfers between devices with their start and end apart: 17, of which 16 were waited for; matrix products, arithmetic and copies ran while one was open for 22% of the time, Pallas kernels for 0%

profile of v4, /device:TPU:32, one launch (start us, length us, event | category | flops | bytes accessed | tf_op | source)
XLA Modules:
  0.0 153.6 jit_solution(10505713367559802844)
XLA Ops:
  4.0 11.2 %all-to-all-start = ((bf16[32,4,256]{2,1,0:T(4,128)(2,1)}), bf16[32,4,256]{2,1,0:T(4,128)(2,1)S(1)}, u32[]{:S(2)}, u32[]{:S(2)}) async-start(bf16[32,4,256]{2,1,0:T(4,128)(2,1)} %broadcast_select_fusion.2), calls=%async_computation | async-start | bytes 131072 | tf_op jit(solution)/shard_map/all_to_all | solution.py:150
  22.3 3.2 %broadcast_select_fusion = bf16[32,128,256]{2,1,0:T(8,128)(2,1)} fusion(bf16[32,128,256]{2,1,0:T(8,128)(2,1)} %gather_fusion.5, pred[32]{0:T(512)(128)(4,1)S(1)} %compare_and_fusion.1), kind=kLoop, calls=%fused_computation.7 | loop fusion | flops 1048576 | bytes 4194336 | tf_op jit(solution)/shard_map/jit(_take)/select_n | solution.py:151
  28.5 10.0 %all-to-all-start.1 = ((bf16[32,128,256]{2,1,0:T(8,128)(2,1)}), bf16[32,128,256]{2,1,0:T(8,128)(2,1)}, u32[]{:S(2)}, u32[]{:S(2)}) async-start(bf16[32,128,256]{2,1,0:T(8,128)(2,1)} %broadcast_select_fusion), calls=%async_computation.1 | async-start | bytes 4194304 | tf_op jit(solution)/shard_map/all_to_all | solution.py:151
  45.3 2.7 %fusion.59 = f32[24,1536]{1,0:T(8,128)} fusion(bf16[256,1536]{1,0:T(8,128)(2,1)} %param.39, f32[24,256]{1,0:T(8,128)S(1)} %get-tuple-element.5, bf16[1536,256]{1,0:T(8,128)(2,1)} %param.33, bf16[24,1536]{1,0:T(8,128)(2,1)S(1)} %copy-done.5, f32[1536]{0:T(1024)S(1)} %copy-done.17, f32[24]{0:T(128)} %add_rsqrt_fusion.2), kind=kOutput, calls=%fused_computation.118 | convolution fusion | flops 37957632 | bytes 1824864 | tf_op jit(solution)/shard_map/dot_general | solution.py:203
  49.6 4.5 %collective-permute-done = f32[24,1536]{1,0:T(8,128)S(1)} collective-permute-done((f32[24,1536]{1,0:T(8,128)}, f32[24,1536]{1,0:T(8,128)S(1)}, u32[]{:S(2)}, u32[]{:S(2)}) %collective-permute-start) | collective-permute-done | bytes 147488 | tf_op jit(solution)/shard_map/ppermute | solution.py:14
  55.7 3.0 %collective-permute-start.1 = (f32[24,1536]{1,0:T(8,128)}, f32[24,1536]{1,0:T(8,128)}, u32[]{:S(2)}, u32[]{:S(2)}) collective-permute-start(f32[24,1536]{1,0:T(8,128)} %add.309), channel_id=1, source_target_pairs={{0,3},{1,2},{2,1},{3,0},{4,7},{5,6},{6,5},{7,4},{8,11},{9,10},{10,... | collective-permute-start | bytes 442376 | tf_op jit(solution)/shard_map/ppermute | solution.py:14
  59.5 2.9 %collective-permute-done.1 = f32[24,1536]{1,0:T(8,128)} collective-permute-done((f32[24,1536]{1,0:T(8,128)}, f32[24,1536]{1,0:T(8,128)}, u32[]{:S(2)}, u32[]{:S(2)}) %collective-permute-start.1) | collective-permute-done | bytes 147488 | tf_op jit(solution)/shard_map/ppermute | solution.py:14
  64.7 4.6 %collective-permute-done.2 = f32[24,1536]{1,0:T(8,128)S(1)} collective-permute-done((f32[24,1536]{1,0:T(8,128)S(1)}, f32[24,1536]{1,0:T(8,128)S(1)}, u32[]{:S(2)}, u32[]{:S(2)}) %collective-permute-start.2) | collective-permute-done | bytes 147488 | tf_op jit(solution)/shard_map/ppermute | solution.py:14
  72.3 3.8 %collective-permute-done.3 = f32[24,1536]{1,0:T(8,128)S(1)} collective-permute-done((f32[24,1536]{1,0:T(8,128)S(1)}, f32[24,1536]{1,0:T(8,128)S(1)}, u32[]{:S(2)}, u32[]{:S(2)}) %collective-permute-start.3) | collective-permute-done | bytes 147488 | tf_op jit(solution)/shard_map/ppermute | solution.py:14
  76.1 3.1 %collective-permute-start.4 = (f32[24,1536]{1,0:T(8,128)S(1)}, f32[24,1536]{1,0:T(8,128)S(1)}, u32[]{:S(2)}, u32[]{:S(2)}) collective-permute-start(f32[24,1536]{1,0:T(8,128)S(1)} %add.322), channel_id=1, source_target_pairs={{0,3},{1,2},{2,1},{3,0},{4,7},{5,6},{6,5},{7,4},{8,11},{9,10},{10,... | collective-permute-start | bytes 442376 | tf_op jit(solution)/shard_map/ppermute | solution.py:14
  79.4 3.2 %collective-permute-done.4 = f32[24,1536]{1,0:T(8,128)S(1)} collective-permute-done((f32[24,1536]{1,0:T(8,128)S(1)}, f32[24,1536]{1,0:T(8,128)S(1)}, u32[]{:S(2)}, u32[]{:S(2)}) %collective-permute-start.4) | collective-permute-done | bytes 147488 | tf_op jit(solution)/shard_map/ppermute | solution.py:14
  83.6 4.3 %collective-permute-done.5 = f32[24,1536]{1,0:T(8,128)S(1)} collective-permute-done((f32[24,1536]{1,0:T(8,128)S(1)}, f32[24,1536]{1,0:T(8,128)S(1)}, u32[]{:S(2)}, u32[]{:S(2)}) %collective-permute-start.5) | collective-permute-done | bytes 147488 | tf_op jit(solution)/shard_map/ppermute | solution.py:14
  91.6 3.6 %gather_fusion.6 = bf16[24,128,256]{2,1,0:T(8,128)(2,1)} fusion(bf16[32,128,256]{2,1,0:T(8,128)(2,1)} %all-to-all-done.1, s32[1024]{0:T(1024)} %pad_clamp_fusion.1), kind=kCustom, calls=%fused_computation.6 | custom fusion | bytes 3145824 | tf_op jit(solution)/shard_map/jit(_take)/gather | solution.py:161
  95.1 2.8 %broadcast_select_fusion.1 = (bf16[24,128,256]{2,1,0:T(8,128)(2,1)}, bf16[24,128,256]{2,1,0:T(8,128)(2,1)S(1)}) fusion(pred[24,128]{1,0:T(8,128)(4,1)} %get-tuple-element.37, bf16[24,256]{1,0:T(8,128)(2,1)S(1)} %pad_maximum_fusion.4, bf16[24,128,256]{2,1,0:T(8,128)(2,1)S(1)} %copy-done.2, bf16[24,128,256]{2,1,0:T(8,128)(2,1)} %gather_fusion.6, ...), kind=kLoop, calls=%fused_computation.9 | loop fusion | flops 2359296 | bytes 6306864 | tf_op jit(solution)/shard_map/jit(_where)/select_n | solution.py:290
  100.9 4.1 %collective-permute-done.6 = f32[24,1664]{1,0:T(8,128)S(1)} collective-permute-done((f32[24,1664]{1,0:T(8,128)S(1)}, f32[24,1664]{1,0:T(8,128)S(1)}, u32[]{:S(2)}, u32[]{:S(2)}) %collective-permute-start.6) | collective-permute-done | bytes 159776 | tf_op jit(solution)/shard_map/ppermute | solution.py:14
  105.4 3.0 %collective-permute-start.7 = (f32[24,1664]{1,0:T(8,128)S(1)}, f32[24,1664]{1,0:T(8,128)S(1)}, u32[]{:S(2)}, u32[]{:S(2)}) collective-permute-start(f32[24,1664]{1,0:T(8,128)S(1)} %concatenate.43), channel_id=1, source_target_pairs={{0,3},{1,2},{2,1},{3,0},{4,7},{5,6},{6,5},{7,4},{8,11},{9,10},{10,... | collective-permute-start | bytes 479240 | tf_op jit(solution)/shard_map/ppermute | solution.py:14
  108.5 3.5 %collective-permute-done.7 = f32[24,1664]{1,0:T(8,128)S(1)} collective-permute-done((f32[24,1664]{1,0:T(8,128)S(1)}, f32[24,1664]{1,0:T(8,128)S(1)}, u32[]{:S(2)}, u32[]{:S(2)}) %collective-permute-start.7) | collective-permute-done | bytes 159776 | tf_op jit(solution)/shard_map/ppermute | solution.py:14
  114.0 4.6 %collective-permute-done.8 = f32[24,1664]{1,0:T(8,128)S(1)} collective-permute-done((f32[24,1664]{1,0:T(8,128)}, f32[24,1664]{1,0:T(8,128)S(1)}, u32[]{:S(2)}, u32[]{:S(2)}) %collective-permute-start.8) | collective-permute-done | bytes 159776 | tf_op jit(solution)/shard_map/ppermute | solution.py:14
  120.7 4.0 %collective-permute-done.9 = bf16[24,1536]{1,0:T(8,128)(2,1)S(1)} collective-permute-done((bf16[24,1536]{1,0:T(8,128)(2,1)S(1)}, bf16[24,1536]{1,0:T(8,128)(2,1)S(1)}, u32[]{:S(2)}, u32[]{:S(2)}) %collective-permute-start.9) | collective-permute-done | bytes 73760 | tf_op jit(solution)/shard_map/ppermute | solution.py:14
  124.7 3.1 %collective-permute-start.10 = (bf16[24,1536]{1,0:T(8,128)(2,1)S(1)}, bf16[24,1536]{1,0:T(8,128)(2,1)S(1)}, u32[]{:S(2)}, u32[]{:S(2)}) collective-permute-start(bf16[24,1536]{1,0:T(8,128)(2,1)S(1)} %fusion.11), channel_id=1, source_target_pairs={{0,3},{1,2},{2,1},{3,0},{4,7},{5,6},{6,5},{7,4},{8,11},{9,10},{10,... | collective-permute-start | bytes 221192 | tf_op jit(solution)/shard_map/ppermute | solution.py:14
  131.1 3.8 %collective-permute-done.11 = bf16[24,1536]{1,0:T(8,128)(2,1)S(1)} collective-permute-done((bf16[24,1536]{1,0:T(8,128)(2,1)S(1)}, bf16[24,1536]{1,0:T(8,128)(2,1)S(1)}, u32[]{:S(2)}, u32[]{:S(2)}) %collective-permute-start.11) | collective-permute-done | bytes 73760 | tf_op jit(solution)/shard_map/ppermute | solution.py:14
  140.4 3.5 %collective-permute-done.12 = bf16[24,4,192]{2,0,1:T(8,128)(2,1)S(1)} collective-permute-done((bf16[24,4,192]{2,0,1:T(8,128)(2,1)S(1)}, bf16[24,4,192]{2,0,1:T(8,128)(2,1)S(1)}, u32[]{:S(2)}, u32[]{:S(2)}) %collective-permute-start.12) | collective-permute-done | bytes 36896 | tf_op jit(solution)/shard_map/ppermute | solution.py:14
  144.0 3.1 %collective-permute-start.13 = (bf16[24,2,192]{2,0,1:T(8,128)(2,1)S(1)}, bf16[24,2,192]{2,0,1:T(8,128)(2,1)S(1)}, u32[]{:S(2)}, u32[]{:S(2)}) collective-permute-start(bf16[24,2,192]{2,0,1:T(8,128)(2,1)S(1)} %select_convert_fusion.1), channel_id=1, source_target_pairs={{0,3},{1,2},{2,1},{3,0},{4,7},{5,6},{6,5},{7,4},{8,11},{9,10},{10,... | collective-permute-start | bytes 55304 | tf_op jit(solution)/shard_map/ppermute | solution.py:14
  149.9 3.0 %collective-permute-done.14 = bf16[24,1,192]{2,0,1:T(8,128)(2,1)S(1)} collective-permute-done((bf16[24,1,192]{2,0,1:T(8,128)(2,1)S(1)}, bf16[24,1,192]{2,0,1:T(8,128)(2,1)S(1)}, u32[]{:S(2)}, u32[]{:S(2)}) %collective-permute-start.14) | collective-permute-done | bytes 9248 | tf_op jit(solution)/shard_map/ppermute | solution.py:14
  (164 shorter events, 54.0 us)
Async XLA Ops:
  0.6 136.4 %copy-start = (bf16[576,1536]{1,0:T(8,128)(2,1)S(1)}, bf16[576,1536]{1,0:T(8,128)(2,1)}, u32[]{:S(2)}) copy-start(bf16[576,1536]{1,0:T(8,128)(2,1)} %param.47) | copy-start | bytes 5308420
  0.6 18.4 %copy-start.5 = (bf16[24,1536]{1,0:T(8,128)(2,1)S(1)}, bf16[24,1536]{1,0:T(8,128)(2,1)}, u32[]{:S(2)}) copy-start(bf16[24,1536]{1,0:T(8,128)(2,1)} %param.24) | copy-start | bytes 221188
  0.7 19.1 %copy-start.23 = (f32[256]{0:T(256)S(1)}, f32[256]{0:T(256)}, u32[]{:S(2)}) copy-start(f32[256]{0:T(256)} %param.38) | copy-start | bytes 3076
  0.7 19.7 %copy-start.2 = (bf16[24,128,256]{2,1,0:T(8,128)(2,1)S(1)}, bf16[24,128,256]{2,1,0:T(8,128)(2,1)}, u32[]{:S(2)}) copy-start(bf16[24,128,256]{2,1,0:T(8,128)(2,1)} %param.28) | copy-start | bytes 4718596
  4.0 24.5 %all-to-all-start = ((bf16[32,4,256]{2,1,0:T(4,128)(2,1)}), bf16[32,4,256]{2,1,0:T(4,128)(2,1)S(1)}, u32[]{:S(2)}, u32[]{:S(2)}) async-start(bf16[32,4,256]{2,1,0:T(4,128)(2,1)} %broadcast_select_fusion.2), calls=%async_computation | async-start | bytes 131072 | tf_op jit(solution)/shard_map/all_to_all | solution.py:150
  28.5 63.0 %all-to-all-start.1 = ((bf16[32,128,256]{2,1,0:T(8,128)(2,1)}), bf16[32,128,256]{2,1,0:T(8,128)(2,1)}, u32[]{:S(2)}, u32[]{:S(2)}) async-start(bf16[32,128,256]{2,1,0:T(8,128)(2,1)} %broadcast_select_fusion), calls=%async_computation.1 | async-start | bytes 4194304 | tf_op jit(solution)/shard_map/all_to_all | solution.py:151
  43.3 26.2 %copy-start.19 = (f32[1536]{0:T(1024)S(1)}, f32[1536]{0:T(1024)}, u32[]{:S(2)}) copy-start(f32[1536]{0:T(1024)} %param.40) | copy-start | bytes 18436
  48.0 6.1 %collective-permute-start = (f32[24,1536]{1,0:T(8,128)}, f32[24,1536]{1,0:T(8,128)S(1)}, u32[]{:S(2)}, u32[]{:S(2)}) collective-permute-start(f32[24,1536]{1,0:T(8,128)} %fusion.59), channel_id=1, source_target_pairs={{0,1},{1,0},{2,3},{3,2},{4,5},{5,4},{6,7},{7,6},{8,9},{9,8},{10,11... | collective-permute-start | bytes 442376 | tf_op jit(solution)/shard_map/ppermute | solution.py:14
  55.7 6.7 %collective-permute-start.1 = (f32[24,1536]{1,0:T(8,128)}, f32[24,1536]{1,0:T(8,128)}, u32[]{:S(2)}, u32[]{:S(2)}) collective-permute-start(f32[24,1536]{1,0:T(8,128)} %add.309), channel_id=1, source_target_pairs={{0,3},{1,2},{2,1},{3,0},{4,7},{5,6},{6,5},{7,4},{8,11},{9,10},{10,... | collective-permute-start | bytes 442376 | tf_op jit(solution)/shard_map/ppermute | solution.py:14
  63.4 5.9 %collective-permute-start.2 = (f32[24,1536]{1,0:T(8,128)S(1)}, f32[24,1536]{1,0:T(8,128)S(1)}, u32[]{:S(2)}, u32[]{:S(2)}) collective-permute-start(f32[24,1536]{1,0:T(8,128)S(1)} %add.310), channel_id=1, source_target_pairs={{0,4},{1,5},{2,6},{3,7},{4,0},{5,1},{6,2},{7,3},{8,12},{9,13},{10,... | collective-permute-start | bytes 442376 | tf_op jit(solution)/shard_map/ppermute | solution.py:14
  69.5 18.4 %copy-start.3 = (f32[24,1536]{1,0:T(8,128)}, f32[24,1536]{1,0:T(8,128)S(1)}, u32[]{:S(2)}) copy-start(f32[24,1536]{1,0:T(8,128)S(1)} %get-tuple-element.26) | copy-start | bytes 442372
  70.9 5.2 %collective-permute-start.3 = (f32[24,1536]{1,0:T(8,128)S(1)}, f32[24,1536]{1,0:T(8,128)S(1)}, u32[]{:S(2)}, u32[]{:S(2)}) collective-permute-start(f32[24,1536]{1,0:T(8,128)S(1)} %fusion.80), channel_id=1, source_target_pairs={{0,1},{1,0},{2,3},{3,2},{4,5},{5,4},{6,7},{7,6},{8,9},{9,8},{10,11... | collective-permute-start | bytes 442376 | tf_op jit(solution)/shard_map/ppermute | solution.py:14
  76.1 6.4 %collective-permute-start.4 = (f32[24,1536]{1,0:T(8,128)S(1)}, f32[24,1536]{1,0:T(8,128)S(1)}, u32[]{:S(2)}, u32[]{:S(2)}) collective-permute-start(f32[24,1536]{1,0:T(8,128)S(1)} %add.322), channel_id=1, source_target_pairs={{0,3},{1,2},{2,1},{3,0},{4,7},{5,6},{6,5},{7,4},{8,11},{9,10},{10,... | collective-permute-start | bytes 442376 | tf_op jit(solution)/shard_map/ppermute | solution.py:14
  82.6 5.3 %collective-permute-start.5 = (f32[24,1536]{1,0:T(8,128)S(1)}, f32[24,1536]{1,0:T(8,128)S(1)}, u32[]{:S(2)}, u32[]{:S(2)}) collective-permute-start(f32[24,1536]{1,0:T(8,128)S(1)} %add.323), channel_id=1, source_target_pairs={{0,4},{1,5},{2,6},{3,7},{4,0},{5,1},{6,2},{7,3},{8,12},{9,13},{10,... | collective-permute-start | bytes 442376 | tf_op jit(solution)/shard_map/ppermute | solution.py:14
  99.3 5.7 %collective-permute-start.6 = (f32[24,1664]{1,0:T(8,128)S(1)}, f32[24,1664]{1,0:T(8,128)S(1)}, u32[]{:S(2)}, u32[]{:S(2)}) collective-permute-start(f32[24,1664]{1,0:T(8,128)S(1)} %concatenate.42), channel_id=1, source_target_pairs={{0,1},{1,0},{2,3},{3,2},{4,5},{5,4},{6,7},{7,6},{8,9},{9,8},{10,11... | collective-permute-start | bytes 479240 | tf_op jit(solution)/shard_map/ppermute | solution.py:14
  105.4 6.5 %collective-permute-start.7 = (f32[24,1664]{1,0:T(8,128)S(1)}, f32[24,1664]{1,0:T(8,128)S(1)}, u32[]{:S(2)}, u32[]{:S(2)}) collective-permute-start(f32[24,1664]{1,0:T(8,128)S(1)} %concatenate.43), channel_id=1, source_target_pairs={{0,3},{1,2},{2,1},{3,0},{4,7},{5,6},{6,5},{7,4},{8,11},{9,10},{10,... | collective-permute-start | bytes 479240 | tf_op jit(solution)/shard_map/ppermute | solution.py:14
  112.3 22.5 %copy-start.4 = (f32[24,1536]{1,0:T(8,128)S(1)}, f32[24,1536]{1,0:T(8,128)}, u32[]{:S(2)}) copy-start(f32[24,1536]{1,0:T(8,128)} %copy-done.3) | copy-start | bytes 442372
  113.1 5.5 %collective-permute-start.8 = (f32[24,1664]{1,0:T(8,128)}, f32[24,1664]{1,0:T(8,128)S(1)}, u32[]{:S(2)}, u32[]{:S(2)}) collective-permute-start(f32[24,1664]{1,0:T(8,128)} %concatenate.44), channel_id=1, source_target_pairs={{0,4},{1,5},{2,6},{3,7},{4,0},{5,1},{6,2},{7,3},{8,12},{9,13},{10,... | collective-permute-start | bytes 479240 | tf_op jit(solution)/shard_map/ppermute | solution.py:14
  120.0 4.6 %collective-permute-start.9 = (bf16[24,1536]{1,0:T(8,128)(2,1)S(1)}, bf16[24,1536]{1,0:T(8,128)(2,1)S(1)}, u32[]{:S(2)}, u32[]{:S(2)}) collective-permute-start(bf16[24,1536]{1,0:T(8,128)(2,1)S(1)} %get-tuple-element.48), channel_id=1, source_target_pairs={{0,1},{1,0},{2,3},{3,2},{4,5},{5,4},{6,7},{7,6},{8,9},{9,8},{10,11... | collective-permute-start | bytes 221192 | tf_op jit(solution)/shard_map/ppermute | solution.py:14
  124.7 5.7 %collective-permute-start.10 = (bf16[24,1536]{1,0:T(8,128)(2,1)S(1)}, bf16[24,1536]{1,0:T(8,128)(2,1)S(1)}, u32[]{:S(2)}, u32[]{:S(2)}) collective-permute-start(bf16[24,1536]{1,0:T(8,128)(2,1)S(1)} %fusion.11), channel_id=1, source_target_pairs={{0,3},{1,2},{2,1},{3,0},{4,7},{5,6},{6,5},{7,4},{8,11},{9,10},{10,... | collective-permute-start | bytes 221192 | tf_op jit(solution)/shard_map/ppermute | solution.py:14
  130.4 4.4 %collective-permute-start.11 = (bf16[24,1536]{1,0:T(8,128)(2,1)S(1)}, bf16[24,1536]{1,0:T(8,128)(2,1)S(1)}, u32[]{:S(2)}, u32[]{:S(2)}) collective-permute-start(bf16[24,1536]{1,0:T(8,128)(2,1)S(1)} %fusion.24), channel_id=1, source_target_pairs={{0,4},{1,5},{2,6},{3,7},{4,0},{5,1},{6,2},{7,3},{8,12},{9,13},{10,... | collective-permute-start | bytes 221192 | tf_op jit(solution)/shard_map/ppermute | solution.py:14
  139.8 4.2 %collective-permute-start.12 = (bf16[24,4,192]{2,0,1:T(8,128)(2,1)S(1)}, bf16[24,4,192]{2,0,1:T(8,128)(2,1)S(1)}, u32[]{:S(2)}, u32[]{:S(2)}) collective-permute-start(bf16[24,4,192]{2,0,1:T(8,128)(2,1)S(1)} %select_convert_fusion), channel_id=1, source_target_pairs={{0,4},{1,5},{2,6},{3,7},{4,0},{5,1},{6,2},{7,3},{8,12},{9,13},{10,... | collective-permute-start | bytes 110600 | tf_op jit(solution)/shard_map/ppermute | solution.py:14
  144.0 5.1 %collective-permute-start.13 = (bf16[24,2,192]{2,0,1:T(8,128)(2,1)S(1)}, bf16[24,2,192]{2,0,1:T(8,128)(2,1)S(1)}, u32[]{:S(2)}, u32[]{:S(2)}) collective-permute-start(bf16[24,2,192]{2,0,1:T(8,128)(2,1)S(1)} %select_convert_fusion.1), channel_id=1, source_target_pairs={{0,3},{1,2},{2,1},{3,0},{4,7},{5,6},{6,5},{7,4},{8,11},{9,10},{10,... | collective-permute-start | bytes 55304 | tf_op jit(solution)/shard_map/ppermute | solution.py:14
  149.1 3.8 %collective-permute-start.14 = (bf16[24,1,192]{2,0,1:T(8,128)(2,1)S(1)}, bf16[24,1,192]{2,0,1:T(8,128)(2,1)S(1)}, u32[]{:S(2)}, u32[]{:S(2)}) collective-permute-start(bf16[24,1,192]{2,0,1:T(8,128)(2,1)S(1)} %select_convert_fusion.2), channel_id=1, source_target_pairs={{0,1},{1,0},{2,3},{3,2},{4,5},{5,4},{6,7},{7,6},{8,9},{9,8},{10,11... | collective-permute-start | bytes 27656 | tf_op jit(solution)/shard_map/ppermute | solution.py:14
  (18 other events, 173.0 us)

commit v5 on v4

--- a/solution.py
+++ b/solution.py
@@ -199,7 +199,7 @@
     lru_out = new_state.astype(jnp.bfloat16)
     conv_out = jnp.concatenate([moved_conv[:, 1:], branch_in[:, None, :]], axis=1)
     gated_rec = (new_state * branch).astype(jnp.bfloat16)
-    resid_one = inputs + across_mlp(
+    resid_one = inputs + across_mlp_narrow(
         jnp.dot(gated_rec, w_rec_out, preferred_element_type=jnp.float32)
     )
     head_size = w_keyval.shape[1] // 2
@@ -211,7 +211,7 @@
         w_query,
         preferred_element_type=jnp.float32,
     )
-    query_full = across_mlp(query_part)
+    query_full = across_mlp_narrow(query_part)
     where_pos = position.astype(jnp.float32)
     queries = rotate(query_full.reshape(req_rows, heads, head_size), where_pos).astype(jnp.bfloat16)
     key_value = jnp.dot(normed_att, w_keyval, preferred_element_type=jnp.float32)

time: 156 us -> 155 us (level)
  waiting for transfers between devices: 54.9 us -> 52.5 us
  other arithmetic: 25 us -> 27 us
    ppermute x15, waiting for transfers between devices: 54.3 us -> 47.9 us  [partner_swap(): return jax.tree.map(lambda part: lax.ppermute(part, axis, pairs), value)]
    all_to_all x1, waiting for transfers between devices: 0.54 us -> 4.6 us  [per_device(): lax.all_to_all(jnp.take(cache, send_slot, axis=0), 'req', 0, 0, tiled=True)]
    add x5 -> x1, other arithmetic: 3.31 us -> 0.7 us  [across_mlp_narrow(): partial_value = partial_value + sent.astype(jnp.float32)]
    convert_element_type x2 -> x6, other arithmetic: 0.05 us -> 2.53 us  [across_mlp_narrow(): sent = partner_swap(partial_value.astype(jnp.bfloat16), 'mlp', mask)]
  transfers between devices with their start and end apart: 17 -> 17, of which waited for: 16 -> 16; matrix products, arithmetic and copies ran while one was open for 22% -> 23% of each run, Pallas kernels for 0% -> 0%
where the time goes in v5:
time: 155 us; the launch traced here: 154 us
  waiting for transfers between devices  52.5 us (34%)
  starting transfers between devices  44.3 us (29%)
  other arithmetic  27 us (17%)
  local copies, waits for them, and re-layouts  14.5 us (9%)
  matrix products  14.2 us (9%)
    ppermute x15, waiting for transfers between devices, partner_swap(): return jax.tree.map(lambda part: lax.ppermute(part, axis, pairs), value)  47.9 us
    ppermute x15, starting transfers between devices, partner_swap(): return jax.tree.map(lambda part: lax.ppermute(part, axis, pairs), value)  23.1 us
    all_to_all x1, starting transfers between devices, per_device(): lax.all_to_all(jnp.take(states, send_slot, axis=0), 'req', 0, 0, tiled=True)  11.2 us
    all_to_all x1, starting transfers between devices, per_device(): lax.all_to_all(jnp.take(cache, send_slot, axis=0), 'req', 0, 0, tiled=True)  10 us
    all_to_all x1, waiting for transfers between devices, per_device(): lax.all_to_all(jnp.take(cache, send_slot, axis=0), 'req', 0, 0, tiled=True)  4.6 us
    gather x1, local copies, waits for them, and re-layouts, per_device(): jnp.take(got_cache, arrive_from, axis=0)  3.55 us
    select_n x1, other arithmetic, per_device(): jnp.take(cache, send_slot, axis=0)  3.18 us
  transfers between devices with their start and end apart: 17, of which 16 were waited for; matrix products, arithmetic and copies ran while one was open for 23% of the time, Pallas kernels for 0%

profile of v5, /device:TPU:32, one launch (start us, length us, event | category | flops | bytes accessed | tf_op | source)
XLA Modules:
  0.0 153.6 jit_solution(1459457484158975582)
XLA Ops:
  4.1 11.2 %all-to-all-start = ((bf16[32,4,256]{2,1,0:T(4,128)(2,1)}), bf16[32,4,256]{2,1,0:T(4,128)(2,1)S(1)}, u32[]{:S(2)}, u32[]{:S(2)}) async-start(bf16[32,4,256]{2,1,0:T(4,128)(2,1)} %broadcast_select_fusion.2), calls=%async_computation | async-start | bytes 131072 | tf_op jit(solution)/shard_map/all_to_all | solution.py:150
  23.7 3.2 %broadcast_select_fusion = bf16[32,128,256]{2,1,0:T(8,128)(2,1)} fusion(bf16[32,128,256]{2,1,0:T(8,128)(2,1)} %gather_fusion.5, pred[32]{0:T(512)(128)(4,1)S(1)} %compare_and_fusion.1), kind=kLoop, calls=%fused_computation.7 | loop fusion | flops 1048576 | bytes 4194336 | tf_op jit(solution)/shard_map/jit(_take)/select_n | solution.py:151
  28.6 10.0 %all-to-all-start.1 = ((bf16[32,128,256]{2,1,0:T(8,128)(2,1)}), bf16[32,128,256]{2,1,0:T(8,128)(2,1)}, u32[]{:S(2)}, u32[]{:S(2)}) async-start(bf16[32,128,256]{2,1,0:T(8,128)(2,1)} %broadcast_select_fusion), calls=%async_computation.1 | async-start | bytes 4194304 | tf_op jit(solution)/shard_map/all_to_all | solution.py:151
  45.3 2.7 %fusion.115 = (bf16[24,1536]{1,0:T(8,128)(2,1)}, f32[24,1536]{1,0:T(8,128)S(1)}) fusion(bf16[256,1536]{1,0:T(8,128)(2,1)} %param.39, f32[24,256]{1,0:T(8,128)S(1)} %get-tuple-element.5, bf16[1536,256]{1,0:T(8,128)(2,1)} %param.33, bf16[24,1536]{1,0:T(8,128)(2,1)} %param.24, f32[1536]{0:T(1024)} %param.31, f32[24]{0:T(128)} %add_rsqrt_fusion.2), kind=kOutput, calls=%fused_computation.231 | convolution fusion | flops 37994496 | bytes 1898592 | tf_op jit(solution)/shard_map/dot_general | solution.py:203
  53.6 3.1 %collective-permute-start.1 = (bf16[24,1536]{1,0:T(8,128)(2,1)S(1)}, bf16[24,1536]{1,0:T(8,128)(2,1)S(1)}, u32[]{:S(2)}, u32[]{:S(2)}) collective-permute-start(bf16[24,1536]{1,0:T(8,128)(2,1)S(1)} %fusion.11), channel_id=1, source_target_pairs={{0,3},{1,2},{2,1},{3,0},{4,7},{5,6},{6,5},{7,4},{8,11},{9,10},{10,... | collective-permute-start | bytes 221192 | tf_op jit(solution)/shard_map/ppermute | solution.py:14
  56.7 2.5 %collective-permute-done.1 = bf16[24,1536]{1,0:T(8,128)(2,1)S(1)} collective-permute-done((bf16[24,1536]{1,0:T(8,128)(2,1)S(1)}, bf16[24,1536]{1,0:T(8,128)(2,1)S(1)}, u32[]{:S(2)}, u32[]{:S(2)}) %collective-permute-start.1) | collective-permute-done | bytes 73760 | tf_op jit(solution)/shard_map/ppermute | solution.py:14
  62.7 3.7 %collective-permute-done.2 = bf16[24,1536]{1,0:T(8,128)(2,1)} collective-permute-done((bf16[24,1536]{1,0:T(8,128)(2,1)}, bf16[24,1536]{1,0:T(8,128)(2,1)}, u32[]{:S(2)}, u32[]{:S(2)}) %collective-permute-start.2) | collective-permute-done | bytes 73760 | tf_op jit(solution)/shard_map/ppermute | solution.py:14
  73.5 3.1 %collective-permute-start.4 = (bf16[24,1536]{1,0:T(8,128)(2,1)S(1)}, bf16[24,1536]{1,0:T(8,128)(2,1)S(1)}, u32[]{:S(2)}, u32[]{:S(2)}) collective-permute-start(bf16[24,1536]{1,0:T(8,128)(2,1)S(1)} %fusion.12), channel_id=1, source_target_pairs={{0,3},{1,2},{2,1},{3,0},{4,7},{5,6},{6,5},{7,4},{8,11},{9,10},{10,... | collective-permute-start | bytes 221192 | tf_op jit(solution)/shard_map/ppermute | solution.py:14
  80.0 3.8 %collective-permute-done.5 = bf16[24,1536]{1,0:T(8,128)(2,1)S(1)} collective-permute-done((bf16[24,1536]{1,0:T(8,128)(2,1)S(1)}, bf16[24,1536]{1,0:T(8,128)(2,1)S(1)}, u32[]{:S(2)}, u32[]{:S(2)}) %collective-permute-start.5) | collective-permute-done | bytes 73760 | tf_op jit(solution)/shard_map/ppermute | solution.py:14
  87.0 4.6 %all-to-all-done.1 = bf16[32,128,256]{2,1,0:T(8,128)(2,1)} async-done(((bf16[32,128,256]{2,1,0:T(8,128)(2,1)}), bf16[32,128,256]{2,1,0:T(8,128)(2,1)}, u32[]{:S(2)}, u32[]{:S(2)}) %all-to-all-start.1) | async-done | bytes 2097184 | tf_op jit(solution)/shard_map/all_to_all | solution.py:151
  91.6 3.6 %gather_fusion.6 = bf16[24,128,256]{2,1,0:T(8,128)(2,1)} fusion(bf16[32,128,256]{2,1,0:T(8,128)(2,1)} %all-to-all-done.1, s32[1024]{0:T(1024)} %pad_clamp_fusion.1), kind=kCustom, calls=%fused_computation.6 | custom fusion | bytes 3145824 | tf_op jit(solution)/shard_map/jit(_take)/gather | solution.py:161
  95.1 2.8 %broadcast_select_fusion.1 = (bf16[24,128,256]{2,1,0:T(8,128)(2,1)}, bf16[24,128,256]{2,1,0:T(8,128)(2,1)S(1)}) fusion(pred[24,128]{1,0:T(8,128)(4,1)} %get-tuple-element.37, bf16[24,256]{1,0:T(8,128)(2,1)S(1)} %pad_maximum_fusion.4, bf16[24,128,256]{2,1,0:T(8,128)(2,1)S(1)} %copy-done.2, bf16[24,128,256]{2,1,0:T(8,128)(2,1)} %gather_fusion.6, ...), kind=kLoop, calls=%fused_computation.9 | loop fusion | flops 2359296 | bytes 6306864 | tf_op jit(solution)/shard_map/jit(_where)/select_n | solution.py:290
  100.9 4.1 %collective-permute-done.6 = f32[24,1664]{1,0:T(8,128)S(1)} collective-permute-done((f32[24,1664]{1,0:T(8,128)S(1)}, f32[24,1664]{1,0:T(8,128)S(1)}, u32[]{:S(2)}, u32[]{:S(2)}) %collective-permute-start.6) | collective-permute-done | bytes 159776 | tf_op jit(solution)/shard_map/ppermute | solution.py:14
  105.4 3.0 %collective-permute-start.7 = (f32[24,1664]{1,0:T(8,128)S(1)}, f32[24,1664]{1,0:T(8,128)S(1)}, u32[]{:S(2)}, u32[]{:S(2)}) collective-permute-start(f32[24,1664]{1,0:T(8,128)S(1)} %concatenate.43), channel_id=1, source_target_pairs={{0,3},{1,2},{2,1},{3,0},{4,7},{5,6},{6,5},{7,4},{8,11},{9,10},{10,... | collective-permute-start | bytes 479240 | tf_op jit(solution)/shard_map/ppermute | solution.py:14
  108.5 3.5 %collective-permute-done.7 = f32[24,1664]{1,0:T(8,128)S(1)} collective-permute-done((f32[24,1664]{1,0:T(8,128)S(1)}, f32[24,1664]{1,0:T(8,128)S(1)}, u32[]{:S(2)}, u32[]{:S(2)}) %collective-permute-start.7) | collective-permute-done | bytes 159776 | tf_op jit(solution)/shard_map/ppermute | solution.py:14
  114.0 4.6 %collective-permute-done.8 = f32[24,1664]{1,0:T(8,128)S(1)} collective-permute-done((f32[24,1664]{1,0:T(8,128)}, f32[24,1664]{1,0:T(8,128)S(1)}, u32[]{:S(2)}, u32[]{:S(2)}) %collective-permute-start.8) | collective-permute-done | bytes 159776 | tf_op jit(solution)/shard_map/ppermute | solution.py:14
  120.7 4.0 %collective-permute-done.9 = bf16[24,1536]{1,0:T(8,128)(2,1)S(1)} collective-permute-done((bf16[24,1536]{1,0:T(8,128)(2,1)S(1)}, bf16[24,1536]{1,0:T(8,128)(2,1)S(1)}, u32[]{:S(2)}, u32[]{:S(2)}) %collective-permute-start.9) | collective-permute-done | bytes 73760 | tf_op jit(solution)/shard_map/ppermute | solution.py:14
  124.7 3.1 %collective-permute-start.10 = (bf16[24,1536]{1,0:T(8,128)(2,1)S(1)}, bf16[24,1536]{1,0:T(8,128)(2,1)S(1)}, u32[]{:S(2)}, u32[]{:S(2)}) collective-permute-start(bf16[24,1536]{1,0:T(8,128)(2,1)S(1)} %fusion.13), channel_id=1, source_target_pairs={{0,3},{1,2},{2,1},{3,0},{4,7},{5,6},{6,5},{7,4},{8,11},{9,10},{10,... | collective-permute-start | bytes 221192 | tf_op jit(solution)/shard_map/ppermute | solution.py:14
  127.8 2.5 %collective-permute-done.10 = bf16[24,1536]{1,0:T(8,128)(2,1)S(1)} collective-permute-done((bf16[24,1536]{1,0:T(8,128)(2,1)S(1)}, bf16[24,1536]{1,0:T(8,128)(2,1)S(1)}, u32[]{:S(2)}, u32[]{:S(2)}) %collective-permute-start.10) | collective-permute-done | bytes 73760 | tf_op jit(solution)/shard_map/ppermute | solution.py:14
  131.0 3.8 %collective-permute-done.11 = bf16[24,1536]{1,0:T(8,128)(2,1)S(1)} collective-permute-done((bf16[24,1536]{1,0:T(8,128)(2,1)S(1)}, bf16[24,1536]{1,0:T(8,128)(2,1)S(1)}, u32[]{:S(2)}, u32[]{:S(2)}) %collective-permute-start.11) | collective-permute-done | bytes 73760 | tf_op jit(solution)/shard_map/ppermute | solution.py:14
  137.1 2.5 %fusion.1 = f32[24,1536]{1,0:T(8,128)S(1)} fusion(bf16[576,1536]{1,0:T(8,128)(2,1)S(1)} %copy-done, bf16[1536,576]{0,1:T(8,128)(2,1)} %param.46, f32[24,576]{1,0:T(8,128)S(1)} %fusion.110, f32[24,1536]{1,0:T(8,128)S(1)} %get-tuple-element.9, f32[1536]{0:T(1024)S(1)} %copy-done.18, f32[24]{0:T(128)S(1)} %add_rsqrt_fusion), kind=kOutput, calls=%fused_computation.14 | convolution fusion | flops 85183488 | bytes 3895392 | tf_op jit(solution)/shard_map/dot_general | solution.py:282
  140.4 3.5 %collective-permute-done.12 = bf16[24,4,192]{2,0,1:T(8,128)(2,1)S(1)} collective-permute-done((bf16[24,4,192]{2,0,1:T(8,128)(2,1)S(1)}, bf16[24,4,192]{2,0,1:T(8,128)(2,1)S(1)}, u32[]{:S(2)}, u32[]{:S(2)}) %collective-permute-start.12) | collective-permute-done | bytes 36896 | tf_op jit(solution)/shard_map/ppermute | solution.py:14
  144.0 3.1 %collective-permute-start.13 = (bf16[24,2,192]{2,0,1:T(8,128)(2,1)S(1)}, bf16[24,2,192]{2,0,1:T(8,128)(2,1)S(1)}, u32[]{:S(2)}, u32[]{:S(2)}) collective-permute-start(bf16[24,2,192]{2,0,1:T(8,128)(2,1)S(1)} %select_convert_fusion.1), channel_id=1, source_target_pairs={{0,3},{1,2},{2,1},{3,0},{4,7},{5,6},{6,5},{7,4},{8,11},{9,10},{10,... | collective-permute-start | bytes 55304 | tf_op jit(solution)/shard_map/ppermute | solution.py:14
  149.9 3.0 %collective-permute-done.14 = bf16[24,1,192]{2,0,1:T(8,128)(2,1)S(1)} collective-permute-done((bf16[24,1,192]{2,0,1:T(8,128)(2,1)S(1)}, bf16[24,1,192]{2,0,1:T(8,128)(2,1)S(1)}, u32[]{:S(2)}, u32[]{:S(2)}) %collective-permute-start.14) | collective-permute-done | bytes 9248 | tf_op jit(solution)/shard_map/ppermute | solution.py:14
  (172 shorter events, 57.4 us)
Async XLA Ops:
  0.6 136.4 %copy-start = (bf16[576,1536]{1,0:T(8,128)(2,1)S(1)}, bf16[576,1536]{1,0:T(8,128)(2,1)}, u32[]{:S(2)}) copy-start(bf16[576,1536]{1,0:T(8,128)(2,1)} %param.47) | copy-start | bytes 5308420
  0.7 21.0 %copy-start.2 = (bf16[24,128,256]{2,1,0:T(8,128)(2,1)S(1)}, bf16[24,128,256]{2,1,0:T(8,128)(2,1)}, u32[]{:S(2)}) copy-start(bf16[24,128,256]{2,1,0:T(8,128)(2,1)} %param.28) | copy-start | bytes 4718596
  4.1 24.5 %all-to-all-start = ((bf16[32,4,256]{2,1,0:T(4,128)(2,1)}), bf16[32,4,256]{2,1,0:T(4,128)(2,1)S(1)}, u32[]{:S(2)}, u32[]{:S(2)}) async-start(bf16[32,4,256]{2,1,0:T(4,128)(2,1)} %broadcast_select_fusion.2), calls=%async_computation | async-start | bytes 131072 | tf_op jit(solution)/shard_map/all_to_all | solution.py:150
  28.6 63.0 %all-to-all-start.1 = ((bf16[32,128,256]{2,1,0:T(8,128)(2,1)}), bf16[32,128,256]{2,1,0:T(8,128)(2,1)}, u32[]{:S(2)}, u32[]{:S(2)}) async-start(bf16[32,128,256]{2,1,0:T(8,128)(2,1)} %broadcast_select_fusion), calls=%async_computation.1 | async-start | bytes 4194304 | tf_op jit(solution)/shard_map/all_to_all | solution.py:151
  40.2 21.8 %copy-start.24 = (s32[24]{0:T(128)S(1)}, s32[24]{0:T(128)}, u32[]{:S(2)}) copy-start(s32[24]{0:T(128)} %get-tuple-element.38) | copy-start | bytes 292
  40.2 21.8 %copy-start.25 = (s32[24]{0:T(128)S(1)}, s32[24]{0:T(128)}, u32[]{:S(2)}) copy-start(s32[24]{0:T(128)} %get-tuple-element.40) | copy-start | bytes 292
  40.2 21.8 %copy-start.26 = (s32[24]{0:T(128)S(1)}, s32[24]{0:T(128)}, u32[]{:S(2)}) copy-start(s32[24]{0:T(128)} %get-tuple-element.41) | copy-start | bytes 292
  43.3 24.3 %copy-start.19 = (f32[1536]{0:T(1024)S(1)}, f32[1536]{0:T(1024)}, u32[]{:S(2)}) copy-start(f32[1536]{0:T(1024)} %param.40) | copy-start | bytes 18436
  48.1 4.7 %collective-permute-start = (bf16[24,1536]{1,0:T(8,128)(2,1)}, bf16[24,1536]{1,0:T(8,128)(2,1)}, u32[]{:S(2)}, u32[]{:S(2)}) collective-permute-start(bf16[24,1536]{1,0:T(8,128)(2,1)} %get-tuple-element.46), channel_id=1, source_target_pairs={{0,1},{1,0},{2,3},{3,2},{4,5},{5,4},{6,7},{7,6},{8,9},{9,8},{10,11... | collective-permute-start | bytes 221192 | tf_op jit(solution)/shard_map/ppermute | solution.py:14
  53.6 5.7 %collective-permute-start.1 = (bf16[24,1536]{1,0:T(8,128)(2,1)S(1)}, bf16[24,1536]{1,0:T(8,128)(2,1)S(1)}, u32[]{:S(2)}, u32[]{:S(2)}) collective-permute-start(bf16[24,1536]{1,0:T(8,128)(2,1)S(1)} %fusion.11), channel_id=1, source_target_pairs={{0,3},{1,2},{2,1},{3,0},{4,7},{5,6},{6,5},{7,4},{8,11},{9,10},{10,... | collective-permute-start | bytes 221192 | tf_op jit(solution)/shard_map/ppermute | solution.py:14
  61.5 5.0 %collective-permute-start.2 = (bf16[24,1536]{1,0:T(8,128)(2,1)}, bf16[24,1536]{1,0:T(8,128)(2,1)}, u32[]{:S(2)}, u32[]{:S(2)}) collective-permute-start(bf16[24,1536]{1,0:T(8,128)(2,1)} %fusion.26), channel_id=1, source_target_pairs={{0,4},{1,5},{2,6},{3,7},{4,0},{5,1},{6,2},{7,3},{8,12},{9,13},{10,... | collective-permute-start | bytes 221192 | tf_op jit(solution)/shard_map/ppermute | solution.py:14
  69.0 4.4 %collective-permute-start.3 = (bf16[24,1536]{1,0:T(8,128)(2,1)S(1)}, bf16[24,1536]{1,0:T(8,128)(2,1)S(1)}, u32[]{:S(2)}, u32[]{:S(2)}) collective-permute-start(bf16[24,1536]{1,0:T(8,128)(2,1)S(1)} %get-tuple-element.48), channel_id=1, source_target_pairs={{0,1},{1,0},{2,3},{3,2},{4,5},{5,4},{6,7},{7,6},{8,9},{9,8},{10,11... | collective-permute-start | bytes 221192 | tf_op jit(solution)/shard_map/ppermute | solution.py:14
  73.5 5.7 %collective-permute-start.4 = (bf16[24,1536]{1,0:T(8,128)(2,1)S(1)}, bf16[24,1536]{1,0:T(8,128)(2,1)S(1)}, u32[]{:S(2)}, u32[]{:S(2)}) collective-permute-start(bf16[24,1536]{1,0:T(8,128)(2,1)S(1)} %fusion.12), channel_id=1, source_target_pairs={{0,3},{1,2},{2,1},{3,0},{4,7},{5,6},{6,5},{7,4},{8,11},{9,10},{10,... | collective-permute-start | bytes 221192 | tf_op jit(solution)/shard_map/ppermute | solution.py:14
  79.2 4.6 %collective-permute-start.5 = (bf16[24,1536]{1,0:T(8,128)(2,1)S(1)}, bf16[24,1536]{1,0:T(8,128)(2,1)S(1)}, u32[]{:S(2)}, u32[]{:S(2)}) collective-permute-start(bf16[24,1536]{1,0:T(8,128)(2,1)S(1)} %fusion.27), channel_id=1, source_target_pairs={{0,4},{1,5},{2,6},{3,7},{4,0},{5,1},{6,2},{7,3},{8,12},{9,13},{10,... | collective-permute-start | bytes 221192 | tf_op jit(solution)/shard_map/ppermute | solution.py:14
  99.3 5.7 %collective-permute-start.6 = (f32[24,1664]{1,0:T(8,128)S(1)}, f32[24,1664]{1,0:T(8,128)S(1)}, u32[]{:S(2)}, u32[]{:S(2)}) collective-permute-start(f32[24,1664]{1,0:T(8,128)S(1)} %concatenate.42), channel_id=1, source_target_pairs={{0,1},{1,0},{2,3},{3,2},{4,5},{5,4},{6,7},{7,6},{8,9},{9,8},{10,11... | collective-permute-start | bytes 479240 | tf_op jit(solution)/shard_map/ppermute | solution.py:14
  105.4 6.5 %collective-permute-start.7 = (f32[24,1664]{1,0:T(8,128)S(1)}, f32[24,1664]{1,0:T(8,128)S(1)}, u32[]{:S(2)}, u32[]{:S(2)}) collective-permute-start(f32[24,1664]{1,0:T(8,128)S(1)} %concatenate.43), channel_id=1, source_target_pairs={{0,3},{1,2},{2,1},{3,0},{4,7},{5,6},{6,5},{7,4},{8,11},{9,10},{10,... | collective-permute-start | bytes 479240 | tf_op jit(solution)/shard_map/ppermute | solution.py:14
  112.3 22.5 %copy-start.4 = (f32[24,1536]{1,0:T(8,128)S(1)}, f32[24,1536]{1,0:T(8,128)}, u32[]{:S(2)}) copy-start(f32[24,1536]{1,0:T(8,128)} %copy-done.3) | copy-start | bytes 442372
  113.1 5.5 %collective-permute-start.8 = (f32[24,1664]{1,0:T(8,128)}, f32[24,1664]{1,0:T(8,128)S(1)}, u32[]{:S(2)}, u32[]{:S(2)}) collective-permute-start(f32[24,1664]{1,0:T(8,128)} %concatenate.44), channel_id=1, source_target_pairs={{0,4},{1,5},{2,6},{3,7},{4,0},{5,1},{6,2},{7,3},{8,12},{9,13},{10,... | collective-permute-start | bytes 479240 | tf_op jit(solution)/shard_map/ppermute | solution.py:14
  120.0 4.6 %collective-permute-start.9 = (bf16[24,1536]{1,0:T(8,128)(2,1)S(1)}, bf16[24,1536]{1,0:T(8,128)(2,1)S(1)}, u32[]{:S(2)}, u32[]{:S(2)}) collective-permute-start(bf16[24,1536]{1,0:T(8,128)(2,1)S(1)} %get-tuple-element.52), channel_id=1, source_target_pairs={{0,1},{1,0},{2,3},{3,2},{4,5},{5,4},{6,7},{7,6},{8,9},{9,8},{10,11... | collective-permute-start | bytes 221192 | tf_op jit(solution)/shard_map/ppermute | solution.py:14
  124.7 5.7 %collective-permute-start.10 = (bf16[24,1536]{1,0:T(8,128)(2,1)S(1)}, bf16[24,1536]{1,0:T(8,128)(2,1)S(1)}, u32[]{:S(2)}, u32[]{:S(2)}) collective-permute-start(bf16[24,1536]{1,0:T(8,128)(2,1)S(1)} %fusion.13), channel_id=1, source_target_pairs={{0,3},{1,2},{2,1},{3,0},{4,7},{5,6},{6,5},{7,4},{8,11},{9,10},{10,... | collective-permute-start | bytes 221192 | tf_op jit(solution)/shard_map/ppermute | solution.py:14
  130.4 4.4 %collective-permute-start.11 = (bf16[24,1536]{1,0:T(8,128)(2,1)S(1)}, bf16[24,1536]{1,0:T(8,128)(2,1)S(1)}, u32[]{:S(2)}, u32[]{:S(2)}) collective-permute-start(bf16[24,1536]{1,0:T(8,128)(2,1)S(1)} %fusion.28), channel_id=1, source_target_pairs={{0,4},{1,5},{2,6},{3,7},{4,0},{5,1},{6,2},{7,3},{8,12},{9,13},{10,... | collective-permute-start | bytes 221192 | tf_op jit(solution)/shard_map/ppermute | solution.py:14
  139.8 4.2 %collective-permute-start.12 = (bf16[24,4,192]{2,0,1:T(8,128)(2,1)S(1)}, bf16[24,4,192]{2,0,1:T(8,128)(2,1)S(1)}, u32[]{:S(2)}, u32[]{:S(2)}) collective-permute-start(bf16[24,4,192]{2,0,1:T(8,128)(2,1)S(1)} %select_convert_fusion), channel_id=1, source_target_pairs={{0,4},{1,5},{2,6},{3,7},{4,0},{5,1},{6,2},{7,3},{8,12},{9,13},{10,... | collective-permute-start | bytes 110600 | tf_op jit(solution)/shard_map/ppermute | solution.py:14
  144.0 5.1 %collective-permute-start.13 = (bf16[24,2,192]{2,0,1:T(8,128)(2,1)S(1)}, bf16[24,2,192]{2,0,1:T(8,128)(2,1)S(1)}, u32[]{:S(2)}, u32[]{:S(2)}) collective-permute-start(bf16[24,2,192]{2,0,1:T(8,128)(2,1)S(1)} %select_convert_fusion.1), channel_id=1, source_target_pairs={{0,3},{1,2},{2,1},{3,0},{4,7},{5,6},{6,5},{7,4},{8,11},{9,10},{10,... | collective-permute-start | bytes 55304 | tf_op jit(solution)/shard_map/ppermute | solution.py:14
  149.1 3.8 %collective-permute-start.14 = (bf16[24,1,192]{2,0,1:T(8,128)(2,1)S(1)}, bf16[24,1,192]{2,0,1:T(8,128)(2,1)S(1)}, u32[]{:S(2)}, u32[]{:S(2)}) collective-permute-start(bf16[24,1,192]{2,0,1:T(8,128)(2,1)S(1)} %select_convert_fusion.2), channel_id=1, source_target_pairs={{0,1},{1,0},{2,3},{3,2},{4,5},{5,4},{6,7},{7,6},{8,9},{9,8},{10,11... | collective-permute-start | bytes 27656 | tf_op jit(solution)/shard_map/ppermute | solution.py:14
  (22 other events, 213.2 us)

commit v6 on v5

--- a/solution.py
+++ b/solution.py
@@ -146,8 +146,12 @@
     conv_rows = conv_state.shape[1]
     states = jnp.concatenate([conv_state, lru_state[:, None, :]], axis=1)
     to_group = owner[own_group][None, :] == group_ids[:, None]
+    rank_of_me = jnp.sum(jnp.where(owner == own_group, rank_ids[None, :], 0), axis=1)
     send_slot = jnp.sum(jnp.where(to_group, my_leave[None, :], 0), axis=1)
-    got_states = lax.all_to_all(jnp.take(states, send_slot, axis=0), "req", 0, 0, tiled=True)
+    leave_states = jnp.take(states, my_leave, axis=0)
+    leave_states = jnp.concatenate([leave_states, jnp.zeros_like(leave_states)], axis=1)
+    all_states = lax.all_gather(leave_states, "req", axis=0, tiled=True)[:, : conv_rows + 1]
+    got_states = jnp.take(all_states, group_ids * leavers + rank_of_me, axis=0)
     got_cache = lax.all_to_all(jnp.take(cache, send_slot, axis=0), "req", 0, 0, tiled=True)
     local_ids = jnp.arange(req_rows, dtype=jnp.int32)
     match_slot = my_leave[None, :] == local_ids[:, None]

time: 155 us -> 216 us (1.39)
  waiting for transfers between devices: 52.5 us -> 117 us
  between operations: 1.18 us -> 14.7 us
  starting transfers between devices: 44.3 us -> 33.2 us
  other arithmetic: 27 us -> 19.2 us
  local copies, waits for them, and re-layouts: 14.5 us -> 18.9 us
  matrix products: 14.2 us -> 11.3 us
    all_gather x0 -> x1, waiting for transfers between devices: none -> 68.9 us  [per_device(): lax.all_gather(leave_states, 'req', axis=0, tiled=True)[:, :conv_rows + 1]]
    all_to_all x1 -> x0, starting transfers between devices: 11.2 us -> none  [per_device(): lax.all_to_all(jnp.take(states, send_slot, axis=0), 'req', 0, 0, tiled=True)]
    all_to_all x1, waiting for transfers between devices: 4.6 us -> 0.01 us  [per_device(): lax.all_to_all(jnp.take(cache, send_slot, axis=0), 'req', 0, 0, tiled=True)]
  transfers between devices with their start and end apart: 17 -> 17, of which waited for: 16 -> 16; matrix products, arithmetic and copies ran while one was open for 23% -> 13% of each run, Pallas kernels for 0% -> 0%
where the time goes in v6:
time: 216 us; the launch traced here: 214 us
  waiting for transfers between devices  117 us (54%)
  starting transfers between devices  33.2 us (15%)
  other arithmetic  19.2 us (9%)
  local copies, waits for them, and re-layouts  18.9 us (9%)
  between operations  14.7 us (7%)
  matrix products  11.3 us (5%)
    all_gather x1, waiting for transfers between devices, per_device(): lax.all_gather(leave_states, 'req', axis=0, tiled=True)[:, :conv_rows + 1]  68.9 us
    ppermute x15, waiting for transfers between devices, partner_swap(): return jax.tree.map(lambda part: lax.ppermute(part, axis, pairs), value)  48 us
    ppermute x15, starting transfers between devices, partner_swap(): return jax.tree.map(lambda part: lax.ppermute(part, axis, pairs), value)  21.8 us
    all_to_all x1, starting transfers between devices, per_device(): lax.all_to_all(jnp.take(cache, send_slot, axis=0), 'req', 0, 0, tiled=True)  11.4 us
  transfers between devices with their start and end apart: 17, of which 16 were waited for; matrix products, arithmetic and copies ran while one was open for 13% of the time, Pallas kernels for 0%

profile of v6, /device:TPU:32, one launch (start us, length us, event | category | flops | bytes accessed | tf_op | source)
XLA Modules:
  0.0 214.2 jit_solution(10597071381298738655)
XLA Ops:
  12.2 3.4 %gather_fusion.6 = bf16[32,128,256]{2,1,0:T(8,128)(2,1)} fusion(bf16[24,128,256]{2,1,0:T(8,128)(2,1)} %param.28, s32[1024]{0:T(1024)S(1)} %pad_clamp_fusion), kind=kCustom, calls=%fused_computation.6 | custom fusion | bytes 4194432 | tf_op jit(solution)/shard_map/jit(_take)/gather | solution.py:155
  15.7 3.2 %broadcast_select_fusion = bf16[32,128,256]{2,1,0:T(8,128)(2,1)} fusion(bf16[32,128,256]{2,1,0:T(8,128)(2,1)} %gather_fusion.6, pred[32]{0:T(512)(128)(4,1)S(1)} %get-tuple-element.56), kind=kLoop, calls=%fused_computation.8 | loop fusion | flops 1048576 | bytes 4194336 | tf_op jit(solution)/shard_map/jit(_take)/select_n | solution.py:155
  18.9 11.4 %all-to-all-start = ((bf16[32,128,256]{2,1,0:T(8,128)(2,1)}), bf16[32,128,256]{2,1,0:T(8,128)(2,1)}, u32[]{:S(2)}, u32[]{:S(2)}) async-start(bf16[32,128,256]{2,1,0:T(8,128)(2,1)} %broadcast_select_fusion), calls=%async_computation | async-start | bytes 4194304 | tf_op jit(solution)/shard_map/all_to_all | solution.py:155
  33.0 68.9 %all-gather.2.cloned.1.call-done = bf16[416,8,256]{2,1,0:T(8,128)(2,1)} async-done(((bf16[13,8,256]{2,1,0:T(8,128)(2,1)}), bf16[416,8,256]{2,1,0:T(8,128)(2,1)}) %all-gather.2.cloned.1.call-update) | async-done | bytes 1703952 | tf_op jit(solution)/shard_map/all_gather | solution.py:153
  114.6 3.1 %collective-permute-start.1 = (bf16[24,1536]{1,0:T(8,128)(2,1)S(1)}, bf16[24,1536]{1,0:T(8,128)(2,1)S(1)}, u32[]{:S(2)}, u32[]{:S(2)}) collective-permute-start(bf16[24,1536]{1,0:T(8,128)(2,1)S(1)} %fusion.11), channel_id=1, source_target_pairs={{0,3},{1,2},{2,1},{3,0},{4,7},{5,6},{6,5},{7,4},{8,11},{9,10},{10,... | collective-permute-start | bytes 221192 | tf_op jit(solution)/shard_map/ppermute | solution.py:14
  122.3 3.3 %collective-permute-done.2 = bf16[24,1536]{1,0:T(8,128)(2,1)} collective-permute-done((bf16[24,1536]{1,0:T(8,128)(2,1)}, bf16[24,1536]{1,0:T(8,128)(2,1)}, u32[]{:S(2)}, u32[]{:S(2)}) %collective-permute-start.2) | collective-permute-done | bytes 73760 | tf_op jit(solution)/shard_map/ppermute | solution.py:14
  128.5 3.0 %collective-permute-done.3 = bf16[24,1536]{1,0:T(8,128)(2,1)S(1)} collective-permute-done((bf16[24,1536]{1,0:T(8,128)(2,1)S(1)}, bf16[24,1536]{1,0:T(8,128)(2,1)S(1)}, u32[]{:S(2)}, u32[]{:S(2)}) %collective-permute-start.3) | collective-permute-done | bytes 73760 | tf_op jit(solution)/shard_map/ppermute | solution.py:14
  131.5 3.1 %collective-permute-start.4 = (bf16[24,1536]{1,0:T(8,128)(2,1)S(1)}, bf16[24,1536]{1,0:T(8,128)(2,1)S(1)}, u32[]{:S(2)}, u32[]{:S(2)}) collective-permute-start(bf16[24,1536]{1,0:T(8,128)(2,1)S(1)} %fusion.12), channel_id=1, source_target_pairs={{0,3},{1,2},{2,1},{3,0},{4,7},{5,6},{6,5},{7,4},{8,11},{9,10},{10,... | collective-permute-start | bytes 221192 | tf_op jit(solution)/shard_map/ppermute | solution.py:14
  138.5 3.1 %collective-permute-done.5 = bf16[24,1536]{1,0:T(8,128)(2,1)S(1)} collective-permute-done((bf16[24,1536]{1,0:T(8,128)(2,1)S(1)}, bf16[24,1536]{1,0:T(8,128)(2,1)S(1)}, u32[]{:S(2)}, u32[]{:S(2)}) %collective-permute-start.5) | collective-permute-done | bytes 73760 | tf_op jit(solution)/shard_map/ppermute | solution.py:14
  143.4 3.6 %gather_fusion.7 = bf16[24,128,256]{2,1,0:T(8,128)(2,1)} fusion(bf16[32,128,256]{2,1,0:T(8,128)(2,1)} %all-to-all-done, s32[1024]{0:T(1024)} %copy-done.25), kind=kCustom, calls=%fused_computation.7 | custom fusion | bytes 3145824 | tf_op jit(solution)/shard_map/jit(_take)/gather | solution.py:165
  146.9 2.8 %broadcast_select_fusion.1 = (bf16[24,128,256]{2,1,0:T(8,128)(2,1)}, bf16[24,128,256]{2,1,0:T(8,128)(2,1)S(1)}) fusion(pred[24,128]{1,0:T(8,128)(4,1)} %get-tuple-element.39, bf16[24,256]{1,0:T(8,128)(2,1)} %pad_maximum_fusion.4, bf16[24,128,256]{2,1,0:T(8,128)(2,1)S(1)} %copy-done.3, bf16[24,128,256]{2,1,0:T(8,128)(2,1)} %gather_fusion.7, ...), kind=kLoop, calls=%fused_computation.10 | loop fusion | flops 2359296 | bytes 6306864 | tf_op jit(solution)/shard_map/jit(_where)/select_n | solution.py:294
  151.2 5.3 %collective-permute-done.6 = f32[24,1664]{1,0:T(8,128)S(1)} collective-permute-done((f32[24,1664]{1,0:T(8,128)S(1)}, f32[24,1664]{1,0:T(8,128)S(1)}, u32[]{:S(2)}, u32[]{:S(2)}) %collective-permute-start.6) | collective-permute-done | bytes 159776 | tf_op jit(solution)/shard_map/ppermute | solution.py:14
  156.9 3.1 %collective-permute-start.7 = (f32[24,1664]{1,0:T(8,128)S(1)}, f32[24,1664]{1,0:T(8,128)S(1)}, u32[]{:S(2)}, u32[]{:S(2)}) collective-permute-start(f32[24,1664]{1,0:T(8,128)S(1)} %concatenate.47), channel_id=1, source_target_pairs={{0,3},{1,2},{2,1},{3,0},{4,7},{5,6},{6,5},{7,4},{8,11},{9,10},{10,... | collective-permute-start | bytes 479240 | tf_op jit(solution)/shard_map/ppermute | solution.py:14
  160.0 3.4 %collective-permute-done.7 = f32[24,1664]{1,0:T(8,128)S(1)} collective-permute-done((f32[24,1664]{1,0:T(8,128)S(1)}, f32[24,1664]{1,0:T(8,128)S(1)}, u32[]{:S(2)}, u32[]{:S(2)}) %collective-permute-start.7) | collective-permute-done | bytes 159776 | tf_op jit(solution)/shard_map/ppermute | solution.py:14
  165.5 4.5 %collective-permute-done.8 = f32[24,1664]{1,0:T(8,128)S(1)} collective-permute-done((f32[24,1664]{1,0:T(8,128)}, f32[24,1664]{1,0:T(8,128)S(1)}, u32[]{:S(2)}, u32[]{:S(2)}) %collective-permute-start.8) | collective-permute-done | bytes 159776 | tf_op jit(solution)/shard_map/ppermute | solution.py:14
  171.1 4.3 %collective-permute-done.9 = bf16[24,1536]{1,0:T(8,128)(2,1)S(1)} collective-permute-done((bf16[24,1536]{1,0:T(8,128)(2,1)S(1)}, bf16[24,1536]{1,0:T(8,128)(2,1)S(1)}, u32[]{:S(2)}, u32[]{:S(2)}) %collective-permute-start.9) | collective-permute-done | bytes 73760 | tf_op jit(solution)/shard_map/ppermute | solution.py:14
  175.4 3.1 %collective-permute-start.10 = (bf16[24,1536]{1,0:T(8,128)(2,1)S(1)}, bf16[24,1536]{1,0:T(8,128)(2,1)S(1)}, u32[]{:S(2)}, u32[]{:S(2)}) collective-permute-start(bf16[24,1536]{1,0:T(8,128)(2,1)S(1)} %fusion.13), channel_id=1, source_target_pairs={{0,3},{1,2},{2,1},{3,0},{4,7},{5,6},{6,5},{7,4},{8,11},{9,10},{10,... | collective-permute-start | bytes 221192 | tf_op jit(solution)/shard_map/ppermute | solution.py:14
  178.6 2.5 %collective-permute-done.10 = bf16[24,1536]{1,0:T(8,128)(2,1)S(1)} collective-permute-done((bf16[24,1536]{1,0:T(8,128)(2,1)S(1)}, bf16[24,1536]{1,0:T(8,128)(2,1)S(1)}, u32[]{:S(2)}, u32[]{:S(2)}) %collective-permute-start.10) | collective-permute-done | bytes 73760 | tf_op jit(solution)/shard_map/ppermute | solution.py:14
  181.9 3.7 %collective-permute-done.11 = bf16[24,1536]{1,0:T(8,128)(2,1)S(1)} collective-permute-done((bf16[24,1536]{1,0:T(8,128)(2,1)S(1)}, bf16[24,1536]{1,0:T(8,128)(2,1)S(1)}, u32[]{:S(2)}, u32[]{:S(2)}) %collective-permute-start.11) | collective-permute-done | bytes 73760 | tf_op jit(solution)/shard_map/ppermute | solution.py:14
  186.4 2.7 %fusion.112 = f32[24,576]{1,0:T(8,128)} fusion(bf16[1536,576]{0,1:T(8,128)(2,1)} %param.45, f32[24,1536]{1,0:T(8,128)S(1)} %get-tuple-element.11, f32[1536]{0:T(1024)S(1)} %copy-done.22, f32[24]{0:T(128)S(1)} %add_rsqrt_fusion), kind=kOutput, calls=%fused_computation.242 | convolution fusion | flops 42577920 | bytes 1978464 | tf_op jit(solution)/shard_map/dot_general | solution.py:281
  189.1 2.6 %fusion.1 = f32[24,1536]{1,0:T(8,128)} fusion(bf16[576,1536]{1,0:T(8,128)(2,1)S(1)} %copy-done, bf16[1536,576]{0,1:T(8,128)(2,1)S(1)} %copy-done.4, f32[24,576]{1,0:T(8,128)} %fusion.112, f32[24,1536]{1,0:T(8,128)} %copy-done.5, f32[1536]{0:T(1024)} %param.44, f32[24]{0:T(128)S(1)} %add_rsqrt_fusion), kind=kOutput, calls=%fused_computation.15 | convolution fusion | flops 85183488 | bytes 3895392 | tf_op jit(solution)/shard_map/dot_general | solution.py:286
  193.5 3.4 %collective-permute-done.12 = bf16[24,4,192]{2,0,1:T(8,128)(2,1)S(1)} collective-permute-done((bf16[24,4,192]{2,0,1:T(8,128)(2,1)S(1)}, bf16[24,4,192]{2,0,1:T(8,128)(2,1)S(1)}, u32[]{:S(2)}, u32[]{:S(2)}) %collective-permute-start.12) | collective-permute-done | bytes 36896 | tf_op jit(solution)/shard_map/ppermute | solution.py:14
  197.0 3.1 %collective-permute-start.13 = (bf16[24,2,192]{2,0,1:T(8,128)(2,1)S(1)}, bf16[24,2,192]{2,0,1:T(8,128)(2,1)S(1)}, u32[]{:S(2)}, u32[]{:S(2)}) collective-permute-start(bf16[24,2,192]{2,0,1:T(8,128)(2,1)S(1)} %select_convert_fusion.1), channel_id=1, source_target_pairs={{0,3},{1,2},{2,1},{3,0},{4,7},{5,6},{6,5},{7,4},{8,11},{9,10},{10,... | collective-permute-start | bytes 55304 | tf_op jit(solution)/shard_map/ppermute | solution.py:14
  202.9 3.0 %collective-permute-done.14 = bf16[24,1,192]{2,0,1:T(8,128)(2,1)S(1)} collective-permute-done((bf16[24,1,192]{2,0,1:T(8,128)(2,1)S(1)}, bf16[24,1,192]{2,0,1:T(8,128)(2,1)S(1)}, u32[]{:S(2)}, u32[]{:S(2)}) %collective-permute-start.14) | collective-permute-done | bytes 9248 | tf_op jit(solution)/shard_map/ppermute | solution.py:14
  (191 shorter events, 45.7 us)
Async XLA Ops:
  7.2 181.9 %copy-start = (bf16[576,1536]{1,0:T(8,128)(2,1)S(1)}, bf16[576,1536]{1,0:T(8,128)(2,1)}, u32[]{:S(2)}) copy-start(bf16[576,1536]{1,0:T(8,128)(2,1)} %param.47) | copy-start | bytes 5308420
  7.2 94.8 %all-gather.2.cloned.1.call-start = ((), (), s32[]{:S(2)}) async-start(), calls=%async_computation.1 | async-start | bytes 1757184 | tf_op jit(solution)/shard_map/all_gather | solution.py:153
  18.9 124.5 %all-to-all-start = ((bf16[32,128,256]{2,1,0:T(8,128)(2,1)}), bf16[32,128,256]{2,1,0:T(8,128)(2,1)}, u32[]{:S(2)}, u32[]{:S(2)}) async-start(bf16[32,128,256]{2,1,0:T(8,128)(2,1)} %broadcast_select_fusion), calls=%async_computation | async-start | bytes 4194304 | tf_op jit(solution)/shard_map/all_to_all | solution.py:155
  30.4 74.6 %copy-start.15 = (bf16[24,3,256]{2,0,1:T(8,128)(2,1)S(1)}, bf16[24,3,256]{2,0,1:T(8,128)(2,1)}, u32[]{:S(2)}) copy-start(bf16[24,3,256]{2,0,1:T(8,128)(2,1)} %param.29) | copy-start | bytes 110596
  30.4 74.6 %copy-start.18 = (bf16[24,256]{1,0:T(8,128)(2,1)S(1)}, bf16[24,256]{1,0:T(8,128)(2,1)}, u32[]{:S(2)}) copy-start(bf16[24,256]{1,0:T(8,128)(2,1)} %param.30) | copy-start | bytes 36868
  32.0 75.1 %copy-start.26 = (pred[24]{0:T(512)(128)(4,1)}, pred[24]{0:T(512)(128)(4,1)S(1)}, u32[]{:S(2)}) copy-start(pred[24]{0:T(512)(128)(4,1)S(1)} %fusion.90) | copy-start | bytes 76
  32.8 79.0 %copy-start.28 = (f32[64]{0:T(128)}, f32[64]{0:T(128)S(1)}, u32[]{:S(2)}) copy-start(f32[64]{0:T(128)S(1)} %multiply_power_fusion) | copy-start | bytes 772
  32.8 74.5 %copy-start.30 = (f32[2,256]{1,0:T(2,128)S(1)}, f32[2,256]{1,0:T(2,128)}, u32[]{:S(2)}) copy-start(f32[2,256]{1,0:T(2,128)} %param.37) | copy-start | bytes 6148
  32.8 74.5 %copy-start.25 = (s32[1024]{0:T(1024)}, s32[1024]{0:T(1024)S(1)}, u32[]{:S(2)}) copy-start(s32[1024]{0:T(1024)S(1)} %pad_clamp_fusion.2) | copy-start | bytes 12292
  110.1 4.5 %collective-permute-start = (bf16[24,1536]{1,0:T(8,128)(2,1)S(1)}, bf16[24,1536]{1,0:T(8,128)(2,1)S(1)}, u32[]{:S(2)}, u32[]{:S(2)}) collective-permute-start(bf16[24,1536]{1,0:T(8,128)(2,1)S(1)} %get-tuple-element.48), channel_id=1, source_target_pairs={{0,1},{1,0},{2,3},{3,2},{4,5},{5,4},{6,7},{7,6},{8,9},{9,8},{10,11... | collective-permute-start | bytes 221192 | tf_op jit(solution)/shard_map/ppermute | solution.py:14
  114.6 5.7 %collective-permute-start.1 = (bf16[24,1536]{1,0:T(8,128)(2,1)S(1)}, bf16[24,1536]{1,0:T(8,128)(2,1)S(1)}, u32[]{:S(2)}, u32[]{:S(2)}) collective-permute-start(bf16[24,1536]{1,0:T(8,128)(2,1)S(1)} %fusion.11), channel_id=1, source_target_pairs={{0,3},{1,2},{2,1},{3,0},{4,7},{5,6},{6,5},{7,4},{8,11},{9,10},{10,... | collective-permute-start | bytes 221192 | tf_op jit(solution)/shard_map/ppermute | solution.py:14
  121.0 4.7 %collective-permute-start.2 = (bf16[24,1536]{1,0:T(8,128)(2,1)}, bf16[24,1536]{1,0:T(8,128)(2,1)}, u32[]{:S(2)}, u32[]{:S(2)}) collective-permute-start(bf16[24,1536]{1,0:T(8,128)(2,1)} %fusion.26), channel_id=1, source_target_pairs={{0,4},{1,5},{2,6},{3,7},{4,0},{5,1},{6,2},{7,3},{8,12},{9,13},{10,... | collective-permute-start | bytes 221192 | tf_op jit(solution)/shard_map/ppermute | solution.py:14
  127.0 4.4 %collective-permute-start.3 = (bf16[24,1536]{1,0:T(8,128)(2,1)S(1)}, bf16[24,1536]{1,0:T(8,128)(2,1)S(1)}, u32[]{:S(2)}, u32[]{:S(2)}) collective-permute-start(bf16[24,1536]{1,0:T(8,128)(2,1)S(1)} %get-tuple-element.50), channel_id=1, source_target_pairs={{0,1},{1,0},{2,3},{3,2},{4,5},{5,4},{6,7},{7,6},{8,9},{9,8},{10,11... | collective-permute-start | bytes 221192 | tf_op jit(solution)/shard_map/ppermute | solution.py:14
  131.5 5.7 %collective-permute-start.4 = (bf16[24,1536]{1,0:T(8,128)(2,1)S(1)}, bf16[24,1536]{1,0:T(8,128)(2,1)S(1)}, u32[]{:S(2)}, u32[]{:S(2)}) collective-permute-start(bf16[24,1536]{1,0:T(8,128)(2,1)S(1)} %fusion.12), channel_id=1, source_target_pairs={{0,3},{1,2},{2,1},{3,0},{4,7},{5,6},{6,5},{7,4},{8,11},{9,10},{10,... | collective-permute-start | bytes 221192 | tf_op jit(solution)/shard_map/ppermute | solution.py:14
  137.2 4.4 %collective-permute-start.5 = (bf16[24,1536]{1,0:T(8,128)(2,1)S(1)}, bf16[24,1536]{1,0:T(8,128)(2,1)S(1)}, u32[]{:S(2)}, u32[]{:S(2)}) collective-permute-start(bf16[24,1536]{1,0:T(8,128)(2,1)S(1)} %fusion.27), channel_id=1, source_target_pairs={{0,4},{1,5},{2,6},{3,7},{4,0},{5,1},{6,2},{7,3},{8,12},{9,13},{10,... | collective-permute-start | bytes 221192 | tf_op jit(solution)/shard_map/ppermute | solution.py:14
  151.1 5.3 %collective-permute-start.6 = (f32[24,1664]{1,0:T(8,128)S(1)}, f32[24,1664]{1,0:T(8,128)S(1)}, u32[]{:S(2)}, u32[]{:S(2)}) collective-permute-start(f32[24,1664]{1,0:T(8,128)S(1)} %concatenate.46), channel_id=1, source_target_pairs={{0,1},{1,0},{2,3},{3,2},{4,5},{5,4},{6,7},{7,6},{8,9},{9,8},{10,11... | collective-permute-start | bytes 479240 | tf_op jit(solution)/shard_map/ppermute | solution.py:14
  156.9 6.5 %collective-permute-start.7 = (f32[24,1664]{1,0:T(8,128)S(1)}, f32[24,1664]{1,0:T(8,128)S(1)}, u32[]{:S(2)}, u32[]{:S(2)}) collective-permute-start(f32[24,1664]{1,0:T(8,128)S(1)} %concatenate.47), channel_id=1, source_target_pairs={{0,3},{1,2},{2,1},{3,0},{4,7},{5,6},{6,5},{7,4},{8,11},{9,10},{10,... | collective-permute-start | bytes 479240 | tf_op jit(solution)/shard_map/ppermute | solution.py:14
  164.5 5.5 %collective-permute-start.8 = (f32[24,1664]{1,0:T(8,128)}, f32[24,1664]{1,0:T(8,128)S(1)}, u32[]{:S(2)}, u32[]{:S(2)}) collective-permute-start(f32[24,1664]{1,0:T(8,128)} %concatenate.48), channel_id=1, source_target_pairs={{0,4},{1,5},{2,6},{3,7},{4,0},{5,1},{6,2},{7,3},{8,12},{9,13},{10,... | collective-permute-start | bytes 479240 | tf_op jit(solution)/shard_map/ppermute | solution.py:14
  170.8 4.6 %collective-permute-start.9 = (bf16[24,1536]{1,0:T(8,128)(2,1)S(1)}, bf16[24,1536]{1,0:T(8,128)(2,1)S(1)}, u32[]{:S(2)}, u32[]{:S(2)}) collective-permute-start(bf16[24,1536]{1,0:T(8,128)(2,1)S(1)} %get-tuple-element.54), channel_id=1, source_target_pairs={{0,1},{1,0},{2,3},{3,2},{4,5},{5,4},{6,7},{7,6},{8,9},{9,8},{10,11... | collective-permute-start | bytes 221192 | tf_op jit(solution)/shard_map/ppermute | solution.py:14
  175.4 5.7 %collective-permute-start.10 = (bf16[24,1536]{1,0:T(8,128)(2,1)S(1)}, bf16[24,1536]{1,0:T(8,128)(2,1)S(1)}, u32[]{:S(2)}, u32[]{:S(2)}) collective-permute-start(bf16[24,1536]{1,0:T(8,128)(2,1)S(1)} %fusion.13), channel_id=1, source_target_pairs={{0,3},{1,2},{2,1},{3,0},{4,7},{5,6},{6,5},{7,4},{8,11},{9,10},{10,... | collective-permute-start | bytes 221192 | tf_op jit(solution)/shard_map/ppermute | solution.py:14
  181.1 4.4 %collective-permute-start.11 = (bf16[24,1536]{1,0:T(8,128)(2,1)S(1)}, bf16[24,1536]{1,0:T(8,128)(2,1)S(1)}, u32[]{:S(2)}, u32[]{:S(2)}) collective-permute-start(bf16[24,1536]{1,0:T(8,128)(2,1)S(1)} %fusion.28), channel_id=1, source_target_pairs={{0,4},{1,5},{2,6},{3,7},{4,0},{5,1},{6,2},{7,3},{8,12},{9,13},{10,... | collective-permute-start | bytes 221192 | tf_op jit(solution)/shard_map/ppermute | solution.py:14
  192.8 4.2 %collective-permute-start.12 = (bf16[24,4,192]{2,0,1:T(8,128)(2,1)S(1)}, bf16[24,4,192]{2,0,1:T(8,128)(2,1)S(1)}, u32[]{:S(2)}, u32[]{:S(2)}) collective-permute-start(bf16[24,4,192]{2,0,1:T(8,128)(2,1)S(1)} %select_convert_fusion), channel_id=1, source_target_pairs={{0,4},{1,5},{2,6},{3,7},{4,0},{5,1},{6,2},{7,3},{8,12},{9,13},{10,... | collective-permute-start | bytes 110600 | tf_op jit(solution)/shard_map/ppermute | solution.py:14
  197.0 5.1 %collective-permute-start.13 = (bf16[24,2,192]{2,0,1:T(8,128)(2,1)S(1)}, bf16[24,2,192]{2,0,1:T(8,128)(2,1)S(1)}, u32[]{:S(2)}, u32[]{:S(2)}) collective-permute-start(bf16[24,2,192]{2,0,1:T(8,128)(2,1)S(1)} %select_convert_fusion.1), channel_id=1, source_target_pairs={{0,3},{1,2},{2,1},{3,0},{4,7},{5,6},{6,5},{7,4},{8,11},{9,10},{10,... | collective-permute-start | bytes 55304 | tf_op jit(solution)/shard_map/ppermute | solution.py:14
  202.1 3.8 %collective-permute-start.14 = (bf16[24,1,192]{2,0,1:T(8,128)(2,1)S(1)}, bf16[24,1,192]{2,0,1:T(8,128)(2,1)S(1)}, u32[]{:S(2)}, u32[]{:S(2)}) collective-permute-start(bf16[24,1,192]{2,0,1:T(8,128)(2,1)S(1)} %select_convert_fusion.2), channel_id=1, source_target_pairs={{0,1},{1,0},{2,3},{3,2},{4,5},{5,4},{6,7},{7,6},{8,9},{9,8},{10,11... | collective-permute-start | bytes 27656 | tf_op jit(solution)/shard_map/ppermute | solution.py:14
  (26 other events, 544.7 us)
Sparse Core Ops, SparseCore 0:
  11.3 90.6 all-gather.1

commit v7 on v5

--- a/solution.py
+++ b/solution.py
@@ -141,31 +141,38 @@
     rank_ids = jnp.arange(leavers, dtype=jnp.int32)
     group_ids = jnp.arange(groups, dtype=jnp.int32)
     my_leave = leaving[own_group]
-    anchor = jnp.sum(jnp.where(owner == own_group, group_ids[:, None], 0), axis=0)
+    my_owner = owner[own_group]
+    to_me = owner == own_group
+    anchor = jnp.sum(jnp.where(to_me, group_ids[:, None], 0), axis=0)
+    anchor_leave = jnp.sum(jnp.where(to_me, leaving, 0), axis=0)
     page_rows = cache.shape[1]
     conv_rows = conv_state.shape[1]
     states = jnp.concatenate([conv_state, lru_state[:, None, :]], axis=1)
-    to_group = owner[own_group][None, :] == group_ids[:, None]
+    to_group = my_owner[None, :] == group_ids[:, None]
     send_slot = jnp.sum(jnp.where(to_group, my_leave[None, :], 0), axis=1)
-    got_states = lax.all_to_all(jnp.take(states, send_slot, axis=0), "req", 0, 0, tiled=True)
-    got_cache = lax.all_to_all(jnp.take(cache, send_slot, axis=0), "req", 0, 0, tiled=True)
+    got_states = lax.all_to_all(
+        jnp.take(states, send_slot, axis=0, mode="clip"), "req", 0, 0, tiled=True
+    )
+    got_cache = lax.all_to_all(
+        jnp.take(cache, send_slot, axis=0, mode="clip"), "req", 0, 0, tiled=True
+    )
     local_ids = jnp.arange(req_rows, dtype=jnp.int32)
     match_slot = my_leave[None, :] == local_ids[:, None]
-    arrive_rank = jnp.sum(jnp.where(match_slot, rank_ids[None, :], 0), axis=1)
     arriving = jnp.any(match_slot, axis=1)
-    arrive_from = anchor[arrive_rank]
+    arrive_from = jnp.sum(jnp.where(match_slot, anchor[None, :], 0), axis=1)
+    anchor_slot = jnp.sum(
+        jnp.where(match_slot, (anchor * req_rows + anchor_leave)[None, :], 0), axis=1
+    )
     moved_states = jnp.where(
-        arriving[:, None, None], jnp.take(got_states, arrive_from, axis=0), states
+        arriving[:, None, None], jnp.take(got_states, arrive_from, axis=0, mode="clip"), states
     )
     moved_cache = jnp.where(
-        arriving[:, None, None], jnp.take(got_cache, arrive_from, axis=0), cache
+        arriving[:, None, None], jnp.take(got_cache, arrive_from, axis=0, mode="clip"), cache
     )
     moved_conv = moved_states[:, :conv_rows]
     moved_lru = moved_states[:, conv_rows]
-    arrive_anchor = anchor[arrive_rank]
-    anchor_slot = arrive_anchor * req_rows + leaving[arrive_anchor, arrive_rank]
     source_slot = jnp.where(arriving, anchor_slot, own_group * req_rows + local_ids)
-    position = lengths[source_slot]
+    position = jnp.take(lengths, source_slot, mode="clip")
     inputs = tokens.astype(jnp.float32)
     normed = rms_norm(inputs, gain_rec)
     branch_in = jnp.dot(normed, w_input, preferred_element_type=jnp.float32).astype(jnp.bfloat16)

time: 155 us -> 153 us (0.987)
  waiting for transfers between devices: 52.5 us -> 60.1 us
  other arithmetic: 27 us -> 20.6 us
  matrix products: 14.2 us -> 10.1 us
    all_to_all x2, waiting for transfers between devices: 4.6 us -> 10.2 us  [the longest x1 10.2 us: per_device(): lax.all_to_all(jnp.take(cache, send_slot, axis=0, mode='clip'), 'req', 0,...]
    select_n x5 -> x1, other arithmetic: 3.94 us -> 0.01 us  [per_device(): jnp.where(arriving, anchor_slot, own_group * req_rows + local_ids)]
    ppermute x15, waiting for transfers between devices: 47.9 us -> 49.9 us  [partner_swap(): return jax.tree.map(lambda part: lax.ppermute(part, axis, pairs), value)]
    convert_element_type x6, other arithmetic: 2.53 us -> 0.77 us  [across_mlp_narrow(): sent = partner_swap(partial_value.astype(jnp.bfloat16), 'mlp', mask)]
    gather x7 -> x5, local copies, waits for them, and re-layouts: 9.78 us -> 10.2 us  [the longest x1 3.55 us: per_device(): jnp.take(got_cache, arrive_from, axis=0, mode='clip')]
  transfers between devices with their start and end apart: 17 -> 17, of which waited for: 16 -> 16; matrix products, arithmetic and copies ran while one was open for 23% -> 16% of each run, Pallas kernels for 0% -> 0%
where the time goes in v7:
time: 153 us; the launch traced here: 152 us
  waiting for transfers between devices  60.1 us (39%)
  starting transfers between devices  44.3 us (29%)
  other arithmetic  20.6 us (13%)
  local copies, waits for them, and re-layouts  15.6 us (10%)
  matrix products  10.1 us (7%)
    ppermute x15, waiting for transfers between devices, partner_swap(): return jax.tree.map(lambda part: lax.ppermute(part, axis, pairs), value)  49.9 us
    ppermute x15, starting transfers between devices, partner_swap(): return jax.tree.map(lambda part: lax.ppermute(part, axis, pairs), value)  23.1 us
    all_to_all x1, starting transfers between devices, per_device(): lax.all_to_all(jnp.take(states, send_slot, axis=0, mode='clip'), 'req', 0...  11.2 us
    all_to_all x1, waiting for transfers between devices, per_device(): lax.all_to_all(jnp.take(cache, send_slot, axis=0, mode='clip'), 'req', 0,...  10.2 us
    all_to_all x1, starting transfers between devices, per_device(): lax.all_to_all(jnp.take(cache, send_slot, axis=0, mode='clip'), 'req', 0,...  10 us
    gather x1, local copies, waits for them, and re-layouts, per_device(): jnp.take(got_cache, arrive_from, axis=0, mode='clip')  3.55 us
    gather x1, local copies, waits for them, and re-layouts, per_device(): jnp.take(cache, send_slot, axis=0, mode='clip')  3.39 us
  transfers between devices with their start and end apart: 17, of which 16 were waited for; matrix products, arithmetic and copies ran while one was open for 16% of the time, Pallas kernels for 0%

profile of v7, /device:TPU:32, one launch (start us, length us, event | category | flops | bytes accessed | tf_op | source)
XLA Modules:
  0.0 152.0 jit_solution(11345244963199781542)
XLA Ops:
  3.8 11.2 %all-to-all-start = ((bf16[32,4,256]{2,1,0:T(4,128)(2,1)}), bf16[32,4,256]{2,1,0:T(4,128)(2,1)S(1)}, u32[]{:S(2)}, u32[]{:S(2)}) async-start(bf16[32,4,256]{2,1,0:T(4,128)(2,1)} %gather_fusion), calls=%async_computation | async-start | bytes 131072 | tf_op jit(solution)/shard_map/all_to_all | solution.py:153
  21.1 3.4 %gather_fusion.3 = bf16[32,128,256]{2,1,0:T(8,128)(2,1)} fusion(bf16[24,128,256]{2,1,0:T(8,128)(2,1)} %param.28, s32[1024]{0:T(1024)S(1)} %pad_clamp_fusion.2), kind=kCustom, calls=%fused_computation.3 | custom fusion | bytes 4194432 | tf_op jit(solution)/shard_map/jit(_take)/gather | solution.py:157
  24.6 10.0 %all-to-all-start.1 = ((bf16[32,128,256]{2,1,0:T(8,128)(2,1)}), bf16[32,128,256]{2,1,0:T(8,128)(2,1)}, u32[]{:S(2)}, u32[]{:S(2)}) async-start(bf16[32,128,256]{2,1,0:T(8,128)(2,1)} %gather_fusion.3), calls=%async_computation.1 | async-start | bytes 4194304 | tf_op jit(solution)/shard_map/all_to_all | solution.py:156
  43.7 3.1 %collective-permute-start.1 = (bf16[24,1536]{1,0:T(8,128)(2,1)S(1)}, bf16[24,1536]{1,0:T(8,128)(2,1)S(1)}, u32[]{:S(2)}, u32[]{:S(2)}) collective-permute-start(bf16[24,1536]{1,0:T(8,128)(2,1)S(1)} %fusion.11), channel_id=1, source_target_pairs={{0,3},{1,2},{2,1},{3,0},{4,7},{5,6},{6,5},{7,4},{8,11},{9,10},{10,... | collective-permute-start | bytes 221192 | tf_op jit(solution)/shard_map/ppermute | solution.py:14
  52.0 6.9 %collective-permute-done.2 = bf16[24,1536]{1,0:T(8,128)(2,1)} collective-permute-done((bf16[24,1536]{1,0:T(8,128)(2,1)}, bf16[24,1536]{1,0:T(8,128)(2,1)}, u32[]{:S(2)}, u32[]{:S(2)}) %collective-permute-start.2) | collective-permute-done | bytes 73760 | tf_op jit(solution)/shard_map/ppermute | solution.py:14
  62.0 2.7 %collective-permute-done.3 = bf16[24,1536]{1,0:T(8,128)(2,1)S(1)} collective-permute-done((bf16[24,1536]{1,0:T(8,128)(2,1)S(1)}, bf16[24,1536]{1,0:T(8,128)(2,1)S(1)}, u32[]{:S(2)}, u32[]{:S(2)}) %collective-permute-start.3) | collective-permute-done | bytes 73760 | tf_op jit(solution)/shard_map/ppermute | solution.py:14
  64.7 3.1 %collective-permute-start.4 = (bf16[24,1536]{1,0:T(8,128)(2,1)S(1)}, bf16[24,1536]{1,0:T(8,128)(2,1)S(1)}, u32[]{:S(2)}, u32[]{:S(2)}) collective-permute-start(bf16[24,1536]{1,0:T(8,128)(2,1)S(1)} %fusion.12), channel_id=1, source_target_pairs={{0,3},{1,2},{2,1},{3,0},{4,7},{5,6},{6,5},{7,4},{8,11},{9,10},{10,... | collective-permute-start | bytes 221192 | tf_op jit(solution)/shard_map/ppermute | solution.py:14
  72.0 3.7 %collective-permute-done.5 = bf16[24,1536]{1,0:T(8,128)(2,1)S(1)} collective-permute-done((bf16[24,1536]{1,0:T(8,128)(2,1)S(1)}, bf16[24,1536]{1,0:T(8,128)(2,1)S(1)}, u32[]{:S(2)}, u32[]{:S(2)}) %collective-permute-start.5) | collective-permute-done | bytes 73760 | tf_op jit(solution)/shard_map/ppermute | solution.py:14
  77.5 10.2 %all-to-all-done.1 = bf16[32,128,256]{2,1,0:T(8,128)(2,1)} async-done(((bf16[32,128,256]{2,1,0:T(8,128)(2,1)}), bf16[32,128,256]{2,1,0:T(8,128)(2,1)}, u32[]{:S(2)}, u32[]{:S(2)}) %all-to-all-start.1) | async-done | bytes 2097184 | tf_op jit(solution)/shard_map/all_to_all | solution.py:156
  87.6 3.6 %gather_fusion.4 = bf16[24,128,256]{2,1,0:T(8,128)(2,1)} fusion(bf16[32,128,256]{2,1,0:T(8,128)(2,1)} %all-to-all-done.1, s32[1024]{0:T(1024)} %copy-done.24), kind=kCustom, calls=%fused_computation.4 | custom fusion | bytes 3145824 | tf_op jit(solution)/shard_map/jit(_take)/gather | solution.py:170
  91.2 2.7 %broadcast_select_fusion.1 = (bf16[24,128,256]{2,1,0:T(8,128)(2,1)}, bf16[24,128,256]{2,1,0:T(8,128)(2,1)S(1)}) fusion(pred[24,128]{1,0:T(8,128)(4,1)} %get-tuple-element.41, bf16[24,256]{1,0:T(8,128)(2,1)} %pad_maximum_fusion.4, bf16[24,128,256]{2,1,0:T(8,128)(2,1)} %gather_fusion.4, bf16[24,128,256]{2,1,0:T(8,128)(2,1)S(1)} %copy-done.1, ...), kind=kLoop, calls=%fused_computation.6 | loop fusion | flops 1572864 | bytes 6306840 | tf_op jit(solution)/shard_map/jit(_where)/select_n | solution.py:297
  97.0 4.1 %collective-permute-done.6 = f32[24,1664]{1,0:T(8,128)S(1)} collective-permute-done((f32[24,1664]{1,0:T(8,128)S(1)}, f32[24,1664]{1,0:T(8,128)S(1)}, u32[]{:S(2)}, u32[]{:S(2)}) %collective-permute-start.6) | collective-permute-done | bytes 159776 | tf_op jit(solution)/shard_map/ppermute | solution.py:14
  101.5 3.0 %collective-permute-start.7 = (f32[24,1664]{1,0:T(8,128)S(1)}, f32[24,1664]{1,0:T(8,128)S(1)}, u32[]{:S(2)}, u32[]{:S(2)}) collective-permute-start(f32[24,1664]{1,0:T(8,128)S(1)} %concatenate.39), channel_id=1, source_target_pairs={{0,3},{1,2},{2,1},{3,0},{4,7},{5,6},{6,5},{7,4},{8,11},{9,10},{10,... | collective-permute-start | bytes 479240 | tf_op jit(solution)/shard_map/ppermute | solution.py:14
  104.5 3.5 %collective-permute-done.7 = f32[24,1664]{1,0:T(8,128)S(1)} collective-permute-done((f32[24,1664]{1,0:T(8,128)S(1)}, f32[24,1664]{1,0:T(8,128)S(1)}, u32[]{:S(2)}, u32[]{:S(2)}) %collective-permute-start.7) | collective-permute-done | bytes 159776 | tf_op jit(solution)/shard_map/ppermute | solution.py:14
  110.0 4.6 %collective-permute-done.8 = f32[24,1664]{1,0:T(8,128)S(1)} collective-permute-done((f32[24,1664]{1,0:T(8,128)}, f32[24,1664]{1,0:T(8,128)S(1)}, u32[]{:S(2)}, u32[]{:S(2)}) %collective-permute-start.8) | collective-permute-done | bytes 159776 | tf_op jit(solution)/shard_map/ppermute | solution.py:14
  115.9 4.0 %collective-permute-done.9 = bf16[24,1536]{1,0:T(8,128)(2,1)S(1)} collective-permute-done((bf16[24,1536]{1,0:T(8,128)(2,1)S(1)}, bf16[24,1536]{1,0:T(8,128)(2,1)S(1)}, u32[]{:S(2)}, u32[]{:S(2)}) %collective-permute-start.9) | collective-permute-done | bytes 73760 | tf_op jit(solution)/shard_map/ppermute | solution.py:14
  119.9 3.3 %collective-permute-start.10 = (bf16[24,1536]{1,0:T(8,128)(2,1)S(1)}, bf16[24,1536]{1,0:T(8,128)(2,1)S(1)}, u32[]{:S(2)}, u32[]{:S(2)}) collective-permute-start(bf16[24,1536]{1,0:T(8,128)(2,1)S(1)} %fusion.13), channel_id=1, source_target_pairs={{0,3},{1,2},{2,1},{3,0},{4,7},{5,6},{6,5},{7,4},{8,11},{9,10},{10,... | collective-permute-start | bytes 221192 | tf_op jit(solution)/shard_map/ppermute | solution.py:14
  123.1 2.5 %collective-permute-done.10 = bf16[24,1536]{1,0:T(8,128)(2,1)S(1)} collective-permute-done((bf16[24,1536]{1,0:T(8,128)(2,1)S(1)}, bf16[24,1536]{1,0:T(8,128)(2,1)S(1)}, u32[]{:S(2)}, u32[]{:S(2)}) %collective-permute-start.10) | collective-permute-done | bytes 73760 | tf_op jit(solution)/shard_map/ppermute | solution.py:14
  126.4 3.8 %collective-permute-done.11 = bf16[24,1536]{1,0:T(8,128)(2,1)S(1)} collective-permute-done((bf16[24,1536]{1,0:T(8,128)(2,1)S(1)}, bf16[24,1536]{1,0:T(8,128)(2,1)S(1)}, u32[]{:S(2)}, u32[]{:S(2)}) %collective-permute-start.11) | collective-permute-done | bytes 73760 | tf_op jit(solution)/shard_map/ppermute | solution.py:14
  131.0 2.7 %fusion.106 = f32[24,576]{1,0:T(8,128)} fusion(bf16[1536,576]{0,1:T(8,128)(2,1)} %param.45, f32[24,1536]{1,0:T(8,128)S(1)} %get-tuple-element.13, f32[1536]{0:T(1024)S(1)} %copy-done.21, f32[24]{0:T(128)S(1)} %add_rsqrt_fusion), kind=kOutput, calls=%fused_computation.211 | convolution fusion | flops 42577920 | bytes 1978464 | tf_op jit(solution)/shard_map/dot_general | solution.py:284
  133.7 2.6 %fusion.1 = f32[24,1536]{1,0:T(8,128)} fusion(bf16[576,1536]{1,0:T(8,128)(2,1)S(1)} %copy-done, bf16[1536,576]{0,1:T(8,128)(2,1)S(1)} %copy-done.2, f32[24,576]{1,0:T(8,128)} %fusion.106, f32[24,1536]{1,0:T(8,128)} %copy-done.3, f32[1536]{0:T(1024)} %param.44, f32[24]{0:T(128)S(1)} %add_rsqrt_fusion), kind=kOutput, calls=%fused_computation.11 | convolution fusion | flops 85183488 | bytes 3895392 | tf_op jit(solution)/shard_map/dot_general | solution.py:289
  138.1 3.5 %collective-permute-done.12 = bf16[24,4,192]{2,0,1:T(8,128)(2,1)S(1)} collective-permute-done((bf16[24,4,192]{2,0,1:T(8,128)(2,1)S(1)}, bf16[24,4,192]{2,0,1:T(8,128)(2,1)S(1)}, u32[]{:S(2)}, u32[]{:S(2)}) %collective-permute-start.12) | collective-permute-done | bytes 36896 | tf_op jit(solution)/shard_map/ppermute | solution.py:14
  141.6 3.1 %collective-permute-start.13 = (bf16[24,2,192]{2,0,1:T(8,128)(2,1)S(1)}, bf16[24,2,192]{2,0,1:T(8,128)(2,1)S(1)}, u32[]{:S(2)}, u32[]{:S(2)}) collective-permute-start(bf16[24,2,192]{2,0,1:T(8,128)(2,1)S(1)} %select_convert_fusion.1), channel_id=1, source_target_pairs={{0,3},{1,2},{2,1},{3,0},{4,7},{5,6},{6,5},{7,4},{8,11},{9,10},{10,... | collective-permute-start | bytes 55304 | tf_op jit(solution)/shard_map/ppermute | solution.py:14
  147.5 3.0 %collective-permute-done.14 = bf16[24,1,192]{2,0,1:T(8,128)(2,1)S(1)} collective-permute-done((bf16[24,1,192]{2,0,1:T(8,128)(2,1)S(1)}, bf16[24,1,192]{2,0,1:T(8,128)(2,1)S(1)}, u32[]{:S(2)}, u32[]{:S(2)}) %collective-permute-start.14) | collective-permute-done | bytes 9248 | tf_op jit(solution)/shard_map/ppermute | solution.py:14
  (164 shorter events, 46.5 us)
Async XLA Ops:
  0.6 133.1 %copy-start = (bf16[576,1536]{1,0:T(8,128)(2,1)S(1)}, bf16[576,1536]{1,0:T(8,128)(2,1)}, u32[]{:S(2)}) copy-start(bf16[576,1536]{1,0:T(8,128)(2,1)} %param.47) | copy-start | bytes 5308420
  3.8 20.7 %all-to-all-start = ((bf16[32,4,256]{2,1,0:T(4,128)(2,1)}), bf16[32,4,256]{2,1,0:T(4,128)(2,1)S(1)}, u32[]{:S(2)}, u32[]{:S(2)}) async-start(bf16[32,4,256]{2,1,0:T(4,128)(2,1)} %gather_fusion), calls=%async_computation | async-start | bytes 131072 | tf_op jit(solution)/shard_map/all_to_all | solution.py:153
  16.0 19.3 %copy-start.25 = (pred[24]{0:T(512)(128)(4,1)}, pred[24]{0:T(512)(128)(4,1)S(1)}, u32[]{:S(2)}) copy-start(pred[24]{0:T(512)(128)(4,1)S(1)} %fusion.89) | copy-start | bytes 76
  17.1 18.3 %copy-start.26 = (f32[24]{0:T(128)}, f32[24]{0:T(128)S(1)}, u32[]{:S(2)}) copy-start(f32[24]{0:T(128)S(1)} %add_rsqrt_fusion.2) | copy-start | bytes 292
  24.6 63.0 %all-to-all-start.1 = ((bf16[32,128,256]{2,1,0:T(8,128)(2,1)}), bf16[32,128,256]{2,1,0:T(8,128)(2,1)}, u32[]{:S(2)}, u32[]{:S(2)}) async-start(bf16[32,128,256]{2,1,0:T(8,128)(2,1)} %gather_fusion.3), calls=%async_computation.1 | async-start | bytes 4194304 | tf_op jit(solution)/shard_map/all_to_all | solution.py:156
  36.4 23.5 %copy-start.22 = (f32[1536]{0:T(1024)S(1)}, f32[1536]{0:T(1024)}, u32[]{:S(2)}) copy-start(f32[1536]{0:T(1024)} %param.40) | copy-start | bytes 18436
  36.5 23.5 %copy-start.11 = (bf16[192,1536]{1,0:T(8,128)(2,1)S(1)}, bf16[192,1536]{1,0:T(8,128)(2,1)}, u32[]{:S(2)}) copy-start(bf16[192,1536]{1,0:T(8,128)(2,1)} %param.41) | copy-start | bytes 1769476
  37.1 23.2 %copy-start.10 = (bf16[1536,256]{1,0:T(8,128)(2,1)S(1)}, bf16[1536,256]{1,0:T(8,128)(2,1)}, u32[]{:S(2)}) copy-start(bf16[1536,256]{1,0:T(8,128)(2,1)} %param.42) | copy-start | bytes 2359300
  39.2 4.4 %collective-permute-start = (bf16[24,1536]{1,0:T(8,128)(2,1)S(1)}, bf16[24,1536]{1,0:T(8,128)(2,1)S(1)}, u32[]{:S(2)}, u32[]{:S(2)}) collective-permute-start(bf16[24,1536]{1,0:T(8,128)(2,1)S(1)} %get-tuple-element.48), channel_id=1, source_target_pairs={{0,1},{1,0},{2,3},{3,2},{4,5},{5,4},{6,7},{7,6},{8,9},{9,8},{10,11... | collective-permute-start | bytes 221192 | tf_op jit(solution)/shard_map/ppermute | solution.py:14
  43.7 5.7 %collective-permute-start.1 = (bf16[24,1536]{1,0:T(8,128)(2,1)S(1)}, bf16[24,1536]{1,0:T(8,128)(2,1)S(1)}, u32[]{:S(2)}, u32[]{:S(2)}) collective-permute-start(bf16[24,1536]{1,0:T(8,128)(2,1)S(1)} %fusion.11), channel_id=1, source_target_pairs={{0,3},{1,2},{2,1},{3,0},{4,7},{5,6},{6,5},{7,4},{8,11},{9,10},{10,... | collective-permute-start | bytes 221192 | tf_op jit(solution)/shard_map/ppermute | solution.py:14
  50.0 8.8 %collective-permute-start.2 = (bf16[24,1536]{1,0:T(8,128)(2,1)}, bf16[24,1536]{1,0:T(8,128)(2,1)}, u32[]{:S(2)}, u32[]{:S(2)}) collective-permute-start(bf16[24,1536]{1,0:T(8,128)(2,1)} %fusion.26), channel_id=1, source_target_pairs={{0,4},{1,5},{2,6},{3,7},{4,0},{5,1},{6,2},{7,3},{8,12},{9,13},{10,... | collective-permute-start | bytes 221192 | tf_op jit(solution)/shard_map/ppermute | solution.py:14
  60.3 4.4 %collective-permute-start.3 = (bf16[24,1536]{1,0:T(8,128)(2,1)S(1)}, bf16[24,1536]{1,0:T(8,128)(2,1)S(1)}, u32[]{:S(2)}, u32[]{:S(2)}) collective-permute-start(bf16[24,1536]{1,0:T(8,128)(2,1)S(1)} %get-tuple-element.50), channel_id=1, source_target_pairs={{0,1},{1,0},{2,3},{3,2},{4,5},{5,4},{6,7},{7,6},{8,9},{9,8},{10,11... | collective-permute-start | bytes 221192 | tf_op jit(solution)/shard_map/ppermute | solution.py:14
  64.7 5.7 %collective-permute-start.4 = (bf16[24,1536]{1,0:T(8,128)(2,1)S(1)}, bf16[24,1536]{1,0:T(8,128)(2,1)S(1)}, u32[]{:S(2)}, u32[]{:S(2)}) collective-permute-start(bf16[24,1536]{1,0:T(8,128)(2,1)S(1)} %fusion.12), channel_id=1, source_target_pairs={{0,3},{1,2},{2,1},{3,0},{4,7},{5,6},{6,5},{7,4},{8,11},{9,10},{10,... | collective-permute-start | bytes 221192 | tf_op jit(solution)/shard_map/ppermute | solution.py:14
  70.4 5.3 %collective-permute-start.5 = (bf16[24,1536]{1,0:T(8,128)(2,1)S(1)}, bf16[24,1536]{1,0:T(8,128)(2,1)S(1)}, u32[]{:S(2)}, u32[]{:S(2)}) collective-permute-start(bf16[24,1536]{1,0:T(8,128)(2,1)S(1)} %fusion.27), channel_id=1, source_target_pairs={{0,4},{1,5},{2,6},{3,7},{4,0},{5,1},{6,2},{7,3},{8,12},{9,13},{10,... | collective-permute-start | bytes 221192 | tf_op jit(solution)/shard_map/ppermute | solution.py:14
  95.4 5.7 %collective-permute-start.6 = (f32[24,1664]{1,0:T(8,128)S(1)}, f32[24,1664]{1,0:T(8,128)S(1)}, u32[]{:S(2)}, u32[]{:S(2)}) collective-permute-start(f32[24,1664]{1,0:T(8,128)S(1)} %concatenate.38), channel_id=1, source_target_pairs={{0,1},{1,0},{2,3},{3,2},{4,5},{5,4},{6,7},{7,6},{8,9},{9,8},{10,11... | collective-permute-start | bytes 479240 | tf_op jit(solution)/shard_map/ppermute | solution.py:14
  101.5 6.5 %collective-permute-start.7 = (f32[24,1664]{1,0:T(8,128)S(1)}, f32[24,1664]{1,0:T(8,128)S(1)}, u32[]{:S(2)}, u32[]{:S(2)}) collective-permute-start(f32[24,1664]{1,0:T(8,128)S(1)} %concatenate.39), channel_id=1, source_target_pairs={{0,3},{1,2},{2,1},{3,0},{4,7},{5,6},{6,5},{7,4},{8,11},{9,10},{10,... | collective-permute-start | bytes 479240 | tf_op jit(solution)/shard_map/ppermute | solution.py:14
  108.4 21.8 %copy-start.5 = (f32[24,1536]{1,0:T(8,128)S(1)}, f32[24,1536]{1,0:T(8,128)}, u32[]{:S(2)}) copy-start(f32[24,1536]{1,0:T(8,128)} %copy-done.4) | copy-start | bytes 442372
  109.1 5.5 %collective-permute-start.8 = (f32[24,1664]{1,0:T(8,128)}, f32[24,1664]{1,0:T(8,128)S(1)}, u32[]{:S(2)}, u32[]{:S(2)}) collective-permute-start(f32[24,1664]{1,0:T(8,128)} %concatenate.40), channel_id=1, source_target_pairs={{0,4},{1,5},{2,6},{3,7},{4,0},{5,1},{6,2},{7,3},{8,12},{9,13},{10,... | collective-permute-start | bytes 479240 | tf_op jit(solution)/shard_map/ppermute | solution.py:14
  115.4 4.4 %collective-permute-start.9 = (bf16[24,1536]{1,0:T(8,128)(2,1)S(1)}, bf16[24,1536]{1,0:T(8,128)(2,1)S(1)}, u32[]{:S(2)}, u32[]{:S(2)}) collective-permute-start(bf16[24,1536]{1,0:T(8,128)(2,1)S(1)} %get-tuple-element.54), channel_id=1, source_target_pairs={{0,1},{1,0},{2,3},{3,2},{4,5},{5,4},{6,7},{7,6},{8,9},{9,8},{10,11... | collective-permute-start | bytes 221192 | tf_op jit(solution)/shard_map/ppermute | solution.py:14
  119.9 5.8 %collective-permute-start.10 = (bf16[24,1536]{1,0:T(8,128)(2,1)S(1)}, bf16[24,1536]{1,0:T(8,128)(2,1)S(1)}, u32[]{:S(2)}, u32[]{:S(2)}) collective-permute-start(bf16[24,1536]{1,0:T(8,128)(2,1)S(1)} %fusion.13), channel_id=1, source_target_pairs={{0,3},{1,2},{2,1},{3,0},{4,7},{5,6},{6,5},{7,4},{8,11},{9,10},{10,... | collective-permute-start | bytes 221192 | tf_op jit(solution)/shard_map/ppermute | solution.py:14
  125.7 4.4 %collective-permute-start.11 = (bf16[24,1536]{1,0:T(8,128)(2,1)S(1)}, bf16[24,1536]{1,0:T(8,128)(2,1)S(1)}, u32[]{:S(2)}, u32[]{:S(2)}) collective-permute-start(bf16[24,1536]{1,0:T(8,128)(2,1)S(1)} %fusion.28), channel_id=1, source_target_pairs={{0,4},{1,5},{2,6},{3,7},{4,0},{5,1},{6,2},{7,3},{8,12},{9,13},{10,... | collective-permute-start | bytes 221192 | tf_op jit(solution)/shard_map/ppermute | solution.py:14
  137.4 4.2 %collective-permute-start.12 = (bf16[24,4,192]{2,0,1:T(8,128)(2,1)S(1)}, bf16[24,4,192]{2,0,1:T(8,128)(2,1)S(1)}, u32[]{:S(2)}, u32[]{:S(2)}) collective-permute-start(bf16[24,4,192]{2,0,1:T(8,128)(2,1)S(1)} %select_convert_fusion), channel_id=1, source_target_pairs={{0,4},{1,5},{2,6},{3,7},{4,0},{5,1},{6,2},{7,3},{8,12},{9,13},{10,... | collective-permute-start | bytes 110600 | tf_op jit(solution)/shard_map/ppermute | solution.py:14
  141.6 5.1 %collective-permute-start.13 = (bf16[24,2,192]{2,0,1:T(8,128)(2,1)S(1)}, bf16[24,2,192]{2,0,1:T(8,128)(2,1)S(1)}, u32[]{:S(2)}, u32[]{:S(2)}) collective-permute-start(bf16[24,2,192]{2,0,1:T(8,128)(2,1)S(1)} %select_convert_fusion.1), channel_id=1, source_target_pairs={{0,3},{1,2},{2,1},{3,0},{4,7},{5,6},{6,5},{7,4},{8,11},{9,10},{10,... | collective-permute-start | bytes 55304 | tf_op jit(solution)/shard_map/ppermute | solution.py:14
  146.8 3.8 %collective-permute-start.14 = (bf16[24,1,192]{2,0,1:T(8,128)(2,1)S(1)}, bf16[24,1,192]{2,0,1:T(8,128)(2,1)S(1)}, u32[]{:S(2)}, u32[]{:S(2)}) collective-permute-start(bf16[24,1,192]{2,0,1:T(8,128)(2,1)S(1)} %select_convert_fusion.2), channel_id=1, source_target_pairs={{0,1},{1,0},{2,3},{3,2},{4,5},{5,4},{6,7},{7,6},{8,9},{9,8},{10,11... | collective-permute-start | bytes 27656 | tf_op jit(solution)/shard_map/ppermute | solution.py:14
  (22 other events, 207.0 us)

commit v8 on v7

--- a/solution.py
+++ b/solution.py
@@ -226,27 +226,46 @@
     value_new = key_value[:, head_size:].astype(jnp.bfloat16)
     window = page_rows * lax.axis_size("mlp")
     score_scale = 1.0 / math.sqrt(head_size)
-    scores = (
-        jnp.einsum(
-            "shd,swd->shw",
-            queries,
-            moved_cache[..., :head_size],
-            preferred_element_type=jnp.float32,
-        )
-        * score_scale
-    )
     slot_ids = mlp_id * page_rows + jnp.arange(page_rows, dtype=jnp.int32)[None, :]
     current = position[:, None]
     held_pos = current - 1 - jnp.mod(current - 1 - slot_ids, window)
     usable = ((held_pos >= 0) & (held_pos != current - window))[:, None, :]
-    local_top = jnp.max(jnp.where(usable, scores, -1e30), axis=-1)
-    weights = jnp.where(usable, jnp.exp(scores - local_top[..., None]), 0.0)
-    local_sum = jnp.sum(weights, axis=-1)
-    local_acc = jnp.einsum(
-        "shw,swd->shd",
-        weights.astype(jnp.bfloat16),
-        moved_cache[..., head_size:],
-        preferred_element_type=jnp.float32,
+
+    def window_part(query_rows, rows, usable_rows):
+        scores = (
+            jnp.einsum(
+                "shd,swd->shw",
+                query_rows,
+                rows[..., :head_size],
+                preferred_element_type=jnp.float32,
+            )
+            * score_scale
+        )
+        top = jnp.max(jnp.where(usable_rows, scores, -1e30), axis=-1)
+        weights = jnp.where(usable_rows, jnp.exp(scores - top[..., None]), 0.0)
+        acc = jnp.einsum(
+            "shw,swd->shd",
+            weights.astype(jnp.bfloat16),
+            rows[..., head_size:],
+            preferred_element_type=jnp.float32,
+        )
+        return top, jnp.sum(weights, axis=-1), acc
+
+    stay_top, stay_sum, stay_acc = window_part(queries, cache, usable)
+    came_top, came_sum, came_acc = window_part(
+        jnp.take(queries, my_leave, axis=0, mode="clip"),
+        jnp.take(got_cache, anchor, axis=0, mode="clip"),
+        jnp.take(usable, my_leave, axis=0, mode="clip"),
+    )
+    arrive_rank = jnp.sum(jnp.where(match_slot, rank_ids[None, :], 0), axis=1)
+    local_top = jnp.where(
+        arriving[:, None], jnp.take(came_top, arrive_rank, axis=0, mode="clip"), stay_top
+    )
+    local_sum = jnp.where(
+        arriving[:, None], jnp.take(came_sum, arrive_rank, axis=0, mode="clip"), stay_sum
+    )
+    local_acc = jnp.where(
+        arriving[:, None, None], jnp.take(came_acc, arrive_rank, axis=0, mode="clip"), stay_acc
     )
     stat_pad = jnp.zeros((req_rows, 128 - 2 * heads), jnp.float32)
     merged = joined(

time: 153 us -> 186 us (1.22)
  local copies, waits for them, and re-layouts: 15.6 us -> 39.3 us
  other arithmetic: 20.6 us -> 30.3 us
  waiting for transfers between devices: 60.1 us -> 52.6 us
  matrix products: 10.1 us -> 17.5 us
    gather x0 -> x6, local copies, waits for them, and re-layouts: none -> 9.9 us  [the longest x1 3.23 us: per_device(): jnp.take(got_cache, anchor, axis=0, mode='clip')]
    all_to_all x1, waiting for transfers between devices: 10.2 us -> 4.35 us  [per_device(): lax.all_to_all(jnp.take(cache, send_slot, axis=0, mode='clip'), 'req', 0,...]
    unnamed x62 -> x84, local copies, waits for them, and re-layouts: 0.95 us -> 6.43 us
    dot_general x2 -> x4, matrix products: 1.03 us -> 6.18 us  [the longest x2 3.29 us: window_part(): jnp.einsum('shw,swd->shd', weights.astype(jnp.bfloat16), rows[..., head_s...]
    reshape x3, local copies, waits for them, and re-layouts: 0.08 us -> 3.25 us  [combine_parts(): second_part[:, :width].reshape(rows, heads, head_size)]
    add x2, other arithmetic: 0.15 us -> 2.92 us  [combine_parts(): first_sum * first_factor + second_sum * second_factor]
    concatenate x2, local copies, waits for them, and re-layouts: 0.83 us -> 3.13 us  [combine_parts(): return jnp.concatenate([acc.reshape(rows, width), stats], axis=-1)]
    add x2, other arithmetic: 0.34 us -> 2.28 us  [combine_parts(): first_part[:, :width].reshape(rows, heads, head_size)]
  transfers between devices with their start and end apart: 17 -> 17, of which waited for: 16 -> 15; matrix products, arithmetic and copies ran while one was open for 16% -> 19% of each run, Pallas kernels for 0% -> 0%
where the time goes in v8:
time: 186 us; the launch traced here: 184 us
  waiting for transfers between devices  52.6 us (28%)
  starting transfers between devices  43 us (23%)
  local copies, waits for them, and re-layouts  39.3 us (21%)
  other arithmetic  30.3 us (16%)
  matrix products  17.5 us (9%)
    ppermute x15, waiting for transfers between devices, partner_swap(): return jax.tree.map(lambda part: lax.ppermute(part, axis, pairs), value)  48.2 us
    ppermute x15, starting transfers between devices, partner_swap(): return jax.tree.map(lambda part: lax.ppermute(part, axis, pairs), value)  21.8 us
    all_to_all x1, starting transfers between devices, per_device(): lax.all_to_all(jnp.take(states, send_slot, axis=0, mode='clip'), 'req', 0...  11.2 us
    all_to_all x1, starting transfers between devices, per_device(): lax.all_to_all(jnp.take(cache, send_slot, axis=0, mode='clip'), 'req', 0,...  10 us
    unnamed x84, local copies, waits for them, and re-layouts  6.43 us
    all_to_all x1, waiting for transfers between devices, per_device(): lax.all_to_all(jnp.take(cache, send_slot, axis=0, mode='clip'), 'req', 0,...  4.35 us
  transfers between devices with their start and end apart: 17, of which 15 were waited for; matrix products, arithmetic and copies ran while one was open for 19% of the time, Pallas kernels for 0%

profile of v8, /device:TPU:32, one launch (start us, length us, event | category | flops | bytes accessed | tf_op | source)
XLA Modules:
  0.0 184.0 jit_solution(18296265866535082077)
XLA Ops:
  3.8 11.2 %all-to-all-start = ((bf16[32,4,256]{2,1,0:T(4,128)(2,1)}), bf16[32,4,256]{2,1,0:T(4,128)(2,1)S(1)}, u32[]{:S(2)}, u32[]{:S(2)}) async-start(bf16[32,4,256]{2,1,0:T(4,128)(2,1)} %gather_fusion), calls=%async_computation | async-start | bytes 131072 | tf_op jit(solution)/shard_map/all_to_all | solution.py:153
  21.4 3.4 %gather_fusion.5 = bf16[32,128,256]{2,1,0:T(8,128)(2,1)} fusion(bf16[24,128,256]{2,1,0:T(8,128)(2,1)} %param.28, s32[1024]{0:T(1024)S(1)} %pad_clamp_fusion.5), kind=kCustom, calls=%fused_computation.5 | custom fusion | bytes 4194432 | tf_op jit(solution)/shard_map/jit(_take)/gather | solution.py:157
  24.9 10.0 %all-to-all-start.1 = ((bf16[32,128,256]{2,1,0:T(8,128)(2,1)}), bf16[32,128,256]{2,1,0:T(8,128)(2,1)}, u32[]{:S(2)}, u32[]{:S(2)}) async-start(bf16[32,128,256]{2,1,0:T(8,128)(2,1)} %gather_fusion.5), calls=%async_computation.1 | async-start | bytes 4194304 | tf_op jit(solution)/shard_map/all_to_all | solution.py:156
  43.9 3.1 %collective-permute-start.1 = (bf16[24,1536]{1,0:T(8,128)(2,1)S(1)}, bf16[24,1536]{1,0:T(8,128)(2,1)S(1)}, u32[]{:S(2)}, u32[]{:S(2)}) collective-permute-start(bf16[24,1536]{1,0:T(8,128)(2,1)S(1)} %fusion.13), channel_id=1, source_target_pairs={{0,3},{1,2},{2,1},{3,0},{4,7},{5,6},{6,5},{7,4},{8,11},{9,10},{10,... | collective-permute-start | bytes 221192 | tf_op jit(solution)/shard_map/ppermute | solution.py:14
  50.9 7.7 %collective-permute-done.2 = bf16[24,1536]{1,0:T(8,128)(2,1)S(1)} collective-permute-done((bf16[24,1536]{1,0:T(8,128)(2,1)S(1)}, bf16[24,1536]{1,0:T(8,128)(2,1)S(1)}, u32[]{:S(2)}, u32[]{:S(2)}) %collective-permute-start.2) | collective-permute-done | bytes 73760 | tf_op jit(solution)/shard_map/ppermute | solution.py:14
  60.9 2.9 %collective-permute-done.3 = bf16[24,1536]{1,0:T(8,128)(2,1)S(1)} collective-permute-done((bf16[24,1536]{1,0:T(8,128)(2,1)S(1)}, bf16[24,1536]{1,0:T(8,128)(2,1)S(1)}, u32[]{:S(2)}, u32[]{:S(2)}) %collective-permute-start.3) | collective-permute-done | bytes 73760 | tf_op jit(solution)/shard_map/ppermute | solution.py:14
  63.8 3.1 %collective-permute-start.4 = (bf16[24,1536]{1,0:T(8,128)(2,1)S(1)}, bf16[24,1536]{1,0:T(8,128)(2,1)S(1)}, u32[]{:S(2)}, u32[]{:S(2)}) collective-permute-start(bf16[24,1536]{1,0:T(8,128)(2,1)S(1)} %fusion.14), channel_id=1, source_target_pairs={{0,3},{1,2},{2,1},{3,0},{4,7},{5,6},{6,5},{7,4},{8,11},{9,10},{10,... | collective-permute-start | bytes 221192 | tf_op jit(solution)/shard_map/ppermute | solution.py:14
  67.0 2.4 %collective-permute-done.4 = bf16[24,1536]{1,0:T(8,128)(2,1)S(1)} collective-permute-done((bf16[24,1536]{1,0:T(8,128)(2,1)S(1)}, bf16[24,1536]{1,0:T(8,128)(2,1)S(1)}, u32[]{:S(2)}, u32[]{:S(2)}) %collective-permute-start.4) | collective-permute-done | bytes 73760 | tf_op jit(solution)/shard_map/ppermute | solution.py:14
  69.6 6.4 %collective-permute-done.5 = bf16[24,1536]{1,0:T(8,128)(2,1)S(1)} collective-permute-done((bf16[24,1536]{1,0:T(8,128)(2,1)S(1)}, bf16[24,1536]{1,0:T(8,128)(2,1)S(1)}, u32[]{:S(2)}, u32[]{:S(2)}) %collective-permute-start.5) | collective-permute-done | bytes 73760 | tf_op jit(solution)/shard_map/ppermute | solution.py:14
  83.6 4.3 %all-to-all-done.1 = bf16[32,128,256]{2,1,0:T(8,128)(2,1)} async-done(((bf16[32,128,256]{2,1,0:T(8,128)(2,1)}), bf16[32,128,256]{2,1,0:T(8,128)(2,1)}, u32[]{:S(2)}, u32[]{:S(2)}) %all-to-all-start.1) | async-done | bytes 2097184 | tf_op jit(solution)/shard_map/all_to_all | solution.py:156
  88.0 3.2 %gather_fusion.6 = bf16[13,128,256]{2,1,0:T(8,128)(2,1)} fusion(bf16[32,128,256]{2,1,0:T(8,128)(2,1)} %all-to-all-done.1, s32[1024]{0:T(1024)} %pad_clamp_fusion.1), kind=kCustom, calls=%fused_computation.6 | custom fusion | bytes 1703988 | tf_op jit(solution)/shard_map/jit(_take)/gather | solution.py:257
  96.7 2.3 %gather_fusion.7 = f32[24,12,128]{2,1,0:T(8,128)} fusion(f32[13,12,128]{2,1,0:T(8,128)} %fusion.4, s32[1024]{0:T(1024)} %pad_clamp_fusion), kind=kCustom, calls=%fused_computation.7 | custom fusion | bytes 295008 | tf_op jit(solution)/shard_map/jit(_take)/gather | solution.py:268
  104.9 4.3 %collective-permute-done.6 = f32[24,1664]{1,0:T(8,128)S(1)} collective-permute-done((f32[24,1664]{1,0:T(8,128)}, f32[24,1664]{1,0:T(8,128)S(1)}, u32[]{:S(2)}, u32[]{:S(2)}) %collective-permute-start.6) | collective-permute-done | bytes 159776 | tf_op jit(solution)/shard_map/ppermute | solution.py:14
  116.2 3.0 %collective-permute-start.7 = (f32[24,1664]{1,0:T(8,128)}, f32[24,1664]{1,0:T(8,128)S(1)}, u32[]{:S(2)}, u32[]{:S(2)}) collective-permute-start(f32[24,1664]{1,0:T(8,128)} %concatenate.39), channel_id=1, source_target_pairs={{0,3},{1,2},{2,1},{3,0},{4,7},{5,6},{6,5},{7,4},{8,11},{9,10},{10,... | collective-permute-start | bytes 479240 | tf_op jit(solution)/shard_map/ppermute | solution.py:14
  119.2 3.7 %collective-permute-done.7 = f32[24,1664]{1,0:T(8,128)S(1)} collective-permute-done((f32[24,1664]{1,0:T(8,128)}, f32[24,1664]{1,0:T(8,128)S(1)}, u32[]{:S(2)}, u32[]{:S(2)}) %collective-permute-start.7) | collective-permute-done | bytes 159776 | tf_op jit(solution)/shard_map/ppermute | solution.py:14
  131.2 3.6 %collective-permute-done.8 = f32[24,1664]{1,0:T(8,128)S(1)} collective-permute-done((f32[24,1664]{1,0:T(8,128)}, f32[24,1664]{1,0:T(8,128)S(1)}, u32[]{:S(2)}, u32[]{:S(2)}) %collective-permute-start.8) | collective-permute-done | bytes 159776 | tf_op jit(solution)/shard_map/ppermute | solution.py:14
  142.4 4.0 %collective-permute-done.9 = bf16[24,1536]{1,0:T(8,128)(2,1)S(1)} collective-permute-done((bf16[24,1536]{1,0:T(8,128)(2,1)S(1)}, bf16[24,1536]{1,0:T(8,128)(2,1)S(1)}, u32[]{:S(2)}, u32[]{:S(2)}) %collective-permute-start.9) | collective-permute-done | bytes 73760 | tf_op jit(solution)/shard_map/ppermute | solution.py:14
  147.7 3.0 %collective-permute-start.10 = (bf16[24,1536]{1,0:T(8,128)(2,1)}, bf16[24,1536]{1,0:T(8,128)(2,1)}, u32[]{:S(2)}, u32[]{:S(2)}) collective-permute-start(bf16[24,1536]{1,0:T(8,128)(2,1)} %fusion.15), channel_id=1, source_target_pairs={{0,3},{1,2},{2,1},{3,0},{4,7},{5,6},{6,5},{7,4},{8,11},{9,10},{10,... | collective-permute-start | bytes 221192 | tf_op jit(solution)/shard_map/ppermute | solution.py:14
  155.8 3.1 %collective-permute-done.11 = bf16[24,1536]{1,0:T(8,128)(2,1)S(1)} collective-permute-done((bf16[24,1536]{1,0:T(8,128)(2,1)S(1)}, bf16[24,1536]{1,0:T(8,128)(2,1)S(1)}, u32[]{:S(2)}, u32[]{:S(2)}) %collective-permute-start.11) | collective-permute-done | bytes 73760 | tf_op jit(solution)/shard_map/ppermute | solution.py:14
  162.8 3.2 %fusion.1 = f32[24,1536]{1,0:T(8,128)} fusion(bf16[576,1536]{1,0:T(8,128)(2,1)S(1)} %copy-done, bf16[1536,576]{0,1:T(8,128)(2,1)} %param.46, f32[24,576]{1,0:T(8,128)S(1)} %fusion.116, f32[24,1536]{1,0:T(8,128)} %copy-done.4, f32[1536]{0:T(1024)S(1)} %copy-done.29, f32[24]{0:T(128)S(1)} %add_rsqrt_fusion), kind=kOutput, calls=%fused_computation.18 | convolution fusion | flops 85183488 | bytes 3895392 | tf_op jit(solution)/shard_map/dot_general | solution.py:308
  167.9 3.4 %collective-permute-done.12 = bf16[24,4,192]{2,0,1:T(8,128)(2,1)S(1)} collective-permute-done((bf16[24,4,192]{2,0,1:T(8,128)(2,1)S(1)}, bf16[24,4,192]{2,0,1:T(8,128)(2,1)S(1)}, u32[]{:S(2)}, u32[]{:S(2)}) %collective-permute-start.12) | collective-permute-done | bytes 36896 | tf_op jit(solution)/shard_map/ppermute | solution.py:14
  171.4 3.1 %collective-permute-start.13 = (bf16[24,2,192]{2,0,1:T(8,128)(2,1)S(1)}, bf16[24,2,192]{2,0,1:T(8,128)(2,1)S(1)}, u32[]{:S(2)}, u32[]{:S(2)}) collective-permute-start(bf16[24,2,192]{2,0,1:T(8,128)(2,1)S(1)} %select_convert_fusion.1), channel_id=1, source_target_pairs={{0,3},{1,2},{2,1},{3,0},{4,7},{5,6},{6,5},{7,4},{8,11},{9,10},{10,... | collective-permute-start | bytes 55304 | tf_op jit(solution)/shard_map/ppermute | solution.py:14
  175.2 3.6 %gather_fusion.10 = bf16[24,128,256]{2,1,0:T(8,128)(2,1)} fusion(bf16[32,128,256]{2,1,0:T(8,128)(2,1)} %all-to-all-done.1, s32[1024]{0:T(1024)} %copy-done.37), kind=kCustom, calls=%fused_computation.10 | custom fusion | bytes 3145824 | tf_op jit(solution)/shard_map/jit(_take)/gather | solution.py:170
  178.9 2.6 %select_select_fusion = bf16[24,128,256]{2,1,0:T(8,128)(2,1)} fusion(bf16[24,128,256]{2,1,0:T(8,128)(2,1)} %gather_fusion.10, bf16[24,128,256]{2,1,0:T(8,128)(2,1)S(1)} %copy-done.1, pred[24]{0:T(512)(128)(4,1)S(1)} %copy-done.32, pred[24,128]{1,0:T(8,128)(4,1)S(1)} %copy-done.33, bf16[24,256]{1,0:T(8,128)(2,1)S(1)} %pad_maximum_fusion.3), kind=kLoop, calls=%fused_computation.11 | loop fusion | flops 1572864 | bytes 4733976 | tf_op jit(solution)/shard_map/jit(_where)/select_n | solution.py:316
  (200 shorter events, 82.1 us)
Async XLA Ops:
  0.6 162.2 %copy-start = (bf16[576,1536]{1,0:T(8,128)(2,1)S(1)}, bf16[576,1536]{1,0:T(8,128)(2,1)}, u32[]{:S(2)}) copy-start(bf16[576,1536]{1,0:T(8,128)(2,1)} %param.47) | copy-start | bytes 5308420
  3.8 21.1 %all-to-all-start = ((bf16[32,4,256]{2,1,0:T(4,128)(2,1)}), bf16[32,4,256]{2,1,0:T(4,128)(2,1)S(1)}, u32[]{:S(2)}, u32[]{:S(2)}) async-start(bf16[32,4,256]{2,1,0:T(4,128)(2,1)} %gather_fusion), calls=%async_computation | async-start | bytes 131072 | tf_op jit(solution)/shard_map/all_to_all | solution.py:153
  20.0 62.2 %copy-start.27 = (pred[24,128]{1,0:T(8,128)(4,1)}, pred[24,128]{1,0:T(8,128)(4,1)S(1)}, u32[]{:S(2)}) copy-start(pred[24,128]{1,0:T(8,128)(4,1)S(1)} %get-tuple-element.42) | copy-start | bytes 9220
  24.9 63.0 %all-to-all-start.1 = ((bf16[32,128,256]{2,1,0:T(8,128)(2,1)}), bf16[32,128,256]{2,1,0:T(8,128)(2,1)}, u32[]{:S(2)}, u32[]{:S(2)}) async-start(bf16[32,128,256]{2,1,0:T(8,128)(2,1)} %gather_fusion.5), calls=%async_computation.1 | async-start | bytes 4194304 | tf_op jit(solution)/shard_map/all_to_all | solution.py:156
  36.6 22.1 %copy-start.34 = (f32[1536]{0:T(1024)S(1)}, f32[1536]{0:T(1024)}, u32[]{:S(2)}) copy-start(f32[1536]{0:T(1024)} %param.40) | copy-start | bytes 18436
  36.8 22.1 %copy-start.10 = (bf16[192,1536]{1,0:T(8,128)(2,1)S(1)}, bf16[192,1536]{1,0:T(8,128)(2,1)}, u32[]{:S(2)}) copy-start(bf16[192,1536]{1,0:T(8,128)(2,1)} %param.41) | copy-start | bytes 1769476
  39.5 4.4 %collective-permute-start = (bf16[24,1536]{1,0:T(8,128)(2,1)S(1)}, bf16[24,1536]{1,0:T(8,128)(2,1)S(1)}, u32[]{:S(2)}, u32[]{:S(2)}) collective-permute-start(bf16[24,1536]{1,0:T(8,128)(2,1)S(1)} %get-tuple-element.51), channel_id=1, source_target_pairs={{0,1},{1,0},{2,3},{3,2},{4,5},{5,4},{6,7},{7,6},{8,9},{9,8},{10,11... | collective-permute-start | bytes 221192 | tf_op jit(solution)/shard_map/ppermute | solution.py:14
  43.9 5.7 %collective-permute-start.1 = (bf16[24,1536]{1,0:T(8,128)(2,1)S(1)}, bf16[24,1536]{1,0:T(8,128)(2,1)S(1)}, u32[]{:S(2)}, u32[]{:S(2)}) collective-permute-start(bf16[24,1536]{1,0:T(8,128)(2,1)S(1)} %fusion.13), channel_id=1, source_target_pairs={{0,3},{1,2},{2,1},{3,0},{4,7},{5,6},{6,5},{7,4},{8,11},{9,10},{10,... | collective-permute-start | bytes 221192 | tf_op jit(solution)/shard_map/ppermute | solution.py:14
  49.6 9.0 %collective-permute-start.2 = (bf16[24,1536]{1,0:T(8,128)(2,1)S(1)}, bf16[24,1536]{1,0:T(8,128)(2,1)S(1)}, u32[]{:S(2)}, u32[]{:S(2)}) collective-permute-start(bf16[24,1536]{1,0:T(8,128)(2,1)S(1)} %fusion.30), channel_id=1, source_target_pairs={{0,4},{1,5},{2,6},{3,7},{4,0},{5,1},{6,2},{7,3},{8,12},{9,13},{10,... | collective-permute-start | bytes 221192 | tf_op jit(solution)/shard_map/ppermute | solution.py:14
  59.4 21.3 %copy-start.1 = (bf16[24,128,256]{2,1,0:T(8,128)(2,1)S(1)}, bf16[24,128,256]{2,1,0:T(8,128)(2,1)}, u32[]{:S(2)}) copy-start(bf16[24,128,256]{2,1,0:T(8,128)(2,1)} %param.28) | copy-start | bytes 4718596
  59.4 4.4 %collective-permute-start.3 = (bf16[24,1536]{1,0:T(8,128)(2,1)S(1)}, bf16[24,1536]{1,0:T(8,128)(2,1)S(1)}, u32[]{:S(2)}, u32[]{:S(2)}) collective-permute-start(bf16[24,1536]{1,0:T(8,128)(2,1)S(1)} %get-tuple-element.53), channel_id=1, source_target_pairs={{0,1},{1,0},{2,3},{3,2},{4,5},{5,4},{6,7},{7,6},{8,9},{9,8},{10,11... | collective-permute-start | bytes 221192 | tf_op jit(solution)/shard_map/ppermute | solution.py:14
  63.8 5.7 %collective-permute-start.4 = (bf16[24,1536]{1,0:T(8,128)(2,1)S(1)}, bf16[24,1536]{1,0:T(8,128)(2,1)S(1)}, u32[]{:S(2)}, u32[]{:S(2)}) collective-permute-start(bf16[24,1536]{1,0:T(8,128)(2,1)S(1)} %fusion.14), channel_id=1, source_target_pairs={{0,3},{1,2},{2,1},{3,0},{4,7},{5,6},{6,5},{7,4},{8,11},{9,10},{10,... | collective-permute-start | bytes 221192 | tf_op jit(solution)/shard_map/ppermute | solution.py:14
  69.5 6.6 %collective-permute-start.5 = (bf16[24,1536]{1,0:T(8,128)(2,1)S(1)}, bf16[24,1536]{1,0:T(8,128)(2,1)S(1)}, u32[]{:S(2)}, u32[]{:S(2)}) collective-permute-start(bf16[24,1536]{1,0:T(8,128)(2,1)S(1)} %fusion.31), channel_id=1, source_target_pairs={{0,4},{1,5},{2,6},{3,7},{4,0},{5,1},{6,2},{7,3},{8,12},{9,13},{10,... | collective-permute-start | bytes 221192 | tf_op jit(solution)/shard_map/ppermute | solution.py:14
  103.3 5.9 %collective-permute-start.6 = (f32[24,1664]{1,0:T(8,128)}, f32[24,1664]{1,0:T(8,128)S(1)}, u32[]{:S(2)}, u32[]{:S(2)}) collective-permute-start(f32[24,1664]{1,0:T(8,128)} %concatenate.38), channel_id=1, source_target_pairs={{0,1},{1,0},{2,3},{3,2},{4,5},{5,4},{6,7},{7,6},{8,9},{9,8},{10,11... | collective-permute-start | bytes 479240 | tf_op jit(solution)/shard_map/ppermute | solution.py:14
  116.2 6.7 %collective-permute-start.7 = (f32[24,1664]{1,0:T(8,128)}, f32[24,1664]{1,0:T(8,128)S(1)}, u32[]{:S(2)}, u32[]{:S(2)}) collective-permute-start(f32[24,1664]{1,0:T(8,128)} %concatenate.39), channel_id=1, source_target_pairs={{0,3},{1,2},{2,1},{3,0},{4,7},{5,6},{6,5},{7,4},{8,11},{9,10},{10,... | collective-permute-start | bytes 479240 | tf_op jit(solution)/shard_map/ppermute | solution.py:14
  129.3 25.9 %copy-start.25 = (bf16[24,256]{1,0:T(8,128)(2,1)S(1)}, bf16[24,256]{1,0:T(8,128)(2,1)}, u32[]{:S(2)}) copy-start(bf16[24,256]{1,0:T(8,128)(2,1)} %get-tuple-element.50) | copy-start | bytes 36868
  129.3 5.5 %collective-permute-start.8 = (f32[24,1664]{1,0:T(8,128)}, f32[24,1664]{1,0:T(8,128)S(1)}, u32[]{:S(2)}, u32[]{:S(2)}) collective-permute-start(f32[24,1664]{1,0:T(8,128)} %concatenate.40), channel_id=1, source_target_pairs={{0,4},{1,5},{2,6},{3,7},{4,0},{5,1},{6,2},{7,3},{8,12},{9,13},{10,... | collective-permute-start | bytes 479240 | tf_op jit(solution)/shard_map/ppermute | solution.py:14
  140.6 20.1 %copy-start.29 = (f32[1536]{0:T(1024)S(1)}, f32[1536]{0:T(1024)}, u32[]{:S(2)}) copy-start(f32[1536]{0:T(1024)} %param.44) | copy-start | bytes 18436
  141.9 4.4 %collective-permute-start.9 = (bf16[24,1536]{1,0:T(8,128)(2,1)S(1)}, bf16[24,1536]{1,0:T(8,128)(2,1)S(1)}, u32[]{:S(2)}, u32[]{:S(2)}) collective-permute-start(bf16[24,1536]{1,0:T(8,128)(2,1)S(1)} %get-tuple-element.59), channel_id=1, source_target_pairs={{0,1},{1,0},{2,3},{3,2},{4,5},{5,4},{6,7},{7,6},{8,9},{9,8},{10,11... | collective-permute-start | bytes 221192 | tf_op jit(solution)/shard_map/ppermute | solution.py:14
  147.7 5.9 %collective-permute-start.10 = (bf16[24,1536]{1,0:T(8,128)(2,1)}, bf16[24,1536]{1,0:T(8,128)(2,1)}, u32[]{:S(2)}, u32[]{:S(2)}) collective-permute-start(bf16[24,1536]{1,0:T(8,128)(2,1)} %fusion.15), channel_id=1, source_target_pairs={{0,3},{1,2},{2,1},{3,0},{4,7},{5,6},{6,5},{7,4},{8,11},{9,10},{10,... | collective-permute-start | bytes 221192 | tf_op jit(solution)/shard_map/ppermute | solution.py:14
  154.5 4.4 %collective-permute-start.11 = (bf16[24,1536]{1,0:T(8,128)(2,1)S(1)}, bf16[24,1536]{1,0:T(8,128)(2,1)S(1)}, u32[]{:S(2)}, u32[]{:S(2)}) collective-permute-start(bf16[24,1536]{1,0:T(8,128)(2,1)S(1)} %fusion.32), channel_id=1, source_target_pairs={{0,4},{1,5},{2,6},{3,7},{4,0},{5,1},{6,2},{7,3},{8,12},{9,13},{10,... | collective-permute-start | bytes 221192 | tf_op jit(solution)/shard_map/ppermute | solution.py:14
  167.2 4.2 %collective-permute-start.12 = (bf16[24,4,192]{2,0,1:T(8,128)(2,1)S(1)}, bf16[24,4,192]{2,0,1:T(8,128)(2,1)S(1)}, u32[]{:S(2)}, u32[]{:S(2)}) collective-permute-start(bf16[24,4,192]{2,0,1:T(8,128)(2,1)S(1)} %select_convert_fusion), channel_id=1, source_target_pairs={{0,4},{1,5},{2,6},{3,7},{4,0},{5,1},{6,2},{7,3},{8,12},{9,13},{10,... | collective-permute-start | bytes 110600 | tf_op jit(solution)/shard_map/ppermute | solution.py:14
  171.4 7.4 %collective-permute-start.13 = (bf16[24,2,192]{2,0,1:T(8,128)(2,1)S(1)}, bf16[24,2,192]{2,0,1:T(8,128)(2,1)S(1)}, u32[]{:S(2)}, u32[]{:S(2)}) collective-permute-start(bf16[24,2,192]{2,0,1:T(8,128)(2,1)S(1)} %select_convert_fusion.1), channel_id=1, source_target_pairs={{0,3},{1,2},{2,1},{3,0},{4,7},{5,6},{6,5},{7,4},{8,11},{9,10},{10,... | collective-permute-start | bytes 55304 | tf_op jit(solution)/shard_map/ppermute | solution.py:14
  178.8 3.8 %collective-permute-start.14 = (bf16[24,1,192]{2,0,1:T(8,128)(2,1)S(1)}, bf16[24,1,192]{2,0,1:T(8,128)(2,1)S(1)}, u32[]{:S(2)}, u32[]{:S(2)}) collective-permute-start(bf16[24,1,192]{2,0,1:T(8,128)(2,1)S(1)} %select_convert_fusion.2), channel_id=1, source_target_pairs={{0,1},{1,0},{2,3},{3,2},{4,5},{5,4},{6,7},{7,6},{8,9},{9,8},{10,11... | collective-permute-start | bytes 27656 | tf_op jit(solution)/shard_map/ppermute | solution.py:14
  (33 other events, 231.4 us)

commit v9 on v7

--- a/solution.py
+++ b/solution.py
@@ -150,12 +150,15 @@
     states = jnp.concatenate([conv_state, lru_state[:, None, :]], axis=1)
     to_group = my_owner[None, :] == group_ids[:, None]
     send_slot = jnp.sum(jnp.where(to_group, my_leave[None, :], 0), axis=1)
-    got_states = lax.all_to_all(
-        jnp.take(states, send_slot, axis=0, mode="clip"), "req", 0, 0, tiled=True
-    )
-    got_cache = lax.all_to_all(
-        jnp.take(cache, send_slot, axis=0, mode="clip"), "req", 0, 0, tiled=True
-    )
+    states_send, cache_send = lax.optimization_barrier(
+        (
+            jnp.take(states, send_slot, axis=0, mode="clip"),
+            jnp.take(cache, send_slot, axis=0, mode="clip"),
+        )
+    )
+    got_states = lax.all_to_all(states_send, "req", 0, 0, tiled=True)
+    got_cache = lax.all_to_all(cache_send, "req", 0, 0, tiled=True)
+    got_states, tokens, lengths = lax.optimization_barrier((got_states, tokens, lengths))
     local_ids = jnp.arange(req_rows, dtype=jnp.int32)
     match_slot = my_leave[None, :] == local_ids[:, None]
     arriving = jnp.any(match_slot, axis=1)

time: 153 us -> 152 us (level)
  waiting for transfers between devices: 60.1 us -> 72.4 us
  other arithmetic: 20.6 us -> 14.2 us
  starting transfers between devices: 44.3 us -> 39.2 us
  local copies, waits for them, and re-layouts: 15.6 us -> 13.8 us
    all_to_all x2, waiting for transfers between devices: 10.2 us -> 19.2 us  [the longest x1 10.3 us: per_device(): got_cache = lax.all_to_all(cache_send, 'req', 0, 0, tiled=True)]
    all_to_all x2, starting transfers between devices: 21.2 us -> 16.9 us  [the longest x1 11.2 us: per_device(): got_states = lax.all_to_all(states_send, 'req', 0, 0, tiled=True)]
    ppermute x15, waiting for transfers between devices: 49.9 us -> 53.2 us  [partner_swap(): return jax.tree.map(lambda part: lax.ppermute(part, axis, pairs), value)]
    reduce_sum x3, other arithmetic: 2.21 us -> 0.45 us  [rms_norm(): mean_square = jnp.mean(values * values, axis=-1, keepdims=True)]
  transfers between devices with their start and end apart: 17 -> 17, of which waited for: 16 -> 17; matrix products, arithmetic and copies ran while one was open for 16% -> 8% of each run, Pallas kernels for 0% -> 0%
where the time goes in v9:
time: 152 us; the launch traced here: 151 us
  waiting for transfers between devices  72.4 us (48%)
  starting transfers between devices  39.2 us (26%)
  other arithmetic  14.2 us (9%)
  local copies, waits for them, and re-layouts  13.8 us (9%)
  matrix products  10.1 us (7%)
    ppermute x15, waiting for transfers between devices, partner_swap(): return jax.tree.map(lambda part: lax.ppermute(part, axis, pairs), value)  53.2 us
    ppermute x15, starting transfers between devices, partner_swap(): return jax.tree.map(lambda part: lax.ppermute(part, axis, pairs), value)  22.3 us
    all_to_all x1, starting transfers between devices, per_device(): got_states = lax.all_to_all(states_send, 'req', 0, 0, tiled=True)  11.2 us
    all_to_all x1, waiting for transfers between devices, per_device(): got_cache = lax.all_to_all(cache_send, 'req', 0, 0, tiled=True)  10.3 us
    all_to_all x1, waiting for transfers between devices, per_device(): got_states = lax.all_to_all(states_send, 'req', 0, 0, tiled=True)  8.85 us
    all_to_all x1, starting transfers between devices, per_device(): got_cache = lax.all_to_all(cache_send, 'req', 0, 0, tiled=True)  5.74 us
    gather x1, local copies, waits for them, and re-layouts, per_device(): jnp.take(got_cache, arrive_from, axis=0, mode='clip')  3.55 us
    gather x1, local copies, waits for them, and re-layouts, per_device(): jnp.take(cache, send_slot, axis=0, mode='clip')  3.49 us
  transfers between devices with their start and end apart: 17, of which 17 were waited for; matrix products, arithmetic and copies ran while one was open for 8% of the time, Pallas kernels for 0%

profile of v9, /device:TPU:32, one launch (start us, length us, event | category | flops | bytes accessed | tf_op | source)
XLA Modules:
  0.0 151.1 jit_solution(16692306051249995312)
XLA Ops:
  3.9 3.5 %gather_fusion.1 = bf16[32,128,256]{2,1,0:T(8,128)(2,1)} fusion(bf16[24,128,256]{2,1,0:T(8,128)(2,1)} %param.28, s32[1024]{0:T(1024)S(1)} %pad_clamp_fusion.2), kind=kCustom, calls=%fused_computation.1 | custom fusion | bytes 4194432 | tf_op jit(solution)/shard_map/jit(_take)/gather | solution.py:156
  7.3 11.2 %all-to-all-start = ((bf16[32,4,256]{2,1,0:T(4,128)(2,1)}), bf16[32,4,256]{2,1,0:T(4,128)(2,1)S(1)}, u32[]{:S(2)}, u32[]{:S(2)}) async-start(bf16[32,4,256]{2,1,0:T(4,128)(2,1)} %gather_fusion), calls=%async_computation | async-start | bytes 131072 | tf_op jit(solution)/shard_map/all_to_all | solution.py:159
  19.1 8.8 %all-to-all-done = bf16[32,4,256]{2,1,0:T(4,128)(2,1)S(1)} async-done(((bf16[32,4,256]{2,1,0:T(4,128)(2,1)}), bf16[32,4,256]{2,1,0:T(4,128)(2,1)S(1)}, u32[]{:S(2)}, u32[]{:S(2)}) %all-to-all-start) | async-done | bytes 65568 | tf_op jit(solution)/shard_map/all_to_all | solution.py:159
  28.0 5.7 %all-to-all-start.1 = ((bf16[32,128,256]{2,1,0:T(8,128)(2,1)}), bf16[32,128,256]{2,1,0:T(8,128)(2,1)}, u32[]{:S(2)}, u32[]{:S(2)}) async-start(bf16[32,128,256]{2,1,0:T(8,128)(2,1)} %gather_fusion.1), calls=%async_computation.1 | async-start | bytes 4194304 | tf_op jit(solution)/shard_map/all_to_all | solution.py:160
  42.9 3.1 %collective-permute-start.1 = (bf16[24,1536]{1,0:T(8,128)(2,1)S(1)}, bf16[24,1536]{1,0:T(8,128)(2,1)S(1)}, u32[]{:S(2)}, u32[]{:S(2)}) collective-permute-start(bf16[24,1536]{1,0:T(8,128)(2,1)S(1)} %fusion.11), channel_id=1, source_target_pairs={{0,3},{1,2},{2,1},{3,0},{4,7},{5,6},{6,5},{7,4},{8,11},{9,10},{10,... | collective-permute-start | bytes 221192 | tf_op jit(solution)/shard_map/ppermute | solution.py:14
  49.9 7.5 %collective-permute-done.2 = bf16[24,1536]{1,0:T(8,128)(2,1)S(1)} collective-permute-done((bf16[24,1536]{1,0:T(8,128)(2,1)S(1)}, bf16[24,1536]{1,0:T(8,128)(2,1)S(1)}, u32[]{:S(2)}, u32[]{:S(2)}) %collective-permute-start.2) | collective-permute-done | bytes 73760 | tf_op jit(solution)/shard_map/ppermute | solution.py:14
  59.1 3.4 %collective-permute-done.3 = bf16[24,1536]{1,0:T(8,128)(2,1)S(1)} collective-permute-done((bf16[24,1536]{1,0:T(8,128)(2,1)S(1)}, bf16[24,1536]{1,0:T(8,128)(2,1)S(1)}, u32[]{:S(2)}, u32[]{:S(2)}) %collective-permute-start.3) | collective-permute-done | bytes 73760 | tf_op jit(solution)/shard_map/ppermute | solution.py:14
  62.4 3.1 %collective-permute-start.4 = (bf16[24,1536]{1,0:T(8,128)(2,1)S(1)}, bf16[24,1536]{1,0:T(8,128)(2,1)S(1)}, u32[]{:S(2)}, u32[]{:S(2)}) collective-permute-start(bf16[24,1536]{1,0:T(8,128)(2,1)S(1)} %fusion.12), channel_id=1, source_target_pairs={{0,3},{1,2},{2,1},{3,0},{4,7},{5,6},{6,5},{7,4},{8,11},{9,10},{10,... | collective-permute-start | bytes 221192 | tf_op jit(solution)/shard_map/ppermute | solution.py:14
  68.8 5.9 %collective-permute-done.5 = bf16[24,1536]{1,0:T(8,128)(2,1)S(1)} collective-permute-done((bf16[24,1536]{1,0:T(8,128)(2,1)S(1)}, bf16[24,1536]{1,0:T(8,128)(2,1)S(1)}, u32[]{:S(2)}, u32[]{:S(2)}) %collective-permute-start.5) | collective-permute-done | bytes 73760 | tf_op jit(solution)/shard_map/ppermute | solution.py:14
  76.5 10.3 %all-to-all-done.1 = bf16[32,128,256]{2,1,0:T(8,128)(2,1)} async-done(((bf16[32,128,256]{2,1,0:T(8,128)(2,1)}), bf16[32,128,256]{2,1,0:T(8,128)(2,1)}, u32[]{:S(2)}, u32[]{:S(2)}) %all-to-all-start.1) | async-done | bytes 2097184 | tf_op jit(solution)/shard_map/all_to_all | solution.py:160
  86.8 3.6 %gather_fusion.4 = bf16[24,128,256]{2,1,0:T(8,128)(2,1)} fusion(bf16[32,128,256]{2,1,0:T(8,128)(2,1)} %all-to-all-done.1, s32[1024]{0:T(1024)} %copy-done.26), kind=kCustom, calls=%fused_computation.4 | custom fusion | bytes 3145824 | tf_op jit(solution)/shard_map/jit(_take)/gather | solution.py:173
  90.4 2.7 %broadcast_select_fusion.1 = (bf16[24,128,256]{2,1,0:T(8,128)(2,1)}, bf16[24,128,256]{2,1,0:T(8,128)(2,1)S(1)}) fusion(pred[24,128]{1,0:T(8,128)(4,1)} %get-tuple-element.51, bf16[24,256]{1,0:T(8,128)(2,1)} %pad_maximum_fusion.4, bf16[24,128,256]{2,1,0:T(8,128)(2,1)} %gather_fusion.4, bf16[24,128,256]{2,1,0:T(8,128)(2,1)S(1)} %copy-done.2, ...), kind=kLoop, calls=%fused_computation.6 | loop fusion | flops 1572864 | bytes 6306840 | tf_op jit(solution)/shard_map/jit(_where)/select_n | solution.py:300
  96.2 4.1 %collective-permute-done.6 = f32[24,1664]{1,0:T(8,128)S(1)} collective-permute-done((f32[24,1664]{1,0:T(8,128)S(1)}, f32[24,1664]{1,0:T(8,128)S(1)}, u32[]{:S(2)}, u32[]{:S(2)}) %collective-permute-start.6) | collective-permute-done | bytes 159776 | tf_op jit(solution)/shard_map/ppermute | solution.py:14
  100.7 3.0 %collective-permute-start.7 = (f32[24,1664]{1,0:T(8,128)S(1)}, f32[24,1664]{1,0:T(8,128)S(1)}, u32[]{:S(2)}, u32[]{:S(2)}) collective-permute-start(f32[24,1664]{1,0:T(8,128)S(1)} %concatenate.39), channel_id=1, source_target_pairs={{0,3},{1,2},{2,1},{3,0},{4,7},{5,6},{6,5},{7,4},{8,11},{9,10},{10,... | collective-permute-start | bytes 479240 | tf_op jit(solution)/shard_map/ppermute | solution.py:14
  103.7 3.5 %collective-permute-done.7 = f32[24,1664]{1,0:T(8,128)S(1)} collective-permute-done((f32[24,1664]{1,0:T(8,128)S(1)}, f32[24,1664]{1,0:T(8,128)S(1)}, u32[]{:S(2)}, u32[]{:S(2)}) %collective-permute-start.7) | collective-permute-done | bytes 159776 | tf_op jit(solution)/shard_map/ppermute | solution.py:14
  108.6 4.4 %collective-permute-done.8 = f32[24,1664]{1,0:T(8,128)S(1)} collective-permute-done((f32[24,1664]{1,0:T(8,128)S(1)}, f32[24,1664]{1,0:T(8,128)S(1)}, u32[]{:S(2)}, u32[]{:S(2)}) %collective-permute-start.8) | collective-permute-done | bytes 159776 | tf_op jit(solution)/shard_map/ppermute | solution.py:14
  114.9 4.0 %collective-permute-done.9 = bf16[24,1536]{1,0:T(8,128)(2,1)S(1)} collective-permute-done((bf16[24,1536]{1,0:T(8,128)(2,1)S(1)}, bf16[24,1536]{1,0:T(8,128)(2,1)S(1)}, u32[]{:S(2)}, u32[]{:S(2)}) %collective-permute-start.9) | collective-permute-done | bytes 73760 | tf_op jit(solution)/shard_map/ppermute | solution.py:14
  118.9 3.3 %collective-permute-start.10 = (bf16[24,1536]{1,0:T(8,128)(2,1)S(1)}, bf16[24,1536]{1,0:T(8,128)(2,1)S(1)}, u32[]{:S(2)}, u32[]{:S(2)}) collective-permute-start(bf16[24,1536]{1,0:T(8,128)(2,1)S(1)} %fusion.13), channel_id=1, source_target_pairs={{0,3},{1,2},{2,1},{3,0},{4,7},{5,6},{6,5},{7,4},{8,11},{9,10},{10,... | collective-permute-start | bytes 221192 | tf_op jit(solution)/shard_map/ppermute | solution.py:14
  125.5 3.8 %collective-permute-done.11 = bf16[24,1536]{1,0:T(8,128)(2,1)S(1)} collective-permute-done((bf16[24,1536]{1,0:T(8,128)(2,1)S(1)}, bf16[24,1536]{1,0:T(8,128)(2,1)S(1)}, u32[]{:S(2)}, u32[]{:S(2)}) %collective-permute-start.11) | collective-permute-done | bytes 73760 | tf_op jit(solution)/shard_map/ppermute | solution.py:14
  130.0 2.7 %fusion.106 = f32[24,576]{1,0:T(8,128)} fusion(bf16[1536,576]{0,1:T(8,128)(2,1)} %param.45, f32[24,1536]{1,0:T(8,128)S(1)} %get-tuple-element.23, f32[1536]{0:T(1024)S(1)} %copy-done.21, f32[24]{0:T(128)S(1)} %add_rsqrt_fusion), kind=kOutput, calls=%fused_computation.211 | convolution fusion | flops 42577920 | bytes 1978464 | tf_op jit(solution)/shard_map/dot_general | solution.py:287
  132.8 2.6 %fusion.1 = f32[24,1536]{1,0:T(8,128)} fusion(bf16[576,1536]{1,0:T(8,128)(2,1)S(1)} %copy-done, bf16[1536,576]{0,1:T(8,128)(2,1)S(1)} %copy-done.3, f32[24,576]{1,0:T(8,128)} %fusion.106, f32[24,1536]{1,0:T(8,128)} %copy-done.4, f32[1536]{0:T(1024)} %param.44, f32[24]{0:T(128)S(1)} %add_rsqrt_fusion), kind=kOutput, calls=%fused_computation.11 | convolution fusion | flops 85183488 | bytes 3895392 | tf_op jit(solution)/shard_map/dot_general | solution.py:292
  137.1 3.5 %collective-permute-done.12 = bf16[24,4,192]{2,0,1:T(8,128)(2,1)S(1)} collective-permute-done((bf16[24,4,192]{2,0,1:T(8,128)(2,1)S(1)}, bf16[24,4,192]{2,0,1:T(8,128)(2,1)S(1)}, u32[]{:S(2)}, u32[]{:S(2)}) %collective-permute-start.12) | collective-permute-done | bytes 36896 | tf_op jit(solution)/shard_map/ppermute | solution.py:14
  140.7 3.1 %collective-permute-start.13 = (bf16[24,2,192]{2,0,1:T(8,128)(2,1)S(1)}, bf16[24,2,192]{2,0,1:T(8,128)(2,1)S(1)}, u32[]{:S(2)}, u32[]{:S(2)}) collective-permute-start(bf16[24,2,192]{2,0,1:T(8,128)(2,1)S(1)} %select_convert_fusion.1), channel_id=1, source_target_pairs={{0,3},{1,2},{2,1},{3,0},{4,7},{5,6},{6,5},{7,4},{8,11},{9,10},{10,... | collective-permute-start | bytes 55304 | tf_op jit(solution)/shard_map/ppermute | solution.py:14
  146.6 3.0 %collective-permute-done.14 = bf16[24,1,192]{2,0,1:T(8,128)(2,1)S(1)} collective-permute-done((bf16[24,1,192]{2,0,1:T(8,128)(2,1)S(1)}, bf16[24,1,192]{2,0,1:T(8,128)(2,1)S(1)}, u32[]{:S(2)}, u32[]{:S(2)}) %collective-permute-start.14) | collective-permute-done | bytes 9248 | tf_op jit(solution)/shard_map/ppermute | solution.py:14
  (172 shorter events, 39.9 us)
Async XLA Ops:
  0.6 132.1 %copy-start = (bf16[576,1536]{1,0:T(8,128)(2,1)S(1)}, bf16[576,1536]{1,0:T(8,128)(2,1)}, u32[]{:S(2)}) copy-start(bf16[576,1536]{1,0:T(8,128)(2,1)} %param.47) | copy-start | bytes 5308420
  7.3 20.6 %all-to-all-start = ((bf16[32,4,256]{2,1,0:T(4,128)(2,1)}), bf16[32,4,256]{2,1,0:T(4,128)(2,1)S(1)}, u32[]{:S(2)}, u32[]{:S(2)}) async-start(bf16[32,4,256]{2,1,0:T(4,128)(2,1)} %gather_fusion), calls=%async_computation | async-start | bytes 131072 | tf_op jit(solution)/shard_map/all_to_all | solution.py:159
  18.6 27.4 %copy-start.28 = (f32[64]{0:T(128)}, f32[64]{0:T(128)S(1)}, u32[]{:S(2)}) copy-start(f32[64]{0:T(128)S(1)} %multiply_power_fusion) | copy-start | bytes 772
  28.0 58.9 %all-to-all-start.1 = ((bf16[32,128,256]{2,1,0:T(8,128)(2,1)}), bf16[32,128,256]{2,1,0:T(8,128)(2,1)}, u32[]{:S(2)}, u32[]{:S(2)}) async-start(bf16[32,128,256]{2,1,0:T(8,128)(2,1)} %gather_fusion.1), calls=%async_computation.1 | async-start | bytes 4194304 | tf_op jit(solution)/shard_map/all_to_all | solution.py:160
  36.3 21.3 %copy-start.24 = (f32[1536]{0:T(1024)S(1)}, f32[1536]{0:T(1024)}, u32[]{:S(2)}) copy-start(f32[1536]{0:T(1024)} %param.40) | copy-start | bytes 18436
  36.3 21.4 %copy-start.12 = (bf16[192,1536]{1,0:T(8,128)(2,1)S(1)}, bf16[192,1536]{1,0:T(8,128)(2,1)}, u32[]{:S(2)}) copy-start(bf16[192,1536]{1,0:T(8,128)(2,1)} %param.41) | copy-start | bytes 1769476
  38.4 19.6 %copy-start.11 = (bf16[1536,256]{1,0:T(8,128)(2,1)S(1)}, bf16[1536,256]{1,0:T(8,128)(2,1)}, u32[]{:S(2)}) copy-start(bf16[1536,256]{1,0:T(8,128)(2,1)} %param.42) | copy-start | bytes 2359300
  38.4 4.4 %collective-permute-start = (bf16[24,1536]{1,0:T(8,128)(2,1)S(1)}, bf16[24,1536]{1,0:T(8,128)(2,1)S(1)}, u32[]{:S(2)}, u32[]{:S(2)}) collective-permute-start(bf16[24,1536]{1,0:T(8,128)(2,1)S(1)} %get-tuple-element.58), channel_id=1, source_target_pairs={{0,1},{1,0},{2,3},{3,2},{4,5},{5,4},{6,7},{7,6},{8,9},{9,8},{10,11... | collective-permute-start | bytes 221192 | tf_op jit(solution)/shard_map/ppermute | solution.py:14
  42.9 5.7 %collective-permute-start.1 = (bf16[24,1536]{1,0:T(8,128)(2,1)S(1)}, bf16[24,1536]{1,0:T(8,128)(2,1)S(1)}, u32[]{:S(2)}, u32[]{:S(2)}) collective-permute-start(bf16[24,1536]{1,0:T(8,128)(2,1)S(1)} %fusion.11), channel_id=1, source_target_pairs={{0,3},{1,2},{2,1},{3,0},{4,7},{5,6},{6,5},{7,4},{8,11},{9,10},{10,... | collective-permute-start | bytes 221192 | tf_op jit(solution)/shard_map/ppermute | solution.py:14
  48.6 8.9 %collective-permute-start.2 = (bf16[24,1536]{1,0:T(8,128)(2,1)S(1)}, bf16[24,1536]{1,0:T(8,128)(2,1)S(1)}, u32[]{:S(2)}, u32[]{:S(2)}) collective-permute-start(bf16[24,1536]{1,0:T(8,128)(2,1)S(1)} %fusion.26), channel_id=1, source_target_pairs={{0,4},{1,5},{2,6},{3,7},{4,0},{5,1},{6,2},{7,3},{8,12},{9,13},{10,... | collective-permute-start | bytes 221192 | tf_op jit(solution)/shard_map/ppermute | solution.py:14
  57.6 17.1 %copy-start.5 = (f32[24,1536]{1,0:T(8,128)}, f32[24,1536]{1,0:T(8,128)S(1)}, u32[]{:S(2)}) copy-start(f32[24,1536]{1,0:T(8,128)S(1)} %get-tuple-element.40) | copy-start | bytes 442372
  58.0 4.4 %collective-permute-start.3 = (bf16[24,1536]{1,0:T(8,128)(2,1)S(1)}, bf16[24,1536]{1,0:T(8,128)(2,1)S(1)}, u32[]{:S(2)}, u32[]{:S(2)}) collective-permute-start(bf16[24,1536]{1,0:T(8,128)(2,1)S(1)} %get-tuple-element.60), channel_id=1, source_target_pairs={{0,1},{1,0},{2,3},{3,2},{4,5},{5,4},{6,7},{7,6},{8,9},{9,8},{10,11... | collective-permute-start | bytes 221192 | tf_op jit(solution)/shard_map/ppermute | solution.py:14
  62.4 5.7 %collective-permute-start.4 = (bf16[24,1536]{1,0:T(8,128)(2,1)S(1)}, bf16[24,1536]{1,0:T(8,128)(2,1)S(1)}, u32[]{:S(2)}, u32[]{:S(2)}) collective-permute-start(bf16[24,1536]{1,0:T(8,128)(2,1)S(1)} %fusion.12), channel_id=1, source_target_pairs={{0,3},{1,2},{2,1},{3,0},{4,7},{5,6},{6,5},{7,4},{8,11},{9,10},{10,... | collective-permute-start | bytes 221192 | tf_op jit(solution)/shard_map/ppermute | solution.py:14
  68.1 6.6 %collective-permute-start.5 = (bf16[24,1536]{1,0:T(8,128)(2,1)S(1)}, bf16[24,1536]{1,0:T(8,128)(2,1)S(1)}, u32[]{:S(2)}, u32[]{:S(2)}) collective-permute-start(bf16[24,1536]{1,0:T(8,128)(2,1)S(1)} %fusion.27), channel_id=1, source_target_pairs={{0,4},{1,5},{2,6},{3,7},{4,0},{5,1},{6,2},{7,3},{8,12},{9,13},{10,... | collective-permute-start | bytes 221192 | tf_op jit(solution)/shard_map/ppermute | solution.py:14
  94.6 5.7 %collective-permute-start.6 = (f32[24,1664]{1,0:T(8,128)S(1)}, f32[24,1664]{1,0:T(8,128)S(1)}, u32[]{:S(2)}, u32[]{:S(2)}) collective-permute-start(f32[24,1664]{1,0:T(8,128)S(1)} %concatenate.38), channel_id=1, source_target_pairs={{0,1},{1,0},{2,3},{3,2},{4,5},{5,4},{6,7},{7,6},{8,9},{9,8},{10,11... | collective-permute-start | bytes 479240 | tf_op jit(solution)/shard_map/ppermute | solution.py:14
  100.7 6.5 %collective-permute-start.7 = (f32[24,1664]{1,0:T(8,128)S(1)}, f32[24,1664]{1,0:T(8,128)S(1)}, u32[]{:S(2)}, u32[]{:S(2)}) collective-permute-start(f32[24,1664]{1,0:T(8,128)S(1)} %concatenate.39), channel_id=1, source_target_pairs={{0,3},{1,2},{2,1},{3,0},{4,7},{5,6},{6,5},{7,4},{8,11},{9,10},{10,... | collective-permute-start | bytes 479240 | tf_op jit(solution)/shard_map/ppermute | solution.py:14
  107.6 21.6 %copy-start.6 = (f32[24,1536]{1,0:T(8,128)S(1)}, f32[24,1536]{1,0:T(8,128)}, u32[]{:S(2)}) copy-start(f32[24,1536]{1,0:T(8,128)} %copy-done.5) | copy-start | bytes 442372
  107.7 5.3 %collective-permute-start.8 = (f32[24,1664]{1,0:T(8,128)S(1)}, f32[24,1664]{1,0:T(8,128)S(1)}, u32[]{:S(2)}, u32[]{:S(2)}) collective-permute-start(f32[24,1664]{1,0:T(8,128)S(1)} %concatenate.40), channel_id=1, source_target_pairs={{0,4},{1,5},{2,6},{3,7},{4,0},{5,1},{6,2},{7,3},{8,12},{9,13},{10,... | collective-permute-start | bytes 479240 | tf_op jit(solution)/shard_map/ppermute | solution.py:14
  114.5 4.4 %collective-permute-start.9 = (bf16[24,1536]{1,0:T(8,128)(2,1)S(1)}, bf16[24,1536]{1,0:T(8,128)(2,1)S(1)}, u32[]{:S(2)}, u32[]{:S(2)}) collective-permute-start(bf16[24,1536]{1,0:T(8,128)(2,1)S(1)} %get-tuple-element.64), channel_id=1, source_target_pairs={{0,1},{1,0},{2,3},{3,2},{4,5},{5,4},{6,7},{7,6},{8,9},{9,8},{10,11... | collective-permute-start | bytes 221192 | tf_op jit(solution)/shard_map/ppermute | solution.py:14
  118.9 5.8 %collective-permute-start.10 = (bf16[24,1536]{1,0:T(8,128)(2,1)S(1)}, bf16[24,1536]{1,0:T(8,128)(2,1)S(1)}, u32[]{:S(2)}, u32[]{:S(2)}) collective-permute-start(bf16[24,1536]{1,0:T(8,128)(2,1)S(1)} %fusion.13), channel_id=1, source_target_pairs={{0,3},{1,2},{2,1},{3,0},{4,7},{5,6},{6,5},{7,4},{8,11},{9,10},{10,... | collective-permute-start | bytes 221192 | tf_op jit(solution)/shard_map/ppermute | solution.py:14
  124.8 4.4 %collective-permute-start.11 = (bf16[24,1536]{1,0:T(8,128)(2,1)S(1)}, bf16[24,1536]{1,0:T(8,128)(2,1)S(1)}, u32[]{:S(2)}, u32[]{:S(2)}) collective-permute-start(bf16[24,1536]{1,0:T(8,128)(2,1)S(1)} %fusion.28), channel_id=1, source_target_pairs={{0,4},{1,5},{2,6},{3,7},{4,0},{5,1},{6,2},{7,3},{8,12},{9,13},{10,... | collective-permute-start | bytes 221192 | tf_op jit(solution)/shard_map/ppermute | solution.py:14
  136.4 4.2 %collective-permute-start.12 = (bf16[24,4,192]{2,0,1:T(8,128)(2,1)S(1)}, bf16[24,4,192]{2,0,1:T(8,128)(2,1)S(1)}, u32[]{:S(2)}, u32[]{:S(2)}) collective-permute-start(bf16[24,4,192]{2,0,1:T(8,128)(2,1)S(1)} %select_convert_fusion), channel_id=1, source_target_pairs={{0,4},{1,5},{2,6},{3,7},{4,0},{5,1},{6,2},{7,3},{8,12},{9,13},{10,... | collective-permute-start | bytes 110600 | tf_op jit(solution)/shard_map/ppermute | solution.py:14
  140.7 5.1 %collective-permute-start.13 = (bf16[24,2,192]{2,0,1:T(8,128)(2,1)S(1)}, bf16[24,2,192]{2,0,1:T(8,128)(2,1)S(1)}, u32[]{:S(2)}, u32[]{:S(2)}) collective-permute-start(bf16[24,2,192]{2,0,1:T(8,128)(2,1)S(1)} %select_convert_fusion.1), channel_id=1, source_target_pairs={{0,3},{1,2},{2,1},{3,0},{4,7},{5,6},{6,5},{7,4},{8,11},{9,10},{10,... | collective-permute-start | bytes 55304 | tf_op jit(solution)/shard_map/ppermute | solution.py:14
  145.8 3.8 %collective-permute-start.14 = (bf16[24,1,192]{2,0,1:T(8,128)(2,1)S(1)}, bf16[24,1,192]{2,0,1:T(8,128)(2,1)S(1)}, u32[]{:S(2)}, u32[]{:S(2)}) collective-permute-start(bf16[24,1,192]{2,0,1:T(8,128)(2,1)S(1)} %select_convert_fusion.2), channel_id=1, source_target_pairs={{0,1},{1,0},{2,3},{3,2},{4,5},{5,4},{6,7},{7,6},{8,9},{9,8},{10,11... | collective-permute-start | bytes 27656 | tf_op jit(solution)/shard_map/ppermute | solution.py:14
  (26 other events, 300.4 us)

commit v10 on v9

--- a/solution.py
+++ b/solution.py
@@ -242,7 +242,9 @@
     current = position[:, None]
     held_pos = current - 1 - jnp.mod(current - 1 - slot_ids, window)
     usable = ((held_pos >= 0) & (held_pos != current - window))[:, None, :]
-    local_top = jnp.max(jnp.where(usable, scores, -1e30), axis=-1)
+    local_top = (
+        jnp.max(jnp.where(usable, scores, -1e30), axis=-1).astype(jnp.bfloat16).astype(jnp.float32)
+    )
     weights = jnp.where(usable, jnp.exp(scores - local_top[..., None]), 0.0)
     local_sum = jnp.sum(weights, axis=-1)
     local_acc = jnp.einsum(
@@ -252,13 +254,12 @@
         preferred_element_type=jnp.float32,
     )
     stat_pad = jnp.zeros((req_rows, 128 - 2 * heads), jnp.float32)
-    merged = joined(
-        jnp.concatenate(
-            [local_acc.reshape(req_rows, width), local_top, local_sum, stat_pad], axis=-1
-        ),
-        "mlp",
-        combine_parts,
-    )
+    merged = jnp.concatenate(
+        [local_acc.reshape(req_rows, width), local_top, local_sum, stat_pad], axis=-1
+    )
+    for mask, _ in axis_stages("mlp"):
+        sent = partner_swap(merged.astype(jnp.bfloat16), "mlp", mask)
+        merged = combine_parts(merged, sent.astype(jnp.float32))
     merged_acc = merged[:, :width].reshape(req_rows, heads, head_size)
     merged_top = merged[:, width : width + heads]
     merged_sum = merged[:, width + heads : width + 2 * heads]

time: 152 us -> 152 us (level)
  waiting for transfers between devices: 72.4 us -> 68.7 us
  other arithmetic: 14.2 us -> 17.8 us
    ppermute x15, waiting for transfers between devices: 53.2 us -> 49.6 us  [partner_swap(): return jax.tree.map(lambda part: lax.ppermute(part, axis, pairs), value)]
    another operation x2 -> x9, other arithmetic: 1.79 us -> 4.38 us
  transfers between devices with their start and end apart: 17 -> 17, of which waited for: 17 -> 17; matrix products, arithmetic and copies ran while one was open for 8% -> 9% of each run, Pallas kernels for 0% -> 0%
where the time goes in v10:
time: 152 us; the launch traced here: 151 us
  waiting for transfers between devices  68.7 us (45%)
  starting transfers between devices  39.3 us (26%)
  other arithmetic  17.8 us (12%)
  local copies, waits for them, and re-layouts  13.7 us (9%)
  matrix products  10.1 us (7%)
    ppermute x15, waiting for transfers between devices, partner_swap(): return jax.tree.map(lambda part: lax.ppermute(part, axis, pairs), value)  49.6 us
    ppermute x15, starting transfers between devices, partner_swap(): return jax.tree.map(lambda part: lax.ppermute(part, axis, pairs), value)  22.4 us
    all_to_all x1, starting transfers between devices, per_device(): got_states = lax.all_to_all(states_send, 'req', 0, 0, tiled=True)  11.2 us
    all_to_all x1, waiting for transfers between devices, per_device(): got_cache = lax.all_to_all(cache_send, 'req', 0, 0, tiled=True)  10.3 us
    all_to_all x1, waiting for transfers between devices, per_device(): got_states = lax.all_to_all(states_send, 'req', 0, 0, tiled=True)  8.85 us
    all_to_all x1, starting transfers between devices, per_device(): got_cache = lax.all_to_all(cache_send, 'req', 0, 0, tiled=True)  5.73 us
    another operation x9, other arithmetic  4.38 us
    gather x1, local copies, waits for them, and re-layouts, per_device(): jnp.take(got_cache, arrive_from, axis=0, mode='clip')  3.55 us
  transfers between devices with their start and end apart: 17, of which 17 were waited for; matrix products, arithmetic and copies ran while one was open for 9% of the time, Pallas kernels for 0%

profile of v10, /device:TPU:32, one launch (start us, length us, event | category | flops | bytes accessed | tf_op | source)
XLA Modules:
  0.0 151.0 jit_solution(11333649654177390420)
XLA Ops:
  3.9 3.5 %gather_fusion.1 = bf16[32,128,256]{2,1,0:T(8,128)(2,1)} fusion(bf16[24,128,256]{2,1,0:T(8,128)(2,1)} %param.28, s32[1024]{0:T(1024)S(1)} %pad_clamp_fusion.2), kind=kCustom, calls=%fused_computation.1 | custom fusion | bytes 4194432 | tf_op jit(solution)/shard_map/jit(_take)/gather | solution.py:156
  7.4 11.2 %all-to-all-start = ((bf16[32,4,256]{2,1,0:T(4,128)(2,1)}), bf16[32,4,256]{2,1,0:T(4,128)(2,1)S(1)}, u32[]{:S(2)}, u32[]{:S(2)}) async-start(bf16[32,4,256]{2,1,0:T(4,128)(2,1)} %gather_fusion), calls=%async_computation | async-start | bytes 131072 | tf_op jit(solution)/shard_map/all_to_all | solution.py:159
  19.1 8.8 %all-to-all-done = bf16[32,4,256]{2,1,0:T(4,128)(2,1)S(1)} async-done(((bf16[32,4,256]{2,1,0:T(4,128)(2,1)}), bf16[32,4,256]{2,1,0:T(4,128)(2,1)S(1)}, u32[]{:S(2)}, u32[]{:S(2)}) %all-to-all-start) | async-done | bytes 65568 | tf_op jit(solution)/shard_map/all_to_all | solution.py:159
  28.0 5.7 %all-to-all-start.1 = ((bf16[32,128,256]{2,1,0:T(8,128)(2,1)}), bf16[32,128,256]{2,1,0:T(8,128)(2,1)}, u32[]{:S(2)}, u32[]{:S(2)}) async-start(bf16[32,128,256]{2,1,0:T(8,128)(2,1)} %gather_fusion.1), calls=%async_computation.1 | async-start | bytes 4194304 | tf_op jit(solution)/shard_map/all_to_all | solution.py:160
  42.9 3.1 %collective-permute-start.1 = (bf16[24,1536]{1,0:T(8,128)(2,1)S(1)}, bf16[24,1536]{1,0:T(8,128)(2,1)S(1)}, u32[]{:S(2)}, u32[]{:S(2)}) collective-permute-start(bf16[24,1536]{1,0:T(8,128)(2,1)S(1)} %fusion.11), channel_id=1, source_target_pairs={{0,3},{1,2},{2,1},{3,0},{4,7},{5,6},{6,5},{7,4},{8,11},{9,10},{10,... | collective-permute-start | bytes 221192 | tf_op jit(solution)/shard_map/ppermute | solution.py:14
  49.4 8.1 %collective-permute-done.2 = bf16[24,1536]{1,0:T(8,128)(2,1)S(1)} collective-permute-done((bf16[24,1536]{1,0:T(8,128)(2,1)S(1)}, bf16[24,1536]{1,0:T(8,128)(2,1)S(1)}, u32[]{:S(2)}, u32[]{:S(2)}) %collective-permute-start.2) | collective-permute-done | bytes 73760 | tf_op jit(solution)/shard_map/ppermute | solution.py:14
  59.1 3.4 %collective-permute-done.3 = bf16[24,1536]{1,0:T(8,128)(2,1)S(1)} collective-permute-done((bf16[24,1536]{1,0:T(8,128)(2,1)S(1)}, bf16[24,1536]{1,0:T(8,128)(2,1)S(1)}, u32[]{:S(2)}, u32[]{:S(2)}) %collective-permute-start.3) | collective-permute-done | bytes 73760 | tf_op jit(solution)/shard_map/ppermute | solution.py:14
  62.4 3.1 %collective-permute-start.4 = (bf16[24,1536]{1,0:T(8,128)(2,1)S(1)}, bf16[24,1536]{1,0:T(8,128)(2,1)S(1)}, u32[]{:S(2)}, u32[]{:S(2)}) collective-permute-start(bf16[24,1536]{1,0:T(8,128)(2,1)S(1)} %fusion.12), channel_id=1, source_target_pairs={{0,3},{1,2},{2,1},{3,0},{4,7},{5,6},{6,5},{7,4},{8,11},{9,10},{10,... | collective-permute-start | bytes 221192 | tf_op jit(solution)/shard_map/ppermute | solution.py:14
  68.8 5.9 %collective-permute-done.5 = bf16[24,1536]{1,0:T(8,128)(2,1)S(1)} collective-permute-done((bf16[24,1536]{1,0:T(8,128)(2,1)S(1)}, bf16[24,1536]{1,0:T(8,128)(2,1)S(1)}, u32[]{:S(2)}, u32[]{:S(2)}) %collective-permute-start.5) | collective-permute-done | bytes 73760 | tf_op jit(solution)/shard_map/ppermute | solution.py:14
  76.5 10.3 %all-to-all-done.1 = bf16[32,128,256]{2,1,0:T(8,128)(2,1)} async-done(((bf16[32,128,256]{2,1,0:T(8,128)(2,1)}), bf16[32,128,256]{2,1,0:T(8,128)(2,1)}, u32[]{:S(2)}, u32[]{:S(2)}) %all-to-all-start.1) | async-done | bytes 2097184 | tf_op jit(solution)/shard_map/all_to_all | solution.py:160
  86.8 3.6 %gather_fusion.4 = bf16[24,128,256]{2,1,0:T(8,128)(2,1)} fusion(bf16[32,128,256]{2,1,0:T(8,128)(2,1)} %all-to-all-done.1, s32[1024]{0:T(1024)} %copy-done.27), kind=kCustom, calls=%fused_computation.4 | custom fusion | bytes 3145824 | tf_op jit(solution)/shard_map/jit(_take)/gather | solution.py:173
  90.4 2.7 %broadcast_select_fusion.1 = (bf16[24,128,256]{2,1,0:T(8,128)(2,1)}, bf16[24,128,256]{2,1,0:T(8,128)(2,1)S(1)}) fusion(pred[24,128]{1,0:T(8,128)(4,1)S(1)} %get-tuple-element.54, bf16[24,256]{1,0:T(8,128)(2,1)} %pad_maximum_fusion.4, bf16[24,128,256]{2,1,0:T(8,128)(2,1)} %gather_fusion.4, bf16[24,128,256]{2,1,0:T(8,128)(2,1)S(1)} %copy-done.2, ...), kind=kLoop, calls=%fused_computation.6 | loop fusion | flops 1572864 | bytes 6306840 | tf_op jit(solution)/shard_map/jit(_where)/select_n | solution.py:301
  96.2 2.8 %collective-permute-done.6 = bf16[24,1664]{1,0:T(8,128)(2,1)S(1)} collective-permute-done((bf16[24,1664]{1,0:T(8,128)(2,1)S(1)}, bf16[24,1664]{1,0:T(8,128)(2,1)S(1)}, u32[]{:S(2)}, u32[]{:S(2)}) %collective-permute-start.6) | collective-permute-done | bytes 79904 | tf_op jit(solution)/shard_map/ppermute | solution.py:14
  100.1 3.1 %collective-permute-start.7 = (bf16[24,1664]{1,0:T(8,128)(2,1)S(1)}, bf16[24,1664]{1,0:T(8,128)(2,1)S(1)}, u32[]{:S(2)}, u32[]{:S(2)}) collective-permute-start(bf16[24,1664]{1,0:T(8,128)(2,1)S(1)} %concatenate.42), channel_id=1, source_target_pairs={{0,3},{1,2},{2,1},{3,0},{4,7},{5,6},{6,5},{7,4},{8,11},{9,10},{10,... | collective-permute-start | bytes 239624 | tf_op jit(solution)/shard_map/ppermute | solution.py:14
  109.3 2.9 %collective-permute-done.8 = bf16[24,1664]{1,0:T(8,128)(2,1)S(1)} collective-permute-done((bf16[24,1664]{1,0:T(8,128)(2,1)S(1)}, bf16[24,1664]{1,0:T(8,128)(2,1)S(1)}, u32[]{:S(2)}, u32[]{:S(2)}) %collective-permute-start.8) | collective-permute-done | bytes 79904 | tf_op jit(solution)/shard_map/ppermute | solution.py:14
  114.9 4.0 %collective-permute-done.9 = bf16[24,1536]{1,0:T(8,128)(2,1)S(1)} collective-permute-done((bf16[24,1536]{1,0:T(8,128)(2,1)S(1)}, bf16[24,1536]{1,0:T(8,128)(2,1)S(1)}, u32[]{:S(2)}, u32[]{:S(2)}) %collective-permute-start.9) | collective-permute-done | bytes 73760 | tf_op jit(solution)/shard_map/ppermute | solution.py:14
  118.9 3.3 %collective-permute-start.10 = (bf16[24,1536]{1,0:T(8,128)(2,1)S(1)}, bf16[24,1536]{1,0:T(8,128)(2,1)S(1)}, u32[]{:S(2)}, u32[]{:S(2)}) collective-permute-start(bf16[24,1536]{1,0:T(8,128)(2,1)S(1)} %fusion.13), channel_id=1, source_target_pairs={{0,3},{1,2},{2,1},{3,0},{4,7},{5,6},{6,5},{7,4},{8,11},{9,10},{10,... | collective-permute-start | bytes 221192 | tf_op jit(solution)/shard_map/ppermute | solution.py:14
  122.2 2.5 %collective-permute-done.10 = bf16[24,1536]{1,0:T(8,128)(2,1)S(1)} collective-permute-done((bf16[24,1536]{1,0:T(8,128)(2,1)S(1)}, bf16[24,1536]{1,0:T(8,128)(2,1)S(1)}, u32[]{:S(2)}, u32[]{:S(2)}) %collective-permute-start.10) | collective-permute-done | bytes 73760 | tf_op jit(solution)/shard_map/ppermute | solution.py:14
  125.4 3.8 %collective-permute-done.11 = bf16[24,1536]{1,0:T(8,128)(2,1)S(1)} collective-permute-done((bf16[24,1536]{1,0:T(8,128)(2,1)S(1)}, bf16[24,1536]{1,0:T(8,128)(2,1)S(1)}, u32[]{:S(2)}, u32[]{:S(2)}) %collective-permute-start.11) | collective-permute-done | bytes 73760 | tf_op jit(solution)/shard_map/ppermute | solution.py:14
  130.0 2.7 %fusion.108 = f32[24,576]{1,0:T(8,128)} fusion(bf16[1536,576]{0,1:T(8,128)(2,1)} %param.45, f32[24,1536]{1,0:T(8,128)S(1)} %get-tuple-element.23, f32[1536]{0:T(1024)S(1)} %copy-done.22, f32[24]{0:T(128)S(1)} %add_rsqrt_fusion), kind=kOutput, calls=%fused_computation.213 | convolution fusion | flops 42577920 | bytes 1978464 | tf_op jit(solution)/shard_map/dot_general | solution.py:288
  132.7 2.6 %fusion.1 = f32[24,1536]{1,0:T(8,128)} fusion(bf16[576,1536]{1,0:T(8,128)(2,1)S(1)} %copy-done, bf16[1536,576]{0,1:T(8,128)(2,1)S(1)} %copy-done.3, f32[24,576]{1,0:T(8,128)} %fusion.108, f32[24,1536]{1,0:T(8,128)} %copy-done.4, f32[1536]{0:T(1024)} %param.44, f32[24]{0:T(128)S(1)} %add_rsqrt_fusion), kind=kOutput, calls=%fused_computation.11 | convolution fusion | flops 85183488 | bytes 3895392 | tf_op jit(solution)/shard_map/dot_general | solution.py:293
  137.1 3.5 %collective-permute-done.12 = bf16[24,4,192]{2,0,1:T(8,128)(2,1)S(1)} collective-permute-done((bf16[24,4,192]{2,0,1:T(8,128)(2,1)S(1)}, bf16[24,4,192]{2,0,1:T(8,128)(2,1)S(1)}, u32[]{:S(2)}, u32[]{:S(2)}) %collective-permute-start.12) | collective-permute-done | bytes 36896 | tf_op jit(solution)/shard_map/ppermute | solution.py:14
  140.6 3.1 %collective-permute-start.13 = (bf16[24,2,192]{2,0,1:T(8,128)(2,1)S(1)}, bf16[24,2,192]{2,0,1:T(8,128)(2,1)S(1)}, u32[]{:S(2)}, u32[]{:S(2)}) collective-permute-start(bf16[24,2,192]{2,0,1:T(8,128)(2,1)S(1)} %select_convert_fusion.1), channel_id=1, source_target_pairs={{0,3},{1,2},{2,1},{3,0},{4,7},{5,6},{6,5},{7,4},{8,11},{9,10},{10,... | collective-permute-start | bytes 55304 | tf_op jit(solution)/shard_map/ppermute | solution.py:14
  146.5 3.0 %collective-permute-done.14 = bf16[24,1,192]{2,0,1:T(8,128)(2,1)S(1)} collective-permute-done((bf16[24,1,192]{2,0,1:T(8,128)(2,1)S(1)}, bf16[24,1,192]{2,0,1:T(8,128)(2,1)S(1)}, u32[]{:S(2)}, u32[]{:S(2)}) %collective-permute-start.14) | collective-permute-done | bytes 9248 | tf_op jit(solution)/shard_map/ppermute | solution.py:14
  (181 shorter events, 42.9 us)
Async XLA Ops:
  0.6 132.1 %copy-start = (bf16[576,1536]{1,0:T(8,128)(2,1)S(1)}, bf16[576,1536]{1,0:T(8,128)(2,1)}, u32[]{:S(2)}) copy-start(bf16[576,1536]{1,0:T(8,128)(2,1)} %param.47) | copy-start | bytes 5308420
  7.4 20.6 %all-to-all-start = ((bf16[32,4,256]{2,1,0:T(4,128)(2,1)}), bf16[32,4,256]{2,1,0:T(4,128)(2,1)S(1)}, u32[]{:S(2)}, u32[]{:S(2)}) async-start(bf16[32,4,256]{2,1,0:T(4,128)(2,1)} %gather_fusion), calls=%async_computation | async-start | bytes 131072 | tf_op jit(solution)/shard_map/all_to_all | solution.py:159
  18.6 27.4 %copy-start.29 = (f32[64]{0:T(128)}, f32[64]{0:T(128)S(1)}, u32[]{:S(2)}) copy-start(f32[64]{0:T(128)S(1)} %multiply_power_fusion) | copy-start | bytes 772
  28.0 58.9 %all-to-all-start.1 = ((bf16[32,128,256]{2,1,0:T(8,128)(2,1)}), bf16[32,128,256]{2,1,0:T(8,128)(2,1)}, u32[]{:S(2)}, u32[]{:S(2)}) async-start(bf16[32,128,256]{2,1,0:T(8,128)(2,1)} %gather_fusion.1), calls=%async_computation.1 | async-start | bytes 4194304 | tf_op jit(solution)/shard_map/all_to_all | solution.py:160
  36.3 21.3 %copy-start.25 = (f32[1536]{0:T(1024)S(1)}, f32[1536]{0:T(1024)}, u32[]{:S(2)}) copy-start(f32[1536]{0:T(1024)} %param.40) | copy-start | bytes 18436
  36.3 21.4 %copy-start.12 = (bf16[192,1536]{1,0:T(8,128)(2,1)S(1)}, bf16[192,1536]{1,0:T(8,128)(2,1)}, u32[]{:S(2)}) copy-start(bf16[192,1536]{1,0:T(8,128)(2,1)} %param.41) | copy-start | bytes 1769476
  38.4 19.6 %copy-start.11 = (bf16[1536,256]{1,0:T(8,128)(2,1)S(1)}, bf16[1536,256]{1,0:T(8,128)(2,1)}, u32[]{:S(2)}) copy-start(bf16[1536,256]{1,0:T(8,128)(2,1)} %param.42) | copy-start | bytes 2359300
  38.4 4.4 %collective-permute-start = (bf16[24,1536]{1,0:T(8,128)(2,1)S(1)}, bf16[24,1536]{1,0:T(8,128)(2,1)S(1)}, u32[]{:S(2)}, u32[]{:S(2)}) collective-permute-start(bf16[24,1536]{1,0:T(8,128)(2,1)S(1)} %get-tuple-element.61), channel_id=1, source_target_pairs={{0,1},{1,0},{2,3},{3,2},{4,5},{5,4},{6,7},{7,6},{8,9},{9,8},{10,11... | collective-permute-start | bytes 221192 | tf_op jit(solution)/shard_map/ppermute | solution.py:14
  42.9 5.7 %collective-permute-start.1 = (bf16[24,1536]{1,0:T(8,128)(2,1)S(1)}, bf16[24,1536]{1,0:T(8,128)(2,1)S(1)}, u32[]{:S(2)}, u32[]{:S(2)}) collective-permute-start(bf16[24,1536]{1,0:T(8,128)(2,1)S(1)} %fusion.11), channel_id=1, source_target_pairs={{0,3},{1,2},{2,1},{3,0},{4,7},{5,6},{6,5},{7,4},{8,11},{9,10},{10,... | collective-permute-start | bytes 221192 | tf_op jit(solution)/shard_map/ppermute | solution.py:14
  48.6 8.9 %collective-permute-start.2 = (bf16[24,1536]{1,0:T(8,128)(2,1)S(1)}, bf16[24,1536]{1,0:T(8,128)(2,1)S(1)}, u32[]{:S(2)}, u32[]{:S(2)}) collective-permute-start(bf16[24,1536]{1,0:T(8,128)(2,1)S(1)} %fusion.26), channel_id=1, source_target_pairs={{0,4},{1,5},{2,6},{3,7},{4,0},{5,1},{6,2},{7,3},{8,12},{9,13},{10,... | collective-permute-start | bytes 221192 | tf_op jit(solution)/shard_map/ppermute | solution.py:14
  58.0 4.4 %collective-permute-start.3 = (bf16[24,1536]{1,0:T(8,128)(2,1)S(1)}, bf16[24,1536]{1,0:T(8,128)(2,1)S(1)}, u32[]{:S(2)}, u32[]{:S(2)}) collective-permute-start(bf16[24,1536]{1,0:T(8,128)(2,1)S(1)} %get-tuple-element.63), channel_id=1, source_target_pairs={{0,1},{1,0},{2,3},{3,2},{4,5},{5,4},{6,7},{7,6},{8,9},{9,8},{10,11... | collective-permute-start | bytes 221192 | tf_op jit(solution)/shard_map/ppermute | solution.py:14
  62.4 5.7 %collective-permute-start.4 = (bf16[24,1536]{1,0:T(8,128)(2,1)S(1)}, bf16[24,1536]{1,0:T(8,128)(2,1)S(1)}, u32[]{:S(2)}, u32[]{:S(2)}) collective-permute-start(bf16[24,1536]{1,0:T(8,128)(2,1)S(1)} %fusion.12), channel_id=1, source_target_pairs={{0,3},{1,2},{2,1},{3,0},{4,7},{5,6},{6,5},{7,4},{8,11},{9,10},{10,... | collective-permute-start | bytes 221192 | tf_op jit(solution)/shard_map/ppermute | solution.py:14
  68.1 6.6 %collective-permute-start.5 = (bf16[24,1536]{1,0:T(8,128)(2,1)S(1)}, bf16[24,1536]{1,0:T(8,128)(2,1)S(1)}, u32[]{:S(2)}, u32[]{:S(2)}) collective-permute-start(bf16[24,1536]{1,0:T(8,128)(2,1)S(1)} %fusion.27), channel_id=1, source_target_pairs={{0,4},{1,5},{2,6},{3,7},{4,0},{5,1},{6,2},{7,3},{8,12},{9,13},{10,... | collective-permute-start | bytes 221192 | tf_op jit(solution)/shard_map/ppermute | solution.py:14
  94.6 4.5 %collective-permute-start.6 = (bf16[24,1664]{1,0:T(8,128)(2,1)S(1)}, bf16[24,1664]{1,0:T(8,128)(2,1)S(1)}, u32[]{:S(2)}, u32[]{:S(2)}) collective-permute-start(bf16[24,1664]{1,0:T(8,128)(2,1)S(1)} %concatenate.41), channel_id=1, source_target_pairs={{0,1},{1,0},{2,3},{3,2},{4,5},{5,4},{6,7},{7,6},{8,9},{9,8},{10,11... | collective-permute-start | bytes 239624 | tf_op jit(solution)/shard_map/ppermute | solution.py:14
  100.1 5.7 %collective-permute-start.7 = (bf16[24,1664]{1,0:T(8,128)(2,1)S(1)}, bf16[24,1664]{1,0:T(8,128)(2,1)S(1)}, u32[]{:S(2)}, u32[]{:S(2)}) collective-permute-start(bf16[24,1664]{1,0:T(8,128)(2,1)S(1)} %concatenate.42), channel_id=1, source_target_pairs={{0,3},{1,2},{2,1},{3,0},{4,7},{5,6},{6,5},{7,4},{8,11},{9,10},{10,... | collective-permute-start | bytes 239624 | tf_op jit(solution)/shard_map/ppermute | solution.py:14
  107.7 21.5 %copy-start.6 = (f32[24,1536]{1,0:T(8,128)S(1)}, f32[24,1536]{1,0:T(8,128)}, u32[]{:S(2)}) copy-start(f32[24,1536]{1,0:T(8,128)} %copy-done.5) | copy-start | bytes 442372
  107.7 4.5 %collective-permute-start.8 = (bf16[24,1664]{1,0:T(8,128)(2,1)S(1)}, bf16[24,1664]{1,0:T(8,128)(2,1)S(1)}, u32[]{:S(2)}, u32[]{:S(2)}) collective-permute-start(bf16[24,1664]{1,0:T(8,128)(2,1)S(1)} %concatenate.43), channel_id=1, source_target_pairs={{0,4},{1,5},{2,6},{3,7},{4,0},{5,1},{6,2},{7,3},{8,12},{9,13},{10,... | collective-permute-start | bytes 239624 | tf_op jit(solution)/shard_map/ppermute | solution.py:14
  112.2 17.8 %copy-start.22 = (f32[1536]{0:T(1024)S(1)}, f32[1536]{0:T(1024)}, u32[]{:S(2)}) copy-start(f32[1536]{0:T(1024)} %param.44) | copy-start | bytes 18436
  114.4 4.4 %collective-permute-start.9 = (bf16[24,1536]{1,0:T(8,128)(2,1)S(1)}, bf16[24,1536]{1,0:T(8,128)(2,1)S(1)}, u32[]{:S(2)}, u32[]{:S(2)}) collective-permute-start(bf16[24,1536]{1,0:T(8,128)(2,1)S(1)} %get-tuple-element.69), channel_id=1, source_target_pairs={{0,1},{1,0},{2,3},{3,2},{4,5},{5,4},{6,7},{7,6},{8,9},{9,8},{10,11... | collective-permute-start | bytes 221192 | tf_op jit(solution)/shard_map/ppermute | solution.py:14
  118.9 5.8 %collective-permute-start.10 = (bf16[24,1536]{1,0:T(8,128)(2,1)S(1)}, bf16[24,1536]{1,0:T(8,128)(2,1)S(1)}, u32[]{:S(2)}, u32[]{:S(2)}) collective-permute-start(bf16[24,1536]{1,0:T(8,128)(2,1)S(1)} %fusion.13), channel_id=1, source_target_pairs={{0,3},{1,2},{2,1},{3,0},{4,7},{5,6},{6,5},{7,4},{8,11},{9,10},{10,... | collective-permute-start | bytes 221192 | tf_op jit(solution)/shard_map/ppermute | solution.py:14
  124.7 4.4 %collective-permute-start.11 = (bf16[24,1536]{1,0:T(8,128)(2,1)S(1)}, bf16[24,1536]{1,0:T(8,128)(2,1)S(1)}, u32[]{:S(2)}, u32[]{:S(2)}) collective-permute-start(bf16[24,1536]{1,0:T(8,128)(2,1)S(1)} %fusion.28), channel_id=1, source_target_pairs={{0,4},{1,5},{2,6},{3,7},{4,0},{5,1},{6,2},{7,3},{8,12},{9,13},{10,... | collective-permute-start | bytes 221192 | tf_op jit(solution)/shard_map/ppermute | solution.py:14
  136.4 4.2 %collective-permute-start.12 = (bf16[24,4,192]{2,0,1:T(8,128)(2,1)S(1)}, bf16[24,4,192]{2,0,1:T(8,128)(2,1)S(1)}, u32[]{:S(2)}, u32[]{:S(2)}) collective-permute-start(bf16[24,4,192]{2,0,1:T(8,128)(2,1)S(1)} %select_convert_fusion), channel_id=1, source_target_pairs={{0,4},{1,5},{2,6},{3,7},{4,0},{5,1},{6,2},{7,3},{8,12},{9,13},{10,... | collective-permute-start | bytes 110600 | tf_op jit(solution)/shard_map/ppermute | solution.py:14
  140.6 5.1 %collective-permute-start.13 = (bf16[24,2,192]{2,0,1:T(8,128)(2,1)S(1)}, bf16[24,2,192]{2,0,1:T(8,128)(2,1)S(1)}, u32[]{:S(2)}, u32[]{:S(2)}) collective-permute-start(bf16[24,2,192]{2,0,1:T(8,128)(2,1)S(1)} %select_convert_fusion.1), channel_id=1, source_target_pairs={{0,3},{1,2},{2,1},{3,0},{4,7},{5,6},{6,5},{7,4},{8,11},{9,10},{10,... | collective-permute-start | bytes 55304 | tf_op jit(solution)/shard_map/ppermute | solution.py:14
  145.8 3.8 %collective-permute-start.14 = (bf16[24,1,192]{2,0,1:T(8,128)(2,1)S(1)}, bf16[24,1,192]{2,0,1:T(8,128)(2,1)S(1)}, u32[]{:S(2)}, u32[]{:S(2)}) collective-permute-start(bf16[24,1,192]{2,0,1:T(8,128)(2,1)S(1)} %select_convert_fusion.2), channel_id=1, source_target_pairs={{0,1},{1,0},{2,3},{3,2},{4,5},{5,4},{6,7},{7,6},{8,9},{9,8},{10,11... | collective-permute-start | bytes 27656 | tf_op jit(solution)/shard_map/ppermute | solution.py:14
  (27 other events, 315.0 us)

commit v11 on v9

--- a/solution.py
+++ b/solution.py
@@ -40,10 +40,8 @@
 
 
 def scatter_sum(value, axis):
-    size = lax.axis_size(axis)
-    rows, cols = value.shape
     me = lax.axis_index(axis)
-    held = value.reshape(rows, size, cols // size)
+    held = value
     for mask, bit in reversed(axis_stages(axis)):
         half = held.shape[1] // 2
         lower, upper = held[:, :half], held[:, half:]
@@ -51,7 +49,7 @@
         keep = jnp.where(mine_upper, upper, lower)
         send = jnp.where(mine_upper, lower, upper)
         held = keep + partner_swap(send.astype(jnp.bfloat16), axis, mask).astype(jnp.float32)
-    return held.reshape(rows, cols // size)
+    return held
 
 
 def rms_norm(values, gain_vec):

time: 152 us -> 152 us (level)
  other arithmetic: 14.2 us -> 16.1 us
where the time goes in v11:
time: 152 us
  waiting for transfers between devices  72.2 us (48%)
  starting transfers between devices  39.2 us (26%)
  other arithmetic  16.1 us (11%)
  local copies, waits for them, and re-layouts  12.7 us (8%)
  matrix products  10.1 us (7%)
    ppermute x15, waiting for transfers between devices, partner_swap(): return jax.tree.map(lambda part: lax.ppermute(part, axis, pairs), value)  53 us
    ppermute x15, starting transfers between devices, partner_swap(): return jax.tree.map(lambda part: lax.ppermute(part, axis, pairs), value)  22.2 us
    all_to_all x1, starting transfers between devices, per_device(): got_states = lax.all_to_all(states_send, 'req', 0, 0, tiled=True)  11.2 us
    all_to_all x1, waiting for transfers between devices, per_device(): got_cache = lax.all_to_all(cache_send, 'req', 0, 0, tiled=True)  10.3 us
    all_to_all x1, waiting for transfers between devices, per_device(): got_states = lax.all_to_all(states_send, 'req', 0, 0, tiled=True)  8.85 us
    all_to_all x1, starting transfers between devices, per_device(): got_cache = lax.all_to_all(cache_send, 'req', 0, 0, tiled=True)  5.74 us
    gather x1, local copies, waits for them, and re-layouts, per_device(): jnp.take(got_cache, arrive_from, axis=0, mode='clip')  3.55 us
    gather x1, local copies, waits for them, and re-layouts, per_device(): jnp.take(cache, send_slot, axis=0, mode='clip')  3.48 us
  transfers between devices with their start and end apart: 17, of which 17 were waited for; matrix products, arithmetic and copies ran while one was open for 8% of the time, Pallas kernels for 0%

profile of v11, /device:TPU:32, one launch (start us, length us, event | category | flops | bytes accessed | tf_op | source)
XLA Modules:
  0.0 151.6 jit_solution(11354207146677937093)
XLA Ops:
  3.9 3.5 %gather_fusion.1 = bf16[32,128,256]{2,1,0:T(8,128)(2,1)} fusion(bf16[24,128,256]{2,1,0:T(8,128)(2,1)} %param.28, s32[1024]{0:T(1024)S(1)} %pad_clamp_fusion.2), kind=kCustom, calls=%fused_computation.1 | custom fusion | bytes 4194432 | tf_op jit(solution)/shard_map/jit(_take)/gather | solution.py:154
  7.3 11.2 %all-to-all-start = ((bf16[32,4,256]{2,1,0:T(4,128)(2,1)}), bf16[32,4,256]{2,1,0:T(4,128)(2,1)S(1)}, u32[]{:S(2)}, u32[]{:S(2)}) async-start(bf16[32,4,256]{2,1,0:T(4,128)(2,1)} %gather_fusion), calls=%async_computation | async-start | bytes 131072 | tf_op jit(solution)/shard_map/all_to_all | solution.py:157
  19.1 8.8 %all-to-all-done = bf16[32,4,256]{2,1,0:T(4,128)(2,1)S(1)} async-done(((bf16[32,4,256]{2,1,0:T(4,128)(2,1)}), bf16[32,4,256]{2,1,0:T(4,128)(2,1)S(1)}, u32[]{:S(2)}, u32[]{:S(2)}) %all-to-all-start) | async-done | bytes 65568 | tf_op jit(solution)/shard_map/all_to_all | solution.py:157
  28.0 5.7 %all-to-all-start.1 = ((bf16[32,128,256]{2,1,0:T(8,128)(2,1)}), bf16[32,128,256]{2,1,0:T(8,128)(2,1)}, u32[]{:S(2)}, u32[]{:S(2)}) async-start(bf16[32,128,256]{2,1,0:T(8,128)(2,1)} %gather_fusion.1), calls=%async_computation.1 | async-start | bytes 4194304 | tf_op jit(solution)/shard_map/all_to_all | solution.py:158
  42.9 3.1 %collective-permute-start.1 = (bf16[24,1536]{1,0:T(8,128)(2,1)S(1)}, bf16[24,1536]{1,0:T(8,128)(2,1)S(1)}, u32[]{:S(2)}, u32[]{:S(2)}) collective-permute-start(bf16[24,1536]{1,0:T(8,128)(2,1)S(1)} %fusion.11), channel_id=1, source_target_pairs={{0,3},{1,2},{2,1},{3,0},{4,7},{5,6},{6,5},{7,4},{8,11},{9,10},{10,... | collective-permute-start | bytes 221192 | tf_op jit(solution)/shard_map/ppermute | solution.py:14
  49.9 7.5 %collective-permute-done.2 = bf16[24,1536]{1,0:T(8,128)(2,1)S(1)} collective-permute-done((bf16[24,1536]{1,0:T(8,128)(2,1)S(1)}, bf16[24,1536]{1,0:T(8,128)(2,1)S(1)}, u32[]{:S(2)}, u32[]{:S(2)}) %collective-permute-start.2) | collective-permute-done | bytes 73760 | tf_op jit(solution)/shard_map/ppermute | solution.py:14
  59.1 3.4 %collective-permute-done.3 = bf16[24,1536]{1,0:T(8,128)(2,1)S(1)} collective-permute-done((bf16[24,1536]{1,0:T(8,128)(2,1)S(1)}, bf16[24,1536]{1,0:T(8,128)(2,1)S(1)}, u32[]{:S(2)}, u32[]{:S(2)}) %collective-permute-start.3) | collective-permute-done | bytes 73760 | tf_op jit(solution)/shard_map/ppermute | solution.py:14
  62.4 3.1 %collective-permute-start.4 = (bf16[24,1536]{1,0:T(8,128)(2,1)S(1)}, bf16[24,1536]{1,0:T(8,128)(2,1)S(1)}, u32[]{:S(2)}, u32[]{:S(2)}) collective-permute-start(bf16[24,1536]{1,0:T(8,128)(2,1)S(1)} %fusion.12), channel_id=1, source_target_pairs={{0,3},{1,2},{2,1},{3,0},{4,7},{5,6},{6,5},{7,4},{8,11},{9,10},{10,... | collective-permute-start | bytes 221192 | tf_op jit(solution)/shard_map/ppermute | solution.py:14
  68.8 5.9 %collective-permute-done.5 = bf16[24,1536]{1,0:T(8,128)(2,1)S(1)} collective-permute-done((bf16[24,1536]{1,0:T(8,128)(2,1)S(1)}, bf16[24,1536]{1,0:T(8,128)(2,1)S(1)}, u32[]{:S(2)}, u32[]{:S(2)}) %collective-permute-start.5) | collective-permute-done | bytes 73760 | tf_op jit(solution)/shard_map/ppermute | solution.py:14
  76.5 10.3 %all-to-all-done.1 = bf16[32,128,256]{2,1,0:T(8,128)(2,1)} async-done(((bf16[32,128,256]{2,1,0:T(8,128)(2,1)}), bf16[32,128,256]{2,1,0:T(8,128)(2,1)}, u32[]{:S(2)}, u32[]{:S(2)}) %all-to-all-start.1) | async-done | bytes 2097184 | tf_op jit(solution)/shard_map/all_to_all | solution.py:158
  86.8 3.6 %gather_fusion.4 = bf16[24,128,256]{2,1,0:T(8,128)(2,1)} fusion(bf16[32,128,256]{2,1,0:T(8,128)(2,1)} %all-to-all-done.1, s32[1024]{0:T(1024)} %copy-done.26), kind=kCustom, calls=%fused_computation.4 | custom fusion | bytes 3145824 | tf_op jit(solution)/shard_map/jit(_take)/gather | solution.py:171
  90.4 2.7 %broadcast_select_fusion.1 = (bf16[24,128,256]{2,1,0:T(8,128)(2,1)}, bf16[24,128,256]{2,1,0:T(8,128)(2,1)S(1)}) fusion(pred[24,128]{1,0:T(8,128)(4,1)} %get-tuple-element.49, bf16[24,256]{1,0:T(8,128)(2,1)} %pad_maximum_fusion.4, bf16[24,128,256]{2,1,0:T(8,128)(2,1)} %gather_fusion.4, bf16[24,128,256]{2,1,0:T(8,128)(2,1)S(1)} %copy-done.2, ...), kind=kLoop, calls=%fused_computation.6 | loop fusion | flops 1572864 | bytes 6306840 | tf_op jit(solution)/shard_map/jit(_where)/select_n | solution.py:298
  96.2 4.1 %collective-permute-done.6 = f32[24,1664]{1,0:T(8,128)S(1)} collective-permute-done((f32[24,1664]{1,0:T(8,128)S(1)}, f32[24,1664]{1,0:T(8,128)S(1)}, u32[]{:S(2)}, u32[]{:S(2)}) %collective-permute-start.6) | collective-permute-done | bytes 159776 | tf_op jit(solution)/shard_map/ppermute | solution.py:14
  100.7 3.0 %collective-permute-start.7 = (f32[24,1664]{1,0:T(8,128)S(1)}, f32[24,1664]{1,0:T(8,128)S(1)}, u32[]{:S(2)}, u32[]{:S(2)}) collective-permute-start(f32[24,1664]{1,0:T(8,128)S(1)} %concatenate.39), channel_id=1, source_target_pairs={{0,3},{1,2},{2,1},{3,0},{4,7},{5,6},{6,5},{7,4},{8,11},{9,10},{10,... | collective-permute-start | bytes 479240 | tf_op jit(solution)/shard_map/ppermute | solution.py:14
  103.7 3.5 %collective-permute-done.7 = f32[24,1664]{1,0:T(8,128)S(1)} collective-permute-done((f32[24,1664]{1,0:T(8,128)S(1)}, f32[24,1664]{1,0:T(8,128)S(1)}, u32[]{:S(2)}, u32[]{:S(2)}) %collective-permute-start.7) | collective-permute-done | bytes 159776 | tf_op jit(solution)/shard_map/ppermute | solution.py:14
  108.6 4.4 %collective-permute-done.8 = f32[24,1664]{1,0:T(8,128)S(1)} collective-permute-done((f32[24,1664]{1,0:T(8,128)S(1)}, f32[24,1664]{1,0:T(8,128)S(1)}, u32[]{:S(2)}, u32[]{:S(2)}) %collective-permute-start.8) | collective-permute-done | bytes 159776 | tf_op jit(solution)/shard_map/ppermute | solution.py:14
  114.9 4.0 %collective-permute-done.9 = bf16[24,1536]{1,0:T(8,128)(2,1)S(1)} collective-permute-done((bf16[24,1536]{1,0:T(8,128)(2,1)S(1)}, bf16[24,1536]{1,0:T(8,128)(2,1)S(1)}, u32[]{:S(2)}, u32[]{:S(2)}) %collective-permute-start.9) | collective-permute-done | bytes 73760 | tf_op jit(solution)/shard_map/ppermute | solution.py:14
  118.9 3.3 %collective-permute-start.10 = (bf16[24,1536]{1,0:T(8,128)(2,1)S(1)}, bf16[24,1536]{1,0:T(8,128)(2,1)S(1)}, u32[]{:S(2)}, u32[]{:S(2)}) collective-permute-start(bf16[24,1536]{1,0:T(8,128)(2,1)S(1)} %fusion.13), channel_id=1, source_target_pairs={{0,3},{1,2},{2,1},{3,0},{4,7},{5,6},{6,5},{7,4},{8,11},{9,10},{10,... | collective-permute-start | bytes 221192 | tf_op jit(solution)/shard_map/ppermute | solution.py:14
  125.5 3.8 %collective-permute-done.11 = bf16[24,1536]{1,0:T(8,128)(2,1)S(1)} collective-permute-done((bf16[24,1536]{1,0:T(8,128)(2,1)S(1)}, bf16[24,1536]{1,0:T(8,128)(2,1)S(1)}, u32[]{:S(2)}, u32[]{:S(2)}) %collective-permute-start.11) | collective-permute-done | bytes 73760 | tf_op jit(solution)/shard_map/ppermute | solution.py:14
  130.1 2.7 %fusion.105 = f32[24,576]{1,0:T(8,128)} fusion(bf16[1536,576]{0,1:T(8,128)(2,1)} %param.45, f32[24,1536]{1,0:T(8,128)S(1)} %get-tuple-element.23, f32[1536]{0:T(1024)S(1)} %copy-done.21, f32[24]{0:T(128)S(1)} %add_rsqrt_fusion), kind=kOutput, calls=%fused_computation.210 | convolution fusion | flops 42577920 | bytes 1978464 | tf_op jit(solution)/shard_map/dot_general | solution.py:285
  132.8 2.6 %fusion.1 = f32[24,1536]{1,0:T(8,128)} fusion(bf16[576,1536]{1,0:T(8,128)(2,1)S(1)} %copy-done, bf16[1536,576]{0,1:T(8,128)(2,1)S(1)} %copy-done.3, f32[24,576]{1,0:T(8,128)} %fusion.105, f32[24,1536]{1,0:T(8,128)} %copy-done.4, f32[1536]{0:T(1024)} %param.44, f32[24]{0:T(128)S(1)} %add_rsqrt_fusion), kind=kOutput, calls=%fused_computation.11 | convolution fusion | flops 85183488 | bytes 3895392 | tf_op jit(solution)/shard_map/dot_general | solution.py:290
  136.9 3.4 %collective-permute-done.12 = bf16[24,768]{1,0:T(8,128)(2,1)S(1)} collective-permute-done((bf16[24,768]{1,0:T(8,128)(2,1)S(1)}, bf16[24,768]{1,0:T(8,128)(2,1)S(1)}, u32[]{:S(2)}, u32[]{:S(2)}) %collective-permute-start.12) | collective-permute-done | bytes 36896 | tf_op jit(solution)/shard_map/ppermute | solution.py:14
  141.3 3.1 %collective-permute-start.13 = (bf16[24,384]{1,0:T(8,128)(2,1)S(1)}, bf16[24,384]{1,0:T(8,128)(2,1)S(1)}, u32[]{:S(2)}, u32[]{:S(2)}) collective-permute-start(bf16[24,384]{1,0:T(8,128)(2,1)S(1)} %select_convert_fusion.1), channel_id=1, source_target_pairs={{0,3},{1,2},{2,1},{3,0},{4,7},{5,6},{6,5},{7,4},{8,11},{9,10},{10,... | collective-permute-start | bytes 55304 | tf_op jit(solution)/shard_map/ppermute | solution.py:14
  147.1 3.0 %collective-permute-done.14 = bf16[24,192]{1,0:T(8,128)(2,1)S(1)} collective-permute-done((bf16[24,192]{1,0:T(8,128)(2,1)S(1)}, bf16[24,192]{1,0:T(8,128)(2,1)S(1)}, u32[]{:S(2)}, u32[]{:S(2)}) %collective-permute-start.14) | collective-permute-done | bytes 9248 | tf_op jit(solution)/shard_map/ppermute | solution.py:14
  (170 shorter events, 40.6 us)
Async XLA Ops:
  0.6 132.1 %copy-start = (bf16[576,1536]{1,0:T(8,128)(2,1)S(1)}, bf16[576,1536]{1,0:T(8,128)(2,1)}, u32[]{:S(2)}) copy-start(bf16[576,1536]{1,0:T(8,128)(2,1)} %param.47) | copy-start | bytes 5308420
  7.3 20.6 %all-to-all-start = ((bf16[32,4,256]{2,1,0:T(4,128)(2,1)}), bf16[32,4,256]{2,1,0:T(4,128)(2,1)S(1)}, u32[]{:S(2)}, u32[]{:S(2)}) async-start(bf16[32,4,256]{2,1,0:T(4,128)(2,1)} %gather_fusion), calls=%async_computation | async-start | bytes 131072 | tf_op jit(solution)/shard_map/all_to_all | solution.py:157
  18.6 27.4 %copy-start.28 = (f32[64]{0:T(128)}, f32[64]{0:T(128)S(1)}, u32[]{:S(2)}) copy-start(f32[64]{0:T(128)S(1)} %multiply_power_fusion) | copy-start | bytes 772
  28.0 58.9 %all-to-all-start.1 = ((bf16[32,128,256]{2,1,0:T(8,128)(2,1)}), bf16[32,128,256]{2,1,0:T(8,128)(2,1)}, u32[]{:S(2)}, u32[]{:S(2)}) async-start(bf16[32,128,256]{2,1,0:T(8,128)(2,1)} %gather_fusion.1), calls=%async_computation.1 | async-start | bytes 4194304 | tf_op jit(solution)/shard_map/all_to_all | solution.py:158
  36.3 21.3 %copy-start.24 = (f32[1536]{0:T(1024)S(1)}, f32[1536]{0:T(1024)}, u32[]{:S(2)}) copy-start(f32[1536]{0:T(1024)} %param.40) | copy-start | bytes 18436
  36.3 21.4 %copy-start.12 = (bf16[192,1536]{1,0:T(8,128)(2,1)S(1)}, bf16[192,1536]{1,0:T(8,128)(2,1)}, u32[]{:S(2)}) copy-start(bf16[192,1536]{1,0:T(8,128)(2,1)} %param.41) | copy-start | bytes 1769476
  38.4 19.6 %copy-start.11 = (bf16[1536,256]{1,0:T(8,128)(2,1)S(1)}, bf16[1536,256]{1,0:T(8,128)(2,1)}, u32[]{:S(2)}) copy-start(bf16[1536,256]{1,0:T(8,128)(2,1)} %param.42) | copy-start | bytes 2359300
  38.4 4.4 %collective-permute-start = (bf16[24,1536]{1,0:T(8,128)(2,1)S(1)}, bf16[24,1536]{1,0:T(8,128)(2,1)S(1)}, u32[]{:S(2)}, u32[]{:S(2)}) collective-permute-start(bf16[24,1536]{1,0:T(8,128)(2,1)S(1)} %get-tuple-element.56), channel_id=1, source_target_pairs={{0,1},{1,0},{2,3},{3,2},{4,5},{5,4},{6,7},{7,6},{8,9},{9,8},{10,11... | collective-permute-start | bytes 221192 | tf_op jit(solution)/shard_map/ppermute | solution.py:14
  42.9 5.7 %collective-permute-start.1 = (bf16[24,1536]{1,0:T(8,128)(2,1)S(1)}, bf16[24,1536]{1,0:T(8,128)(2,1)S(1)}, u32[]{:S(2)}, u32[]{:S(2)}) collective-permute-start(bf16[24,1536]{1,0:T(8,128)(2,1)S(1)} %fusion.11), channel_id=1, source_target_pairs={{0,3},{1,2},{2,1},{3,0},{4,7},{5,6},{6,5},{7,4},{8,11},{9,10},{10,... | collective-permute-start | bytes 221192 | tf_op jit(solution)/shard_map/ppermute | solution.py:14
  48.6 8.9 %collective-permute-start.2 = (bf16[24,1536]{1,0:T(8,128)(2,1)S(1)}, bf16[24,1536]{1,0:T(8,128)(2,1)S(1)}, u32[]{:S(2)}, u32[]{:S(2)}) collective-permute-start(bf16[24,1536]{1,0:T(8,128)(2,1)S(1)} %fusion.26), channel_id=1, source_target_pairs={{0,4},{1,5},{2,6},{3,7},{4,0},{5,1},{6,2},{7,3},{8,12},{9,13},{10,... | collective-permute-start | bytes 221192 | tf_op jit(solution)/shard_map/ppermute | solution.py:14
  57.6 17.1 %copy-start.5 = (f32[24,1536]{1,0:T(8,128)}, f32[24,1536]{1,0:T(8,128)S(1)}, u32[]{:S(2)}) copy-start(f32[24,1536]{1,0:T(8,128)S(1)} %get-tuple-element.40) | copy-start | bytes 442372
  58.0 4.4 %collective-permute-start.3 = (bf16[24,1536]{1,0:T(8,128)(2,1)S(1)}, bf16[24,1536]{1,0:T(8,128)(2,1)S(1)}, u32[]{:S(2)}, u32[]{:S(2)}) collective-permute-start(bf16[24,1536]{1,0:T(8,128)(2,1)S(1)} %get-tuple-element.58), channel_id=1, source_target_pairs={{0,1},{1,0},{2,3},{3,2},{4,5},{5,4},{6,7},{7,6},{8,9},{9,8},{10,11... | collective-permute-start | bytes 221192 | tf_op jit(solution)/shard_map/ppermute | solution.py:14
  62.4 5.7 %collective-permute-start.4 = (bf16[24,1536]{1,0:T(8,128)(2,1)S(1)}, bf16[24,1536]{1,0:T(8,128)(2,1)S(1)}, u32[]{:S(2)}, u32[]{:S(2)}) collective-permute-start(bf16[24,1536]{1,0:T(8,128)(2,1)S(1)} %fusion.12), channel_id=1, source_target_pairs={{0,3},{1,2},{2,1},{3,0},{4,7},{5,6},{6,5},{7,4},{8,11},{9,10},{10,... | collective-permute-start | bytes 221192 | tf_op jit(solution)/shard_map/ppermute | solution.py:14
  68.1 6.6 %collective-permute-start.5 = (bf16[24,1536]{1,0:T(8,128)(2,1)S(1)}, bf16[24,1536]{1,0:T(8,128)(2,1)S(1)}, u32[]{:S(2)}, u32[]{:S(2)}) collective-permute-start(bf16[24,1536]{1,0:T(8,128)(2,1)S(1)} %fusion.27), channel_id=1, source_target_pairs={{0,4},{1,5},{2,6},{3,7},{4,0},{5,1},{6,2},{7,3},{8,12},{9,13},{10,... | collective-permute-start | bytes 221192 | tf_op jit(solution)/shard_map/ppermute | solution.py:14
  94.6 5.7 %collective-permute-start.6 = (f32[24,1664]{1,0:T(8,128)S(1)}, f32[24,1664]{1,0:T(8,128)S(1)}, u32[]{:S(2)}, u32[]{:S(2)}) collective-permute-start(f32[24,1664]{1,0:T(8,128)S(1)} %concatenate.38), channel_id=1, source_target_pairs={{0,1},{1,0},{2,3},{3,2},{4,5},{5,4},{6,7},{7,6},{8,9},{9,8},{10,11... | collective-permute-start | bytes 479240 | tf_op jit(solution)/shard_map/ppermute | solution.py:14
  100.7 6.5 %collective-permute-start.7 = (f32[24,1664]{1,0:T(8,128)S(1)}, f32[24,1664]{1,0:T(8,128)S(1)}, u32[]{:S(2)}, u32[]{:S(2)}) collective-permute-start(f32[24,1664]{1,0:T(8,128)S(1)} %concatenate.39), channel_id=1, source_target_pairs={{0,3},{1,2},{2,1},{3,0},{4,7},{5,6},{6,5},{7,4},{8,11},{9,10},{10,... | collective-permute-start | bytes 479240 | tf_op jit(solution)/shard_map/ppermute | solution.py:14
  107.6 21.6 %copy-start.6 = (f32[24,1536]{1,0:T(8,128)S(1)}, f32[24,1536]{1,0:T(8,128)}, u32[]{:S(2)}) copy-start(f32[24,1536]{1,0:T(8,128)} %copy-done.5) | copy-start | bytes 442372
  107.7 5.3 %collective-permute-start.8 = (f32[24,1664]{1,0:T(8,128)S(1)}, f32[24,1664]{1,0:T(8,128)S(1)}, u32[]{:S(2)}, u32[]{:S(2)}) collective-permute-start(f32[24,1664]{1,0:T(8,128)S(1)} %concatenate.40), channel_id=1, source_target_pairs={{0,4},{1,5},{2,6},{3,7},{4,0},{5,1},{6,2},{7,3},{8,12},{9,13},{10,... | collective-permute-start | bytes 479240 | tf_op jit(solution)/shard_map/ppermute | solution.py:14
  114.5 4.4 %collective-permute-start.9 = (bf16[24,1536]{1,0:T(8,128)(2,1)S(1)}, bf16[24,1536]{1,0:T(8,128)(2,1)S(1)}, u32[]{:S(2)}, u32[]{:S(2)}) collective-permute-start(bf16[24,1536]{1,0:T(8,128)(2,1)S(1)} %get-tuple-element.62), channel_id=1, source_target_pairs={{0,1},{1,0},{2,3},{3,2},{4,5},{5,4},{6,7},{7,6},{8,9},{9,8},{10,11... | collective-permute-start | bytes 221192 | tf_op jit(solution)/shard_map/ppermute | solution.py:14
  118.9 5.8 %collective-permute-start.10 = (bf16[24,1536]{1,0:T(8,128)(2,1)S(1)}, bf16[24,1536]{1,0:T(8,128)(2,1)S(1)}, u32[]{:S(2)}, u32[]{:S(2)}) collective-permute-start(bf16[24,1536]{1,0:T(8,128)(2,1)S(1)} %fusion.13), channel_id=1, source_target_pairs={{0,3},{1,2},{2,1},{3,0},{4,7},{5,6},{6,5},{7,4},{8,11},{9,10},{10,... | collective-permute-start | bytes 221192 | tf_op jit(solution)/shard_map/ppermute | solution.py:14
  124.8 4.4 %collective-permute-start.11 = (bf16[24,1536]{1,0:T(8,128)(2,1)S(1)}, bf16[24,1536]{1,0:T(8,128)(2,1)S(1)}, u32[]{:S(2)}, u32[]{:S(2)}) collective-permute-start(bf16[24,1536]{1,0:T(8,128)(2,1)S(1)} %fusion.28), channel_id=1, source_target_pairs={{0,4},{1,5},{2,6},{3,7},{4,0},{5,1},{6,2},{7,3},{8,12},{9,13},{10,... | collective-permute-start | bytes 221192 | tf_op jit(solution)/shard_map/ppermute | solution.py:14
  136.3 4.0 %collective-permute-start.12 = (bf16[24,768]{1,0:T(8,128)(2,1)S(1)}, bf16[24,768]{1,0:T(8,128)(2,1)S(1)}, u32[]{:S(2)}, u32[]{:S(2)}) collective-permute-start(bf16[24,768]{1,0:T(8,128)(2,1)S(1)} %select_convert_fusion), channel_id=1, source_target_pairs={{0,4},{1,5},{2,6},{3,7},{4,0},{5,1},{6,2},{7,3},{8,12},{9,13},{10,... | collective-permute-start | bytes 110600 | tf_op jit(solution)/shard_map/ppermute | solution.py:14
  141.3 5.1 %collective-permute-start.13 = (bf16[24,384]{1,0:T(8,128)(2,1)S(1)}, bf16[24,384]{1,0:T(8,128)(2,1)S(1)}, u32[]{:S(2)}, u32[]{:S(2)}) collective-permute-start(bf16[24,384]{1,0:T(8,128)(2,1)S(1)} %select_convert_fusion.1), channel_id=1, source_target_pairs={{0,3},{1,2},{2,1},{3,0},{4,7},{5,6},{6,5},{7,4},{8,11},{9,10},{10,... | collective-permute-start | bytes 55304 | tf_op jit(solution)/shard_map/ppermute | solution.py:14
  146.4 3.7 %collective-permute-start.14 = (bf16[24,192]{1,0:T(8,128)(2,1)S(1)}, bf16[24,192]{1,0:T(8,128)(2,1)S(1)}, u32[]{:S(2)}, u32[]{:S(2)}) collective-permute-start(bf16[24,192]{1,0:T(8,128)(2,1)S(1)} %select_convert_fusion.2), channel_id=1, source_target_pairs={{0,1},{1,0},{2,3},{3,2},{4,5},{5,4},{6,7},{7,6},{8,9},{9,8},{10,11... | collective-permute-start | bytes 27656 | tf_op jit(solution)/shard_map/ppermute | solution.py:14
  (26 other events, 300.9 us)

commit v12 on v11

--- a/solution.py
+++ b/solution.py
@@ -249,33 +249,58 @@
         moved_cache[..., head_size:],
         preferred_element_type=jnp.float32,
     )
-    stat_pad = jnp.zeros((req_rows, 128 - 2 * heads), jnp.float32)
-    merged = joined(
-        jnp.concatenate(
-            [local_acc.reshape(req_rows, width), local_top, local_sum, stat_pad], axis=-1
-        ),
-        "mlp",
-        combine_parts,
-    )
-    merged_acc = merged[:, :width].reshape(req_rows, heads, head_size)
-    merged_top = merged[:, width : width + heads]
-    merged_sum = merged[:, width + heads : width + 2 * heads]
+    acc = local_acc.reshape(req_rows, width)
+    top, total = local_top, local_sum
+    held = heads
+    head_base = jnp.zeros((), jnp.int32)
+    for mask, bit in reversed(axis_stages("mlp")):
+        if held % 2 == 0 and (held // 2) * head_size >= 2 * slice_rows:
+            held = held // 2
+            upper = (mlp_id & bit) != 0
+            cut = held * head_size
+            keep_acc = jnp.where(upper, acc[:, cut:], acc[:, :cut])
+            send_acc = jnp.where(upper, acc[:, :cut], acc[:, cut:])
+            keep_top = jnp.where(upper, top[:, held:], top[:, :held])
+            send_top = jnp.where(upper, top[:, :held], top[:, held:])
+            keep_total = jnp.where(upper, total[:, held:], total[:, :held])
+            send_total = jnp.where(upper, total[:, :held], total[:, held:])
+            head_base = head_base + jnp.where(upper, held, 0)
+        else:
+            keep_acc = send_acc = acc
+            keep_top = send_top = top
+            keep_total = send_total = total
+        cut = held * head_size
+        stat_pad = jnp.zeros((req_rows, head_size - 2 * held), jnp.float32)
+        got = partner_swap(
+            jnp.concatenate([send_acc, send_top, send_total, stat_pad], axis=1), "mlp", mask
+        )
+        got_top = got[:, cut : cut + held]
+        got_total = got[:, cut + held : cut + 2 * held]
+        top = jnp.maximum(keep_top, got_top)
+        keep_factor = jnp.exp(keep_top - top)
+        got_factor = jnp.exp(got_top - top)
+        acc = keep_acc * jnp.repeat(keep_factor, head_size, axis=1) + got[:, :cut] * jnp.repeat(
+            got_factor, head_size, axis=1
+        )
+        total = keep_total * keep_factor + got_total * got_factor
     own_score = (
         jnp.sum(queries.astype(jnp.float32) * key_new.astype(jnp.float32)[:, None, :], axis=-1)
         * score_scale
     )
-    top_score = jnp.maximum(merged_top, own_score)
-    rescale = jnp.exp(merged_top - top_score)
+    own_score = lax.dynamic_slice_in_dim(own_score, head_base, held, 1)
+    top_score = jnp.maximum(top, own_score)
+    rescale = jnp.exp(top - top_score)
     own_weight = jnp.exp(own_score - top_score)
     own_rounded = lax.optimization_barrier(own_weight.astype(jnp.bfloat16)).astype(jnp.float32)
-    denominator = merged_sum * rescale + own_weight
-    numerator = (
-        merged_acc * rescale[..., None]
-        + own_rounded[..., None] * value_new.astype(jnp.float32)[:, None, :]
-    )
-    attended = (numerator / denominator[..., None]).reshape(req_rows, width).astype(jnp.bfloat16)
+    denominator = total * rescale + own_weight
+    numerator = acc * jnp.repeat(rescale, head_size, axis=1) + jnp.repeat(
+        own_rounded, head_size, axis=1
+    ) * jnp.tile(value_new.astype(jnp.float32), (1, held))
+    attended = (numerator / jnp.repeat(denominator, head_size, axis=1)).astype(jnp.bfloat16)
     attn_part = jnp.dot(
-        lax.dynamic_slice_in_dim(attended, mlp_id * slice_rows, slice_rows, 1),
+        lax.dynamic_slice_in_dim(
+            attended, mlp_id * slice_rows - head_base * head_size, slice_rows, 1
+        ),
         w_attn_out,
         preferred_element_type=jnp.float32,
     )

time: 152 us -> 147 us (0.967)
  waiting for transfers between devices: 72.2 us -> 69.1 us
    ppermute x15, waiting for transfers between devices: 53 us -> 50.5 us  [partner_swap(): return jax.tree.map(lambda part: lax.ppermute(part, axis, pairs), value)]
  transfers between devices with their start and end apart: 17 -> 17, of which waited for: 17 -> 17; matrix products, arithmetic and copies ran while one was open for 8% -> 9% of each run, Pallas kernels for 0% -> 0%
where the time goes in v12:
time: 147 us
  waiting for transfers between devices  69.1 us (47%)
  starting transfers between devices  38.2 us (26%)
  other arithmetic  15.5 us (11%)
  local copies, waits for them, and re-layouts  13.7 us (9%)
  matrix products  8.68 us (6%)
    ppermute x15, waiting for transfers between devices, partner_swap(): return jax.tree.map(lambda part: lax.ppermute(part, axis, pairs), value)  50.5 us
    ppermute x15, starting transfers between devices, partner_swap(): return jax.tree.map(lambda part: lax.ppermute(part, axis, pairs), value)  21.3 us
    all_to_all x1, starting transfers between devices, per_device(): got_states = lax.all_to_all(states_send, 'req', 0, 0, tiled=True)  11.2 us
    all_to_all x1, waiting for transfers between devices, per_device(): got_cache = lax.all_to_all(cache_send, 'req', 0, 0, tiled=True)  10.3 us
    all_to_all x1, waiting for transfers between devices, per_device(): got_states = lax.all_to_all(states_send, 'req', 0, 0, tiled=True)  8.19 us
    all_to_all x1, starting transfers between devices, per_device(): got_cache = lax.all_to_all(cache_send, 'req', 0, 0, tiled=True)  5.75 us
    gather x1, local copies, waits for them, and re-layouts, per_device(): jnp.take(got_cache, arrive_from, axis=0, mode='clip')  3.55 us
    gather x1, local copies, waits for them, and re-layouts, per_device(): jnp.take(cache, send_slot, axis=0, mode='clip')  3.5 us
  transfers between devices with their start and end apart: 17, of which 17 were waited for; matrix products, arithmetic and copies ran while one was open for 9% of the time, Pallas kernels for 0%

profile of v12, /device:TPU:32, one launch (start us, length us, event | category | flops | bytes accessed | tf_op | source)
XLA Modules:
  0.0 146.5 jit_solution(13517759083006567057)
XLA Ops:
  3.9 3.5 %gather_fusion.1 = bf16[32,128,256]{2,1,0:T(8,128)(2,1)} fusion(bf16[24,128,256]{2,1,0:T(8,128)(2,1)} %param.28, s32[1024]{0:T(1024)S(1)} %pad_clamp_fusion.2), kind=kCustom, calls=%fused_computation.1 | custom fusion | bytes 4194432 | tf_op jit(solution)/shard_map/jit(_take)/gather | solution.py:154
  7.4 11.2 %all-to-all-start = ((bf16[32,4,256]{2,1,0:T(4,128)(2,1)}), bf16[32,4,256]{2,1,0:T(4,128)(2,1)S(1)}, u32[]{:S(2)}, u32[]{:S(2)}) async-start(bf16[32,4,256]{2,1,0:T(4,128)(2,1)} %gather_fusion), calls=%async_computation | async-start | bytes 131072 | tf_op jit(solution)/shard_map/all_to_all | solution.py:157
  19.8 8.2 %all-to-all-done = bf16[32,4,256]{2,1,0:T(4,128)(2,1)S(1)} async-done(((bf16[32,4,256]{2,1,0:T(4,128)(2,1)}), bf16[32,4,256]{2,1,0:T(4,128)(2,1)S(1)}, u32[]{:S(2)}, u32[]{:S(2)}) %all-to-all-start) | async-done | bytes 65568 | tf_op jit(solution)/shard_map/all_to_all | solution.py:157
  28.0 5.7 %all-to-all-start.1 = ((bf16[32,128,256]{2,1,0:T(8,128)(2,1)}), bf16[32,128,256]{2,1,0:T(8,128)(2,1)}, u32[]{:S(2)}, u32[]{:S(2)}) async-start(bf16[32,128,256]{2,1,0:T(8,128)(2,1)} %gather_fusion.1), calls=%async_computation.1 | async-start | bytes 4194304 | tf_op jit(solution)/shard_map/all_to_all | solution.py:158
  42.9 3.1 %collective-permute-start.1 = (bf16[24,1536]{1,0:T(8,128)(2,1)S(1)}, bf16[24,1536]{1,0:T(8,128)(2,1)S(1)}, u32[]{:S(2)}, u32[]{:S(2)}) collective-permute-start(bf16[24,1536]{1,0:T(8,128)(2,1)S(1)} %fusion.11), channel_id=1, source_target_pairs={{0,3},{1,2},{2,1},{3,0},{4,7},{5,6},{6,5},{7,4},{8,11},{9,10},{10,... | collective-permute-start | bytes 221192 | tf_op jit(solution)/shard_map/ppermute | solution.py:14
  50.0 7.5 %collective-permute-done.2 = bf16[24,1536]{1,0:T(8,128)(2,1)S(1)} collective-permute-done((bf16[24,1536]{1,0:T(8,128)(2,1)S(1)}, bf16[24,1536]{1,0:T(8,128)(2,1)S(1)}, u32[]{:S(2)}, u32[]{:S(2)}) %collective-permute-start.2) | collective-permute-done | bytes 73760 | tf_op jit(solution)/shard_map/ppermute | solution.py:14
  59.1 3.4 %collective-permute-done.3 = bf16[24,1536]{1,0:T(8,128)(2,1)S(1)} collective-permute-done((bf16[24,1536]{1,0:T(8,128)(2,1)S(1)}, bf16[24,1536]{1,0:T(8,128)(2,1)S(1)}, u32[]{:S(2)}, u32[]{:S(2)}) %collective-permute-start.3) | collective-permute-done | bytes 73760 | tf_op jit(solution)/shard_map/ppermute | solution.py:14
  62.5 3.1 %collective-permute-start.4 = (bf16[24,1536]{1,0:T(8,128)(2,1)S(1)}, bf16[24,1536]{1,0:T(8,128)(2,1)S(1)}, u32[]{:S(2)}, u32[]{:S(2)}) collective-permute-start(bf16[24,1536]{1,0:T(8,128)(2,1)S(1)} %fusion.12), channel_id=1, source_target_pairs={{0,3},{1,2},{2,1},{3,0},{4,7},{5,6},{6,5},{7,4},{8,11},{9,10},{10,... | collective-permute-start | bytes 221192 | tf_op jit(solution)/shard_map/ppermute | solution.py:14
  65.6 2.5 %collective-permute-done.4 = bf16[24,1536]{1,0:T(8,128)(2,1)S(1)} collective-permute-done((bf16[24,1536]{1,0:T(8,128)(2,1)S(1)}, bf16[24,1536]{1,0:T(8,128)(2,1)S(1)}, u32[]{:S(2)}, u32[]{:S(2)}) %collective-permute-start.4) | collective-permute-done | bytes 73760 | tf_op jit(solution)/shard_map/ppermute | solution.py:14
  68.8 5.9 %collective-permute-done.5 = bf16[24,1536]{1,0:T(8,128)(2,1)S(1)} collective-permute-done((bf16[24,1536]{1,0:T(8,128)(2,1)S(1)}, bf16[24,1536]{1,0:T(8,128)(2,1)S(1)}, u32[]{:S(2)}, u32[]{:S(2)}) %collective-permute-start.5) | collective-permute-done | bytes 73760 | tf_op jit(solution)/shard_map/ppermute | solution.py:14
  76.5 10.3 %all-to-all-done.1 = bf16[32,128,256]{2,1,0:T(8,128)(2,1)} async-done(((bf16[32,128,256]{2,1,0:T(8,128)(2,1)}), bf16[32,128,256]{2,1,0:T(8,128)(2,1)}, u32[]{:S(2)}, u32[]{:S(2)}) %all-to-all-start.1) | async-done | bytes 2097184 | tf_op jit(solution)/shard_map/all_to_all | solution.py:158
  86.9 3.6 %gather_fusion.4 = bf16[24,128,256]{2,1,0:T(8,128)(2,1)} fusion(bf16[32,128,256]{2,1,0:T(8,128)(2,1)} %all-to-all-done.1, s32[1024]{0:T(1024)} %copy-done.29), kind=kCustom, calls=%fused_computation.4 | custom fusion | bytes 3145824 | tf_op jit(solution)/shard_map/jit(_take)/gather | solution.py:171
  90.4 2.7 %broadcast_select_fusion.1 = (bf16[24,128,256]{2,1,0:T(8,128)(2,1)}, bf16[24,128,256]{2,1,0:T(8,128)(2,1)S(1)}) fusion(pred[24,128]{1,0:T(8,128)(4,1)} %get-tuple-element.49, bf16[24,256]{1,0:T(8,128)(2,1)} %pad_maximum_fusion.4, bf16[24,128,256]{2,1,0:T(8,128)(2,1)} %gather_fusion.4, bf16[24,128,256]{2,1,0:T(8,128)(2,1)S(1)} %copy-done.2, ...), kind=kLoop, calls=%fused_computation.6 | loop fusion | flops 1572864 | bytes 6306840 | tf_op jit(solution)/shard_map/jit(_where)/select_n | solution.py:323
  95.5 3.8 %collective-permute-done.6 = f32[24,896]{1,0:T(8,128)S(1)} collective-permute-done((f32[24,896]{1,0:T(8,128)S(1)}, f32[24,896]{1,0:T(8,128)S(1)}, u32[]{:S(2)}, u32[]{:S(2)}) %collective-permute-start.6) | collective-permute-done | bytes 86048 | tf_op jit(solution)/shard_map/ppermute | solution.py:14
  99.8 3.0 %collective-permute-start.7 = (f32[24,512]{1,0:T(8,128)S(1)}, f32[24,512]{1,0:T(8,128)S(1)}, u32[]{:S(2)}, u32[]{:S(2)}) collective-permute-start(f32[24,512]{1,0:T(8,128)S(1)} %maximum_maximum_fusion.1), channel_id=1, source_target_pairs={{0,3},{1,2},{2,1},{3,0},{4,7},{5,6},{6,5},{7,4},{8,11},{9,10},{10,... | collective-permute-start | bytes 147464 | tf_op jit(solution)/shard_map/ppermute | solution.py:14
  106.2 3.6 %collective-permute-done.8 = f32[24,512]{1,0:T(8,128)S(1)} collective-permute-done((f32[24,512]{1,0:T(8,128)S(1)}, f32[24,512]{1,0:T(8,128)S(1)}, u32[]{:S(2)}, u32[]{:S(2)}) %collective-permute-start.8) | collective-permute-done | bytes 49184 | tf_op jit(solution)/shard_map/ppermute | solution.py:14
  111.4 3.9 %collective-permute-done.9 = bf16[24,1536]{1,0:T(8,128)(2,1)S(1)} collective-permute-done((bf16[24,1536]{1,0:T(8,128)(2,1)S(1)}, bf16[24,1536]{1,0:T(8,128)(2,1)S(1)}, u32[]{:S(2)}, u32[]{:S(2)}) %collective-permute-start.9) | collective-permute-done | bytes 73760 | tf_op jit(solution)/shard_map/ppermute | solution.py:14
  115.3 3.2 %collective-permute-start.10 = (bf16[24,1536]{1,0:T(8,128)(2,1)S(1)}, bf16[24,1536]{1,0:T(8,128)(2,1)S(1)}, u32[]{:S(2)}, u32[]{:S(2)}) collective-permute-start(bf16[24,1536]{1,0:T(8,128)(2,1)S(1)} %fusion.13), channel_id=1, source_target_pairs={{0,3},{1,2},{2,1},{3,0},{4,7},{5,6},{6,5},{7,4},{8,11},{9,10},{10,... | collective-permute-start | bytes 221192 | tf_op jit(solution)/shard_map/ppermute | solution.py:14
  118.5 2.5 %collective-permute-done.10 = bf16[24,1536]{1,0:T(8,128)(2,1)S(1)} collective-permute-done((bf16[24,1536]{1,0:T(8,128)(2,1)S(1)}, bf16[24,1536]{1,0:T(8,128)(2,1)S(1)}, u32[]{:S(2)}, u32[]{:S(2)}) %collective-permute-start.10) | collective-permute-done | bytes 73760 | tf_op jit(solution)/shard_map/ppermute | solution.py:14
  121.8 3.8 %collective-permute-done.11 = bf16[24,1536]{1,0:T(8,128)(2,1)S(1)} collective-permute-done((bf16[24,1536]{1,0:T(8,128)(2,1)S(1)}, bf16[24,1536]{1,0:T(8,128)(2,1)S(1)}, u32[]{:S(2)}, u32[]{:S(2)}) %collective-permute-start.11) | collective-permute-done | bytes 73760 | tf_op jit(solution)/shard_map/ppermute | solution.py:14
  127.7 2.6 %fusion.1 = f32[24,1536]{1,0:T(8,128)} fusion(bf16[576,1536]{1,0:T(8,128)(2,1)S(1)} %copy-done, bf16[1536,576]{0,1:T(8,128)(2,1)S(1)} %copy-done.3, f32[24,576]{1,0:T(8,128)} %fusion.109, f32[24,1536]{1,0:T(8,128)} %copy-done.5, f32[1536]{0:T(1024)} %param.44, f32[24]{0:T(128)S(1)} %add_rsqrt_fusion), kind=kOutput, calls=%fused_computation.11 | convolution fusion | flops 85183488 | bytes 3895392 | tf_op jit(solution)/shard_map/dot_general | solution.py:315
  131.9 3.4 %collective-permute-done.12 = bf16[24,768]{1,0:T(8,128)(2,1)S(1)} collective-permute-done((bf16[24,768]{1,0:T(8,128)(2,1)S(1)}, bf16[24,768]{1,0:T(8,128)(2,1)S(1)}, u32[]{:S(2)}, u32[]{:S(2)}) %collective-permute-start.12) | collective-permute-done | bytes 36896 | tf_op jit(solution)/shard_map/ppermute | solution.py:14
  136.2 3.2 %collective-permute-start.13 = (bf16[24,384]{1,0:T(8,128)(2,1)S(1)}, bf16[24,384]{1,0:T(8,128)(2,1)S(1)}, u32[]{:S(2)}, u32[]{:S(2)}) collective-permute-start(bf16[24,384]{1,0:T(8,128)(2,1)S(1)} %select_convert_fusion.1), channel_id=1, source_target_pairs={{0,3},{1,2},{2,1},{3,0},{4,7},{5,6},{6,5},{7,4},{8,11},{9,10},{10,... | collective-permute-start | bytes 55304 | tf_op jit(solution)/shard_map/ppermute | solution.py:14
  142.0 3.0 %collective-permute-done.14 = bf16[24,192]{1,0:T(8,128)(2,1)S(1)} collective-permute-done((bf16[24,192]{1,0:T(8,128)(2,1)S(1)}, bf16[24,192]{1,0:T(8,128)(2,1)S(1)}, u32[]{:S(2)}, u32[]{:S(2)}) %collective-permute-start.14) | collective-permute-done | bytes 9248 | tf_op jit(solution)/shard_map/ppermute | solution.py:14
  (190 shorter events, 38.4 us)
Async XLA Ops:
  0.6 127.0 %copy-start = (bf16[576,1536]{1,0:T(8,128)(2,1)S(1)}, bf16[576,1536]{1,0:T(8,128)(2,1)}, u32[]{:S(2)}) copy-start(bf16[576,1536]{1,0:T(8,128)(2,1)} %param.47) | copy-start | bytes 5308420
  7.4 20.6 %all-to-all-start = ((bf16[32,4,256]{2,1,0:T(4,128)(2,1)}), bf16[32,4,256]{2,1,0:T(4,128)(2,1)S(1)}, u32[]{:S(2)}, u32[]{:S(2)}) async-start(bf16[32,4,256]{2,1,0:T(4,128)(2,1)} %gather_fusion), calls=%async_computation | async-start | bytes 131072 | tf_op jit(solution)/shard_map/all_to_all | solution.py:157
  18.6 27.4 %copy-start.31 = (f32[64]{0:T(128)}, f32[64]{0:T(128)S(1)}, u32[]{:S(2)}) copy-start(f32[64]{0:T(128)S(1)} %multiply_power_fusion) | copy-start | bytes 772
  28.0 58.9 %all-to-all-start.1 = ((bf16[32,128,256]{2,1,0:T(8,128)(2,1)}), bf16[32,128,256]{2,1,0:T(8,128)(2,1)}, u32[]{:S(2)}, u32[]{:S(2)}) async-start(bf16[32,128,256]{2,1,0:T(8,128)(2,1)} %gather_fusion.1), calls=%async_computation.1 | async-start | bytes 4194304 | tf_op jit(solution)/shard_map/all_to_all | solution.py:158
  36.4 21.3 %copy-start.27 = (f32[1536]{0:T(1024)S(1)}, f32[1536]{0:T(1024)}, u32[]{:S(2)}) copy-start(f32[1536]{0:T(1024)} %param.40) | copy-start | bytes 18436
  36.4 21.4 %copy-start.13 = (bf16[192,1536]{1,0:T(8,128)(2,1)S(1)}, bf16[192,1536]{1,0:T(8,128)(2,1)}, u32[]{:S(2)}) copy-start(bf16[192,1536]{1,0:T(8,128)(2,1)} %param.41) | copy-start | bytes 1769476
  38.5 4.4 %collective-permute-start = (bf16[24,1536]{1,0:T(8,128)(2,1)S(1)}, bf16[24,1536]{1,0:T(8,128)(2,1)S(1)}, u32[]{:S(2)}, u32[]{:S(2)}) collective-permute-start(bf16[24,1536]{1,0:T(8,128)(2,1)S(1)} %get-tuple-element.56), channel_id=1, source_target_pairs={{0,1},{1,0},{2,3},{3,2},{4,5},{5,4},{6,7},{7,6},{8,9},{9,8},{10,11... | collective-permute-start | bytes 221192 | tf_op jit(solution)/shard_map/ppermute | solution.py:14
  42.9 5.7 %collective-permute-start.1 = (bf16[24,1536]{1,0:T(8,128)(2,1)S(1)}, bf16[24,1536]{1,0:T(8,128)(2,1)S(1)}, u32[]{:S(2)}, u32[]{:S(2)}) collective-permute-start(bf16[24,1536]{1,0:T(8,128)(2,1)S(1)} %fusion.11), channel_id=1, source_target_pairs={{0,3},{1,2},{2,1},{3,0},{4,7},{5,6},{6,5},{7,4},{8,11},{9,10},{10,... | collective-permute-start | bytes 221192 | tf_op jit(solution)/shard_map/ppermute | solution.py:14
  48.6 8.9 %collective-permute-start.2 = (bf16[24,1536]{1,0:T(8,128)(2,1)S(1)}, bf16[24,1536]{1,0:T(8,128)(2,1)S(1)}, u32[]{:S(2)}, u32[]{:S(2)}) collective-permute-start(bf16[24,1536]{1,0:T(8,128)(2,1)S(1)} %fusion.27), channel_id=1, source_target_pairs={{0,4},{1,5},{2,6},{3,7},{4,0},{5,1},{6,2},{7,3},{8,12},{9,13},{10,... | collective-permute-start | bytes 221192 | tf_op jit(solution)/shard_map/ppermute | solution.py:14
  58.0 4.4 %collective-permute-start.3 = (bf16[24,1536]{1,0:T(8,128)(2,1)S(1)}, bf16[24,1536]{1,0:T(8,128)(2,1)S(1)}, u32[]{:S(2)}, u32[]{:S(2)}) collective-permute-start(bf16[24,1536]{1,0:T(8,128)(2,1)S(1)} %get-tuple-element.58), channel_id=1, source_target_pairs={{0,1},{1,0},{2,3},{3,2},{4,5},{5,4},{6,7},{7,6},{8,9},{9,8},{10,11... | collective-permute-start | bytes 221192 | tf_op jit(solution)/shard_map/ppermute | solution.py:14
  62.5 5.7 %collective-permute-start.4 = (bf16[24,1536]{1,0:T(8,128)(2,1)S(1)}, bf16[24,1536]{1,0:T(8,128)(2,1)S(1)}, u32[]{:S(2)}, u32[]{:S(2)}) collective-permute-start(bf16[24,1536]{1,0:T(8,128)(2,1)S(1)} %fusion.12), channel_id=1, source_target_pairs={{0,3},{1,2},{2,1},{3,0},{4,7},{5,6},{6,5},{7,4},{8,11},{9,10},{10,... | collective-permute-start | bytes 221192 | tf_op jit(solution)/shard_map/ppermute | solution.py:14
  68.1 6.6 %collective-permute-start.5 = (bf16[24,1536]{1,0:T(8,128)(2,1)S(1)}, bf16[24,1536]{1,0:T(8,128)(2,1)S(1)}, u32[]{:S(2)}, u32[]{:S(2)}) collective-permute-start(bf16[24,1536]{1,0:T(8,128)(2,1)S(1)} %fusion.28), channel_id=1, source_target_pairs={{0,4},{1,5},{2,6},{3,7},{4,0},{5,1},{6,2},{7,3},{8,12},{9,13},{10,... | collective-permute-start | bytes 221192 | tf_op jit(solution)/shard_map/ppermute | solution.py:14
  94.8 4.5 %collective-permute-start.6 = (f32[24,896]{1,0:T(8,128)S(1)}, f32[24,896]{1,0:T(8,128)S(1)}, u32[]{:S(2)}, u32[]{:S(2)}) collective-permute-start(f32[24,896]{1,0:T(8,128)S(1)} %maximum_maximum_fusion), channel_id=1, source_target_pairs={{0,4},{1,5},{2,6},{3,7},{4,0},{5,1},{6,2},{7,3},{8,12},{9,13},{10,... | collective-permute-start | bytes 258056 | tf_op jit(solution)/shard_map/ppermute | solution.py:14
  99.8 5.3 %collective-permute-start.7 = (f32[24,512]{1,0:T(8,128)S(1)}, f32[24,512]{1,0:T(8,128)S(1)}, u32[]{:S(2)}, u32[]{:S(2)}) collective-permute-start(f32[24,512]{1,0:T(8,128)S(1)} %maximum_maximum_fusion.1), channel_id=1, source_target_pairs={{0,3},{1,2},{2,1},{3,0},{4,7},{5,6},{6,5},{7,4},{8,11},{9,10},{10,... | collective-permute-start | bytes 147464 | tf_op jit(solution)/shard_map/ppermute | solution.py:14
  103.0 22.6 %copy-start.7 = (f32[24,1536]{1,0:T(8,128)S(1)}, f32[24,1536]{1,0:T(8,128)}, u32[]{:S(2)}) copy-start(f32[24,1536]{1,0:T(8,128)} %copy-done.6) | copy-start | bytes 442372
  105.5 20.9 %copy-start.4 = (bf16[1536,576]{0,1:T(8,128)(2,1)S(1)}, bf16[1536,576]{0,1:T(8,128)(2,1)}, u32[]{:S(2)}) copy-start(bf16[1536,576]{0,1:T(8,128)(2,1)} %param.45) | copy-start | bytes 5308420
  105.5 20.9 %copy-start.23 = (f32[1536]{0:T(1024)S(1)}, f32[1536]{0:T(1024)}, u32[]{:S(2)}) copy-start(f32[1536]{0:T(1024)} %param.44) | copy-start | bytes 18436
  105.5 4.3 %collective-permute-start.8 = (f32[24,512]{1,0:T(8,128)S(1)}, f32[24,512]{1,0:T(8,128)S(1)}, u32[]{:S(2)}, u32[]{:S(2)}) collective-permute-start(f32[24,512]{1,0:T(8,128)S(1)} %maximum_maximum_fusion.2), channel_id=1, source_target_pairs={{0,1},{1,0},{2,3},{3,2},{4,5},{5,4},{6,7},{7,6},{8,9},{9,8},{10,11... | collective-permute-start | bytes 147464 | tf_op jit(solution)/shard_map/ppermute | solution.py:14
  110.8 4.4 %collective-permute-start.9 = (bf16[24,1536]{1,0:T(8,128)(2,1)S(1)}, bf16[24,1536]{1,0:T(8,128)(2,1)S(1)}, u32[]{:S(2)}, u32[]{:S(2)}) collective-permute-start(bf16[24,1536]{1,0:T(8,128)(2,1)S(1)} %get-tuple-element.62), channel_id=1, source_target_pairs={{0,1},{1,0},{2,3},{3,2},{4,5},{5,4},{6,7},{7,6},{8,9},{9,8},{10,11... | collective-permute-start | bytes 221192 | tf_op jit(solution)/shard_map/ppermute | solution.py:14
  115.3 5.7 %collective-permute-start.10 = (bf16[24,1536]{1,0:T(8,128)(2,1)S(1)}, bf16[24,1536]{1,0:T(8,128)(2,1)S(1)}, u32[]{:S(2)}, u32[]{:S(2)}) collective-permute-start(bf16[24,1536]{1,0:T(8,128)(2,1)S(1)} %fusion.13), channel_id=1, source_target_pairs={{0,3},{1,2},{2,1},{3,0},{4,7},{5,6},{6,5},{7,4},{8,11},{9,10},{10,... | collective-permute-start | bytes 221192 | tf_op jit(solution)/shard_map/ppermute | solution.py:14
  121.0 4.6 %collective-permute-start.11 = (bf16[24,1536]{1,0:T(8,128)(2,1)S(1)}, bf16[24,1536]{1,0:T(8,128)(2,1)S(1)}, u32[]{:S(2)}, u32[]{:S(2)}) collective-permute-start(bf16[24,1536]{1,0:T(8,128)(2,1)S(1)} %fusion.29), channel_id=1, source_target_pairs={{0,4},{1,5},{2,6},{3,7},{4,0},{5,1},{6,2},{7,3},{8,12},{9,13},{10,... | collective-permute-start | bytes 221192 | tf_op jit(solution)/shard_map/ppermute | solution.py:14
  131.2 4.0 %collective-permute-start.12 = (bf16[24,768]{1,0:T(8,128)(2,1)S(1)}, bf16[24,768]{1,0:T(8,128)(2,1)S(1)}, u32[]{:S(2)}, u32[]{:S(2)}) collective-permute-start(bf16[24,768]{1,0:T(8,128)(2,1)S(1)} %select_convert_fusion), channel_id=1, source_target_pairs={{0,4},{1,5},{2,6},{3,7},{4,0},{5,1},{6,2},{7,3},{8,12},{9,13},{10,... | collective-permute-start | bytes 110600 | tf_op jit(solution)/shard_map/ppermute | solution.py:14
  136.2 5.1 %collective-permute-start.13 = (bf16[24,384]{1,0:T(8,128)(2,1)S(1)}, bf16[24,384]{1,0:T(8,128)(2,1)S(1)}, u32[]{:S(2)}, u32[]{:S(2)}) collective-permute-start(bf16[24,384]{1,0:T(8,128)(2,1)S(1)} %select_convert_fusion.1), channel_id=1, source_target_pairs={{0,3},{1,2},{2,1},{3,0},{4,7},{5,6},{6,5},{7,4},{8,11},{9,10},{10,... | collective-permute-start | bytes 55304 | tf_op jit(solution)/shard_map/ppermute | solution.py:14
  141.3 3.7 %collective-permute-start.14 = (bf16[24,192]{1,0:T(8,128)(2,1)S(1)}, bf16[24,192]{1,0:T(8,128)(2,1)S(1)}, u32[]{:S(2)}, u32[]{:S(2)}) collective-permute-start(bf16[24,192]{1,0:T(8,128)(2,1)S(1)} %select_convert_fusion.2), channel_id=1, source_target_pairs={{0,1},{1,0},{2,3},{3,2},{4,5},{5,4},{6,7},{7,6},{8,9},{9,8},{10,11... | collective-permute-start | bytes 27656 | tf_op jit(solution)/shard_map/ppermute | solution.py:14
  (29 other events, 354.7 us)

commit v13 on v12

--- a/solution.py
+++ b/solution.py
@@ -148,14 +148,12 @@
     states = jnp.concatenate([conv_state, lru_state[:, None, :]], axis=1)
     to_group = my_owner[None, :] == group_ids[:, None]
     send_slot = jnp.sum(jnp.where(to_group, my_leave[None, :], 0), axis=1)
-    states_send, cache_send = lax.optimization_barrier(
-        (
-            jnp.take(states, send_slot, axis=0, mode="clip"),
-            jnp.take(cache, send_slot, axis=0, mode="clip"),
-        )
-    )
-    got_states = lax.all_to_all(states_send, "req", 0, 0, tiled=True)
-    got_cache = lax.all_to_all(cache_send, "req", 0, 0, tiled=True)
+    got_states = lax.all_to_all(
+        jnp.take(states, send_slot, axis=0, mode="clip"), "req", 0, 0, tiled=True
+    )
+    got_cache = lax.all_to_all(
+        jnp.take(cache, send_slot, axis=0, mode="clip"), "req", 0, 0, tiled=True
+    )
     got_states, tokens, lengths = lax.optimization_barrier((got_states, tokens, lengths))
     local_ids = jnp.arange(req_rows, dtype=jnp.int32)
     match_slot = my_leave[None, :] == local_ids[:, None]

time: 147 us -> 145 us (0.986)
  waiting for transfers between devices: 69.1 us -> 63.6 us
  other arithmetic: 15.5 us -> 17 us
  starting transfers between devices: 38.2 us -> 39.7 us
    all_to_all x2, waiting for transfers between devices: 18.5 us -> 12.9 us  [the longest x1 10.2 us: per_device(): lax.all_to_all(jnp.take(cache, send_slot, axis=0, mode='clip'), 'req', 0,...]
    all_to_all x2, starting transfers between devices: 16.9 us -> 18.4 us  [the longest x1 11.2 us: per_device(): lax.all_to_all(jnp.take(states, send_slot, axis=0, mode='clip'), 'req', 0...]
  transfers between devices with their start and end apart: 17 -> 17, of which waited for: 17 -> 17; matrix products, arithmetic and copies ran while one was open for 9% -> 13% of each run, Pallas kernels for 0% -> 0%
where the time goes in v13:
time: 145 us; the launch traced here: 144 us
  waiting for transfers between devices  63.6 us (44%)
  starting transfers between devices  39.7 us (27%)
  other arithmetic  17 us (12%)
  local copies, waits for them, and re-layouts  14.1 us (10%)
  matrix products  8.65 us (6%)
    ppermute x15, waiting for transfers between devices, partner_swap(): return jax.tree.map(lambda part: lax.ppermute(part, axis, pairs), value)  50.6 us
    ppermute x15, starting transfers between devices, partner_swap(): return jax.tree.map(lambda part: lax.ppermute(part, axis, pairs), value)  21.3 us
    all_to_all x1, starting transfers between devices, per_device(): lax.all_to_all(jnp.take(states, send_slot, axis=0, mode='clip'), 'req', 0...  11.2 us
    all_to_all x1, waiting for transfers between devices, per_device(): lax.all_to_all(jnp.take(cache, send_slot, axis=0, mode='clip'), 'req', 0,...  10.2 us
    all_to_all x1, starting transfers between devices, per_device(): lax.all_to_all(jnp.take(cache, send_slot, axis=0, mode='clip'), 'req', 0,...  7.24 us
    gather x1, local copies, waits for them, and re-layouts, per_device(): jnp.take(got_cache, arrive_from, axis=0, mode='clip')  3.55 us
    gather x1, local copies, waits for them, and re-layouts, per_device(): jnp.take(cache, send_slot, axis=0, mode='clip')  3.39 us
  transfers between devices with their start and end apart: 17, of which 17 were waited for; matrix products, arithmetic and copies ran while one was open for 13% of the time, Pallas kernels for 0%

profile of v13, /device:TPU:32, one launch (start us, length us, event | category | flops | bytes accessed | tf_op | source)
XLA Modules:
  0.0 144.4 jit_solution(9684113544618977411)
XLA Ops:
  3.8 11.2 %all-to-all-start = ((bf16[32,4,256]{2,1,0:T(4,128)(2,1)}), bf16[32,4,256]{2,1,0:T(4,128)(2,1)S(1)}, u32[]{:S(2)}, u32[]{:S(2)}) async-start(bf16[32,4,256]{2,1,0:T(4,128)(2,1)} %gather_fusion), calls=%async_computation | async-start | bytes 131072 | tf_op jit(solution)/shard_map/all_to_all | solution.py:151
  17.5 3.4 %gather_fusion.3 = bf16[32,128,256]{2,1,0:T(8,128)(2,1)} fusion(bf16[24,128,256]{2,1,0:T(8,128)(2,1)} %param.28, s32[1024]{0:T(1024)S(1)} %pad_clamp_fusion.2), kind=kCustom, calls=%fused_computation.3 | custom fusion | bytes 4194432 | tf_op jit(solution)/shard_map/jit(_take)/gather | solution.py:155
  21.7 2.8 %all-to-all-done = bf16[32,4,256]{2,1,0:T(4,128)(2,1)S(1)} async-done(((bf16[32,4,256]{2,1,0:T(4,128)(2,1)}), bf16[32,4,256]{2,1,0:T(4,128)(2,1)S(1)}, u32[]{:S(2)}, u32[]{:S(2)}) %all-to-all-start) | async-done | bytes 65568 | tf_op jit(solution)/shard_map/all_to_all | solution.py:151
  24.5 7.2 %all-to-all-start.1 = ((bf16[32,128,256]{2,1,0:T(8,128)(2,1)}), bf16[32,128,256]{2,1,0:T(8,128)(2,1)}, u32[]{:S(2)}, u32[]{:S(2)}) async-start(bf16[32,128,256]{2,1,0:T(8,128)(2,1)} %gather_fusion.3), calls=%async_computation.1 | async-start | bytes 4194304 | tf_op jit(solution)/shard_map/all_to_all | solution.py:154
  40.9 3.1 %collective-permute-start.1 = (bf16[24,1536]{1,0:T(8,128)(2,1)S(1)}, bf16[24,1536]{1,0:T(8,128)(2,1)S(1)}, u32[]{:S(2)}, u32[]{:S(2)}) collective-permute-start(bf16[24,1536]{1,0:T(8,128)(2,1)S(1)} %fusion.11), channel_id=1, source_target_pairs={{0,3},{1,2},{2,1},{3,0},{4,7},{5,6},{6,5},{7,4},{8,11},{9,10},{10,... | collective-permute-start | bytes 221192 | tf_op jit(solution)/shard_map/ppermute | solution.py:14
  48.0 7.5 %collective-permute-done.2 = bf16[24,1536]{1,0:T(8,128)(2,1)S(1)} collective-permute-done((bf16[24,1536]{1,0:T(8,128)(2,1)S(1)}, bf16[24,1536]{1,0:T(8,128)(2,1)S(1)}, u32[]{:S(2)}, u32[]{:S(2)}) %collective-permute-start.2) | collective-permute-done | bytes 73760 | tf_op jit(solution)/shard_map/ppermute | solution.py:14
  57.1 3.4 %collective-permute-done.3 = bf16[24,1536]{1,0:T(8,128)(2,1)S(1)} collective-permute-done((bf16[24,1536]{1,0:T(8,128)(2,1)S(1)}, bf16[24,1536]{1,0:T(8,128)(2,1)S(1)}, u32[]{:S(2)}, u32[]{:S(2)}) %collective-permute-start.3) | collective-permute-done | bytes 73760 | tf_op jit(solution)/shard_map/ppermute | solution.py:14
  60.5 3.1 %collective-permute-start.4 = (bf16[24,1536]{1,0:T(8,128)(2,1)S(1)}, bf16[24,1536]{1,0:T(8,128)(2,1)S(1)}, u32[]{:S(2)}, u32[]{:S(2)}) collective-permute-start(bf16[24,1536]{1,0:T(8,128)(2,1)S(1)} %fusion.12), channel_id=1, source_target_pairs={{0,3},{1,2},{2,1},{3,0},{4,7},{5,6},{6,5},{7,4},{8,11},{9,10},{10,... | collective-permute-start | bytes 221192 | tf_op jit(solution)/shard_map/ppermute | solution.py:14
  63.6 2.5 %collective-permute-done.4 = bf16[24,1536]{1,0:T(8,128)(2,1)S(1)} collective-permute-done((bf16[24,1536]{1,0:T(8,128)(2,1)S(1)}, bf16[24,1536]{1,0:T(8,128)(2,1)S(1)}, u32[]{:S(2)}, u32[]{:S(2)}) %collective-permute-start.4) | collective-permute-done | bytes 73760 | tf_op jit(solution)/shard_map/ppermute | solution.py:14
  66.9 6.0 %collective-permute-done.5 = bf16[24,1536]{1,0:T(8,128)(2,1)S(1)} collective-permute-done((bf16[24,1536]{1,0:T(8,128)(2,1)S(1)}, bf16[24,1536]{1,0:T(8,128)(2,1)S(1)}, u32[]{:S(2)}, u32[]{:S(2)}) %collective-permute-start.5) | collective-permute-done | bytes 73760 | tf_op jit(solution)/shard_map/ppermute | solution.py:14
  74.6 10.2 %all-to-all-done.1 = bf16[32,128,256]{2,1,0:T(8,128)(2,1)} async-done(((bf16[32,128,256]{2,1,0:T(8,128)(2,1)}), bf16[32,128,256]{2,1,0:T(8,128)(2,1)}, u32[]{:S(2)}, u32[]{:S(2)}) %all-to-all-start.1) | async-done | bytes 2097184 | tf_op jit(solution)/shard_map/all_to_all | solution.py:154
  84.7 3.6 %gather_fusion.4 = bf16[24,128,256]{2,1,0:T(8,128)(2,1)} fusion(bf16[32,128,256]{2,1,0:T(8,128)(2,1)} %all-to-all-done.1, s32[1024]{0:T(1024)} %copy-done.27), kind=kCustom, calls=%fused_computation.4 | custom fusion | bytes 3145824 | tf_op jit(solution)/shard_map/jit(_take)/gather | solution.py:169
  88.3 2.7 %broadcast_select_fusion.1 = (bf16[24,128,256]{2,1,0:T(8,128)(2,1)}, bf16[24,128,256]{2,1,0:T(8,128)(2,1)S(1)}) fusion(pred[24,128]{1,0:T(8,128)(4,1)} %get-tuple-element.45, bf16[24,256]{1,0:T(8,128)(2,1)} %pad_maximum_fusion.4, bf16[24,128,256]{2,1,0:T(8,128)(2,1)} %gather_fusion.4, bf16[24,128,256]{2,1,0:T(8,128)(2,1)S(1)} %copy-done.2, ...), kind=kLoop, calls=%fused_computation.6 | loop fusion | flops 1572864 | bytes 6306840 | tf_op jit(solution)/shard_map/jit(_where)/select_n | solution.py:321
  93.4 3.8 %collective-permute-done.6 = f32[24,896]{1,0:T(8,128)S(1)} collective-permute-done((f32[24,896]{1,0:T(8,128)S(1)}, f32[24,896]{1,0:T(8,128)S(1)}, u32[]{:S(2)}, u32[]{:S(2)}) %collective-permute-start.6) | collective-permute-done | bytes 86048 | tf_op jit(solution)/shard_map/ppermute | solution.py:14
  97.7 3.0 %collective-permute-start.7 = (f32[24,512]{1,0:T(8,128)S(1)}, f32[24,512]{1,0:T(8,128)S(1)}, u32[]{:S(2)}, u32[]{:S(2)}) collective-permute-start(f32[24,512]{1,0:T(8,128)S(1)} %maximum_maximum_fusion.1), channel_id=1, source_target_pairs={{0,3},{1,2},{2,1},{3,0},{4,7},{5,6},{6,5},{7,4},{8,11},{9,10},{10,... | collective-permute-start | bytes 147464 | tf_op jit(solution)/shard_map/ppermute | solution.py:14
  104.1 3.6 %collective-permute-done.8 = f32[24,512]{1,0:T(8,128)S(1)} collective-permute-done((f32[24,512]{1,0:T(8,128)S(1)}, f32[24,512]{1,0:T(8,128)S(1)}, u32[]{:S(2)}, u32[]{:S(2)}) %collective-permute-start.8) | collective-permute-done | bytes 49184 | tf_op jit(solution)/shard_map/ppermute | solution.py:14
  109.2 3.9 %collective-permute-done.9 = bf16[24,1536]{1,0:T(8,128)(2,1)S(1)} collective-permute-done((bf16[24,1536]{1,0:T(8,128)(2,1)S(1)}, bf16[24,1536]{1,0:T(8,128)(2,1)S(1)}, u32[]{:S(2)}, u32[]{:S(2)}) %collective-permute-start.9) | collective-permute-done | bytes 73760 | tf_op jit(solution)/shard_map/ppermute | solution.py:14
  113.2 3.2 %collective-permute-start.10 = (bf16[24,1536]{1,0:T(8,128)(2,1)S(1)}, bf16[24,1536]{1,0:T(8,128)(2,1)S(1)}, u32[]{:S(2)}, u32[]{:S(2)}) collective-permute-start(bf16[24,1536]{1,0:T(8,128)(2,1)S(1)} %fusion.13), channel_id=1, source_target_pairs={{0,3},{1,2},{2,1},{3,0},{4,7},{5,6},{6,5},{7,4},{8,11},{9,10},{10,... | collective-permute-start | bytes 221192 | tf_op jit(solution)/shard_map/ppermute | solution.py:14
  116.4 2.5 %collective-permute-done.10 = bf16[24,1536]{1,0:T(8,128)(2,1)S(1)} collective-permute-done((bf16[24,1536]{1,0:T(8,128)(2,1)S(1)}, bf16[24,1536]{1,0:T(8,128)(2,1)S(1)}, u32[]{:S(2)}, u32[]{:S(2)}) %collective-permute-start.10) | collective-permute-done | bytes 73760 | tf_op jit(solution)/shard_map/ppermute | solution.py:14
  119.7 3.8 %collective-permute-done.11 = bf16[24,1536]{1,0:T(8,128)(2,1)S(1)} collective-permute-done((bf16[24,1536]{1,0:T(8,128)(2,1)S(1)}, bf16[24,1536]{1,0:T(8,128)(2,1)S(1)}, u32[]{:S(2)}, u32[]{:S(2)}) %collective-permute-start.11) | collective-permute-done | bytes 73760 | tf_op jit(solution)/shard_map/ppermute | solution.py:14
  125.5 2.6 %fusion.1 = f32[24,1536]{1,0:T(8,128)} fusion(bf16[576,1536]{1,0:T(8,128)(2,1)S(1)} %copy-done, bf16[1536,576]{0,1:T(8,128)(2,1)S(1)} %copy-done.3, f32[24,576]{1,0:T(8,128)} %fusion.109, f32[24,1536]{1,0:T(8,128)} %copy-done.5, f32[1536]{0:T(1024)} %param.44, f32[24]{0:T(128)S(1)} %add_rsqrt_fusion), kind=kOutput, calls=%fused_computation.11 | convolution fusion | flops 85183488 | bytes 3895392 | tf_op jit(solution)/shard_map/dot_general | solution.py:313
  129.7 3.4 %collective-permute-done.12 = bf16[24,768]{1,0:T(8,128)(2,1)S(1)} collective-permute-done((bf16[24,768]{1,0:T(8,128)(2,1)S(1)}, bf16[24,768]{1,0:T(8,128)(2,1)S(1)}, u32[]{:S(2)}, u32[]{:S(2)}) %collective-permute-start.12) | collective-permute-done | bytes 36896 | tf_op jit(solution)/shard_map/ppermute | solution.py:14
  134.1 3.2 %collective-permute-start.13 = (bf16[24,384]{1,0:T(8,128)(2,1)S(1)}, bf16[24,384]{1,0:T(8,128)(2,1)S(1)}, u32[]{:S(2)}, u32[]{:S(2)}) collective-permute-start(bf16[24,384]{1,0:T(8,128)(2,1)S(1)} %select_convert_fusion.1), channel_id=1, source_target_pairs={{0,3},{1,2},{2,1},{3,0},{4,7},{5,6},{6,5},{7,4},{8,11},{9,10},{10,... | collective-permute-start | bytes 55304 | tf_op jit(solution)/shard_map/ppermute | solution.py:14
  139.9 3.0 %collective-permute-done.14 = bf16[24,192]{1,0:T(8,128)(2,1)S(1)} collective-permute-done((bf16[24,192]{1,0:T(8,128)(2,1)S(1)}, bf16[24,192]{1,0:T(8,128)(2,1)S(1)}, u32[]{:S(2)}, u32[]{:S(2)}) %collective-permute-start.14) | collective-permute-done | bytes 9248 | tf_op jit(solution)/shard_map/ppermute | solution.py:14
  (184 shorter events, 40.5 us)
Async XLA Ops:
  0.6 124.9 %copy-start = (bf16[576,1536]{1,0:T(8,128)(2,1)S(1)}, bf16[576,1536]{1,0:T(8,128)(2,1)}, u32[]{:S(2)}) copy-start(bf16[576,1536]{1,0:T(8,128)(2,1)} %param.47) | copy-start | bytes 5308420
  3.8 20.6 %all-to-all-start = ((bf16[32,4,256]{2,1,0:T(4,128)(2,1)}), bf16[32,4,256]{2,1,0:T(4,128)(2,1)S(1)}, u32[]{:S(2)}, u32[]{:S(2)}) async-start(bf16[32,4,256]{2,1,0:T(4,128)(2,1)} %gather_fusion), calls=%async_computation | async-start | bytes 131072 | tf_op jit(solution)/shard_map/all_to_all | solution.py:151
  16.0 28.0 %copy-start.29 = (f32[64]{0:T(128)}, f32[64]{0:T(128)S(1)}, u32[]{:S(2)}) copy-start(f32[64]{0:T(128)S(1)} %multiply_power_fusion) | copy-start | bytes 772
  24.5 60.3 %all-to-all-start.1 = ((bf16[32,128,256]{2,1,0:T(8,128)(2,1)}), bf16[32,128,256]{2,1,0:T(8,128)(2,1)}, u32[]{:S(2)}, u32[]{:S(2)}) async-start(bf16[32,128,256]{2,1,0:T(8,128)(2,1)} %gather_fusion.3), calls=%async_computation.1 | async-start | bytes 4194304 | tf_op jit(solution)/shard_map/all_to_all | solution.py:154
  34.4 21.3 %copy-start.25 = (f32[1536]{0:T(1024)S(1)}, f32[1536]{0:T(1024)}, u32[]{:S(2)}) copy-start(f32[1536]{0:T(1024)} %param.40) | copy-start | bytes 18436
  34.4 21.4 %copy-start.13 = (bf16[192,1536]{1,0:T(8,128)(2,1)S(1)}, bf16[192,1536]{1,0:T(8,128)(2,1)}, u32[]{:S(2)}) copy-start(bf16[192,1536]{1,0:T(8,128)(2,1)} %param.41) | copy-start | bytes 1769476
  36.4 4.4 %collective-permute-start = (bf16[24,1536]{1,0:T(8,128)(2,1)S(1)}, bf16[24,1536]{1,0:T(8,128)(2,1)S(1)}, u32[]{:S(2)}, u32[]{:S(2)}) collective-permute-start(bf16[24,1536]{1,0:T(8,128)(2,1)S(1)} %get-tuple-element.52), channel_id=1, source_target_pairs={{0,1},{1,0},{2,3},{3,2},{4,5},{5,4},{6,7},{7,6},{8,9},{9,8},{10,11... | collective-permute-start | bytes 221192 | tf_op jit(solution)/shard_map/ppermute | solution.py:14
  40.9 5.7 %collective-permute-start.1 = (bf16[24,1536]{1,0:T(8,128)(2,1)S(1)}, bf16[24,1536]{1,0:T(8,128)(2,1)S(1)}, u32[]{:S(2)}, u32[]{:S(2)}) collective-permute-start(bf16[24,1536]{1,0:T(8,128)(2,1)S(1)} %fusion.11), channel_id=1, source_target_pairs={{0,3},{1,2},{2,1},{3,0},{4,7},{5,6},{6,5},{7,4},{8,11},{9,10},{10,... | collective-permute-start | bytes 221192 | tf_op jit(solution)/shard_map/ppermute | solution.py:14
  46.6 8.9 %collective-permute-start.2 = (bf16[24,1536]{1,0:T(8,128)(2,1)S(1)}, bf16[24,1536]{1,0:T(8,128)(2,1)S(1)}, u32[]{:S(2)}, u32[]{:S(2)}) collective-permute-start(bf16[24,1536]{1,0:T(8,128)(2,1)S(1)} %fusion.27), channel_id=1, source_target_pairs={{0,4},{1,5},{2,6},{3,7},{4,0},{5,1},{6,2},{7,3},{8,12},{9,13},{10,... | collective-permute-start | bytes 221192 | tf_op jit(solution)/shard_map/ppermute | solution.py:14
  56.0 4.4 %collective-permute-start.3 = (bf16[24,1536]{1,0:T(8,128)(2,1)S(1)}, bf16[24,1536]{1,0:T(8,128)(2,1)S(1)}, u32[]{:S(2)}, u32[]{:S(2)}) collective-permute-start(bf16[24,1536]{1,0:T(8,128)(2,1)S(1)} %get-tuple-element.54), channel_id=1, source_target_pairs={{0,1},{1,0},{2,3},{3,2},{4,5},{5,4},{6,7},{7,6},{8,9},{9,8},{10,11... | collective-permute-start | bytes 221192 | tf_op jit(solution)/shard_map/ppermute | solution.py:14
  60.5 5.7 %collective-permute-start.4 = (bf16[24,1536]{1,0:T(8,128)(2,1)S(1)}, bf16[24,1536]{1,0:T(8,128)(2,1)S(1)}, u32[]{:S(2)}, u32[]{:S(2)}) collective-permute-start(bf16[24,1536]{1,0:T(8,128)(2,1)S(1)} %fusion.12), channel_id=1, source_target_pairs={{0,3},{1,2},{2,1},{3,0},{4,7},{5,6},{6,5},{7,4},{8,11},{9,10},{10,... | collective-permute-start | bytes 221192 | tf_op jit(solution)/shard_map/ppermute | solution.py:14
  66.2 6.7 %collective-permute-start.5 = (bf16[24,1536]{1,0:T(8,128)(2,1)S(1)}, bf16[24,1536]{1,0:T(8,128)(2,1)S(1)}, u32[]{:S(2)}, u32[]{:S(2)}) collective-permute-start(bf16[24,1536]{1,0:T(8,128)(2,1)S(1)} %fusion.28), channel_id=1, source_target_pairs={{0,4},{1,5},{2,6},{3,7},{4,0},{5,1},{6,2},{7,3},{8,12},{9,13},{10,... | collective-permute-start | bytes 221192 | tf_op jit(solution)/shard_map/ppermute | solution.py:14
  92.7 4.5 %collective-permute-start.6 = (f32[24,896]{1,0:T(8,128)S(1)}, f32[24,896]{1,0:T(8,128)S(1)}, u32[]{:S(2)}, u32[]{:S(2)}) collective-permute-start(f32[24,896]{1,0:T(8,128)S(1)} %maximum_maximum_fusion), channel_id=1, source_target_pairs={{0,4},{1,5},{2,6},{3,7},{4,0},{5,1},{6,2},{7,3},{8,12},{9,13},{10,... | collective-permute-start | bytes 258056 | tf_op jit(solution)/shard_map/ppermute | solution.py:14
  97.7 5.3 %collective-permute-start.7 = (f32[24,512]{1,0:T(8,128)S(1)}, f32[24,512]{1,0:T(8,128)S(1)}, u32[]{:S(2)}, u32[]{:S(2)}) collective-permute-start(f32[24,512]{1,0:T(8,128)S(1)} %maximum_maximum_fusion.1), channel_id=1, source_target_pairs={{0,3},{1,2},{2,1},{3,0},{4,7},{5,6},{6,5},{7,4},{8,11},{9,10},{10,... | collective-permute-start | bytes 147464 | tf_op jit(solution)/shard_map/ppermute | solution.py:14
  100.9 22.6 %copy-start.7 = (f32[24,1536]{1,0:T(8,128)S(1)}, f32[24,1536]{1,0:T(8,128)}, u32[]{:S(2)}) copy-start(f32[24,1536]{1,0:T(8,128)} %copy-done.6) | copy-start | bytes 442372
  103.4 20.9 %copy-start.4 = (bf16[1536,576]{0,1:T(8,128)(2,1)S(1)}, bf16[1536,576]{0,1:T(8,128)(2,1)}, u32[]{:S(2)}) copy-start(bf16[1536,576]{0,1:T(8,128)(2,1)} %param.45) | copy-start | bytes 5308420
  103.4 20.9 %copy-start.23 = (f32[1536]{0:T(1024)S(1)}, f32[1536]{0:T(1024)}, u32[]{:S(2)}) copy-start(f32[1536]{0:T(1024)} %param.44) | copy-start | bytes 18436
  103.4 4.3 %collective-permute-start.8 = (f32[24,512]{1,0:T(8,128)S(1)}, f32[24,512]{1,0:T(8,128)S(1)}, u32[]{:S(2)}, u32[]{:S(2)}) collective-permute-start(f32[24,512]{1,0:T(8,128)S(1)} %maximum_maximum_fusion.2), channel_id=1, source_target_pairs={{0,1},{1,0},{2,3},{3,2},{4,5},{5,4},{6,7},{7,6},{8,9},{9,8},{10,11... | collective-permute-start | bytes 147464 | tf_op jit(solution)/shard_map/ppermute | solution.py:14
  108.7 4.4 %collective-permute-start.9 = (bf16[24,1536]{1,0:T(8,128)(2,1)S(1)}, bf16[24,1536]{1,0:T(8,128)(2,1)S(1)}, u32[]{:S(2)}, u32[]{:S(2)}) collective-permute-start(bf16[24,1536]{1,0:T(8,128)(2,1)S(1)} %get-tuple-element.58), channel_id=1, source_target_pairs={{0,1},{1,0},{2,3},{3,2},{4,5},{5,4},{6,7},{7,6},{8,9},{9,8},{10,11... | collective-permute-start | bytes 221192 | tf_op jit(solution)/shard_map/ppermute | solution.py:14
  113.2 5.7 %collective-permute-start.10 = (bf16[24,1536]{1,0:T(8,128)(2,1)S(1)}, bf16[24,1536]{1,0:T(8,128)(2,1)S(1)}, u32[]{:S(2)}, u32[]{:S(2)}) collective-permute-start(bf16[24,1536]{1,0:T(8,128)(2,1)S(1)} %fusion.13), channel_id=1, source_target_pairs={{0,3},{1,2},{2,1},{3,0},{4,7},{5,6},{6,5},{7,4},{8,11},{9,10},{10,... | collective-permute-start | bytes 221192 | tf_op jit(solution)/shard_map/ppermute | solution.py:14
  118.9 4.6 %collective-permute-start.11 = (bf16[24,1536]{1,0:T(8,128)(2,1)S(1)}, bf16[24,1536]{1,0:T(8,128)(2,1)S(1)}, u32[]{:S(2)}, u32[]{:S(2)}) collective-permute-start(bf16[24,1536]{1,0:T(8,128)(2,1)S(1)} %fusion.29), channel_id=1, source_target_pairs={{0,4},{1,5},{2,6},{3,7},{4,0},{5,1},{6,2},{7,3},{8,12},{9,13},{10,... | collective-permute-start | bytes 221192 | tf_op jit(solution)/shard_map/ppermute | solution.py:14
  129.1 4.0 %collective-permute-start.12 = (bf16[24,768]{1,0:T(8,128)(2,1)S(1)}, bf16[24,768]{1,0:T(8,128)(2,1)S(1)}, u32[]{:S(2)}, u32[]{:S(2)}) collective-permute-start(bf16[24,768]{1,0:T(8,128)(2,1)S(1)} %select_convert_fusion), channel_id=1, source_target_pairs={{0,4},{1,5},{2,6},{3,7},{4,0},{5,1},{6,2},{7,3},{8,12},{9,13},{10,... | collective-permute-start | bytes 110600 | tf_op jit(solution)/shard_map/ppermute | solution.py:14
  134.1 5.1 %collective-permute-start.13 = (bf16[24,384]{1,0:T(8,128)(2,1)S(1)}, bf16[24,384]{1,0:T(8,128)(2,1)S(1)}, u32[]{:S(2)}, u32[]{:S(2)}) collective-permute-start(bf16[24,384]{1,0:T(8,128)(2,1)S(1)} %select_convert_fusion.1), channel_id=1, source_target_pairs={{0,3},{1,2},{2,1},{3,0},{4,7},{5,6},{6,5},{7,4},{8,11},{9,10},{10,... | collective-permute-start | bytes 55304 | tf_op jit(solution)/shard_map/ppermute | solution.py:14
  139.2 3.7 %collective-permute-start.14 = (bf16[24,192]{1,0:T(8,128)(2,1)S(1)}, bf16[24,192]{1,0:T(8,128)(2,1)S(1)}, u32[]{:S(2)}, u32[]{:S(2)}) collective-permute-start(bf16[24,192]{1,0:T(8,128)(2,1)S(1)} %select_convert_fusion.2), channel_id=1, source_target_pairs={{0,1},{1,0},{2,3},{3,2},{4,5},{5,4},{6,7},{7,6},{8,9},{9,8},{10,11... | collective-permute-start | bytes 27656 | tf_op jit(solution)/shard_map/ppermute | solution.py:14
  (26 other events, 276.9 us)

commit v14 on v13

--- a/solution.py
+++ b/solution.py
@@ -251,6 +251,14 @@
     top, total = local_top, local_sum
     held = heads
     head_base = jnp.zeros((), jnp.int32)
+    column_half = None
+
+    def spread(per_head):
+        cols = jnp.repeat(per_head, head_size, axis=1)
+        if column_half is None:
+            return cols
+        return jnp.where(column_half, cols[:, slice_rows:], cols[:, :slice_rows])
+
     for mask, bit in reversed(axis_stages("mlp")):
         if held % 2 == 0 and (held // 2) * head_size >= 2 * slice_rows:
             held = held // 2
@@ -264,10 +272,15 @@
             send_total = jnp.where(upper, total[:, :held], total[:, held:])
             head_base = head_base + jnp.where(upper, held, 0)
         else:
-            keep_acc = send_acc = acc
             keep_top = send_top = top
             keep_total = send_total = total
-        cut = held * head_size
+            if column_half is None and acc.shape[1] == 2 * slice_rows:
+                column_half = (mlp_id & bit) != 0
+                keep_acc = jnp.where(column_half, acc[:, slice_rows:], acc[:, :slice_rows])
+                send_acc = jnp.where(column_half, acc[:, :slice_rows], acc[:, slice_rows:])
+            else:
+                keep_acc = send_acc = acc
+        cut = keep_acc.shape[1]
         stat_pad = jnp.zeros((req_rows, head_size - 2 * held), jnp.float32)
         got = partner_swap(
             jnp.concatenate([send_acc, send_top, send_total, stat_pad], axis=1), "mlp", mask
@@ -277,9 +290,7 @@
         top = jnp.maximum(keep_top, got_top)
         keep_factor = jnp.exp(keep_top - top)
         got_factor = jnp.exp(got_top - top)
-        acc = keep_acc * jnp.repeat(keep_factor, head_size, axis=1) + got[:, :cut] * jnp.repeat(
-            got_factor, head_size, axis=1
-        )
+        acc = keep_acc * spread(keep_factor) + got[:, :cut] * spread(got_factor)
         total = keep_total * keep_factor + got_total * got_factor
     own_score = (
         jnp.sum(queries.astype(jnp.float32) * key_new.astype(jnp.float32)[:, None, :], axis=-1)
@@ -291,17 +302,13 @@
     own_weight = jnp.exp(own_score - top_score)
     own_rounded = lax.optimization_barrier(own_weight.astype(jnp.bfloat16)).astype(jnp.float32)
     denominator = total * rescale + own_weight
-    numerator = acc * jnp.repeat(rescale, head_size, axis=1) + jnp.repeat(
-        own_rounded, head_size, axis=1
-    ) * jnp.tile(value_new.astype(jnp.float32), (1, held))
-    attended = (numerator / jnp.repeat(denominator, head_size, axis=1)).astype(jnp.bfloat16)
-    attn_part = jnp.dot(
-        lax.dynamic_slice_in_dim(
-            attended, mlp_id * slice_rows - head_base * head_size, slice_rows, 1
-        ),
-        w_attn_out,
-        preferred_element_type=jnp.float32,
-    )
+    values_tiled = jnp.tile(value_new.astype(jnp.float32), (1, held))
+    values_tiled = jnp.where(
+        column_half, values_tiled[:, slice_rows:], values_tiled[:, :slice_rows]
+    )
+    numerator = acc * spread(rescale) + spread(own_rounded) * values_tiled
+    attended = (numerator / spread(denominator)).astype(jnp.bfloat16)
+    attn_part = jnp.dot(attended, w_attn_out, preferred_element_type=jnp.float32)
     resid_two = resid_one + across_mlp_narrow(attn_part)
     normed_mlp = rms_norm(resid_two, gain_mlp)
     gate_act = jax.nn.gelu(

time: 145 us -> 145 us (level)
  no operation moved by 1% of the time
where the time goes in v14:
time: 145 us; the launch traced here: 144 us
  waiting for transfers between devices  64 us (44%)
  starting transfers between devices  39.7 us (27%)
  other arithmetic  16.4 us (11%)
  local copies, waits for them, and re-layouts  14.2 us (10%)
  matrix products  8.64 us (6%)
    ppermute x15, waiting for transfers between devices, partner_swap(): return jax.tree.map(lambda part: lax.ppermute(part, axis, pairs), value)  51.1 us
    ppermute x15, starting transfers between devices, partner_swap(): return jax.tree.map(lambda part: lax.ppermute(part, axis, pairs), value)  21.3 us
    all_to_all x1, starting transfers between devices, per_device(): lax.all_to_all(jnp.take(states, send_slot, axis=0, mode='clip'), 'req', 0...  11.2 us
    all_to_all x1, waiting for transfers between devices, per_device(): lax.all_to_all(jnp.take(cache, send_slot, axis=0, mode='clip'), 'req', 0,...  10.2 us
    all_to_all x1, starting transfers between devices, per_device(): lax.all_to_all(jnp.take(cache, send_slot, axis=0, mode='clip'), 'req', 0,...  7.24 us
    gather x1, local copies, waits for them, and re-layouts, per_device(): jnp.take(got_cache, arrive_from, axis=0, mode='clip')  3.55 us
    gather x1, local copies, waits for them, and re-layouts, per_device(): jnp.take(cache, send_slot, axis=0, mode='clip')  3.39 us
  transfers between devices with their start and end apart: 17, of which 17 were waited for; matrix products, arithmetic and copies ran while one was open for 13% of the time, Pallas kernels for 0%

profile of v14, /device:TPU:32, one launch (start us, length us, event | category | flops | bytes accessed | tf_op | source)
XLA Modules:
  0.0 144.3 jit_solution(5091253746933790214)
XLA Ops:
  3.8 11.2 %all-to-all-start = ((bf16[32,4,256]{2,1,0:T(4,128)(2,1)}), bf16[32,4,256]{2,1,0:T(4,128)(2,1)S(1)}, u32[]{:S(2)}, u32[]{:S(2)}) async-start(bf16[32,4,256]{2,1,0:T(4,128)(2,1)} %gather_fusion), calls=%async_computation | async-start | bytes 131072 | tf_op jit(solution)/shard_map/all_to_all | solution.py:151
  17.5 3.4 %gather_fusion.3 = bf16[32,128,256]{2,1,0:T(8,128)(2,1)} fusion(bf16[24,128,256]{2,1,0:T(8,128)(2,1)} %param.28, s32[1024]{0:T(1024)S(1)} %pad_clamp_fusion.2), kind=kCustom, calls=%fused_computation.3 | custom fusion | bytes 4194432 | tf_op jit(solution)/shard_map/jit(_take)/gather | solution.py:155
  21.7 2.8 %all-to-all-done = bf16[32,4,256]{2,1,0:T(4,128)(2,1)S(1)} async-done(((bf16[32,4,256]{2,1,0:T(4,128)(2,1)}), bf16[32,4,256]{2,1,0:T(4,128)(2,1)S(1)}, u32[]{:S(2)}, u32[]{:S(2)}) %all-to-all-start) | async-done | bytes 65568 | tf_op jit(solution)/shard_map/all_to_all | solution.py:151
  24.5 7.2 %all-to-all-start.1 = ((bf16[32,128,256]{2,1,0:T(8,128)(2,1)}), bf16[32,128,256]{2,1,0:T(8,128)(2,1)}, u32[]{:S(2)}, u32[]{:S(2)}) async-start(bf16[32,128,256]{2,1,0:T(8,128)(2,1)} %gather_fusion.3), calls=%async_computation.1 | async-start | bytes 4194304 | tf_op jit(solution)/shard_map/all_to_all | solution.py:154
  40.9 3.1 %collective-permute-start.1 = (bf16[24,1536]{1,0:T(8,128)(2,1)S(1)}, bf16[24,1536]{1,0:T(8,128)(2,1)S(1)}, u32[]{:S(2)}, u32[]{:S(2)}) collective-permute-start(bf16[24,1536]{1,0:T(8,128)(2,1)S(1)} %fusion.11), channel_id=1, source_target_pairs={{0,3},{1,2},{2,1},{3,0},{4,7},{5,6},{6,5},{7,4},{8,11},{9,10},{10,... | collective-permute-start | bytes 221192 | tf_op jit(solution)/shard_map/ppermute | solution.py:14
  48.0 7.5 %collective-permute-done.2 = bf16[24,1536]{1,0:T(8,128)(2,1)S(1)} collective-permute-done((bf16[24,1536]{1,0:T(8,128)(2,1)S(1)}, bf16[24,1536]{1,0:T(8,128)(2,1)S(1)}, u32[]{:S(2)}, u32[]{:S(2)}) %collective-permute-start.2) | collective-permute-done | bytes 73760 | tf_op jit(solution)/shard_map/ppermute | solution.py:14
  56.5 3.9 %collective-permute-done.3 = bf16[24,1536]{1,0:T(8,128)(2,1)S(1)} collective-permute-done((bf16[24,1536]{1,0:T(8,128)(2,1)S(1)}, bf16[24,1536]{1,0:T(8,128)(2,1)S(1)}, u32[]{:S(2)}, u32[]{:S(2)}) %collective-permute-start.3) | collective-permute-done | bytes 73760 | tf_op jit(solution)/shard_map/ppermute | solution.py:14
  60.5 3.1 %collective-permute-start.4 = (bf16[24,1536]{1,0:T(8,128)(2,1)S(1)}, bf16[24,1536]{1,0:T(8,128)(2,1)S(1)}, u32[]{:S(2)}, u32[]{:S(2)}) collective-permute-start(bf16[24,1536]{1,0:T(8,128)(2,1)S(1)} %fusion.12), channel_id=1, source_target_pairs={{0,3},{1,2},{2,1},{3,0},{4,7},{5,6},{6,5},{7,4},{8,11},{9,10},{10,... | collective-permute-start | bytes 221192 | tf_op jit(solution)/shard_map/ppermute | solution.py:14
  63.6 2.5 %collective-permute-done.4 = bf16[24,1536]{1,0:T(8,128)(2,1)S(1)} collective-permute-done((bf16[24,1536]{1,0:T(8,128)(2,1)S(1)}, bf16[24,1536]{1,0:T(8,128)(2,1)S(1)}, u32[]{:S(2)}, u32[]{:S(2)}) %collective-permute-start.4) | collective-permute-done | bytes 73760 | tf_op jit(solution)/shard_map/ppermute | solution.py:14
  66.9 6.0 %collective-permute-done.5 = bf16[24,1536]{1,0:T(8,128)(2,1)S(1)} collective-permute-done((bf16[24,1536]{1,0:T(8,128)(2,1)S(1)}, bf16[24,1536]{1,0:T(8,128)(2,1)S(1)}, u32[]{:S(2)}, u32[]{:S(2)}) %collective-permute-start.5) | collective-permute-done | bytes 73760 | tf_op jit(solution)/shard_map/ppermute | solution.py:14
  74.6 10.2 %all-to-all-done.1 = bf16[32,128,256]{2,1,0:T(8,128)(2,1)} async-done(((bf16[32,128,256]{2,1,0:T(8,128)(2,1)}), bf16[32,128,256]{2,1,0:T(8,128)(2,1)}, u32[]{:S(2)}, u32[]{:S(2)}) %all-to-all-start.1) | async-done | bytes 2097184 | tf_op jit(solution)/shard_map/all_to_all | solution.py:154
  84.7 3.6 %gather_fusion.4 = bf16[24,128,256]{2,1,0:T(8,128)(2,1)} fusion(bf16[32,128,256]{2,1,0:T(8,128)(2,1)} %all-to-all-done.1, s32[1024]{0:T(1024)} %copy-done.28), kind=kCustom, calls=%fused_computation.4 | custom fusion | bytes 3145824 | tf_op jit(solution)/shard_map/jit(_take)/gather | solution.py:169
  88.3 2.7 %broadcast_select_fusion.1 = (bf16[24,128,256]{2,1,0:T(8,128)(2,1)}, bf16[24,128,256]{2,1,0:T(8,128)(2,1)S(1)}) fusion(pred[24,128]{1,0:T(8,128)(4,1)} %get-tuple-element.43, bf16[24,256]{1,0:T(8,128)(2,1)} %pad_maximum_fusion.6, bf16[24,128,256]{2,1,0:T(8,128)(2,1)} %gather_fusion.4, bf16[24,128,256]{2,1,0:T(8,128)(2,1)S(1)} %copy-done.2, ...), kind=kLoop, calls=%fused_computation.6 | loop fusion | flops 1572864 | bytes 6306840 | tf_op jit(solution)/shard_map/jit(_where)/select_n | solution.py:328
  93.3 3.9 %collective-permute-done.6 = f32[24,896]{1,0:T(8,128)S(1)} collective-permute-done((f32[24,896]{1,0:T(8,128)S(1)}, f32[24,896]{1,0:T(8,128)S(1)}, u32[]{:S(2)}, u32[]{:S(2)}) %collective-permute-start.6) | collective-permute-done | bytes 86048 | tf_op jit(solution)/shard_map/ppermute | solution.py:14
  97.7 3.0 %collective-permute-start.7 = (f32[24,512]{1,0:T(8,128)S(1)}, f32[24,512]{1,0:T(8,128)S(1)}, u32[]{:S(2)}, u32[]{:S(2)}) collective-permute-start(f32[24,512]{1,0:T(8,128)S(1)} %pad_maximum_fusion.2), channel_id=1, source_target_pairs={{0,3},{1,2},{2,1},{3,0},{4,7},{5,6},{6,5},{7,4},{8,11},{9,10},{10,... | collective-permute-start | bytes 147464 | tf_op jit(solution)/shard_map/ppermute | solution.py:14
  104.2 3.5 %collective-permute-done.8 = f32[24,320]{1,0:T(8,128)S(1)} collective-permute-done((f32[24,320]{1,0:T(8,128)S(1)}, f32[24,320]{1,0:T(8,128)S(1)}, u32[]{:S(2)}, u32[]{:S(2)}) %collective-permute-start.8) | collective-permute-done | bytes 30752 | tf_op jit(solution)/shard_map/ppermute | solution.py:14
  109.2 3.9 %collective-permute-done.9 = bf16[24,1536]{1,0:T(8,128)(2,1)S(1)} collective-permute-done((bf16[24,1536]{1,0:T(8,128)(2,1)S(1)}, bf16[24,1536]{1,0:T(8,128)(2,1)S(1)}, u32[]{:S(2)}, u32[]{:S(2)}) %collective-permute-start.9) | collective-permute-done | bytes 73760 | tf_op jit(solution)/shard_map/ppermute | solution.py:14
  113.1 3.2 %collective-permute-start.10 = (bf16[24,1536]{1,0:T(8,128)(2,1)S(1)}, bf16[24,1536]{1,0:T(8,128)(2,1)S(1)}, u32[]{:S(2)}, u32[]{:S(2)}) collective-permute-start(bf16[24,1536]{1,0:T(8,128)(2,1)S(1)} %fusion.13), channel_id=1, source_target_pairs={{0,3},{1,2},{2,1},{3,0},{4,7},{5,6},{6,5},{7,4},{8,11},{9,10},{10,... | collective-permute-start | bytes 221192 | tf_op jit(solution)/shard_map/ppermute | solution.py:14
  116.3 2.5 %collective-permute-done.10 = bf16[24,1536]{1,0:T(8,128)(2,1)S(1)} collective-permute-done((bf16[24,1536]{1,0:T(8,128)(2,1)S(1)}, bf16[24,1536]{1,0:T(8,128)(2,1)S(1)}, u32[]{:S(2)}, u32[]{:S(2)}) %collective-permute-start.10) | collective-permute-done | bytes 73760 | tf_op jit(solution)/shard_map/ppermute | solution.py:14
  119.7 3.8 %collective-permute-done.11 = bf16[24,1536]{1,0:T(8,128)(2,1)S(1)} collective-permute-done((bf16[24,1536]{1,0:T(8,128)(2,1)S(1)}, bf16[24,1536]{1,0:T(8,128)(2,1)S(1)}, u32[]{:S(2)}, u32[]{:S(2)}) %collective-permute-start.11) | collective-permute-done | bytes 73760 | tf_op jit(solution)/shard_map/ppermute | solution.py:14
  125.5 2.6 %fusion.1 = f32[24,1536]{1,0:T(8,128)} fusion(bf16[576,1536]{1,0:T(8,128)(2,1)S(1)} %copy-done, bf16[1536,576]{0,1:T(8,128)(2,1)S(1)} %copy-done.3, f32[24,576]{1,0:T(8,128)} %fusion.115, f32[24,1536]{1,0:T(8,128)} %copy-done.5, f32[1536]{0:T(1024)} %param.44, f32[24]{0:T(128)S(1)} %add_rsqrt_fusion), kind=kOutput, calls=%fused_computation.11 | convolution fusion | flops 85183488 | bytes 3895392 | tf_op jit(solution)/shard_map/dot_general | solution.py:320
  129.7 3.4 %collective-permute-done.12 = bf16[24,768]{1,0:T(8,128)(2,1)S(1)} collective-permute-done((bf16[24,768]{1,0:T(8,128)(2,1)S(1)}, bf16[24,768]{1,0:T(8,128)(2,1)S(1)}, u32[]{:S(2)}, u32[]{:S(2)}) %collective-permute-start.12) | collective-permute-done | bytes 36896 | tf_op jit(solution)/shard_map/ppermute | solution.py:14
  134.0 3.2 %collective-permute-start.13 = (bf16[24,384]{1,0:T(8,128)(2,1)S(1)}, bf16[24,384]{1,0:T(8,128)(2,1)S(1)}, u32[]{:S(2)}, u32[]{:S(2)}) collective-permute-start(bf16[24,384]{1,0:T(8,128)(2,1)S(1)} %select_convert_fusion.1), channel_id=1, source_target_pairs={{0,3},{1,2},{2,1},{3,0},{4,7},{5,6},{6,5},{7,4},{8,11},{9,10},{10,... | collective-permute-start | bytes 55304 | tf_op jit(solution)/shard_map/ppermute | solution.py:14
  139.8 3.0 %collective-permute-done.14 = bf16[24,192]{1,0:T(8,128)(2,1)S(1)} collective-permute-done((bf16[24,192]{1,0:T(8,128)(2,1)S(1)}, bf16[24,192]{1,0:T(8,128)(2,1)S(1)}, u32[]{:S(2)}, u32[]{:S(2)}) %collective-permute-start.14) | collective-permute-done | bytes 9248 | tf_op jit(solution)/shard_map/ppermute | solution.py:14
  (186 shorter events, 39.9 us)
Async XLA Ops:
  0.6 124.9 %copy-start = (bf16[576,1536]{1,0:T(8,128)(2,1)S(1)}, bf16[576,1536]{1,0:T(8,128)(2,1)}, u32[]{:S(2)}) copy-start(bf16[576,1536]{1,0:T(8,128)(2,1)} %param.47) | copy-start | bytes 5308420
  3.8 20.6 %all-to-all-start = ((bf16[32,4,256]{2,1,0:T(4,128)(2,1)}), bf16[32,4,256]{2,1,0:T(4,128)(2,1)S(1)}, u32[]{:S(2)}, u32[]{:S(2)}) async-start(bf16[32,4,256]{2,1,0:T(4,128)(2,1)} %gather_fusion), calls=%async_computation | async-start | bytes 131072 | tf_op jit(solution)/shard_map/all_to_all | solution.py:151
  16.0 28.0 %copy-start.30 = (f32[64]{0:T(128)}, f32[64]{0:T(128)S(1)}, u32[]{:S(2)}) copy-start(f32[64]{0:T(128)S(1)} %multiply_power_fusion) | copy-start | bytes 772
  24.5 60.3 %all-to-all-start.1 = ((bf16[32,128,256]{2,1,0:T(8,128)(2,1)}), bf16[32,128,256]{2,1,0:T(8,128)(2,1)}, u32[]{:S(2)}, u32[]{:S(2)}) async-start(bf16[32,128,256]{2,1,0:T(8,128)(2,1)} %gather_fusion.3), calls=%async_computation.1 | async-start | bytes 4194304 | tf_op jit(solution)/shard_map/all_to_all | solution.py:154
  34.3 21.3 %copy-start.26 = (f32[1536]{0:T(1024)S(1)}, f32[1536]{0:T(1024)}, u32[]{:S(2)}) copy-start(f32[1536]{0:T(1024)} %param.40) | copy-start | bytes 18436
  34.4 21.4 %copy-start.13 = (bf16[192,1536]{1,0:T(8,128)(2,1)S(1)}, bf16[192,1536]{1,0:T(8,128)(2,1)}, u32[]{:S(2)}) copy-start(bf16[192,1536]{1,0:T(8,128)(2,1)} %param.41) | copy-start | bytes 1769476
  36.4 4.4 %collective-permute-start = (bf16[24,1536]{1,0:T(8,128)(2,1)S(1)}, bf16[24,1536]{1,0:T(8,128)(2,1)S(1)}, u32[]{:S(2)}, u32[]{:S(2)}) collective-permute-start(bf16[24,1536]{1,0:T(8,128)(2,1)S(1)} %get-tuple-element.50), channel_id=1, source_target_pairs={{0,1},{1,0},{2,3},{3,2},{4,5},{5,4},{6,7},{7,6},{8,9},{9,8},{10,11... | collective-permute-start | bytes 221192 | tf_op jit(solution)/shard_map/ppermute | solution.py:14
  40.9 5.7 %collective-permute-start.1 = (bf16[24,1536]{1,0:T(8,128)(2,1)S(1)}, bf16[24,1536]{1,0:T(8,128)(2,1)S(1)}, u32[]{:S(2)}, u32[]{:S(2)}) collective-permute-start(bf16[24,1536]{1,0:T(8,128)(2,1)S(1)} %fusion.11), channel_id=1, source_target_pairs={{0,3},{1,2},{2,1},{3,0},{4,7},{5,6},{6,5},{7,4},{8,11},{9,10},{10,... | collective-permute-start | bytes 221192 | tf_op jit(solution)/shard_map/ppermute | solution.py:14
  46.6 8.9 %collective-permute-start.2 = (bf16[24,1536]{1,0:T(8,128)(2,1)S(1)}, bf16[24,1536]{1,0:T(8,128)(2,1)S(1)}, u32[]{:S(2)}, u32[]{:S(2)}) collective-permute-start(bf16[24,1536]{1,0:T(8,128)(2,1)S(1)} %fusion.27), channel_id=1, source_target_pairs={{0,4},{1,5},{2,6},{3,7},{4,0},{5,1},{6,2},{7,3},{8,12},{9,13},{10,... | collective-permute-start | bytes 221192 | tf_op jit(solution)/shard_map/ppermute | solution.py:14
  56.0 4.4 %collective-permute-start.3 = (bf16[24,1536]{1,0:T(8,128)(2,1)S(1)}, bf16[24,1536]{1,0:T(8,128)(2,1)S(1)}, u32[]{:S(2)}, u32[]{:S(2)}) collective-permute-start(bf16[24,1536]{1,0:T(8,128)(2,1)S(1)} %get-tuple-element.52), channel_id=1, source_target_pairs={{0,1},{1,0},{2,3},{3,2},{4,5},{5,4},{6,7},{7,6},{8,9},{9,8},{10,11... | collective-permute-start | bytes 221192 | tf_op jit(solution)/shard_map/ppermute | solution.py:14
  60.5 5.7 %collective-permute-start.4 = (bf16[24,1536]{1,0:T(8,128)(2,1)S(1)}, bf16[24,1536]{1,0:T(8,128)(2,1)S(1)}, u32[]{:S(2)}, u32[]{:S(2)}) collective-permute-start(bf16[24,1536]{1,0:T(8,128)(2,1)S(1)} %fusion.12), channel_id=1, source_target_pairs={{0,3},{1,2},{2,1},{3,0},{4,7},{5,6},{6,5},{7,4},{8,11},{9,10},{10,... | collective-permute-start | bytes 221192 | tf_op jit(solution)/shard_map/ppermute | solution.py:14
  66.2 6.7 %collective-permute-start.5 = (bf16[24,1536]{1,0:T(8,128)(2,1)S(1)}, bf16[24,1536]{1,0:T(8,128)(2,1)S(1)}, u32[]{:S(2)}, u32[]{:S(2)}) collective-permute-start(bf16[24,1536]{1,0:T(8,128)(2,1)S(1)} %fusion.28), channel_id=1, source_target_pairs={{0,4},{1,5},{2,6},{3,7},{4,0},{5,1},{6,2},{7,3},{8,12},{9,13},{10,... | collective-permute-start | bytes 221192 | tf_op jit(solution)/shard_map/ppermute | solution.py:14
  92.7 4.5 %collective-permute-start.6 = (f32[24,896]{1,0:T(8,128)S(1)}, f32[24,896]{1,0:T(8,128)S(1)}, u32[]{:S(2)}, u32[]{:S(2)}) collective-permute-start(f32[24,896]{1,0:T(8,128)S(1)} %maximum_maximum_fusion), channel_id=1, source_target_pairs={{0,4},{1,5},{2,6},{3,7},{4,0},{5,1},{6,2},{7,3},{8,12},{9,13},{10,... | collective-permute-start | bytes 258056 | tf_op jit(solution)/shard_map/ppermute | solution.py:14
  97.7 5.3 %collective-permute-start.7 = (f32[24,512]{1,0:T(8,128)S(1)}, f32[24,512]{1,0:T(8,128)S(1)}, u32[]{:S(2)}, u32[]{:S(2)}) collective-permute-start(f32[24,512]{1,0:T(8,128)S(1)} %pad_maximum_fusion.2), channel_id=1, source_target_pairs={{0,3},{1,2},{2,1},{3,0},{4,7},{5,6},{6,5},{7,4},{8,11},{9,10},{10,... | collective-permute-start | bytes 147464 | tf_op jit(solution)/shard_map/ppermute | solution.py:14
  100.9 22.5 %copy-start.7 = (f32[24,1536]{1,0:T(8,128)S(1)}, f32[24,1536]{1,0:T(8,128)}, u32[]{:S(2)}) copy-start(f32[24,1536]{1,0:T(8,128)} %copy-done.6) | copy-start | bytes 442372
  103.5 20.7 %copy-start.4 = (bf16[1536,576]{0,1:T(8,128)(2,1)S(1)}, bf16[1536,576]{0,1:T(8,128)(2,1)}, u32[]{:S(2)}) copy-start(bf16[1536,576]{0,1:T(8,128)(2,1)} %param.45) | copy-start | bytes 5308420
  103.5 20.7 %copy-start.24 = (f32[1536]{0:T(1024)S(1)}, f32[1536]{0:T(1024)}, u32[]{:S(2)}) copy-start(f32[1536]{0:T(1024)} %param.44) | copy-start | bytes 18436
  103.6 4.1 %collective-permute-start.8 = (f32[24,320]{1,0:T(8,128)S(1)}, f32[24,320]{1,0:T(8,128)S(1)}, u32[]{:S(2)}, u32[]{:S(2)}) collective-permute-start(f32[24,320]{1,0:T(8,128)S(1)} %pad_maximum_fusion.3), channel_id=1, source_target_pairs={{0,1},{1,0},{2,3},{3,2},{4,5},{5,4},{6,7},{7,6},{8,9},{9,8},{10,11... | collective-permute-start | bytes 92168 | tf_op jit(solution)/shard_map/ppermute | solution.py:14
  108.7 4.4 %collective-permute-start.9 = (bf16[24,1536]{1,0:T(8,128)(2,1)S(1)}, bf16[24,1536]{1,0:T(8,128)(2,1)S(1)}, u32[]{:S(2)}, u32[]{:S(2)}) collective-permute-start(bf16[24,1536]{1,0:T(8,128)(2,1)S(1)} %get-tuple-element.56), channel_id=1, source_target_pairs={{0,1},{1,0},{2,3},{3,2},{4,5},{5,4},{6,7},{7,6},{8,9},{9,8},{10,11... | collective-permute-start | bytes 221192 | tf_op jit(solution)/shard_map/ppermute | solution.py:14
  113.1 5.7 %collective-permute-start.10 = (bf16[24,1536]{1,0:T(8,128)(2,1)S(1)}, bf16[24,1536]{1,0:T(8,128)(2,1)S(1)}, u32[]{:S(2)}, u32[]{:S(2)}) collective-permute-start(bf16[24,1536]{1,0:T(8,128)(2,1)S(1)} %fusion.13), channel_id=1, source_target_pairs={{0,3},{1,2},{2,1},{3,0},{4,7},{5,6},{6,5},{7,4},{8,11},{9,10},{10,... | collective-permute-start | bytes 221192 | tf_op jit(solution)/shard_map/ppermute | solution.py:14
  118.8 4.6 %collective-permute-start.11 = (bf16[24,1536]{1,0:T(8,128)(2,1)S(1)}, bf16[24,1536]{1,0:T(8,128)(2,1)S(1)}, u32[]{:S(2)}, u32[]{:S(2)}) collective-permute-start(bf16[24,1536]{1,0:T(8,128)(2,1)S(1)} %fusion.29), channel_id=1, source_target_pairs={{0,4},{1,5},{2,6},{3,7},{4,0},{5,1},{6,2},{7,3},{8,12},{9,13},{10,... | collective-permute-start | bytes 221192 | tf_op jit(solution)/shard_map/ppermute | solution.py:14
  129.0 4.0 %collective-permute-start.12 = (bf16[24,768]{1,0:T(8,128)(2,1)S(1)}, bf16[24,768]{1,0:T(8,128)(2,1)S(1)}, u32[]{:S(2)}, u32[]{:S(2)}) collective-permute-start(bf16[24,768]{1,0:T(8,128)(2,1)S(1)} %select_convert_fusion), channel_id=1, source_target_pairs={{0,4},{1,5},{2,6},{3,7},{4,0},{5,1},{6,2},{7,3},{8,12},{9,13},{10,... | collective-permute-start | bytes 110600 | tf_op jit(solution)/shard_map/ppermute | solution.py:14
  134.0 5.1 %collective-permute-start.13 = (bf16[24,384]{1,0:T(8,128)(2,1)S(1)}, bf16[24,384]{1,0:T(8,128)(2,1)S(1)}, u32[]{:S(2)}, u32[]{:S(2)}) collective-permute-start(bf16[24,384]{1,0:T(8,128)(2,1)S(1)} %select_convert_fusion.1), channel_id=1, source_target_pairs={{0,3},{1,2},{2,1},{3,0},{4,7},{5,6},{6,5},{7,4},{8,11},{9,10},{10,... | collective-permute-start | bytes 55304 | tf_op jit(solution)/shard_map/ppermute | solution.py:14
  139.1 3.7 %collective-permute-start.14 = (bf16[24,192]{1,0:T(8,128)(2,1)S(1)}, bf16[24,192]{1,0:T(8,128)(2,1)S(1)}, u32[]{:S(2)}, u32[]{:S(2)}) collective-permute-start(bf16[24,192]{1,0:T(8,128)(2,1)S(1)} %select_convert_fusion.2), channel_id=1, source_target_pairs={{0,1},{1,0},{2,3},{3,2},{4,5},{5,4},{6,7},{7,6},{8,9},{9,8},{10,11... | collective-permute-start | bytes 27656 | tf_op jit(solution)/shard_map/ppermute | solution.py:14
  (27 other events, 286.0 us)
